TPU v7x, 128 devices: a whole 4x4x4 slice. The times are simulated.
128 devices in a mesh: dp: 4 (over x_lo, core), expert: 32 (over z, x_hi, y).
Axes of the slice: x: 4 (x_hi: 2, x_lo: 2; x = x_hi * 2 + x_lo), y: 4, z: 4, core: 2. Of those that a mesh axis runs over, the one named last changes fastest.
Arguments:
- tokens_in: bfloat16 [16384, 2048], P(('dp', 'expert')), may hold values from -6 to 6
- out_grad: bfloat16 [16384, 2048], P(('dp', 'expert')), may hold values from -6 to 6
- gate_logits: float32 [16384, 8], P(('dp', 'expert')), may hold values from -6 to 6
- route_ids: int32 [16384, 8], P(('dp', 'expert')), may hold values from 0 to 63, all different within a row; in each aligned block of 128 rows (0 to 127, 128 to 255, ...) at most 18 rows name the same one
- w_gate: bfloat16 [2048, 64, 768], P(None, 'expert'), may hold values from -0.125 to 0.125
- w_up: bfloat16 [2048, 64, 768], P(None, 'expert'), may hold values from -0.125 to 0.125
- w_down: bfloat16 [2048, 64, 768], P(None, 'expert'), may hold values from -0.21875 to 0.21875
Outputs:
- input_grad: bfloat16 [16384, 2048], P(('dp', 'expert'))
- router_grad: float32 [16384, 8], P(('dp', 'expert'))
- weight_grads: bfloat16 [2048, 3, 64, 768], P('dp', None, 'expert')
Inputs may be any that keep to these rules, and one draw needn't show every extreme that they name: `route_ids`: the 8 experts of a token differ. In each aligned block of 128 rows (the rows of one device) no expert is named by more than 18 rows, a bound that some block reaches.
All inputs are finite; a program needn't handle non-finite values.
Results may differ from a plain program's by a relative error of at most 0.015.
Values may be sent and summed in bfloat16 or wider, within the bound.
No kernel may reach another device: no remote copies, remote signals or barrier semaphores. Data moves between devices by JAX's collectives and lax.ppermute only.
A program may use at most 192 MiB of HBM per device.

v0:
```python
import jax
import jax.numpy as jnp
from jax import lax
from jax.sharding import PartitionSpec as P


def combine_weights(gate_logits):
    raised = jnp.exp(gate_logits)
    return raised / jnp.sum(raised, axis=1, keepdims=True)


def rounded(term):
    return lax.optimization_barrier(term.astype(jnp.bfloat16)).astype(jnp.float32)


def per_device(tokens_in, out_grad, gate_logits, route_ids, w_gate, w_up, w_down):
    tok_rows, model_width = tokens_in.shape
    topk_count = route_ids.shape[1]
    local_experts = w_gate.shape[1]
    owners = lax.axis_size("expert")
    expert_count = local_experts * owners
    capacity = 9 * tok_rows * topk_count // (8 * expert_count)
    pair_count = tok_rows * topk_count
    slot_count = expert_count * capacity
    weights = combine_weights(gate_logits)
    scaled = (weights[:, :, None] * out_grad[:, None, :].astype(jnp.float32)).astype(jnp.bfloat16)
    flat_ids = route_ids.reshape(-1)
    onehot = (flat_ids[:, None] == jnp.arange(expert_count, dtype=jnp.int32)[None, :]).astype(
        jnp.int32
    )
    before = jnp.cumsum(onehot, axis=0) - onehot
    slot_rank = jnp.sum(before * onehot, axis=1)
    slot_of_pair = flat_ids * capacity + slot_rank
    pair_of_slot = (
        jnp.full((slot_count,), pair_count, jnp.int32)
        .at[slot_of_pair]
        .set(jnp.arange(pair_count, dtype=jnp.int32))
    )
    zero_row = jnp.zeros((1, model_width), jnp.bfloat16)
    token_table = jnp.concatenate([tokens_in, zero_row], axis=0)
    scaled_table = jnp.concatenate([scaled.reshape(pair_count, model_width), zero_row], axis=0)
    send_shape = (owners, local_experts * capacity, model_width)
    send_tokens = jnp.take(token_table, pair_of_slot // topk_count, axis=0).reshape(send_shape)
    send_scaled = jnp.take(scaled_table, pair_of_slot, axis=0).reshape(send_shape)
    recv_tokens, recv_scaled = (
        lax.all_to_all(send_tokens, "expert", split_axis=0, concat_axis=0, tiled=True),
        lax.all_to_all(send_scaled, "expert", split_axis=0, concat_axis=0, tiled=True),
    )
    block_shape = (owners, local_experts, capacity, model_width)
    recv_tokens = recv_tokens.reshape(block_shape)
    recv_scaled = recv_scaled.reshape(block_shape)
    gate_pre = jnp.einsum("nemd,deh->nemh", recv_tokens, w_gate, preferred_element_type=jnp.float32)
    up_pre = jnp.einsum("nemd,deh->nemh", recv_tokens, w_up, preferred_element_type=jnp.float32)
    sigmoid_gate = jax.nn.sigmoid(gate_pre)
    active = gate_pre * sigmoid_gate
    hidden = (active * up_pre).astype(jnp.bfloat16)
    hidden_grad = jnp.einsum(
        "nemd,deh->nemh", recv_scaled, w_down, preferred_element_type=jnp.float32
    )
    prob_part = jnp.sum(hidden_grad * hidden.astype(jnp.float32), axis=3).astype(jnp.bfloat16)
    gate_grad = (
        hidden_grad * up_pre * sigmoid_gate * (1.0 + gate_pre * (1.0 - sigmoid_gate))
    ).astype(jnp.bfloat16)
    up_grad = (hidden_grad * active).astype(jnp.bfloat16)
    row_grad = (
        jnp.einsum("nemh,deh->nemd", gate_grad, w_gate, preferred_element_type=jnp.float32)
        + jnp.einsum("nemh,deh->nemd", up_grad, w_up, preferred_element_type=jnp.float32)
    ).astype(jnp.bfloat16)
    back_rows, back_probs = (
        lax.all_to_all(
            row_grad.reshape(send_shape), "expert", split_axis=0, concat_axis=0, tiled=True
        ),
        lax.all_to_all(
            prob_part.reshape(owners, local_experts * capacity),
            "expert",
            split_axis=0,
            concat_axis=0,
            tiled=True,
        ),
    )
    pair_rows = jnp.take(back_rows.reshape(slot_count, model_width), slot_of_pair, axis=0)
    input_grad = jnp.sum(
        pair_rows.reshape(tok_rows, topk_count, model_width).astype(jnp.float32), axis=1
    ).astype(jnp.bfloat16)
    pair_probs = (
        jnp.take(back_probs.reshape(slot_count), slot_of_pair, axis=0)
        .reshape(tok_rows, topk_count)
        .astype(jnp.float32)
    )
    router_grad = pair_probs - weights * jnp.sum(pair_probs, axis=1, keepdims=True)
    grad_gate = jnp.einsum(
        "nemd,nemh->deh", recv_tokens, gate_grad, preferred_element_type=jnp.float32
    )
    grad_up = jnp.einsum("nemd,nemh->deh", recv_tokens, up_grad, preferred_element_type=jnp.float32)
    grad_down = jnp.einsum(
        "nemd,nemh->deh", recv_scaled, hidden, preferred_element_type=jnp.float32
    )
    shares = lax.psum_scatter(
        rounded(jnp.stack([grad_gate, grad_up, grad_down], axis=1)).astype(jnp.bfloat16),
        "dp",
        scatter_dimension=0,
        tiled=True,
    )
    return (input_grad, router_grad, shares)


def solution(mesh):
    in_specs = (
        P(("dp", "expert"), None),
        P(("dp", "expert"), None),
        P(("dp", "expert"), None),
        P(("dp", "expert"), None),
        P(None, "expert", None),
        P(None, "expert", None),
        P(None, "expert", None),
    )
    out_specs = (
        P(("dp", "expert"), None),
        P(("dp", "expert"), None),
        P("dp", None, "expert", None),
    )
    return jax.shard_map(
        per_device, mesh=mesh, in_specs=in_specs, out_specs=out_specs, check_vma=False
    )
```

profile of v0, /device:TPU:0, one launch (start us, length us, event | category | flops | bytes accessed | tf_op | source)
XLA Modules:
  0.0 500.6 jit_solution(5124495065527904248)
XLA Ops:
  8.6 18.0 %reduce-window.6 = s32[64,8,128]{2,1,0:T(8,128)S(1)} reduce-window(s32[64,8,128]{2,1,0:T(8,128)S(1)} %fusion.30, s32[]{:T(128)} %constant.73.clone.1), window={size=1x1x128 pad=0_0x0_0x127_0}, to_apply=%region_0.0 | reduce-window | flops 8323072 | bytes 524292 | tf_op jit(solution)/shard_map/reduce-window
  33.3 5.9 %gather_fusion.1 = bf16[1152,2048]{1,0:T(8,128)(2,1)} fusion(bf16[129,2048]{1,0:T(8,128)(2,1)S(1)} %concatenate.7, s32[2048]{0:T(1024)S(1)} %pad_clamp_fusion), kind=kCustom, calls=%fused_computation.1 | custom fusion | bytes 9441792 | tf_op jit(solution)/shard_map/jit(_take)/gather | solution.py:43
  39.2 7.2 %gather.27 = bf16[32,36,2048]{2,1,0:T(8,128)(2,1)} reshape(bf16[1152,2048]{1,0:T(8,128)(2,1)} %gather_fusion.1) | data formatting | bytes 9437184 | tf_op jit(solution)/shard_map/jit(_take)/gather | solution.py:43
  51.9 11.1 %all-to-all-start.1 = ((bf16[32,36,2048]{2,1,0:T(8,128)(2,1)}), bf16[32,36,2048]{2,1,0:T(8,128)(2,1)}, u32[]{:S(2)}, u32[]{:S(2)}) async-start(bf16[32,36,2048]{2,1,0:T(8,128)(2,1)} %broadcast_select_fusion), calls=%async_computation.1 | async-start | bytes 10485760 | tf_op jit(solution)/shard_map/all_to_all | solution.py:46
  67.4 13.4 %gather_fusion = bf16[1152,2048]{1,0:T(8,128)(2,1)} fusion(bf16[1025,2048]{1,0:T(8,128)(2,1)} %concatenate.6, s32[2048]{0:T(1024)S(1)} %pad_clamp_fusion.1), kind=kCustom, calls=%fused_computation | custom fusion | bytes 9441792 | tf_op jit(solution)/shard_map/jit(_take)/gather | solution.py:44
  80.8 7.2 %gather.25 = bf16[32,36,2048]{2,1,0:T(8,128)(2,1)} reshape(bf16[1152,2048]{1,0:T(8,128)(2,1)} %gather_fusion) | data formatting | bytes 9437184 | tf_op jit(solution)/shard_map/jit(_take)/gather | solution.py:44
  93.5 40.9 %all-to-all-done.1 = bf16[32,36,2048]{2,1,0:T(8,128)(2,1)} async-done(((bf16[32,36,2048]{2,1,0:T(8,128)(2,1)}), bf16[32,36,2048]{2,1,0:T(8,128)(2,1)}, u32[]{:S(2)}, u32[]{:S(2)}) %all-to-all-start.1) | async-done | bytes 4718624 | tf_op jit(solution)/shard_map/all_to_all | solution.py:46
  134.4 6.5 %all-to-all-start = ((bf16[32,36,2048]{2,1,0:T(8,128)(2,1)}), bf16[32,36,2048]{2,1,0:T(8,128)(2,1)}, u32[]{:S(2)}, u32[]{:S(2)}) async-start(bf16[32,36,2048]{2,1,0:T(8,128)(2,1)} %broadcast_select_fusion.1), calls=%async_computation | async-start | bytes 10485760 | tf_op jit(solution)/shard_map/all_to_all | solution.py:47
  146.8 10.1 %fusion.12 = f32[2,32,18,768]{3,1,2,0:T(8,128)} fusion(bf16[32,2,18,2048]{3,0,2,1:T(8,128)(2,1)S(1)} %bitcast.121, bf16[2048,2,768,1]{2,1,0,3:T(2,128)(2,1)} %bitcast.140), kind=kOutput, calls=%fused_computation.23 | convolution fusion | flops 3623878656 | bytes 14548992 | tf_op jit(solution)/shard_map/nemd,deh->nemh/dot_general | solution.py:53
  156.9 5.6 %fusion.8 = f32[2,32,18,768]{3,1,2,0:T(8,128)} fusion(bf16[32,2,18,2048]{3,0,2,1:T(8,128)(2,1)S(1)} %bitcast.122, bf16[2048,2,768,1]{2,1,0,3:T(2,128)(2,1)S(1)} %bitcast.139), kind=kOutput, calls=%fused_computation.19 | convolution fusion | flops 3623878656 | bytes 14548992 | tf_op jit(solution)/shard_map/nemd,deh->nemh/dot_general | solution.py:52
  162.5 50.2 %all-to-all-done = bf16[32,36,2048]{2,1,0:T(8,128)(2,1)} async-done(((bf16[32,36,2048]{2,1,0:T(8,128)(2,1)}), bf16[32,36,2048]{2,1,0:T(8,128)(2,1)}, u32[]{:S(2)}, u32[]{:S(2)}) %all-to-all-start) | async-done | bytes 4718624 | tf_op jit(solution)/shard_map/all_to_all | solution.py:47
  218.0 10.4 %fusion.26 = (bf16[32,2,18]{0,2,1:T(8,128)(2,1)S(1)}, bf16[32,2,18,768]{3,0,2,1:T(8,128)(2,1)}, bf16[32,2,18,768]{3,0,2,1:T(8,128)(2,1)S(1)}, bf16[32,2,18,768]{3,0,2,1:T(8,128)(2,1)S(1)}) fusion(f32[2,32,18,768]{3,1,2,0:T(8,128)S(1)} %copy-done.14, f32[2,32,18,768]{3,1,2,0:T(8,128)} %fusion.8, bf16[32,2,18,2048]{3,0,2,1:T(8,128)(2,1)S(1)} %bitcast.127, ...), kind=kOutput, calls=%fused_computation.45 | convolution fusion | flops 3639802880 | bytes 23398656 | tf_op jit(solution)/shard_map/nemd,deh->nemh/dot_general | solution.py:57
  228.4 7.6 %fusion.3 = bf16[2048,1,2,768]{0,3,2,1:T(8,128)(2,1)S(1)} fusion(bf16[32,2,18,768]{3,0,2,1:T(8,128)(2,1)} %get-tuple-element.18, bf16[32,2,18,2048]{3,0,2,1:T(8,128)(2,1)S(1)} %bitcast.128), kind=kOutput, calls=%fused_computation.14 | convolution fusion | flops 3627024384 | bytes 12779520 | tf_op jit(solution)/shard_map/nemd,nemh->deh/dot_general | solution.py:95
  247.0 8.3 %pad_maximum_fusion = bf16[2048,3,2,768]{0,3,2,1:T(8,128)(2,1)} fusion(bf16[2048,1,2,768]{0,3,2,1:T(8,128)(2,1)S(1)} %fusion.3, bf16[2048,1,2,768]{0,3,2,1:T(8,128)(2,1)S(1)} %fusion.2, bf16[2048,1,2,768]{0,3,2,1:T(8,128)(2,1)S(1)} %fusion.1), kind=kLoop, calls=%fused_computation.5 | loop fusion | flops 18874368 | bytes 37748736 | tf_op jit(solution)/shard_map/stack | solution.py:99
  256.0 6.4 %all-to-all-start.3 = ((bf16[32,1,36]{2,1,0:T(2,128)(2,1)}), bf16[32,1,36]{2,1,0:T(2,128)(2,1)S(1)}, u32[]{:S(2)}, u32[]{:S(2)}) async-start(bf16[32,1,36]{2,1,0:T(2,128)(2,1)} %copy.67), calls=%async_computation.3 | async-start | bytes 32768 | tf_op jit(solution)/shard_map/all_to_all | solution.py:73
  262.4 10.9 %fusion.6 = f32[2,32,18,2048]{3,1,2,0:T(8,128)} fusion(bf16[32,2,18,768]{3,0,2,1:T(8,128)(2,1)} %copy-done.13, bf16[2048,2,768,1]{2,1,0,3:T(2,128)(2,1)} %bitcast.136), kind=kOutput, calls=%fused_computation.17 | convolution fusion | flops 3623878656 | bytes 17498112 | tf_op jit(solution)/shard_map/nemh,deh->nemd/dot_general | solution.py:66
  273.3 8.5 %add_convert_fusion = bf16[2,32,18,2048]{3,1,2,0:T(8,128)(2,1)S(1)} fusion(f32[2,32,18,2048]{3,1,2,0:T(8,128)} %fusion.6, bf16[32,2,18,768]{3,0,2,1:T(8,128)(2,1)S(1)} %get-tuple-element.22, bf16[2048,2,768,1]{2,1,0,3:T(2,128)(2,1)} %bitcast.141), kind=kOutput, calls=%fused_computation.9 | convolution fusion | flops 3628597248 | bytes 22216704 | tf_op jit(solution)/shard_map/nemh,deh->nemd/dot_general | solution.py:67
  286.8 10.3 %all-to-all-start.2 = ((bf16[32,36,2048]{2,1,0:T(8,128)(2,1)}), bf16[32,36,2048]{2,1,0:T(8,128)(2,1)}, u32[]{:S(2)}, u32[]{:S(2)}) async-start(bf16[32,36,2048]{2,1,0:T(8,128)(2,1)} %copy.66), calls=%async_computation.2 | async-start | bytes 10485760 | tf_op jit(solution)/shard_map/all_to_all | solution.py:70
  297.4 6.8 %gather_fusion.3 = bf16[1024]{0:T(1024)(128)(2,1)S(1)} fusion(bf16[1152]{0:T(1024)(128)(2,1)S(1)} %reshape.141, s32[1024]{0:T(1024)S(1)} %broadcast_clamp_fusion), kind=kCustom, calls=%fused_computation.3 | custom fusion | bytes 8192 | tf_op jit(solution)/shard_map/jit(_take)/gather | solution.py:86
  305.2 111.9 %all-to-all-done.2 = bf16[32,36,2048]{2,1,0:T(8,128)(2,1)} async-done(((bf16[32,36,2048]{2,1,0:T(8,128)(2,1)}), bf16[32,36,2048]{2,1,0:T(8,128)(2,1)}, u32[]{:S(2)}, u32[]{:S(2)}) %all-to-all-start.2) | async-done | bytes 4718624 | tf_op jit(solution)/shard_map/all_to_all | solution.py:70
  417.1 7.2 %reshape.140 = bf16[1152,2048]{1,0:T(8,128)(2,1)} reshape(bf16[32,36,2048]{2,1,0:T(8,128)(2,1)} %all-to-all-done.2) | data formatting | bytes 9437184 | tf_op jit(solution)/shard_map/reshape | solution.py:81
  424.3 11.9 %gather_fusion.2 = bf16[1024,2048]{1,0:T(8,128)(2,1)} fusion(bf16[1152,2048]{1,0:T(8,128)(2,1)} %reshape.140, s32[1024]{0:T(1024)S(1)} %broadcast_clamp_fusion), kind=kCustom, calls=%fused_computation.2 | custom fusion | bytes 8392704 | tf_op jit(solution)/shard_map/jit(_take)/gather | solution.py:81
  441.5 39.6 %reduce-scatter.2.cloned.1.call-done = bf16[512,3,2,768]{0,3,2,1:T(8,128)(2,1)} async-done(((bf16[2048,3,2,768]{0,3,2,1:T(8,128)(2,1)}), bf16[512,3,2,768]{0,3,2,1:T(8,128)(2,1)}) %reduce-scatter.2.cloned.1.call-update) | async-done | bytes 4718608 | tf_op jit(solution)/shard_map/reduce_scatter | solution.py:98
  481.1 12.4 %copy.69 = bf16[512,3,2,768]{3,2,1,0:T(2,128)(2,1)} copy(bf16[512,3,2,768]{0,3,2,1:T(8,128)(2,1)} %reduce-scatter.2.cloned.1.call-done) | data formatting | bytes 9437184
  (91 shorter events, 57.5 us)
Async XLA Ops:
  8.0 0.6 copy-start.1
  27.2 0.6 copy-start.6
  27.3 4.9 copy-start.8
  51.9 11.1 %copy-start.5 = (bf16[128,2048]{1,0:T(8,128)(2,1)S(1)}, bf16[128,2048]{1,0:T(8,128)(2,1)}, u32[]{:S(2)}) copy-start(bf16[128,2048]{1,0:T(8,128)(2,1)} %param.8) | copy-start | bytes 1572868
  51.9 11.3 %copy-start.12 = (f32[128,8]{0,1:T(8,128)S(1)}, f32[128,8]{0,1:T(8,128)}, u32[]{:S(2)}) copy-start(f32[128,8]{0,1:T(8,128)} %param.9) | copy-start | bytes 12292
  51.9 82.5 %all-to-all-start.1 = ((bf16[32,36,2048]{2,1,0:T(8,128)(2,1)}), bf16[32,36,2048]{2,1,0:T(8,128)(2,1)}, u32[]{:S(2)}, u32[]{:S(2)}) async-start(bf16[32,36,2048]{2,1,0:T(8,128)(2,1)} %broadcast_select_fusion), calls=%async_computation.1 | async-start | bytes 10485760 | tf_op jit(solution)/shard_map/all_to_all | solution.py:46
  63.2 4.1 copy-start.3
  63.3 0.5 copy-start.10
  134.4 78.4 %all-to-all-start = ((bf16[32,36,2048]{2,1,0:T(8,128)(2,1)}), bf16[32,36,2048]{2,1,0:T(8,128)(2,1)}, u32[]{:S(2)}, u32[]{:S(2)}) async-start(bf16[32,36,2048]{2,1,0:T(8,128)(2,1)} %broadcast_select_fusion.1), calls=%async_computation | async-start | bytes 10485760 | tf_op jit(solution)/shard_map/all_to_all | solution.py:47
  140.9 340.2 %reduce-scatter.2.cloned.1.call-start = ((), (), s32[]{:S(2)}) async-start(), calls=%async_computation.5 | async-start | bytes 23592960 | tf_op jit(solution)/shard_map/reduce_scatter | solution.py:98
  141.5 15.4 %slice-start.2 = ((s8[6291456]{0:T(1024)(128)(4,1)}), s8[4194304]{0:T(1024)(128)(4,1)S(1)}, s32[]{:S(2)}) async-start(s8[6291456]{0:T(1024)(128)(4,1)} %bitcast.137), calls=%async_computation.8 | async-start | bytes 8388608
  146.7 10.2 %copy-start = (bf16[32,36,2048]{2,0,1:T(8,128)(2,1)}, bf16[32,36,2048]{2,0,1:T(8,128)(2,1)S(1)}, u32[]{:S(2)}) copy-start(bf16[32,36,2048]{2,0,1:T(8,128)(2,1)S(1)} %copy.61) | copy-start | bytes 14155780
  146.7 10.2 %slice-start.3 = ((s8[6291456]{0:T(1024)(128)(4,1)}), s8[2097152]{0:T(1024)(128)(4,1)S(1)}, s32[]{:S(2)}) async-start(s8[6291456]{0:T(1024)(128)(4,1)} %bitcast.137), calls=%async_computation.9 | async-start | bytes 4194304
  212.8 5.2 %copy-start.14 = (f32[2,32,18,768]{3,1,2,0:T(8,128)S(1)}, f32[2,32,18,768]{3,1,2,0:T(8,128)}, u32[]{:S(2)}) copy-start(f32[2,32,18,768]{3,1,2,0:T(8,128)} %fusion.12) | copy-start | bytes 10616836
  218.0 18.0 %slice-start = ((s8[4718592]{0:T(1024)(128)(4,1)}), s8[524288]{0:T(1024)(128)(4,1)S(1)}, s32[]{:S(2)}) async-start(s8[4718592]{0:T(1024)(128)(4,1)} %bitcast.123), calls=%async_computation.6 | async-start | bytes 1048576
  228.4 13.1 %copy-start.13 = (bf16[32,2,18,768]{3,0,2,1:T(8,128)(2,1)}, bf16[32,2,18,768]{3,0,2,1:T(8,128)(2,1)S(1)}, u32[]{:S(2)}) copy-start(bf16[32,2,18,768]{3,0,2,1:T(8,128)(2,1)S(1)} %get-tuple-element.21) | copy-start | bytes 5308420
  228.4 7.6 %slice-start.1 = ((s8[4718592]{0:T(1024)(128)(4,1)}), s8[4194304]{0:T(1024)(128)(4,1)S(1)}, s32[]{:S(2)}) async-start(s8[4718592]{0:T(1024)(128)(4,1)} %bitcast.123), calls=%async_computation.7 | async-start | bytes 8388608
  256.0 30.8 %all-to-all-start.3 = ((bf16[32,1,36]{2,1,0:T(2,128)(2,1)}), bf16[32,1,36]{2,1,0:T(2,128)(2,1)S(1)}, u32[]{:S(2)}, u32[]{:S(2)}) async-start(bf16[32,1,36]{2,1,0:T(2,128)(2,1)} %copy.67), calls=%async_computation.3 | async-start | bytes 32768 | tf_op jit(solution)/shard_map/all_to_all | solution.py:73
  286.7 10.3 %copy-start.7 = (s32[1024]{0:T(1024)S(1)}, s32[1024]{0:T(1024)}, u32[]{:S(2)}) copy-start(s32[1024]{0:T(1024)} %copy-done.6) | copy-start | bytes 12292
  286.7 10.4 %copy-start.9 = (s32[1024,1]{0,1:T(1,128)S(1)}, s32[1024,1]{0,1:T(1,128)}, u32[]{:S(2)}) copy-start(s32[1024,1]{0,1:T(1,128)} %copy-done.8) | copy-start | bytes 12292
  286.7 17.5 %copy-start.2 = (s32[128,8]{1,0:T(8,128)S(1)}, s32[128,8]{1,0:T(8,128)}, u32[]{:S(2)}) copy-start(s32[128,8]{1,0:T(8,128)} %copy-done.1) | copy-start | bytes 12292
  286.7 17.7 %copy-start.4 = (f32[128,8]{1,0:T(8,128)S(1)}, f32[128,8]{1,0:T(8,128)}, u32[]{:S(2)}) copy-start(f32[128,8]{1,0:T(8,128)} %copy-done.3) | copy-start | bytes 12292
  286.7 17.7 %copy-start.11 = (f32[128]{0:T(128)S(1)}, f32[128]{0:T(128)}, u32[]{:S(2)}) copy-start(f32[128]{0:T(128)} %copy-done.10) | copy-start | bytes 1540
  286.8 130.3 %all-to-all-start.2 = ((bf16[32,36,2048]{2,1,0:T(8,128)(2,1)}), bf16[32,36,2048]{2,1,0:T(8,128)(2,1)}, u32[]{:S(2)}, u32[]{:S(2)}) async-start(bf16[32,36,2048]{2,1,0:T(8,128)(2,1)} %copy.66), calls=%async_computation.2 | async-start | bytes 10485760 | tf_op jit(solution)/shard_map/all_to_all | solution.py:70
Sparse Core Ops, SparseCore 0:
  255.4 225.6 reduce-scatter.1
where the time goes:
time: 510 us; the launch traced here: 501 us
  waiting for transfers between devices  243 us (48%)
  local copies, waits for them, and re-layouts  100 us (20%)
  matrix products  64.1 us (13%)
  other arithmetic  44.2 us (9%)
  starting transfers between devices  34.9 us (7%)
  between operations  14.7 us (3%)
    all_to_all x1, waiting for transfers between devices, per_device(): lax.all_to_all(row_grad.reshape(send_shape), 'expert', split_axis=0, conc...  112 us
    all_to_all x1, waiting for transfers between devices, per_device(): lax.all_to_all(send_scaled, 'expert', split_axis=0, concat_axis=0, tiled=...  50.2 us
    all_to_all x1, waiting for transfers between devices, per_device(): lax.all_to_all(send_tokens, 'expert', split_axis=0, concat_axis=0, tiled=...  40.9 us
    reduce_scatter x1, waiting for transfers between devices, per_device(): lax.psum_scatter(rounded(jnp.stack([grad_gate, grad_up, grad_down], axis=...  39.6 us
    gather x2, local copies, waits for them, and re-layouts, per_device(): jnp.take(scaled_table, pair_of_slot, axis=0).reshape(send_shape)  20.6 us
    another operation x3, other arithmetic  18.2 us
    unnamed x42, local copies, waits for them, and re-layouts  15.4 us
    gather x2, local copies, waits for them, and re-layouts, per_device(): jnp.take(token_table, pair_of_slot // topk_count, axis=0)  13.1 us
  transfers between devices with their start and end apart: 5, of which 4 were waited for; matrix products, arithmetic and copies ran while one was open for 22% of the time, Pallas kernels for 0%

commit v1 on v0

v1 whole, which is shorter than its diff:
```python
import jax
import jax.numpy as jnp
from jax import lax
from jax.sharding import Mesh
from jax.sharding import PartitionSpec as P


def combine_weights(gate_logits):
    raised = jnp.exp(gate_logits)
    return raised / jnp.sum(raised, axis=1, keepdims=True)


def per_device(tokens_in, out_grad, gate_logits, route_ids, w_gate, w_up, w_down):
    tok_rows, model_width = tokens_in.shape
    topk_count = route_ids.shape[1]
    local_experts = w_gate.shape[1]
    hidden_width = w_gate.shape[2]
    xlo_count = lax.axis_size("xlo")
    core_count = lax.axis_size("core")
    expert_devs = lax.axis_size("expert")
    assert local_experts == xlo_count
    expert_count = local_experts * expert_devs
    dest_count = xlo_count * expert_devs
    capacity = 9 * tok_rows * topk_count // (8 * expert_count)
    pair_count = tok_rows * topk_count
    slot_count = dest_count * capacity
    xlo = lax.axis_index("xlo")
    core = lax.axis_index("core")

    weights = combine_weights(gate_logits)
    flat_ids = route_ids.reshape(-1)
    flat_weights = weights.reshape(-1)

    onehot = (flat_ids[:, None] == jnp.arange(expert_count, dtype=jnp.int32)[None, :]).astype(
        jnp.bfloat16
    )
    pos = jnp.arange(pair_count, dtype=jnp.int32)
    earlier = (pos[None, :] < pos[:, None]).astype(jnp.bfloat16)
    before = jnp.dot(earlier, onehot, preferred_element_type=jnp.float32)
    slot_rank = jnp.sum(before * onehot.astype(jnp.float32), axis=1).astype(jnp.int32)
    dest = (flat_ids % local_experts) * expert_devs + flat_ids // local_experts
    slot_of_pair = dest * capacity + slot_rank

    slot_ids = jnp.arange(slot_count, dtype=jnp.int32)
    pair_hit = slot_of_pair[None, :] == slot_ids[:, None]
    token_hit = jnp.any(pair_hit.reshape(slot_count, tok_rows, topk_count), axis=2)
    dispatch = token_hit.astype(jnp.bfloat16)
    slot_weight = jnp.sum(jnp.where(pair_hit, flat_weights[None, :], 0.0), axis=1)

    send_tokens = jnp.dot(dispatch, tokens_in, preferred_element_type=jnp.float32).astype(
        jnp.bfloat16
    )
    send_grads = jnp.dot(dispatch, out_grad, preferred_element_type=jnp.float32)
    send_scaled = (slot_weight[:, None] * send_grads).astype(jnp.bfloat16)
    send = jnp.concatenate([send_tokens, send_scaled], axis=1).reshape(
        dest_count, capacity, 2 * model_width
    )
    recv = lax.all_to_all(send, ("xlo", "expert"), split_axis=0, concat_axis=0, tiled=True)
    recv = recv.reshape(slot_count, 2 * model_width)
    rows_in = recv[:, :model_width]
    rows_scaled = recv[:, model_width:]

    wg = lax.dynamic_index_in_dim(w_gate, xlo, axis=1, keepdims=False)
    wu = lax.dynamic_index_in_dim(w_up, xlo, axis=1, keepdims=False)
    wd = lax.dynamic_index_in_dim(w_down, xlo, axis=1, keepdims=False)

    gate_pre = jnp.dot(rows_in, wg, preferred_element_type=jnp.float32)
    up_pre = jnp.dot(rows_in, wu, preferred_element_type=jnp.float32)
    sigmoid_gate = jax.nn.sigmoid(gate_pre)
    active = gate_pre * sigmoid_gate
    hidden = (active * up_pre).astype(jnp.bfloat16)
    hidden_grad = jnp.dot(rows_scaled, wd, preferred_element_type=jnp.float32)
    prob_part = jnp.sum(hidden_grad * hidden.astype(jnp.float32), axis=1).astype(jnp.bfloat16)
    gate_grad = (
        hidden_grad * up_pre * sigmoid_gate * (1.0 + gate_pre * (1.0 - sigmoid_gate))
    ).astype(jnp.bfloat16)
    up_grad = (hidden_grad * active).astype(jnp.bfloat16)
    row_grad = (
        jnp.dot(gate_grad, wg.T, preferred_element_type=jnp.float32)
        + jnp.dot(up_grad, wu.T, preferred_element_type=jnp.float32)
    ).astype(jnp.bfloat16)

    back_rows = lax.all_to_all(
        row_grad.reshape(dest_count, capacity, model_width),
        ("xlo", "expert"),
        split_axis=0,
        concat_axis=0,
        tiled=True,
    ).reshape(slot_count, model_width)
    back_probs = lax.all_to_all(
        prob_part.reshape(dest_count, capacity),
        ("xlo", "expert"),
        split_axis=0,
        concat_axis=0,
        tiled=True,
    ).reshape(slot_count)

    input_grad = lax.dot_general(
        dispatch, back_rows, (((0,), (0,)), ((), ())), preferred_element_type=jnp.float32
    ).astype(jnp.bfloat16)
    pair_probs = jnp.sum(
        jnp.where(pair_hit, back_probs.astype(jnp.float32)[:, None], 0.0), axis=0
    ).reshape(tok_rows, topk_count)
    router_grad = pair_probs - weights * jnp.sum(pair_probs, axis=1, keepdims=True)

    contract = (((0,), (0,)), ((), ()))
    grad_gate = lax.dot_general(rows_in, gate_grad, contract, preferred_element_type=jnp.float32)
    grad_up = lax.dot_general(rows_in, up_grad, contract, preferred_element_type=jnp.float32)
    grad_down = lax.dot_general(rows_scaled, hidden, contract, preferred_element_type=jnp.float32)
    block_rows = model_width // (xlo_count * core_count)
    grads = jnp.stack([grad_gate, grad_up, grad_down], axis=1).astype(jnp.bfloat16)
    grads = grads.reshape(xlo_count, core_count, block_rows, 3, hidden_width)

    core_pairs = [(i, (i + 1) % core_count) for i in range(core_count)]
    sibling = lax.dynamic_index_in_dim(grads, 1 - core, axis=1, keepdims=False)
    own = lax.dynamic_index_in_dim(grads, core, axis=1, keepdims=False)
    summed = (
        own.astype(jnp.float32) + lax.ppermute(sibling, "core", core_pairs).astype(jnp.float32)
    ).astype(jnp.bfloat16)

    xlo_pairs = [(i, (i + 1) % xlo_count) for i in range(xlo_count)]
    mine = lax.dynamic_index_in_dim(summed, xlo, axis=0, keepdims=False)
    theirs = lax.ppermute(
        lax.dynamic_index_in_dim(summed, 1 - xlo, axis=0, keepdims=False), "xlo", xlo_pairs
    )
    shares = jnp.where(
        xlo == 0, jnp.stack([mine, theirs], axis=2), jnp.stack([theirs, mine], axis=2)
    )
    return (input_grad, router_grad, shares)


def solution(mesh):
    dp_count, expert_devs = mesh.devices.shape
    core_count = 2
    split_mesh = Mesh(
        mesh.devices.reshape(dp_count // core_count, core_count, expert_devs),
        ("xlo", "core", "expert"),
    )
    rows = ("xlo", "core", "expert")
    in_specs = (
        P(rows, None),
        P(rows, None),
        P(rows, None),
        P(rows, None),
        P(None, "expert", None),
        P(None, "expert", None),
        P(None, "expert", None),
    )
    out_specs = (
        P(rows, None),
        P(rows, None),
        P(("xlo", "core"), None, "expert", None),
    )
    return jax.shard_map(
        per_device, mesh=split_mesh, in_specs=in_specs, out_specs=out_specs, check_vma=False
    )
```

time: 510 us -> 556 us (1.090)
  the two profiles are of different devices: /device:TPU:0 before, /device:TPU:36 now
where the time goes in v1:
time: 556 us; the launch traced here: 546 us
  waiting for transfers between devices  331 us (60%)
  local copies, waits for them, and re-layouts  92.4 us (17%)
  matrix products  62.6 us (11%)
  starting transfers between devices  32 us (6%)
  other arithmetic  26.3 us (5%)
    all_to_all x1, waiting for transfers between devices, per_device(): lax.all_to_all(send, ('xlo', 'expert'), split_axis=0, concat_axis=0, tile...  210 us
    all_to_all x1, waiting for transfers between devices, per_device(): lax.all_to_all(row_grad.reshape(dest_count, capacity, model_width), ('xlo...  84.4 us
    ppermute x1, waiting for transfers between devices, per_device(): lax.ppermute(lax.dynamic_index_in_dim(summed, 1 - xlo, axis=0, keepdims=F...  37.3 us
    dynamic_slice x1, local copies, waits for them, and re-layouts, per_device(): wg = lax.dynamic_index_in_dim(w_gate, xlo, axis=1, keepdims=False)  15.6 us
    unnamed x35, local copies, waits for them, and re-layouts  15.2 us
    reshape x1, local copies, waits for them, and re-layouts, per_device(): recv = recv.reshape(slot_count, 2 * model_width)  14.1 us
    reshape x1, local copies, waits for them, and re-layouts, per_device(): jnp.concatenate([send_tokens, send_scaled], axis=1)  13.9 us
    all_to_all x1, starting transfers between devices, per_device(): lax.all_to_all(send, ('xlo', 'expert'), split_axis=0, concat_axis=0, tile...  11.5 us
  transfers between devices with their start and end apart: 5, of which 3 were waited for; matrix products, arithmetic and copies ran while one was open for 12% of the time, Pallas kernels for 0%

profile of v1, /device:TPU:36, one launch (start us, length us, event | category | flops | bytes accessed | tf_op | source)
XLA Modules:
  0.0 546.2 jit_solution(8657567422653006562)
XLA Ops:
  16.5 13.9 %reshape.130 = bf16[64,18,4096]{2,1,0:T(8,128)(2,1)} reshape(bf16[1152,4096]{1,0:T(8,128)(2,1)} %pad_maximum_fusion) | data formatting | bytes 18874368 | tf_op jit(solution)/shard_map/reshape | solution.py:55
  30.5 11.5 %all-to-all-start = ((bf16[64,18,4096]{2,1,0:T(8,128)(2,1)}), bf16[64,18,4096]{2,1,0:T(8,128)(2,1)}, u32[]{:S(2)}, u32[]{:S(2)}) async-start(bf16[64,18,4096]{2,1,0:T(8,128)(2,1)} %reshape.130), calls=%async_computation | async-start | bytes 25165824 | tf_op jit(solution)/shard_map/all_to_all | solution.py:58
  42.0 8.6 %constant_dynamic-slice_fusion.4 = bf16[2048,1,768]{2,1,0:T(2,128)(2,1)} fusion(bf16[2048,2,768]{2,1,0:T(2,128)(2,1)} %param.13, s32[]{:T(128)S(6)} %select_n.65), kind=kLoop, calls=%fused_computation.85 | loop fusion | bytes 6291460 | tf_op jit(solution)/shard_map/jit(dynamic_index_in_dim)/dynamic_slice | solution.py:65
  50.6 15.6 %constant_dynamic-slice_fusion.2 = (bf16[2048,1,768]{2,1,0:T(2,128)(2,1)}, bf16[2048,1,768]{2,1,0:T(2,128)(2,1)}) fusion(bf16[2048,2,768]{2,1,0:T(2,128)(2,1)} %param.11, s32[]{:T(128)S(6)} %select_n.65, bf16[2048,2,768]{2,1,0:T(2,128)(2,1)} %param.12), kind=kLoop, calls=%fused_computation.83 | loop fusion | bytes 12582916 | tf_op jit(solution)/shard_map/jit(dynamic_index_in_dim)/dynamic_slice | solution.py:63
  66.2 209.6 %all-to-all-done = bf16[64,18,4096]{2,1,0:T(8,128)(2,1)} async-done(((bf16[64,18,4096]{2,1,0:T(8,128)(2,1)}), bf16[64,18,4096]{2,1,0:T(8,128)(2,1)}, u32[]{:S(2)}, u32[]{:S(2)}) %all-to-all-start) | async-done | bytes 9437216 | tf_op jit(solution)/shard_map/all_to_all | solution.py:58
  275.8 14.1 %reshape.131 = bf16[1152,4096]{1,0:T(8,128)(2,1)} reshape(bf16[64,18,4096]{2,1,0:T(8,128)(2,1)} %all-to-all-done) | data formatting | bytes 18874368 | tf_op jit(solution)/shard_map/reshape | solution.py:59
  290.0 8.0 %fusion.14 = f32[1152,768]{0,1:T(8,128)S(1)} fusion(bf16[1152,4096]{1,0:T(8,128)(2,1)} %reshape.131, bf16[2048,1,768]{2,1,0:T(2,128)(2,1)} %get-tuple-element.23), kind=kOutput, calls=%fused_computation.36 | convolution fusion | flops 3623878656 | bytes 14548992 | tf_op jit(solution)/shard_map/dot_general | solution.py:67
  298.6 6.1 %fusion.16 = f32[1152,768]{0,1:T(8,128)} fusion(bf16[1152,4096]{1,0:T(8,128)(2,1)S(1)} %copy-done.2, bf16[2048,1,768]{2,1,0:T(2,128)(2,1)S(1)} %copy-done.3), kind=kOutput, calls=%fused_computation.38 | convolution fusion | flops 3623878656 | bytes 14548992 | tf_op jit(solution)/shard_map/dot_general | solution.py:68
  304.7 11.4 %multiply_reduce_fusion = (bf16[1152]{0:T(1024)(128)(2,1)S(1)}, bf16[1152,768]{0,1:T(8,128)(2,1)}, bf16[1152,768]{0,1:T(8,128)(2,1)}, bf16[1152,768]{0,1:T(8,128)(2,1)}) fusion(f32[1152,768]{0,1:T(8,128)} %fusion.16, f32[1152,768]{0,1:T(8,128)S(1)} %fusion.14, bf16[2048,1,768]{2,1,0:T(2,128)(2,1)} %constant_dynamic-slice_fusion.4, ...), kind=kOutput, calls=%fused_computation.22 | convolution fusion | flops 3639802880 | bytes 20252928 | tf_op jit(solution)/shard_map/dot_general | solution.py:72
  316.1 6.3 %convolution_convert_fusion.2 = bf16[2048,768]{1,0:T(8,128)(2,1)S(1)} fusion(bf16[1152,768]{0,1:T(8,128)(2,1)} %get-tuple-element.17, bf16[1152,4096]{1,0:T(8,128)(2,1)S(1)} %copy-done.2), kind=kOutput, calls=%fused_computation.30 | convolution fusion | flops 3625451520 | bytes 9633792 | tf_op jit(solution)/shard_map/dot_general | solution.py:107
  322.4 4.6 convolution_convert_fusion.1
  327.0 4.6 fusion.9
  336.1 6.5 %constant_dynamic-slice_fusion.1 = (bf16[2,1,512,3,768]{4,2,1,0,3:T(8,128)(2,1)}, bf16[2,1,512,3,768]{4,2,1,0,3:T(8,128)(2,1)S(1)}) fusion(bf16[2,2,512,3,768]{4,2,1,0,3:T(8,128)(2,1)} %pad_maximum_fusion.1, s32[]{:T(128)S(6)} %select_n.68, s32[]{:T(128)S(6)} %select_n.69), kind=kLoop, calls=%fused_computation.82 | loop fusion | bytes 18874376 | tf_op jit(solution)/shard_map/jit(dynamic_index_in_dim)/dynamic_slice | solution.py:116
  345.8 8.8 %all-to-all-start.2 = ((bf16[64,1,18]{2,1,0:T(2,128)(2,1)}), bf16[64,1,18]{2,1,0:T(2,128)(2,1)S(1)}, u32[]{:S(2)}, u32[]{:S(2)}) async-start(bf16[64,1,18]{2,1,0:T(2,128)(2,1)} %convert_element_type.103), calls=%async_computation.2 | async-start | bytes 65536 | tf_op jit(solution)/shard_map/all_to_all | solution.py:90
  354.6 6.9 %fusion.18 = f32[1152,2048]{1,0:T(8,128)S(1)} fusion(bf16[1152,768]{0,1:T(8,128)(2,1)} %get-tuple-element.17, bf16[2048,1,768]{2,1,0:T(2,128)(2,1)} %get-tuple-element.23), kind=kOutput, calls=%fused_computation.43 | convolution fusion | flops 3623878656 | bytes 14352384 | tf_op jit(solution)/shard_map/dot_general | solution.py:79
  361.5 7.4 %add_convert_fusion = bf16[1152,2048]{1,0:T(8,128)(2,1)} fusion(f32[1152,2048]{1,0:T(8,128)S(1)} %fusion.18, bf16[1152,768]{0,1:T(8,128)(2,1)} %get-tuple-element.20, bf16[2048,1,768]{2,1,0:T(2,128)(2,1)S(1)} %bitcast.41), kind=kOutput, calls=%fused_computation.5 | convolution fusion | flops 3628597248 | bytes 19070976 | tf_op jit(solution)/shard_map/dot_general | solution.py:80
  368.9 7.5 %reshape.132 = bf16[64,18,2048]{2,1,0:T(8,128)(2,1)} reshape(bf16[1152,2048]{1,0:T(8,128)(2,1)} %add_convert_fusion) | data formatting | bytes 9437184 | tf_op jit(solution)/shard_map/reshape | solution.py:84
  376.5 10.4 %all-to-all-start.1 = ((bf16[64,18,2048]{2,1,0:T(8,128)(2,1)}), bf16[64,18,2048]{2,1,0:T(8,128)(2,1)}, u32[]{:S(2)}, u32[]{:S(2)}) async-start(bf16[64,18,2048]{2,1,0:T(8,128)(2,1)} %reshape.132), calls=%async_computation.1 | async-start | bytes 12582912 | tf_op jit(solution)/shard_map/all_to_all | solution.py:83
  386.8 4.9 fusion
  396.6 84.4 %all-to-all-done.1 = bf16[64,18,2048]{2,1,0:T(8,128)(2,1)} async-done(((bf16[64,18,2048]{2,1,0:T(8,128)(2,1)}), bf16[64,18,2048]{2,1,0:T(8,128)(2,1)}, u32[]{:S(2)}, u32[]{:S(2)}) %all-to-all-start.1) | async-done | bytes 4718624 | tf_op jit(solution)/shard_map/all_to_all | solution.py:83
  481.0 8.0 %reshape.133 = bf16[1152,2048]{1,0:T(8,128)(2,1)} reshape(bf16[64,18,2048]{2,1,0:T(8,128)(2,1)} %all-to-all-done.1) | data formatting | bytes 9437184 | tf_op jit(solution)/shard_map/reshape | solution.py:89
  493.0 37.3 %collective-permute-done.1 = bf16[512,3,768]{2,0,1:T(8,128)(2,1)} collective-permute-done((bf16[512,3,768]{2,0,1:T(8,128)(2,1)}, bf16[512,3,768]{2,0,1:T(8,128)(2,1)}, u32[]{:S(2)}, u32[]{:S(2)}) %collective-permute-start.1) | collective-permute-done | bytes 2359328 | tf_op jit(solution)/shard_map/ppermute | solution.py:123
  530.2 6.0 %maximum_select_fusion = bf16[512,3,2,768]{3,0,2,1:T(8,128)(2,1)} fusion(bf16[512,3,1,768]{3,0,2,1:T(8,128)(2,1)} %bitcast.10, bf16[512,3,1,768]{3,0,2,1:T(8,128)(2,1)S(1)} %get-tuple-element.21, pred[]{:T(512)S(6)} %eq.50), kind=kLoop, calls=%fused_computation.8 | loop fusion | flops 7077888 | bytes 9437185 | tf_op jit(solution)/shard_map/jit(_where)/select_n | solution.py:126
  536.3 9.4 %copy.69 = bf16[512,3,2,768]{3,2,1,0:T(2,128)(2,1)} copy(bf16[512,3,2,768]{3,0,2,1:T(8,128)(2,1)} %maximum_select_fusion) | data formatting | bytes 9437184
  (64 shorter events, 33.0 us)
Async XLA Ops:
  0.6 8.8 %copy-start = (bf16[128,2048]{1,0:T(8,128)(2,1)S(1)}, bf16[128,2048]{1,0:T(8,128)(2,1)}, u32[]{:S(2)}) copy-start(bf16[128,2048]{1,0:T(8,128)(2,1)} %param.7) | copy-start | bytes 1572868
  2.2 8.6 %copy-start.7 = (s32[1024]{0:T(1024)}, s32[1024]{0:T(1024)S(1)}, u32[]{:S(2)}) copy-start(s32[1024]{0:T(1024)S(1)} %fusion.30) | copy-start | bytes 12292
  3.0 7.8 %copy-start.4 = (f32[128,8]{1,0:T(8,128)}, f32[128,8]{1,0:T(8,128)S(1)}, u32[]{:S(2)}) copy-start(f32[128,8]{1,0:T(8,128)S(1)} %copy.60) | copy-start | bytes 12292
  3.1 0.6 copy-start.9
  3.8 7.0 %copy-start.6 = (bf16[128,2048]{1,0:T(8,128)(2,1)S(1)}, bf16[128,2048]{1,0:T(8,128)(2,1)}, u32[]{:S(2)}) copy-start(bf16[128,2048]{1,0:T(8,128)(2,1)} %param.8) | copy-start | bytes 1572868
  30.5 245.4 %all-to-all-start = ((bf16[64,18,4096]{2,1,0:T(8,128)(2,1)}), bf16[64,18,4096]{2,1,0:T(8,128)(2,1)}, u32[]{:S(2)}, u32[]{:S(2)}) async-start(bf16[64,18,4096]{2,1,0:T(8,128)(2,1)} %reshape.130), calls=%async_computation | async-start | bytes 25165824 | tf_op jit(solution)/shard_map/all_to_all | solution.py:58
  289.9 8.0 %copy-start.2 = (bf16[1152,4096]{1,0:T(8,128)(2,1)S(1)}, bf16[1152,4096]{1,0:T(8,128)(2,1)}, u32[]{:S(2)}) copy-start(bf16[1152,4096]{1,0:T(8,128)(2,1)} %reshape.131) | copy-start | bytes 28311556
  289.9 8.7 %copy-start.3 = (bf16[2048,1,768]{2,1,0:T(2,128)(2,1)S(1)}, bf16[2048,1,768]{2,1,0:T(2,128)(2,1)}, u32[]{:S(2)}) copy-start(bf16[2048,1,768]{2,1,0:T(2,128)(2,1)} %get-tuple-element.24) | copy-start | bytes 9437188
  316.1 6.3 %copy-start.11 = (bf16[1152,768]{0,1:T(8,128)(2,1)S(1)}, bf16[1152,768]{0,1:T(8,128)(2,1)}, u32[]{:S(2)}) copy-start(bf16[1152,768]{0,1:T(8,128)(2,1)} %get-tuple-element.20) | copy-start | bytes 5308420
  322.4 4.6 copy-start.12
  342.6 18.9 %slice-start = ((s8[6291456]{0:T(1024)(128)(4,1)}), s8[2097152]{0:T(1024)(128)(4,1)S(1)}, s32[]{:S(2)}) async-start(s8[6291456]{0:T(1024)(128)(4,1)} %bitcast.40), calls=%async_computation.3 | async-start | bytes 4194304
  345.0 41.8 %collective-permute-start = (bf16[2,512,3,768]{3,1,2,0:T(8,128)(2,1)}, bf16[2,512,3,768]{3,1,2,0:T(8,128)(2,1)}, u32[]{:S(2)}, u32[]{:S(2)}) collective-permute-start(bf16[2,512,3,768]{3,1,2,0:T(8,128)(2,1)} %bitcast.39), channel_id=1, source_target_pairs={{0,32},{32,0},{1,33},{33,1},{2,34},{34,2},{3,35},{35,3},{4,36},{36... | collective-permute-start | bytes 14155784 | tf_op jit(solution)/shard_map/ppermute | solution.py:118
  345.8 30.7 %all-to-all-start.2 = ((bf16[64,1,18]{2,1,0:T(2,128)(2,1)}), bf16[64,1,18]{2,1,0:T(2,128)(2,1)S(1)}, u32[]{:S(2)}, u32[]{:S(2)}) async-start(bf16[64,1,18]{2,1,0:T(2,128)(2,1)} %convert_element_type.103), calls=%async_computation.2 | async-start | bytes 65536 | tf_op jit(solution)/shard_map/all_to_all | solution.py:90
  354.6 6.9 %slice-start.1 = ((s8[6291456]{0:T(1024)(128)(4,1)}), s8[4194304]{0:T(1024)(128)(4,1)S(1)}, s32[]{:S(2)}) async-start(s8[6291456]{0:T(1024)(128)(4,1)} %bitcast.40), calls=%async_computation.4 | async-start | bytes 8388608
  376.5 104.5 %all-to-all-start.1 = ((bf16[64,18,2048]{2,1,0:T(8,128)(2,1)}), bf16[64,18,2048]{2,1,0:T(8,128)(2,1)}, u32[]{:S(2)}, u32[]{:S(2)}) async-start(bf16[64,18,2048]{2,1,0:T(8,128)(2,1)} %reshape.132), calls=%async_computation.1 | async-start | bytes 12582912 | tf_op jit(solution)/shard_map/all_to_all | solution.py:83
  391.7 3.3 copy-start.8
  391.7 4.1 copy-start.5
  391.8 4.1 copy-start.10
  393.5 136.8 %collective-permute-start.1 = (bf16[512,3,768]{2,0,1:T(8,128)(2,1)}, bf16[512,3,768]{2,0,1:T(8,128)(2,1)}, u32[]{:S(2)}, u32[]{:S(2)}) collective-permute-start(bf16[512,3,768]{2,0,1:T(8,128)(2,1)} %get-tuple-element.22), channel_id=1, source_target_pairs={{0,64},{64,0},{1,65},{65,1},{2,66},{66,2},{3,67},{67,3},{4,68},{68... | collective-permute-start | bytes 7077896 | tf_op jit(solution)/shard_map/ppermute | solution.py:123
  530.2 15.4 %copy-start.1 = (bf16[128,2048]{1,0:T(8,128)(2,1)S(1)}, bf16[128,2048]{1,0:T(8,128)(2,1)}, u32[]{:S(2)}) copy-start(bf16[128,2048]{1,0:T(8,128)(2,1)} %param.7) | copy-start | bytes 1572868

commit v2 on v1

v2 whole, which is shorter than its diff:
```python
import jax
import jax.numpy as jnp
from jax import lax
from jax.sharding import Mesh
from jax.sharding import PartitionSpec as P


def combine_weights(gate_logits):
    raised = jnp.exp(gate_logits)
    return raised / jnp.sum(raised, axis=1, keepdims=True)


def per_device(tokens_in, out_grad, gate_logits, route_ids, w_gate, w_up, w_down):
    tok_rows, model_width = tokens_in.shape
    topk_count = route_ids.shape[1]
    local_experts = w_gate.shape[1]
    hidden_width = w_gate.shape[2]
    xlo_count = lax.axis_size("xlo")
    core_count = lax.axis_size("core")
    owners = lax.axis_size("expert")
    expert_count = local_experts * owners
    capacity = 9 * tok_rows * topk_count // (8 * expert_count)
    pair_count = tok_rows * topk_count
    slot_count = expert_count * capacity
    xlo = lax.axis_index("xlo")
    core = lax.axis_index("core")

    weights = combine_weights(gate_logits)
    flat_ids = route_ids.reshape(-1)
    flat_weights = weights.reshape(-1)

    onehot = (flat_ids[:, None] == jnp.arange(expert_count, dtype=jnp.int32)[None, :]).astype(
        jnp.bfloat16
    )
    pos = jnp.arange(pair_count, dtype=jnp.int32)
    earlier = (pos[None, :] < pos[:, None]).astype(jnp.bfloat16)
    before = jnp.dot(earlier, onehot, preferred_element_type=jnp.float32)
    slot_rank = jnp.sum(before * onehot.astype(jnp.float32), axis=1).astype(jnp.int32)
    slot_of_pair = flat_ids * capacity + slot_rank

    slot_ids = jnp.arange(slot_count, dtype=jnp.int32)
    pair_hit = slot_of_pair[None, :] == slot_ids[:, None]
    token_hit = jnp.any(pair_hit.reshape(slot_count, tok_rows, topk_count), axis=2)
    dispatch = token_hit.astype(jnp.bfloat16)
    slot_weight = jnp.sum(jnp.where(pair_hit, flat_weights[None, :], 0.0), axis=1)

    send_shape = (owners, local_experts * capacity, model_width)
    send_tokens = jnp.dot(dispatch, tokens_in, preferred_element_type=jnp.float32).astype(
        jnp.bfloat16
    )
    send_grads = jnp.dot(dispatch, out_grad, preferred_element_type=jnp.float32)
    send_scaled = (slot_weight[:, None] * send_grads).astype(jnp.bfloat16)
    recv_tokens = lax.all_to_all(
        send_tokens.reshape(send_shape), "expert", split_axis=0, concat_axis=0, tiled=True
    )
    recv_scaled = lax.all_to_all(
        send_scaled.reshape(send_shape), "expert", split_axis=0, concat_axis=0, tiled=True
    )
    block_shape = (owners, local_experts, capacity, model_width)
    recv_tokens = recv_tokens.reshape(block_shape)
    recv_scaled = recv_scaled.reshape(block_shape)

    gate_pre = jnp.einsum("nemd,deh->nemh", recv_tokens, w_gate, preferred_element_type=jnp.float32)
    up_pre = jnp.einsum("nemd,deh->nemh", recv_tokens, w_up, preferred_element_type=jnp.float32)
    sigmoid_gate = jax.nn.sigmoid(gate_pre)
    active = gate_pre * sigmoid_gate
    hidden = (active * up_pre).astype(jnp.bfloat16)
    hidden_grad = jnp.einsum(
        "nemd,deh->nemh", recv_scaled, w_down, preferred_element_type=jnp.float32
    )
    prob_part = jnp.sum(hidden_grad * hidden.astype(jnp.float32), axis=3).astype(jnp.bfloat16)
    gate_grad = (
        hidden_grad * up_pre * sigmoid_gate * (1.0 + gate_pre * (1.0 - sigmoid_gate))
    ).astype(jnp.bfloat16)
    up_grad = (hidden_grad * active).astype(jnp.bfloat16)
    row_grad = (
        jnp.einsum("nemh,deh->nemd", gate_grad, w_gate, preferred_element_type=jnp.float32)
        + jnp.einsum("nemh,deh->nemd", up_grad, w_up, preferred_element_type=jnp.float32)
    ).astype(jnp.bfloat16)
    back_rows = lax.all_to_all(
        row_grad.reshape(send_shape), "expert", split_axis=0, concat_axis=0, tiled=True
    ).reshape(slot_count, model_width)
    back_probs = lax.all_to_all(
        prob_part.reshape(owners, local_experts * capacity),
        "expert",
        split_axis=0,
        concat_axis=0,
        tiled=True,
    ).reshape(slot_count)

    input_grad = lax.dot_general(
        dispatch, back_rows, (((0,), (0,)), ((), ())), preferred_element_type=jnp.float32
    ).astype(jnp.bfloat16)
    pair_probs = jnp.sum(
        jnp.where(pair_hit, back_probs.astype(jnp.float32)[:, None], 0.0), axis=0
    ).reshape(tok_rows, topk_count)
    router_grad = pair_probs - weights * jnp.sum(pair_probs, axis=1, keepdims=True)

    grad_gate = jnp.einsum(
        "nemd,nemh->deh", recv_tokens, gate_grad, preferred_element_type=jnp.float32
    )
    grad_up = jnp.einsum("nemd,nemh->deh", recv_tokens, up_grad, preferred_element_type=jnp.float32)
    grad_down = jnp.einsum(
        "nemd,nemh->deh", recv_scaled, hidden, preferred_element_type=jnp.float32
    )
    block_rows = model_width // (xlo_count * core_count)
    grads = jnp.stack([grad_gate, grad_up, grad_down], axis=1).astype(jnp.bfloat16)
    grads = grads.reshape(xlo_count, core_count, block_rows, 3, local_experts, hidden_width)

    core_pairs = [(i, (i + 1) % core_count) for i in range(core_count)]
    sibling = lax.dynamic_index_in_dim(grads, 1 - core, axis=1, keepdims=False)
    own = lax.dynamic_index_in_dim(grads, core, axis=1, keepdims=False)
    summed = (
        own.astype(jnp.float32) + lax.ppermute(sibling, "core", core_pairs).astype(jnp.float32)
    ).astype(jnp.bfloat16)

    xlo_pairs = [(i, (i + 1) % xlo_count) for i in range(xlo_count)]
    mine = lax.dynamic_index_in_dim(summed, xlo, axis=0, keepdims=False)
    theirs = lax.ppermute(
        lax.dynamic_index_in_dim(summed, 1 - xlo, axis=0, keepdims=False), "xlo", xlo_pairs
    )
    shares = (mine.astype(jnp.float32) + theirs.astype(jnp.float32)).astype(jnp.bfloat16)
    return (input_grad, router_grad, shares)


def solution(mesh):
    dp_count, expert_devs = mesh.devices.shape
    core_count = 2
    split_mesh = Mesh(
        mesh.devices.reshape(dp_count // core_count, core_count, expert_devs),
        ("xlo", "core", "expert"),
    )
    rows = ("xlo", "core", "expert")
    in_specs = (
        P(rows, None),
        P(rows, None),
        P(rows, None),
        P(rows, None),
        P(None, "expert", None),
        P(None, "expert", None),
        P(None, "expert", None),
    )
    out_specs = (
        P(rows, None),
        P(rows, None),
        P(("xlo", "core"), None, "expert", None),
    )
    return jax.shard_map(
        per_device, mesh=split_mesh, in_specs=in_specs, out_specs=out_specs, check_vma=False
    )
```

time: 556 us -> 630 us (1.13)
  the two profiles are of different devices: /device:TPU:36 before, /device:TPU:20 now
where the time goes in v2:
time: 630 us; the launch traced here: 620 us
  waiting for transfers between devices  249 us (40%)
  local copies, waits for them, and re-layouts  180 us (29%)
  matrix products  84.1 us (13%)
  other arithmetic  55.8 us (9%)
  starting transfers between devices  50.8 us (8%)
    another operation x6, local copies, waits for them, and re-layouts, per_device(): jnp.stack([grad_gate, grad_up, grad_down], axis=1).astype(jnp.bfloat16)  122 us
    ppermute x1, waiting for transfers between devices, per_device(): lax.ppermute(lax.dynamic_index_in_dim(summed, 1 - xlo, axis=0, keepdims=F...  97 us
    all_to_all x1, waiting for transfers between devices, per_device(): lax.all_to_all(send_tokens.reshape(send_shape), 'expert', split_axis=0, c...  56.2 us
    all_to_all x1, waiting for transfers between devices, per_device(): lax.all_to_all(row_grad.reshape(send_shape), 'expert', split_axis=0, conc...  48.8 us
    all_to_all x1, waiting for transfers between devices, per_device(): lax.all_to_all(send_scaled.reshape(send_shape), 'expert', split_axis=0, c...  46.6 us
    another operation x1, other arithmetic, per_device(): jnp.stack([grad_gate, grad_up, grad_down], axis=1).astype(jnp.bfloat16)  28.9 us
  transfers between devices with their start and end apart: 6, of which 4 were waited for; matrix products, arithmetic and copies ran while one was open for 15% of the time, Pallas kernels for 0%

profile of v2, /device:TPU:20, one launch (start us, length us, event | category | flops | bytes accessed | tf_op | source)
XLA Modules:
  0.0 620.5 jit_solution(1942673985413192669)
XLA Ops:
  18.0 11.0 %all-to-all-start.1 = ((bf16[32,36,2048]{2,1,0:T(8,128)(2,1)}), bf16[32,36,2048]{2,1,0:T(8,128)(2,1)}, u32[]{:S(2)}, u32[]{:S(2)}) async-start(bf16[32,36,2048]{2,1,0:T(8,128)(2,1)} %reshape.93), calls=%async_computation.1 | async-start | bytes 10485760 | tf_op jit(solution)/shard_map/all_to_all | solution.py:53
  41.4 56.2 %all-to-all-done.1 = bf16[32,36,2048]{2,1,0:T(8,128)(2,1)} async-done(((bf16[32,36,2048]{2,1,0:T(8,128)(2,1)}), bf16[32,36,2048]{2,1,0:T(8,128)(2,1)}, u32[]{:S(2)}, u32[]{:S(2)}) %all-to-all-start.1) | async-done | bytes 4718624 | tf_op jit(solution)/shard_map/all_to_all | solution.py:53
  97.6 10.0 %all-to-all-start = ((bf16[32,36,2048]{2,1,0:T(8,128)(2,1)}), bf16[32,36,2048]{2,1,0:T(8,128)(2,1)}, u32[]{:S(2)}, u32[]{:S(2)}) async-start(bf16[32,36,2048]{2,1,0:T(8,128)(2,1)} %reshape.91), calls=%async_computation | async-start | bytes 10485760 | tf_op jit(solution)/shard_map/all_to_all | solution.py:56
  112.9 10.1 %fusion.14 = f32[2,32,18,768]{3,1,2,0:T(8,128)} fusion(bf16[32,2,18,2048]{3,0,2,1:T(8,128)(2,1)S(1)} %bitcast.109, bf16[2048,2,768,1]{2,1,0,3:T(2,128)(2,1)} %bitcast.121), kind=kOutput, calls=%fused_computation.24 | convolution fusion | flops 3623878656 | bytes 14548992 | tf_op jit(solution)/shard_map/nemd,deh->nemh/dot_general | solution.py:64
  128.6 46.6 %all-to-all-done = bf16[32,36,2048]{2,1,0:T(8,128)(2,1)} async-done(((bf16[32,36,2048]{2,1,0:T(8,128)(2,1)}), bf16[32,36,2048]{2,1,0:T(8,128)(2,1)}, u32[]{:S(2)}, u32[]{:S(2)}) %all-to-all-start) | async-done | bytes 4718624 | tf_op jit(solution)/shard_map/all_to_all | solution.py:56
  180.5 9.8 %fusion.29 = (bf16[32,2,18]{0,2,1:T(8,128)(2,1)S(1)}, bf16[32,2,18,768]{3,0,2,1:T(8,128)(2,1)}, bf16[32,2,18,768]{3,0,2,1:T(8,128)(2,1)}, bf16[32,2,18,768]{3,0,2,1:T(8,128)(2,1)S(1)}) fusion(f32[2,32,18,768]{3,1,2,0:T(8,128)S(1)} %copy-done.14, f32[2,32,18,768]{3,1,2,0:T(8,128)S(1)} %copy-done.15, bf16[32,2,18,2048]{3,0,2,1:T(8,128)(2,1)S(1)} %bitcast.113, ...), kind=kOutput, calls=%fused_computation.50 | convolution fusion | flops 3639802880 | bytes 23398656 | tf_op jit(solution)/shard_map/nemd,deh->nemh/dot_general | solution.py:68
  190.3 8.6 %fusion.5 = bf16[2048,2,768]{0,2,1:T(8,128)(2,1)} fusion(bf16[32,2,18,768]{3,0,2,1:T(8,128)(2,1)} %get-tuple-element.19, bf16[32,2,18,2048]{3,0,2,1:T(8,128)(2,1)S(1)} %bitcast.114), kind=kOutput, calls=%fused_computation.15 | convolution fusion | flops 3627024384 | bytes 12779520 | tf_op jit(solution)/shard_map/nemd,nemh->deh/dot_general | solution.py:103
  199.0 11.1 %stack.14 = bf16[2,2,512,1,2,768]{2,1,0,5,4,3:T(2,128)(2,1)} reshape(bf16[2048,2,768]{0,2,1:T(8,128)(2,1)} %fusion.5) | data formatting | bytes 12582912 | tf_op jit(solution)/shard_map/stack | solution.py:107
  210.1 29.5 %copy.103 = bf16[2,2,512,1,2,768]{5,4,3,2,0,1:T(2,128)(2,1)} copy(bf16[2,2,512,1,2,768]{2,1,0,5,4,3:T(2,128)(2,1)} %stack.14) | data formatting | bytes 12582912 | tf_op jit(solution)/shard_map/stack | solution.py:107
  239.6 9.3 %fusion.4 = bf16[2048,2,768]{0,2,1:T(8,128)(2,1)} fusion(bf16[32,2,18,768]{3,0,2,1:T(8,128)(2,1)S(1)} %get-tuple-element.21, bf16[32,2,18,2048]{3,0,2,1:T(8,128)(2,1)} %bitcast.111), kind=kOutput, calls=%fused_computation.14 | convolution fusion | flops 3627024384 | bytes 12779520 | tf_op jit(solution)/shard_map/nemd,nemh->deh/dot_general | solution.py:102
  249.0 11.1 %stack.13 = bf16[2,2,512,1,2,768]{2,1,0,5,4,3:T(2,128)(2,1)} reshape(bf16[2048,2,768]{0,2,1:T(8,128)(2,1)} %fusion.4) | data formatting | bytes 12582912 | tf_op jit(solution)/shard_map/stack | solution.py:107
  260.1 29.5 %copy.102 = bf16[2,2,512,1,2,768]{5,4,3,2,0,1:T(2,128)(2,1)} copy(bf16[2,2,512,1,2,768]{2,1,0,5,4,3:T(2,128)(2,1)} %stack.13) | data formatting | bytes 12582912 | tf_op jit(solution)/shard_map/stack | solution.py:107
  289.6 9.6 %fusion.3 = bf16[2048,2,768]{0,2,1:T(8,128)(2,1)} fusion(bf16[32,2,18,768]{3,0,2,1:T(8,128)(2,1)} %get-tuple-element.20, bf16[32,2,18,2048]{3,0,2,1:T(8,128)(2,1)} %bitcast.112), kind=kOutput, calls=%fused_computation.13 | convolution fusion | flops 3627024384 | bytes 12779520 | tf_op jit(solution)/shard_map/nemd,nemh->deh/dot_general | solution.py:99
  299.2 11.3 %stack.12 = bf16[2,2,512,1,2,768]{2,1,0,5,4,3:T(2,128)(2,1)} reshape(bf16[2048,2,768]{0,2,1:T(8,128)(2,1)} %fusion.3) | data formatting | bytes 12582912 | tf_op jit(solution)/shard_map/stack | solution.py:107
  310.5 29.5 %copy.101 = bf16[2,2,512,1,2,768]{5,4,3,2,0,1:T(2,128)(2,1)} copy(bf16[2,2,512,1,2,768]{2,1,0,5,4,3:T(2,128)(2,1)} %stack.12) | data formatting | bytes 12582912 | tf_op jit(solution)/shard_map/stack | solution.py:107
  340.0 28.9 %pad_maximum_fusion = bf16[2,2,512,3,2,768]{5,4,3,2,0,1:T(2,128)(2,1)S(1)} fusion(bf16[2,2,512,1,2,768]{5,4,3,2,0,1:T(2,128)(2,1)} %copy.103, bf16[2,2,512,1,2,768]{5,4,3,2,0,1:T(2,128)(2,1)} %copy.102, bf16[2,2,512,1,2,768]{5,4,3,2,0,1:T(2,128)(2,1)} %copy.101), kind=kLoop, calls=%fused_computation | loop fusion | flops 18874368 | bytes 37748736 | tf_op jit(solution)/shard_map/stack | solution.py:107
  369.0 9.0 %dynamic-slice_bitcast_fusion = bf16[2,512,3,2,768]{4,3,2,1,0:T(2,128)(2,1)} fusion(bf16[2,2,512,3,2,768]{5,4,3,2,0,1:T(2,128)(2,1)S(1)} %pad_maximum_fusion, s32[]{:T(128)S(6)} %select_n.25), kind=kLoop, calls=%fused_computation.9 | loop fusion | bytes 18874372 | tf_op jit(solution)/shard_map/jit(dynamic_index_in_dim)/squeeze | solution.py:111
  378.3 10.8 %fusion.8 = f32[2,32,18,2048]{3,1,2,0:T(8,128)} fusion(bf16[32,2,18,768]{3,0,2,1:T(8,128)(2,1)} %get-tuple-element.20, bf16[2048,2,768,1]{2,1,0,3:T(2,128)(2,1)} %bitcast.117), kind=kOutput, calls=%fused_computation.18 | convolution fusion | flops 3623878656 | bytes 17498112 | tf_op jit(solution)/shard_map/nemh,deh->nemd/dot_general | solution.py:77
  403.2 10.5 %all-to-all-start.3 = ((bf16[32,1,36]{2,1,0:T(2,128)(2,1)}), bf16[32,1,36]{2,1,0:T(2,128)(2,1)S(1)}, u32[]{:S(2)}, u32[]{:S(2)}) async-start(bf16[32,1,36]{2,1,0:T(2,128)(2,1)} %copy.100), calls=%async_computation.3 | async-start | bytes 32768 | tf_op jit(solution)/shard_map/all_to_all | solution.py:83
  413.7 12.5 %fusion = bf16[2,512,3,2,768]{4,3,2,1,0:T(2,128)(2,1)} fusion(bf16[2,512,3,2,768]{4,3,2,1,0:T(2,128)(2,1)} %collective-permute-done, bf16[2,2,512,3,2,768]{5,4,3,2,0,1:T(2,128)(2,1)} %copy-done.2, s32[]{:T(128)S(6)} %select_n.24), kind=kLoop, calls=%fused_computation.2 | loop fusion | flops 18874368 | bytes 28311556 | tf_op jit(solution)/shard_map/convert_element_type | solution.py:115
  426.2 10.3 %all-to-all-start.2 = ((bf16[32,36,2048]{2,1,0:T(8,128)(2,1)}), bf16[32,36,2048]{2,1,0:T(8,128)(2,1)}, u32[]{:S(2)}, u32[]{:S(2)}) async-start(bf16[32,36,2048]{2,1,0:T(8,128)(2,1)} %copy.99), calls=%async_computation.2 | async-start | bytes 10485760 | tf_op jit(solution)/shard_map/all_to_all | solution.py:80
  444.3 8.9 %collective-permute-start.1 = (bf16[512,3,2,768]{3,2,1,0:T(2,128)(2,1)}, bf16[512,3,2,768]{3,2,1,0:T(2,128)(2,1)}, u32[]{:S(2)}, u32[]{:S(2)}) collective-permute-start(bf16[512,3,2,768]{3,2,1,0:T(2,128)(2,1)} %dynamic-slice_bitcast_fusion.1), channel_id=1, source_target_pairs={{0,64},{64,0},{1,65},{65,1},{2,66},{66,2},{3,67},{67,3},{4,68},{68... | collective-permute-start | bytes 14155784 | tf_op jit(solution)/shard_map/ppermute | solution.py:119
  455.0 48.8 %all-to-all-done.2 = bf16[32,36,2048]{2,1,0:T(8,128)(2,1)} async-done(((bf16[32,36,2048]{2,1,0:T(8,128)(2,1)}), bf16[32,36,2048]{2,1,0:T(8,128)(2,1)}, u32[]{:S(2)}, u32[]{:S(2)}) %all-to-all-start.2) | async-done | bytes 4718624 | tf_op jit(solution)/shard_map/all_to_all | solution.py:80
  515.1 97.0 %collective-permute-done.1 = bf16[512,3,2,768]{3,2,1,0:T(2,128)(2,1)} collective-permute-done((bf16[512,3,2,768]{3,2,1,0:T(2,128)(2,1)}, bf16[512,3,2,768]{3,2,1,0:T(2,128)(2,1)}, u32[]{:S(2)}, u32[]{:S(2)}) %collective-permute-start.1) | collective-permute-done | bytes 4718624 | tf_op jit(solution)/shard_map/ppermute | solution.py:119
  (76 shorter events, 88.8 us)
Async XLA Ops:
  0.6 6.6 %copy-start = (bf16[128,2048]{1,0:T(8,128)(2,1)S(1)}, bf16[128,2048]{1,0:T(8,128)(2,1)}, u32[]{:S(2)}) copy-start(bf16[128,2048]{1,0:T(8,128)(2,1)} %param.7) | copy-start | bytes 1572868
  7.2 23.4 %copy-start.4 = (pred[1152,128]{1,0:T(8,128)(4,1)}, pred[1152,128]{1,0:T(8,128)(4,1)S(1)}, u32[]{:S(2)}) copy-start(pred[1152,128]{1,0:T(8,128)(4,1)S(1)} %fusion.16) | copy-start | bytes 442372
  18.0 11.0 %copy-start.13 = (f32[128,8]{0,1:T(8,128)S(1)}, f32[128,8]{0,1:T(8,128)}, u32[]{:S(2)}) copy-start(f32[128,8]{0,1:T(8,128)} %param.9) | copy-start | bytes 12292
  18.0 12.6 %copy-start.8 = (bf16[128,2048]{1,0:T(8,128)(2,1)S(1)}, bf16[128,2048]{1,0:T(8,128)(2,1)}, u32[]{:S(2)}) copy-start(bf16[128,2048]{1,0:T(8,128)(2,1)} %param.8) | copy-start | bytes 1572868
  18.0 79.6 %all-to-all-start.1 = ((bf16[32,36,2048]{2,1,0:T(8,128)(2,1)}), bf16[32,36,2048]{2,1,0:T(8,128)(2,1)}, u32[]{:S(2)}, u32[]{:S(2)}) async-start(bf16[32,36,2048]{2,1,0:T(8,128)(2,1)} %reshape.93), calls=%async_computation.1 | async-start | bytes 10485760 | tf_op jit(solution)/shard_map/all_to_all | solution.py:53
  29.2 5.0 copy-start.6
  29.3 0.6 copy-start.11
  30.1 11.4 %copy-start.9 = (s32[1024]{0:T(1024)}, s32[1024]{0:T(1024)S(1)}, u32[]{:S(2)}) copy-start(s32[1024]{0:T(1024)S(1)} %multiply_add_fusion) | copy-start | bytes 12292
  97.6 77.6 %all-to-all-start = ((bf16[32,36,2048]{2,1,0:T(8,128)(2,1)}), bf16[32,36,2048]{2,1,0:T(8,128)(2,1)}, u32[]{:S(2)}, u32[]{:S(2)}) async-start(bf16[32,36,2048]{2,1,0:T(8,128)(2,1)} %reshape.91), calls=%async_computation | async-start | bytes 10485760 | tf_op jit(solution)/shard_map/all_to_all | solution.py:56
  107.7 15.4 %slice-start = ((s8[6291456]{0:T(1024)(128)(4,1)}), s8[4194304]{0:T(1024)(128)(4,1)S(1)}, s32[]{:S(2)}) async-start(s8[6291456]{0:T(1024)(128)(4,1)} %bitcast.118), calls=%async_computation.4 | async-start | bytes 8388608
  112.9 10.1 %copy-start.3 = (bf16[32,36,2048]{2,0,1:T(8,128)(2,1)}, bf16[32,36,2048]{2,0,1:T(8,128)(2,1)S(1)}, u32[]{:S(2)}) copy-start(bf16[32,36,2048]{2,0,1:T(8,128)(2,1)S(1)} %copy.94) | copy-start | bytes 14155780
  112.9 10.1 %slice-start.1 = ((s8[6291456]{0:T(1024)(128)(4,1)}), s8[2097152]{0:T(1024)(128)(4,1)S(1)}, s32[]{:S(2)}) async-start(s8[6291456]{0:T(1024)(128)(4,1)} %bitcast.118), calls=%async_computation.5 | async-start | bytes 4194304
  175.3 5.2 copy-start.14
  175.3 5.2 copy-start.15
  369.0 9.3 %copy-start.2 = (bf16[2,2,512,3,2,768]{5,4,3,2,0,1:T(2,128)(2,1)}, bf16[2,2,512,3,2,768]{5,4,3,2,0,1:T(2,128)(2,1)S(1)}, u32[]{:S(2)}) copy-start(bf16[2,2,512,3,2,768]{5,4,3,2,0,1:T(2,128)(2,1)S(1)} %pad_maximum_fusion) | copy-start | bytes 56623108
  378.3 35.4 %collective-permute-start = (bf16[2,512,3,2,768]{4,3,2,1,0:T(2,128)(2,1)}, bf16[2,512,3,2,768]{4,3,2,1,0:T(2,128)(2,1)}, u32[]{:S(2)}, u32[]{:S(2)}) collective-permute-start(bf16[2,512,3,2,768]{4,3,2,1,0:T(2,128)(2,1)} %dynamic-slice_bitcast_fusion), channel_id=1, source_target_pairs={{0,32},{32,0},{1,33},{33,1},{2,34},{34,2},{3,35},{35,3},{4,36},{36... | collective-permute-start | bytes 28311560 | tf_op jit(solution)/shard_map/ppermute | solution.py:114
  403.2 23.0 %all-to-all-start.3 = ((bf16[32,1,36]{2,1,0:T(2,128)(2,1)}), bf16[32,1,36]{2,1,0:T(2,128)(2,1)S(1)}, u32[]{:S(2)}, u32[]{:S(2)}) async-start(bf16[32,1,36]{2,1,0:T(2,128)(2,1)} %copy.100), calls=%async_computation.3 | async-start | bytes 32768 | tf_op jit(solution)/shard_map/all_to_all | solution.py:83
  426.2 77.6 %all-to-all-start.2 = ((bf16[32,36,2048]{2,1,0:T(8,128)(2,1)}), bf16[32,36,2048]{2,1,0:T(8,128)(2,1)}, u32[]{:S(2)}, u32[]{:S(2)}) async-start(bf16[32,36,2048]{2,1,0:T(8,128)(2,1)} %copy.99), calls=%async_computation.2 | async-start | bytes 10485760 | tf_op jit(solution)/shard_map/all_to_all | solution.py:80
  436.5 16.9 %copy-start.10 = (s32[1024]{0:T(1024)S(1)}, s32[1024]{0:T(1024)}, u32[]{:S(2)}) copy-start(s32[1024]{0:T(1024)} %copy-done.9) | copy-start | bytes 12292
  436.5 17.7 %copy-start.7 = (f32[128,8]{1,0:T(8,128)S(1)}, f32[128,8]{1,0:T(8,128)}, u32[]{:S(2)}) copy-start(f32[128,8]{1,0:T(8,128)} %copy-done.6) | copy-start | bytes 12292
  436.5 17.7 %copy-start.12 = (f32[128]{0:T(128)S(1)}, f32[128]{0:T(128)}, u32[]{:S(2)}) copy-start(f32[128]{0:T(128)} %copy-done.11) | copy-start | bytes 1540
  444.3 167.8 %collective-permute-start.1 = (bf16[512,3,2,768]{3,2,1,0:T(2,128)(2,1)}, bf16[512,3,2,768]{3,2,1,0:T(2,128)(2,1)}, u32[]{:S(2)}, u32[]{:S(2)}) collective-permute-start(bf16[512,3,2,768]{3,2,1,0:T(2,128)(2,1)} %dynamic-slice_bitcast_fusion.1), channel_id=1, source_target_pairs={{0,64},{64,0},{1,65},{65,1},{2,66},{66,2},{3,67},{67,3},{4,68},{68... | collective-permute-start | bytes 14155784 | tf_op jit(solution)/shard_map/ppermute | solution.py:119
  455.0 56.0 %copy-start.5 = (pred[1152,128]{1,0:T(8,128)(4,1)S(1)}, pred[1152,128]{1,0:T(8,128)(4,1)}, u32[]{:S(2)}) copy-start(pred[1152,128]{1,0:T(8,128)(4,1)} %copy-done.4) | copy-start | bytes 442372
  511.0 109.0 %copy-start.1 = (bf16[128,2048]{1,0:T(8,128)(2,1)S(1)}, bf16[128,2048]{1,0:T(8,128)(2,1)}, u32[]{:S(2)}) copy-start(bf16[128,2048]{1,0:T(8,128)(2,1)} %param.7) | copy-start | bytes 1572868

commit v3 on v2

--- a/solution.py
+++ b/solution.py
@@ -8,6 +8,14 @@
 def combine_weights(gate_logits):
     raised = jnp.exp(gate_logits)
     return raised / jnp.sum(raised, axis=1, keepdims=True)
+
+
+def diagonal_groups(xlo_count, owners, hi_stride):
+    groups = [[], []]
+    for xlo in range(xlo_count):
+        for holder in range(owners):
+            groups[xlo ^ ((holder // hi_stride) % 2)].append(xlo * owners + holder)
+    return groups
 
 
 def per_device(tokens_in, out_grad, gate_logits, route_ids, w_gate, w_up, w_down):
@@ -24,6 +32,11 @@
     slot_count = expert_count * capacity
     xlo = lax.axis_index("xlo")
     core = lax.axis_index("core")
+    hi_stride = 4
+    group_half = owners // 2
+    my_xhi = (lax.axis_index("expert") // hi_stride) % 2
+    my_group = xlo ^ my_xhi
+    groups = diagonal_groups(xlo_count, owners, hi_stride)
 
     weights = combine_weights(gate_logits)
     flat_ids = route_ids.reshape(-1)
@@ -36,7 +49,12 @@
     earlier = (pos[None, :] < pos[:, None]).astype(jnp.bfloat16)
     before = jnp.dot(earlier, onehot, preferred_element_type=jnp.float32)
     slot_rank = jnp.sum(before * onehot.astype(jnp.float32), axis=1).astype(jnp.int32)
-    slot_of_pair = flat_ids * capacity + slot_rank
+    holder = flat_ids // local_experts
+    holder_xhi = (holder // hi_stride) % 2
+    group_pos = (my_group ^ holder_xhi) * group_half + (holder // (2 * hi_stride)) * hi_stride + (
+        holder % hi_stride
+    )
+    slot_of_pair = (group_pos * local_experts + flat_ids % local_experts) * capacity + slot_rank
 
     slot_ids = jnp.arange(slot_count, dtype=jnp.int32)
     pair_hit = slot_of_pair[None, :] == slot_ids[:, None]
@@ -51,10 +69,18 @@
     send_grads = jnp.dot(dispatch, out_grad, preferred_element_type=jnp.float32)
     send_scaled = (slot_weight[:, None] * send_grads).astype(jnp.bfloat16)
     recv_tokens = lax.all_to_all(
-        send_tokens.reshape(send_shape), "expert", split_axis=0, concat_axis=0, tiled=True
+        send_tokens.reshape(send_shape), ("xlo", "expert"),
+        split_axis=0,
+        concat_axis=0,
+        tiled=True,
+        axis_index_groups=groups,
     )
     recv_scaled = lax.all_to_all(
-        send_scaled.reshape(send_shape), "expert", split_axis=0, concat_axis=0, tiled=True
+        send_scaled.reshape(send_shape), ("xlo", "expert"),
+        split_axis=0,
+        concat_axis=0,
+        tiled=True,
+        axis_index_groups=groups,
     )
     block_shape = (owners, local_experts, capacity, model_width)
     recv_tokens = recv_tokens.reshape(block_shape)
@@ -78,14 +104,19 @@
         + jnp.einsum("nemh,deh->nemd", up_grad, w_up, preferred_element_type=jnp.float32)
     ).astype(jnp.bfloat16)
     back_rows = lax.all_to_all(
-        row_grad.reshape(send_shape), "expert", split_axis=0, concat_axis=0, tiled=True
+        row_grad.reshape(send_shape), ("xlo", "expert"),
+        split_axis=0,
+        concat_axis=0,
+        tiled=True,
+        axis_index_groups=groups,
     ).reshape(slot_count, model_width)
     back_probs = lax.all_to_all(
         prob_part.reshape(owners, local_experts * capacity),
-        "expert",
+        ("xlo", "expert"),
         split_axis=0,
         concat_axis=0,
         tiled=True,
+        axis_index_groups=groups,
     ).reshape(slot_count)
 
     input_grad = lax.dot_general(
@@ -104,22 +135,24 @@
         "nemd,nemh->deh", recv_scaled, hidden, preferred_element_type=jnp.float32
     )
     block_rows = model_width // (xlo_count * core_count)
-    grads = jnp.stack([grad_gate, grad_up, grad_down], axis=1).astype(jnp.bfloat16)
-    grads = grads.reshape(xlo_count, core_count, block_rows, 3, local_experts, hidden_width)
+    grads = jnp.stack([grad_gate, grad_up, grad_down], axis=0).astype(jnp.bfloat16)
+    grads = grads.reshape(3, xlo_count, core_count, block_rows, local_experts, hidden_width)
 
     core_pairs = [(i, (i + 1) % core_count) for i in range(core_count)]
-    sibling = lax.dynamic_index_in_dim(grads, 1 - core, axis=1, keepdims=False)
-    own = lax.dynamic_index_in_dim(grads, core, axis=1, keepdims=False)
+    sibling = lax.dynamic_index_in_dim(grads, 1 - core, axis=2, keepdims=False)
+    own = lax.dynamic_index_in_dim(grads, core, axis=2, keepdims=False)
     summed = (
         own.astype(jnp.float32) + lax.ppermute(sibling, "core", core_pairs).astype(jnp.float32)
     ).astype(jnp.bfloat16)
 
     xlo_pairs = [(i, (i + 1) % xlo_count) for i in range(xlo_count)]
-    mine = lax.dynamic_index_in_dim(summed, xlo, axis=0, keepdims=False)
+    mine = lax.dynamic_index_in_dim(summed, xlo, axis=1, keepdims=False)
     theirs = lax.ppermute(
-        lax.dynamic_index_in_dim(summed, 1 - xlo, axis=0, keepdims=False), "xlo", xlo_pairs
+        lax.dynamic_index_in_dim(summed, 1 - xlo, axis=1, keepdims=False), "xlo", xlo_pairs
     )
-    shares = (mine.astype(jnp.float32) + theirs.astype(jnp.float32)).astype(jnp.bfloat16)
+    shares = jnp.transpose(
+        (mine.astype(jnp.float32) + theirs.astype(jnp.float32)).astype(jnp.bfloat16), (1, 0, 2, 3)
+    )
     return (input_grad, router_grad, shares)
 
 

time: 630 us -> 569 us (0.903)
  the two profiles are of different devices: /device:TPU:20 before, /device:TPU:0 now
where the time goes in v3:
time: 569 us; the launch traced here: 559 us
  waiting for transfers between devices  196 us (34%)
  local copies, waits for them, and re-layouts  180 us (32%)
  matrix products  84.1 us (15%)
  other arithmetic  55.9 us (10%)
  starting transfers between devices  42.1 us (7%)
    another operation x6, local copies, waits for them, and re-layouts, per_device(): jnp.stack([grad_gate, grad_up, grad_down], axis=0).astype(jnp.bfloat16)  122 us
    all_to_all x1, waiting for transfers between devices, per_device(): lax.all_to_all(row_grad.reshape(send_shape), ('xlo', 'expert'), split_axi...  59.4 us
    all_to_all x1, waiting for transfers between devices, per_device(): lax.all_to_all(send_tokens.reshape(send_shape), ('xlo', 'expert'), split_...  57.3 us
    all_to_all x1, waiting for transfers between devices, per_device(): lax.all_to_all(send_scaled.reshape(send_shape), ('xlo', 'expert'), split_...  48.2 us
    ppermute x1, waiting for transfers between devices, per_device(): lax.ppermute(lax.dynamic_index_in_dim(summed, 1 - xlo, axis=1, keepdims=F...  31.3 us
    another operation x1, other arithmetic, per_device(): jnp.stack([grad_gate, grad_up, grad_down], axis=0).astype(jnp.bfloat16)  28.9 us
    convert_element_type x1, other arithmetic, per_device(): summed = (own.astype(jnp.float32) + lax.ppermute(sibling, 'core', core_pa...  12.5 us
  transfers between devices with their start and end apart: 6, of which 4 were waited for; matrix products, arithmetic and copies ran while one was open for 16% of the time, Pallas kernels for 0%

profile of v3, /device:TPU:0, one launch (start us, length us, event | category | flops | bytes accessed | tf_op | source)
XLA Modules:
  0.0 559.4 jit_solution(10514842551805046984)
XLA Ops:
  18.1 10.9 %all-to-all-start.1 = ((bf16[32,36,2048]{2,1,0:T(8,128)(2,1)}), bf16[32,36,2048]{2,1,0:T(8,128)(2,1)}, u32[]{:S(2)}, u32[]{:S(2)}) async-start(bf16[32,36,2048]{2,1,0:T(8,128)(2,1)} %reshape.191), calls=%async_computation.1 | async-start | bytes 10485760 | tf_op jit(solution)/shard_map/all_to_all | solution.py:71
  41.4 57.3 %all-to-all-done.1 = bf16[32,36,2048]{2,1,0:T(8,128)(2,1)} async-done(((bf16[32,36,2048]{2,1,0:T(8,128)(2,1)}), bf16[32,36,2048]{2,1,0:T(8,128)(2,1)}, u32[]{:S(2)}, u32[]{:S(2)}) %all-to-all-start.1) | async-done | bytes 4718624 | tf_op jit(solution)/shard_map/all_to_all | solution.py:71
  98.7 10.9 %all-to-all-start = ((bf16[32,36,2048]{2,1,0:T(8,128)(2,1)}), bf16[32,36,2048]{2,1,0:T(8,128)(2,1)}, u32[]{:S(2)}, u32[]{:S(2)}) async-start(bf16[32,36,2048]{2,1,0:T(8,128)(2,1)} %reshape.189), calls=%async_computation | async-start | bytes 10485760 | tf_op jit(solution)/shard_map/all_to_all | solution.py:78
  114.9 10.1 %fusion.14 = f32[2,32,18,768]{3,1,2,0:T(8,128)} fusion(bf16[32,2,18,2048]{3,0,2,1:T(8,128)(2,1)S(1)} %bitcast.111, bf16[2048,2,768,1]{2,1,0,3:T(2,128)(2,1)} %bitcast.123), kind=kOutput, calls=%fused_computation.24 | convolution fusion | flops 3623878656 | bytes 14548992 | tf_op jit(solution)/shard_map/nemd,deh->nemh/dot_general | solution.py:90
  130.6 48.2 %all-to-all-done = bf16[32,36,2048]{2,1,0:T(8,128)(2,1)} async-done(((bf16[32,36,2048]{2,1,0:T(8,128)(2,1)}), bf16[32,36,2048]{2,1,0:T(8,128)(2,1)}, u32[]{:S(2)}, u32[]{:S(2)}) %all-to-all-start) | async-done | bytes 4718624 | tf_op jit(solution)/shard_map/all_to_all | solution.py:78
  184.1 9.8 %fusion.30 = (bf16[32,2,18]{0,2,1:T(8,128)(2,1)S(1)}, bf16[32,2,18,768]{3,0,2,1:T(8,128)(2,1)}, bf16[32,2,18,768]{3,0,2,1:T(8,128)(2,1)}, bf16[32,2,18,768]{3,0,2,1:T(8,128)(2,1)S(1)}) fusion(f32[2,32,18,768]{3,1,2,0:T(8,128)S(1)} %copy-done.14, f32[2,32,18,768]{3,1,2,0:T(8,128)S(1)} %copy-done.15, bf16[32,2,18,2048]{3,0,2,1:T(8,128)(2,1)S(1)} %bitcast.115, ...), kind=kOutput, calls=%fused_computation.51 | convolution fusion | flops 3639802880 | bytes 23398656 | tf_op jit(solution)/shard_map/nemd,deh->nemh/dot_general | solution.py:94
  193.9 8.6 %fusion.5 = bf16[2048,2,768]{0,2,1:T(8,128)(2,1)} fusion(bf16[32,2,18,768]{3,0,2,1:T(8,128)(2,1)} %get-tuple-element.19, bf16[32,2,18,2048]{3,0,2,1:T(8,128)(2,1)S(1)} %bitcast.116), kind=kOutput, calls=%fused_computation.15 | convolution fusion | flops 3627024384 | bytes 12779520 | tf_op jit(solution)/shard_map/nemd,nemh->deh/dot_general | solution.py:134
  202.5 11.1 %stack.14 = bf16[1,2,2,512,2,768]{3,2,1,5,4,0:T(2,128)(2,1)} reshape(bf16[2048,2,768]{0,2,1:T(8,128)(2,1)} %fusion.5) | data formatting | bytes 12582912 | tf_op jit(solution)/shard_map/stack | solution.py:138
  213.6 29.5 %copy.111 = bf16[1,2,2,512,2,768]{5,4,0,3,1,2:T(2,128)(2,1)} copy(bf16[1,2,2,512,2,768]{3,2,1,5,4,0:T(2,128)(2,1)} %stack.14) | data formatting | bytes 12582912 | tf_op jit(solution)/shard_map/stack | solution.py:138
  243.2 9.3 %fusion.4 = bf16[2048,2,768]{0,2,1:T(8,128)(2,1)} fusion(bf16[32,2,18,768]{3,0,2,1:T(8,128)(2,1)S(1)} %get-tuple-element.21, bf16[32,2,18,2048]{3,0,2,1:T(8,128)(2,1)} %bitcast.113), kind=kOutput, calls=%fused_computation.14 | convolution fusion | flops 3627024384 | bytes 12779520 | tf_op jit(solution)/shard_map/nemd,nemh->deh/dot_general | solution.py:133
  252.5 11.1 %stack.13 = bf16[1,2,2,512,2,768]{3,2,1,5,4,0:T(2,128)(2,1)} reshape(bf16[2048,2,768]{0,2,1:T(8,128)(2,1)} %fusion.4) | data formatting | bytes 12582912 | tf_op jit(solution)/shard_map/stack | solution.py:138
  263.6 29.5 %copy.110 = bf16[1,2,2,512,2,768]{5,4,0,3,1,2:T(2,128)(2,1)} copy(bf16[1,2,2,512,2,768]{3,2,1,5,4,0:T(2,128)(2,1)} %stack.13) | data formatting | bytes 12582912 | tf_op jit(solution)/shard_map/stack | solution.py:138
  293.1 9.6 %fusion.3 = bf16[2048,2,768]{0,2,1:T(8,128)(2,1)} fusion(bf16[32,2,18,768]{3,0,2,1:T(8,128)(2,1)} %get-tuple-element.20, bf16[32,2,18,2048]{3,0,2,1:T(8,128)(2,1)} %bitcast.114), kind=kOutput, calls=%fused_computation.13 | convolution fusion | flops 3627024384 | bytes 12779520 | tf_op jit(solution)/shard_map/nemd,nemh->deh/dot_general | solution.py:130
  302.7 11.3 %stack.12 = bf16[1,2,2,512,2,768]{3,2,1,5,4,0:T(2,128)(2,1)} reshape(bf16[2048,2,768]{0,2,1:T(8,128)(2,1)} %fusion.3) | data formatting | bytes 12582912 | tf_op jit(solution)/shard_map/stack | solution.py:138
  314.1 29.5 %copy.109 = bf16[1,2,2,512,2,768]{5,4,0,3,1,2:T(2,128)(2,1)} copy(bf16[1,2,2,512,2,768]{3,2,1,5,4,0:T(2,128)(2,1)} %stack.12) | data formatting | bytes 12582912 | tf_op jit(solution)/shard_map/stack | solution.py:138
  343.6 28.9 %pad_maximum_fusion = bf16[3,2,2,512,2,768]{5,4,0,3,1,2:T(2,128)(2,1)S(1)} fusion(bf16[1,2,2,512,2,768]{5,4,0,3,1,2:T(2,128)(2,1)} %copy.111, bf16[1,2,2,512,2,768]{5,4,0,3,1,2:T(2,128)(2,1)} %copy.110, bf16[1,2,2,512,2,768]{5,4,0,3,1,2:T(2,128)(2,1)} %copy.109), kind=kLoop, calls=%fused_computation | loop fusion | flops 18874368 | bytes 37748736 | tf_op jit(solution)/shard_map/stack | solution.py:138
  372.5 9.0 %dynamic-slice_bitcast_fusion = bf16[3,2,512,2,768]{4,3,0,2,1:T(2,128)(2,1)} fusion(bf16[3,2,2,512,2,768]{5,4,0,3,1,2:T(2,128)(2,1)S(1)} %pad_maximum_fusion, s32[]{:T(128)S(6)} %select_n.117), kind=kLoop, calls=%fused_computation.9 | loop fusion | bytes 18874372 | tf_op jit(solution)/shard_map/jit(dynamic_index_in_dim)/squeeze | solution.py:142
  381.8 10.8 %fusion.8 = f32[2,32,18,2048]{3,1,2,0:T(8,128)} fusion(bf16[32,2,18,768]{3,0,2,1:T(8,128)(2,1)} %get-tuple-element.20, bf16[2048,2,768,1]{2,1,0,3:T(2,128)(2,1)} %bitcast.119), kind=kOutput, calls=%fused_computation.18 | convolution fusion | flops 3623878656 | bytes 17498112 | tf_op jit(solution)/shard_map/nemh,deh->nemd/dot_general | solution.py:103
  392.6 8.4 %add_convert_fusion = bf16[2,32,18,2048]{3,1,2,0:T(8,128)(2,1)S(1)} fusion(f32[2,32,18,2048]{3,1,2,0:T(8,128)} %fusion.8, bf16[32,2,18,768]{3,0,2,1:T(8,128)(2,1)S(1)} %get-tuple-element.21, bf16[2048,2,768,1]{2,1,0,3:T(2,128)(2,1)} %bitcast.124), kind=kOutput, calls=%fused_computation.10 | convolution fusion | flops 3628597248 | bytes 22216704 | tf_op jit(solution)/shard_map/nemh,deh->nemd/dot_general | solution.py:104
  406.7 10.4 %all-to-all-start.3 = ((bf16[32,1,36]{2,1,0:T(2,128)(2,1)}), bf16[32,1,36]{2,1,0:T(2,128)(2,1)S(1)}, u32[]{:S(2)}, u32[]{:S(2)}) async-start(bf16[32,1,36]{2,1,0:T(2,128)(2,1)} %copy.108), calls=%async_computation.3 | async-start | bytes 32768 | tf_op jit(solution)/shard_map/all_to_all | solution.py:113
  417.1 12.5 %fusion = bf16[3,2,512,2,768]{4,3,0,2,1:T(2,128)(2,1)} fusion(bf16[3,2,512,2,768]{4,3,0,2,1:T(2,128)(2,1)} %collective-permute-done, bf16[3,2,2,512,2,768]{5,4,0,3,1,2:T(2,128)(2,1)} %copy-done.2, s32[]{:T(128)S(6)} %select_n.116), kind=kLoop, calls=%fused_computation.2 | loop fusion | flops 18874368 | bytes 28311556 | tf_op jit(solution)/shard_map/convert_element_type | solution.py:146
  429.7 9.9 %all-to-all-start.2 = ((bf16[32,36,2048]{2,1,0:T(8,128)(2,1)}), bf16[32,36,2048]{2,1,0:T(8,128)(2,1)}, u32[]{:S(2)}, u32[]{:S(2)}) async-start(bf16[32,36,2048]{2,1,0:T(8,128)(2,1)} %copy.107), calls=%async_computation.2 | async-start | bytes 10485760 | tf_op jit(solution)/shard_map/all_to_all | solution.py:106
  449.1 59.4 %all-to-all-done.2 = bf16[32,36,2048]{2,1,0:T(8,128)(2,1)} async-done(((bf16[32,36,2048]{2,1,0:T(8,128)(2,1)}), bf16[32,36,2048]{2,1,0:T(8,128)(2,1)}, u32[]{:S(2)}, u32[]{:S(2)}) %all-to-all-start.2) | async-done | bytes 4718624 | tf_op jit(solution)/shard_map/all_to_all | solution.py:106
  519.8 31.3 %collective-permute-done.1 = bf16[3,512,2,768]{3,2,0,1:T(2,128)(2,1)} collective-permute-done((bf16[3,512,2,768]{3,2,0,1:T(2,128)(2,1)}, bf16[3,512,2,768]{3,2,0,1:T(2,128)(2,1)}, u32[]{:S(2)}, u32[]{:S(2)}) %collective-permute-start.1) | collective-permute-done | bytes 4718624 | tf_op jit(solution)/shard_map/ppermute | solution.py:150
  (76 shorter events, 80.4 us)
Async XLA Ops:
  0.6 6.7 %copy-start = (bf16[128,2048]{1,0:T(8,128)(2,1)S(1)}, bf16[128,2048]{1,0:T(8,128)(2,1)}, u32[]{:S(2)}) copy-start(bf16[128,2048]{1,0:T(8,128)(2,1)} %param.7) | copy-start | bytes 1572868
  7.3 23.3 %copy-start.4 = (pred[1152,128]{1,0:T(8,128)(4,1)}, pred[1152,128]{1,0:T(8,128)(4,1)S(1)}, u32[]{:S(2)}) copy-start(pred[1152,128]{1,0:T(8,128)(4,1)S(1)} %fusion.17) | copy-start | bytes 442372
  18.1 10.9 %copy-start.13 = (f32[128,8]{0,1:T(8,128)S(1)}, f32[128,8]{0,1:T(8,128)}, u32[]{:S(2)}) copy-start(f32[128,8]{0,1:T(8,128)} %param.9) | copy-start | bytes 12292
  18.1 12.5 %copy-start.8 = (bf16[128,2048]{1,0:T(8,128)(2,1)S(1)}, bf16[128,2048]{1,0:T(8,128)(2,1)}, u32[]{:S(2)}) copy-start(bf16[128,2048]{1,0:T(8,128)(2,1)} %param.8) | copy-start | bytes 1572868
  18.1 80.6 %all-to-all-start.1 = ((bf16[32,36,2048]{2,1,0:T(8,128)(2,1)}), bf16[32,36,2048]{2,1,0:T(8,128)(2,1)}, u32[]{:S(2)}, u32[]{:S(2)}) async-start(bf16[32,36,2048]{2,1,0:T(8,128)(2,1)} %reshape.191), calls=%async_computation.1 | async-start | bytes 10485760 | tf_op jit(solution)/shard_map/all_to_all | solution.py:71
  29.1 5.1 copy-start.6
  29.2 0.6 copy-start.11
  30.0 11.4 %copy-start.9 = (s32[1024]{0:T(1024)}, s32[1024]{0:T(1024)S(1)}, u32[]{:S(2)}) copy-start(s32[1024]{0:T(1024)S(1)} %fusion.54) | copy-start | bytes 12292
  98.7 80.1 %all-to-all-start = ((bf16[32,36,2048]{2,1,0:T(8,128)(2,1)}), bf16[32,36,2048]{2,1,0:T(8,128)(2,1)}, u32[]{:S(2)}, u32[]{:S(2)}) async-start(bf16[32,36,2048]{2,1,0:T(8,128)(2,1)} %reshape.189), calls=%async_computation | async-start | bytes 10485760 | tf_op jit(solution)/shard_map/all_to_all | solution.py:78
  109.6 15.4 %slice-start = ((s8[6291456]{0:T(1024)(128)(4,1)}), s8[4194304]{0:T(1024)(128)(4,1)S(1)}, s32[]{:S(2)}) async-start(s8[6291456]{0:T(1024)(128)(4,1)} %bitcast.120), calls=%async_computation.4 | async-start | bytes 8388608
  114.8 10.1 %copy-start.3 = (bf16[32,36,2048]{2,0,1:T(8,128)(2,1)}, bf16[32,36,2048]{2,0,1:T(8,128)(2,1)S(1)}, u32[]{:S(2)}) copy-start(bf16[32,36,2048]{2,0,1:T(8,128)(2,1)S(1)} %copy.102) | copy-start | bytes 14155780
  114.9 10.1 %slice-start.1 = ((s8[6291456]{0:T(1024)(128)(4,1)}), s8[2097152]{0:T(1024)(128)(4,1)S(1)}, s32[]{:S(2)}) async-start(s8[6291456]{0:T(1024)(128)(4,1)} %bitcast.120), calls=%async_computation.5 | async-start | bytes 4194304
  178.8 5.2 copy-start.14
  178.8 5.2 copy-start.15
  372.5 9.3 %copy-start.2 = (bf16[3,2,2,512,2,768]{5,4,0,3,1,2:T(2,128)(2,1)}, bf16[3,2,2,512,2,768]{5,4,0,3,1,2:T(2,128)(2,1)S(1)}, u32[]{:S(2)}) copy-start(bf16[3,2,2,512,2,768]{5,4,0,3,1,2:T(2,128)(2,1)S(1)} %pad_maximum_fusion) | copy-start | bytes 56623108
  381.8 35.3 %collective-permute-start = (bf16[3,2,512,2,768]{4,3,0,2,1:T(2,128)(2,1)}, bf16[3,2,512,2,768]{4,3,0,2,1:T(2,128)(2,1)}, u32[]{:S(2)}, u32[]{:S(2)}) collective-permute-start(bf16[3,2,512,2,768]{4,3,0,2,1:T(2,128)(2,1)} %dynamic-slice_bitcast_fusion), channel_id=1, source_target_pairs={{0,32},{32,0},{1,33},{33,1},{2,34},{34,2},{3,35},{35,3},{4,36},{36... | collective-permute-start | bytes 28311560 | tf_op jit(solution)/shard_map/ppermute | solution.py:145
  406.7 23.0 %all-to-all-start.3 = ((bf16[32,1,36]{2,1,0:T(2,128)(2,1)}), bf16[32,1,36]{2,1,0:T(2,128)(2,1)S(1)}, u32[]{:S(2)}, u32[]{:S(2)}) async-start(bf16[32,1,36]{2,1,0:T(2,128)(2,1)} %copy.108), calls=%async_computation.3 | async-start | bytes 32768 | tf_op jit(solution)/shard_map/all_to_all | solution.py:113
  429.7 78.9 %all-to-all-start.2 = ((bf16[32,36,2048]{2,1,0:T(8,128)(2,1)}), bf16[32,36,2048]{2,1,0:T(8,128)(2,1)}, u32[]{:S(2)}, u32[]{:S(2)}) async-start(bf16[32,36,2048]{2,1,0:T(8,128)(2,1)} %copy.107), calls=%async_computation.2 | async-start | bytes 10485760 | tf_op jit(solution)/shard_map/all_to_all | solution.py:106
  439.6 8.0 %copy-start.10 = (s32[1024]{0:T(1024)S(1)}, s32[1024]{0:T(1024)}, u32[]{:S(2)}) copy-start(s32[1024]{0:T(1024)} %copy-done.9) | copy-start | bytes 12292
  439.6 8.8 %copy-start.7 = (f32[128,8]{1,0:T(8,128)S(1)}, f32[128,8]{1,0:T(8,128)}, u32[]{:S(2)}) copy-start(f32[128,8]{1,0:T(8,128)} %copy-done.6) | copy-start | bytes 12292
  439.6 8.8 %copy-start.12 = (f32[128]{0:T(128)S(1)}, f32[128]{0:T(128)}, u32[]{:S(2)}) copy-start(f32[128]{0:T(128)} %copy-done.11) | copy-start | bytes 1540
  447.4 103.7 %collective-permute-start.1 = (bf16[3,512,2,768]{3,2,0,1:T(2,128)(2,1)}, bf16[3,512,2,768]{3,2,0,1:T(2,128)(2,1)}, u32[]{:S(2)}, u32[]{:S(2)}) collective-permute-start(bf16[3,512,2,768]{3,2,0,1:T(2,128)(2,1)} %dynamic-slice_bitcast_fusion.1), channel_id=1, source_target_pairs={{0,64},{64,0},{1,65},{65,1},{2,66},{66,2},{3,67},{67,3},{4,68},{68... | collective-permute-start | bytes 14155784 | tf_op jit(solution)/shard_map/ppermute | solution.py:150
  449.1 66.6 %copy-start.5 = (pred[1152,128]{1,0:T(8,128)(4,1)S(1)}, pred[1152,128]{1,0:T(8,128)(4,1)}, u32[]{:S(2)}) copy-start(pred[1152,128]{1,0:T(8,128)(4,1)} %copy-done.4) | copy-start | bytes 442372
  515.7 43.3 %copy-start.1 = (bf16[128,2048]{1,0:T(8,128)(2,1)S(1)}, bf16[128,2048]{1,0:T(8,128)(2,1)}, u32[]{:S(2)}) copy-start(bf16[128,2048]{1,0:T(8,128)(2,1)} %param.7) | copy-start | bytes 1572868

commit v4 on v3

--- a/solution.py
+++ b/solution.py
@@ -127,31 +127,52 @@
     ).reshape(tok_rows, topk_count)
     router_grad = pair_probs - weights * jnp.sum(pair_probs, axis=1, keepdims=True)
 
-    grad_gate = jnp.einsum(
-        "nemd,nemh->deh", recv_tokens, gate_grad, preferred_element_type=jnp.float32
-    )
-    grad_up = jnp.einsum("nemd,nemh->deh", recv_tokens, up_grad, preferred_element_type=jnp.float32)
-    grad_down = jnp.einsum(
-        "nemd,nemh->deh", recv_scaled, hidden, preferred_element_type=jnp.float32
-    )
-    block_rows = model_width // (xlo_count * core_count)
-    grads = jnp.stack([grad_gate, grad_up, grad_down], axis=0).astype(jnp.bfloat16)
-    grads = grads.reshape(3, xlo_count, core_count, block_rows, local_experts, hidden_width)
+    block_count = xlo_count * core_count
+    block_rows = model_width // block_count
+    blocks = []
+    for block in range(block_count):
+        rows = slice(block * block_rows, (block + 1) * block_rows)
+        blocks.append(
+            jnp.stack(
+                [
+                    jnp.einsum(
+                        "nemh,nemd->ehd",
+                        gate_grad,
+                        recv_tokens[..., rows],
+                        preferred_element_type=jnp.float32,
+                    ),
+                    jnp.einsum(
+                        "nemh,nemd->ehd",
+                        up_grad,
+                        recv_tokens[..., rows],
+                        preferred_element_type=jnp.float32,
+                    ),
+                    jnp.einsum(
+                        "nemh,nemd->ehd",
+                        hidden,
+                        recv_scaled[..., rows],
+                        preferred_element_type=jnp.float32,
+                    ),
+                ]
+            )
+        )
+    grads = jnp.stack(blocks).astype(jnp.bfloat16)
+    grads = grads.reshape((xlo_count, core_count) + grads.shape[1:])
 
     core_pairs = [(i, (i + 1) % core_count) for i in range(core_count)]
-    sibling = lax.dynamic_index_in_dim(grads, 1 - core, axis=2, keepdims=False)
-    own = lax.dynamic_index_in_dim(grads, core, axis=2, keepdims=False)
+    sibling = lax.dynamic_index_in_dim(grads, 1 - core, axis=1, keepdims=False)
+    own = lax.dynamic_index_in_dim(grads, core, axis=1, keepdims=False)
     summed = (
         own.astype(jnp.float32) + lax.ppermute(sibling, "core", core_pairs).astype(jnp.float32)
     ).astype(jnp.bfloat16)
 
     xlo_pairs = [(i, (i + 1) % xlo_count) for i in range(xlo_count)]
-    mine = lax.dynamic_index_in_dim(summed, xlo, axis=1, keepdims=False)
+    mine = lax.dynamic_index_in_dim(summed, xlo, axis=0, keepdims=False)
     theirs = lax.ppermute(
-        lax.dynamic_index_in_dim(summed, 1 - xlo, axis=1, keepdims=False), "xlo", xlo_pairs
+        lax.dynamic_index_in_dim(summed, 1 - xlo, axis=0, keepdims=False), "xlo", xlo_pairs
     )
     shares = jnp.transpose(
-        (mine.astype(jnp.float32) + theirs.astype(jnp.float32)).astype(jnp.bfloat16), (1, 0, 2, 3)
+        (mine.astype(jnp.float32) + theirs.astype(jnp.float32)).astype(jnp.bfloat16), (3, 0, 1, 2)
     )
     return (input_grad, router_grad, shares)
 

time: 569 us -> 456 us (0.80)
  local copies, waits for them, and re-layouts: 180 us -> 103 us
  other arithmetic: 55.9 us -> 31.6 us
  matrix products: 84.1 us -> 73.7 us
    another operation x6 -> x0, local copies, waits for them, and re-layouts: 122 us -> none  [per_device(): jnp.stack([grad_gate, grad_up, grad_down], axis=0).astype(jnp.bfloat16)]
    dynamic_slice x0 -> x2, local copies, waits for them, and re-layouts: none -> 30.6 us  [the longest x1 23.9 us: per_device(): sibling = lax.dynamic_index_in_dim(grads, 1 - core, axis=1, keepdims=False)]
    another operation x1 -> x3, other arithmetic: 28.9 us -> 4.67 us  [per_device(): grads = jnp.stack(blocks).astype(jnp.bfloat16)]
    unnamed x39 -> x42, local copies, waits for them, and re-layouts: 2.55 us -> 26.4 us
    dot_general x3 -> x12, matrix products: 27.5 us -> 17.6 us  [the longest x4 6.16 us: per_device(): jnp.einsum('nemh,nemd->ehd', hidden, recv_scaled[..., rows], preferred_el...]
    squeeze x2 -> x1, local copies, waits for them, and re-layouts: 16.8 us -> 7.81 us  [per_device(): lax.dynamic_index_in_dim(summed, 1 - xlo, axis=0, keepdims=False)]
  transfers between devices with their start and end apart: 6 -> 6, of which waited for: 4 -> 4; matrix products, arithmetic and copies ran while one was open for 16% -> 26% of each run, Pallas kernels for 0% -> 0%
where the time goes in v4:
time: 456 us; the launch traced here: 448 us
  waiting for transfers between devices  196 us (43%)
  local copies, waits for them, and re-layouts  103 us (23%)
  matrix products  73.7 us (16%)
  starting transfers between devices  41.9 us (9%)
  other arithmetic  31.6 us (7%)
    all_to_all x1, waiting for transfers between devices, per_device(): lax.all_to_all(row_grad.reshape(send_shape), ('xlo', 'expert'), split_axi...  59.4 us
    all_to_all x1, waiting for transfers between devices, per_device(): lax.all_to_all(send_tokens.reshape(send_shape), ('xlo', 'expert'), split_...  57.4 us
    all_to_all x1, waiting for transfers between devices, per_device(): lax.all_to_all(send_scaled.reshape(send_shape), ('xlo', 'expert'), split_...  48.2 us
    ppermute x1, waiting for transfers between devices, per_device(): lax.ppermute(lax.dynamic_index_in_dim(summed, 1 - xlo, axis=0, keepdims=F...  31.3 us
    unnamed x42, local copies, waits for them, and re-layouts  26.4 us
    dynamic_slice x1, local copies, waits for them, and re-layouts, per_device(): sibling = lax.dynamic_index_in_dim(grads, 1 - core, axis=1, keepdims=False)  23.9 us
    convert_element_type x1, other arithmetic, per_device(): summed = (own.astype(jnp.float32) + lax.ppermute(sibling, 'core', core_pa...  12.5 us
    all_to_all x1, starting transfers between devices, per_device(): lax.all_to_all(send_scaled.reshape(send_shape), ('xlo', 'expert'), split_...  10.9 us
  transfers between devices with their start and end apart: 6, of which 4 were waited for; matrix products, arithmetic and copies ran while one was open for 26% of the time, Pallas kernels for 0%

profile of v4, /device:TPU:0, one launch (start us, length us, event | category | flops | bytes accessed | tf_op | source)
XLA Modules:
  0.0 447.8 jit_solution(10746255883051351267)
XLA Ops:
  10.9 7.2 %reshape.184 = bf16[32,36,2048]{2,1,0:T(8,128)(2,1)} reshape(bf16[1152,2048]{1,0:T(8,128)(2,1)} %convolution_convert_fusion) | data formatting | bytes 9437184 | tf_op jit(solution)/shard_map/reshape | solution.py:72
  18.1 10.9 %all-to-all-start.1 = ((bf16[32,36,2048]{2,1,0:T(8,128)(2,1)}), bf16[32,36,2048]{2,1,0:T(8,128)(2,1)}, u32[]{:S(2)}, u32[]{:S(2)}) async-start(bf16[32,36,2048]{2,1,0:T(8,128)(2,1)} %reshape.184), calls=%async_computation.1 | async-start | bytes 10485760 | tf_op jit(solution)/shard_map/all_to_all | solution.py:71
  34.0 7.2 %reshape.182 = bf16[32,36,2048]{2,1,0:T(8,128)(2,1)} reshape(bf16[1152,2048]{1,0:T(8,128)(2,1)} %fusion.2) | data formatting | bytes 9437184 | tf_op jit(solution)/shard_map/reshape | solution.py:79
  41.3 57.4 %all-to-all-done.1 = bf16[32,36,2048]{2,1,0:T(8,128)(2,1)} async-done(((bf16[32,36,2048]{2,1,0:T(8,128)(2,1)}), bf16[32,36,2048]{2,1,0:T(8,128)(2,1)}, u32[]{:S(2)}, u32[]{:S(2)}) %all-to-all-start.1) | async-done | bytes 4718624 | tf_op jit(solution)/shard_map/all_to_all | solution.py:71
  98.7 10.9 %all-to-all-start = ((bf16[32,36,2048]{2,1,0:T(8,128)(2,1)}), bf16[32,36,2048]{2,1,0:T(8,128)(2,1)}, u32[]{:S(2)}, u32[]{:S(2)}) async-start(bf16[32,36,2048]{2,1,0:T(8,128)(2,1)} %reshape.182), calls=%async_computation | async-start | bytes 10485760 | tf_op jit(solution)/shard_map/all_to_all | solution.py:78
  109.6 5.2 %copy.97 = bf16[32,36,2048]{2,0,1:T(8,128)(2,1)S(1)} copy(bf16[32,36,2048]{2,1,0:T(8,128)(2,1)} %all-to-all-done.1) | data formatting | bytes 9437184 | tf_op jit(solution)/shard_map/all_to_all | solution.py:71
  114.8 10.1 %fusion.11 = f32[2,32,18,768]{3,1,2,0:T(8,128)} fusion(bf16[32,2,18,2048]{3,0,2,1:T(8,128)(2,1)S(1)} %bitcast.184, bf16[2048,2,768,1]{2,1,0,3:T(2,128)(2,1)} %bitcast.207), kind=kOutput, calls=%fused_computation.17 | convolution fusion | flops 3623878656 | bytes 14548992 | tf_op jit(solution)/shard_map/nemd,deh->nemh/dot_general | solution.py:90
  125.0 5.6 %fusion.7 = f32[2,32,18,768]{3,1,2,0:T(8,128)} fusion(bf16[32,2,18,2048]{3,0,2,1:T(8,128)(2,1)S(1)} %bitcast.185, bf16[2048,2,768,1]{2,1,0,3:T(2,128)(2,1)S(1)} %bitcast.206), kind=kOutput, calls=%fused_computation.13 | convolution fusion | flops 3623878656 | bytes 14548992 | tf_op jit(solution)/shard_map/nemd,deh->nemh/dot_general | solution.py:89
  130.6 48.2 %all-to-all-done = bf16[32,36,2048]{2,1,0:T(8,128)(2,1)} async-done(((bf16[32,36,2048]{2,1,0:T(8,128)(2,1)}), bf16[32,36,2048]{2,1,0:T(8,128)(2,1)}, u32[]{:S(2)}, u32[]{:S(2)}) %all-to-all-start) | async-done | bytes 4718624 | tf_op jit(solution)/shard_map/all_to_all | solution.py:78
  178.8 5.2 %copy.95 = bf16[32,36,2048]{2,0,1:T(8,128)(2,1)S(1)} copy(bf16[32,36,2048]{2,1,0:T(8,128)(2,1)} %all-to-all-done) | data formatting | bytes 9437184 | tf_op jit(solution)/shard_map/all_to_all | solution.py:78
  184.0 9.1 %fusion.27 = (bf16[32,2,18]{0,2,1:T(8,128)(2,1)S(1)}, bf16[32,2,18,768]{3,0,2,1:T(8,128)(2,1)S(1)}, bf16[32,2,18,768]{3,0,2,1:T(8,128)(2,1)S(1)}, bf16[32,2,18,768]{3,0,2,1:T(8,128)(2,1)S(1)}) fusion(f32[2,32,18,768]{3,1,2,0:T(8,128)S(1)} %copy-done.14, f32[2,32,18,768]{3,1,2,0:T(8,128)} %fusion.7, bf16[32,2,18,2048]{3,0,2,1:T(8,128)(2,1)S(1)} %bitcast.196, ...), kind=kOutput, calls=%fused_computation.48 | convolution fusion | flops 3639802880 | bytes 23398656 | tf_op jit(solution)/shard_map/nemd,deh->nemh/dot_general | solution.py:94
  215.8 6.7 %constant_dynamic-slice_fusion.1 = (bf16[2,1,3,2,768,512]{5,4,3,2,1,0:T(8,128)(2,1)}, bf16[2,1,3,2,768,512]{5,4,3,2,1,0:T(8,128)(2,1)}) fusion(bf16[2,2,3,2,768,512]{5,4,3,2,1,0:T(8,128)(2,1)S(1)} %bitcast.182, s32[]{:T(128)S(6)} %select_n.116, s32[]{:T(128)S(6)} %select_n.117), kind=kLoop, calls=%fused_computation.164 | loop fusion | bytes 37748744 | tf_op jit(solution)/shard_map/jit(dynamic_index_in_dim)/dynamic_slice | solution.py:164
  222.5 23.9 %copy.105 = bf16[2,1,3,2,768,512]{4,3,2,5,0,1:T(2,128)(2,1)} copy(bf16[2,1,3,2,768,512]{5,4,3,2,1,0:T(8,128)(2,1)} %get-tuple-element.21) | data formatting | bytes 18874368 | tf_op jit(solution)/shard_map/jit(dynamic_index_in_dim)/dynamic_slice | solution.py:163
  246.4 10.9 %fusion.5 = f32[2,32,18,2048]{3,1,2,0:T(8,128)} fusion(bf16[32,2,18,768]{3,0,2,1:T(8,128)(2,1)} %copy-done.13, bf16[2048,2,768,1]{2,1,0,3:T(2,128)(2,1)} %bitcast.203), kind=kOutput, calls=%fused_computation.11 | convolution fusion | flops 3623878656 | bytes 17498112 | tf_op jit(solution)/shard_map/nemh,deh->nemd/dot_general | solution.py:103
  257.3 8.6 %add_convert_fusion = bf16[2,32,18,2048]{3,1,2,0:T(8,128)(2,1)S(1)} fusion(f32[2,32,18,2048]{3,1,2,0:T(8,128)} %fusion.5, bf16[32,2,18,768]{3,0,2,1:T(8,128)(2,1)S(1)} %get-tuple-element.23, bf16[2048,2,768,1]{2,1,0,3:T(2,128)(2,1)} %bitcast.208), kind=kOutput, calls=%fused_computation.6 | convolution fusion | flops 3628597248 | bytes 22216704 | tf_op jit(solution)/shard_map/nemh,deh->nemd/dot_general | solution.py:104
  271.5 10.4 %all-to-all-start.3 = ((bf16[32,1,36]{2,1,0:T(2,128)(2,1)}), bf16[32,1,36]{2,1,0:T(2,128)(2,1)S(1)}, u32[]{:S(2)}, u32[]{:S(2)}) async-start(bf16[32,1,36]{2,1,0:T(2,128)(2,1)} %copy.103), calls=%async_computation.3 | async-start | bytes 32768 | tf_op jit(solution)/shard_map/all_to_all | solution.py:113
  282.0 24.0 %copy.134 = bf16[2,1,3,2,768,512]{4,3,2,5,0,1:T(2,128)(2,1)} copy(bf16[2,1,3,2,768,512]{5,4,3,2,1,0:T(8,128)(2,1)} %get-tuple-element.20) | data formatting | bytes 18874368
  306.0 12.5 %fusion = bf16[2,3,2,768,512]{3,2,1,4,0:T(2,128)(2,1)} fusion(bf16[2,3,2,768,512]{3,2,1,4,0:T(2,128)(2,1)} %collective-permute-done, bf16[2,1,3,2,768,512]{4,3,2,5,0,1:T(2,128)(2,1)} %copy.134), kind=kLoop, calls=%fused_computation.2 | loop fusion | flops 18874368 | bytes 28311552 | tf_op jit(solution)/shard_map/convert_element_type | solution.py:167
  318.5 9.7 %all-to-all-start.2 = ((bf16[32,36,2048]{2,1,0:T(8,128)(2,1)}), bf16[32,36,2048]{2,1,0:T(8,128)(2,1)}, u32[]{:S(2)}, u32[]{:S(2)}) async-start(bf16[32,36,2048]{2,1,0:T(8,128)(2,1)} %copy.102), calls=%async_computation.2 | async-start | bytes 10485760 | tf_op jit(solution)/shard_map/all_to_all | solution.py:106
  328.2 7.8 %dynamic-slice_bitcast_fusion = bf16[3,2,768,512]{2,1,0,3:T(2,128)(2,1)} fusion(bf16[2,3,2,768,512]{3,2,1,4,0:T(2,128)(2,1)} %fusion, s32[]{:T(128)S(6)} %select_n.119), kind=kLoop, calls=%fused_computation.24 | loop fusion | bytes 9437188 | tf_op jit(solution)/shard_map/jit(dynamic_index_in_dim)/squeeze | solution.py:172
  337.7 59.4 %all-to-all-done.2 = bf16[32,36,2048]{2,1,0:T(8,128)(2,1)} async-done(((bf16[32,36,2048]{2,1,0:T(8,128)(2,1)}), bf16[32,36,2048]{2,1,0:T(8,128)(2,1)}, u32[]{:S(2)}, u32[]{:S(2)}) %all-to-all-start.2) | async-done | bytes 4718624 | tf_op jit(solution)/shard_map/all_to_all | solution.py:106
  397.1 7.2 %reshape.187 = bf16[1152,2048]{1,0:T(8,128)(2,1)} reshape(bf16[32,36,2048]{2,1,0:T(8,128)(2,1)} %all-to-all-done.2) | data formatting | bytes 9437184 | tf_op jit(solution)/shard_map/reshape | solution.py:112
  408.4 31.3 %collective-permute-done.1 = bf16[3,2,768,512]{2,1,0,3:T(2,128)(2,1)} collective-permute-done((bf16[3,2,768,512]{2,1,0,3:T(2,128)(2,1)}, bf16[3,2,768,512]{2,1,0,3:T(2,128)(2,1)}, u32[]{:S(2)}, u32[]{:S(2)}) %collective-permute-start.1) | collective-permute-done | bytes 4718624 | tf_op jit(solution)/shard_map/ppermute | solution.py:171
  439.7 7.9 %fusion.13 = bf16[512,3,2,768]{3,2,1,0:T(2,128)(2,1)} fusion(bf16[3,2,768,512]{2,1,0,3:T(2,128)(2,1)} %collective-permute-done.1, bf16[2,3,2,768,512]{3,2,1,4,0:T(2,128)(2,1)} %fusion, s32[]{:T(128)S(6)} %select_n.118), kind=kLoop, calls=%fused_computation.19 | loop fusion | flops 9437184 | bytes 14155780 | tf_op jit(solution)/shard_map/transpose | solution.py:174
  (86 shorter events, 49.2 us)
Async XLA Ops:
  0.6 6.7 %copy-start = (bf16[128,2048]{1,0:T(8,128)(2,1)S(1)}, bf16[128,2048]{1,0:T(8,128)(2,1)}, u32[]{:S(2)}) copy-start(bf16[128,2048]{1,0:T(8,128)(2,1)} %param.7) | copy-start | bytes 1572868
  7.3 23.2 %copy-start.3 = (pred[1152,128]{1,0:T(8,128)(4,1)}, pred[1152,128]{1,0:T(8,128)(4,1)S(1)}, u32[]{:S(2)}) copy-start(pred[1152,128]{1,0:T(8,128)(4,1)S(1)} %fusion.14) | copy-start | bytes 442372
  18.1 10.9 %copy-start.12 = (f32[128,8]{0,1:T(8,128)S(1)}, f32[128,8]{0,1:T(8,128)}, u32[]{:S(2)}) copy-start(f32[128,8]{0,1:T(8,128)} %param.9) | copy-start | bytes 12292
  18.1 12.4 %copy-start.7 = (bf16[128,2048]{1,0:T(8,128)(2,1)S(1)}, bf16[128,2048]{1,0:T(8,128)(2,1)}, u32[]{:S(2)}) copy-start(bf16[128,2048]{1,0:T(8,128)(2,1)} %param.8) | copy-start | bytes 1572868
  18.1 80.6 %all-to-all-start.1 = ((bf16[32,36,2048]{2,1,0:T(8,128)(2,1)}), bf16[32,36,2048]{2,1,0:T(8,128)(2,1)}, u32[]{:S(2)}, u32[]{:S(2)}) async-start(bf16[32,36,2048]{2,1,0:T(8,128)(2,1)} %reshape.184), calls=%async_computation.1 | async-start | bytes 10485760 | tf_op jit(solution)/shard_map/all_to_all | solution.py:71
  29.0 5.0 %copy-start.5 = (f32[128,8]{1,0:T(8,128)}, f32[128,8]{1,0:T(8,128)S(1)}, u32[]{:S(2)}) copy-start(f32[128,8]{1,0:T(8,128)S(1)} %copy.94) | copy-start | bytes 12292
  29.9 11.4 %copy-start.8 = (s32[1024]{0:T(1024)}, s32[1024]{0:T(1024)S(1)}, u32[]{:S(2)}) copy-start(s32[1024]{0:T(1024)S(1)} %fusion.75) | copy-start | bytes 12292
  98.7 80.1 %all-to-all-start = ((bf16[32,36,2048]{2,1,0:T(8,128)(2,1)}), bf16[32,36,2048]{2,1,0:T(8,128)(2,1)}, u32[]{:S(2)}, u32[]{:S(2)}) async-start(bf16[32,36,2048]{2,1,0:T(8,128)(2,1)} %reshape.182), calls=%async_computation | async-start | bytes 10485760 | tf_op jit(solution)/shard_map/all_to_all | solution.py:78
  109.6 15.4 %slice-start.2 = ((s8[6291456]{0:T(1024)(128)(4,1)}), s8[4194304]{0:T(1024)(128)(4,1)S(1)}, s32[]{:S(2)}) async-start(s8[6291456]{0:T(1024)(128)(4,1)} %bitcast.204), calls=%async_computation.6 | async-start | bytes 8388608
  114.8 10.1 %copy-start.2 = (bf16[32,36,2048]{2,0,1:T(8,128)(2,1)}, bf16[32,36,2048]{2,0,1:T(8,128)(2,1)S(1)}, u32[]{:S(2)}) copy-start(bf16[32,36,2048]{2,0,1:T(8,128)(2,1)S(1)} %copy.97) | copy-start | bytes 14155780
  114.8 10.1 %slice-start.3 = ((s8[6291456]{0:T(1024)(128)(4,1)}), s8[2097152]{0:T(1024)(128)(4,1)S(1)}, s32[]{:S(2)}) async-start(s8[6291456]{0:T(1024)(128)(4,1)} %bitcast.204), calls=%async_computation.7 | async-start | bytes 4194304
  178.8 5.2 %copy-start.14 = (f32[2,32,18,768]{3,1,2,0:T(8,128)S(1)}, f32[2,32,18,768]{3,1,2,0:T(8,128)}, u32[]{:S(2)}) copy-start(f32[2,32,18,768]{3,1,2,0:T(8,128)} %fusion.11) | copy-start | bytes 10616836
  193.2 16.5 %copy-start.13 = (bf16[32,2,18,768]{3,0,2,1:T(8,128)(2,1)}, bf16[32,2,18,768]{3,0,2,1:T(8,128)(2,1)S(1)}, u32[]{:S(2)}) copy-start(bf16[32,2,18,768]{3,0,2,1:T(8,128)(2,1)S(1)} %get-tuple-element.22) | copy-start | bytes 5308420
  193.2 2.9 slice-start
  194.6 1.7 slice-start.1
  246.4 59.5 %collective-permute-start = (bf16[2,3,2,768,512]{3,2,1,4,0:T(2,128)(2,1)}, bf16[2,3,2,768,512]{3,2,1,4,0:T(2,128)(2,1)}, u32[]{:S(2)}, u32[]{:S(2)}) collective-permute-start(bf16[2,3,2,768,512]{3,2,1,4,0:T(2,128)(2,1)} %bitcast.183), channel_id=1, source_target_pairs={{0,32},{32,0},{1,33},{33,1},{2,34},{34,2},{3,35},{35,3},{4,36},{36... | collective-permute-start | bytes 28311560 | tf_op jit(solution)/shard_map/ppermute | solution.py:166
  271.5 47.0 %all-to-all-start.3 = ((bf16[32,1,36]{2,1,0:T(2,128)(2,1)}), bf16[32,1,36]{2,1,0:T(2,128)(2,1)S(1)}, u32[]{:S(2)}, u32[]{:S(2)}) async-start(bf16[32,1,36]{2,1,0:T(2,128)(2,1)} %copy.103), calls=%async_computation.3 | async-start | bytes 32768 | tf_op jit(solution)/shard_map/all_to_all | solution.py:113
  318.5 78.6 %all-to-all-start.2 = ((bf16[32,36,2048]{2,1,0:T(8,128)(2,1)}), bf16[32,36,2048]{2,1,0:T(8,128)(2,1)}, u32[]{:S(2)}, u32[]{:S(2)}) async-start(bf16[32,36,2048]{2,1,0:T(8,128)(2,1)} %copy.102), calls=%async_computation.2 | async-start | bytes 10485760 | tf_op jit(solution)/shard_map/all_to_all | solution.py:106
  328.1 8.0 %copy-start.9 = (s32[1024]{0:T(1024)S(1)}, s32[1024]{0:T(1024)}, u32[]{:S(2)}) copy-start(s32[1024]{0:T(1024)} %copy-done.8) | copy-start | bytes 12292
  328.1 8.8 %copy-start.6 = (f32[128,8]{1,0:T(8,128)S(1)}, f32[128,8]{1,0:T(8,128)}, u32[]{:S(2)}) copy-start(f32[128,8]{1,0:T(8,128)} %copy-done.5) | copy-start | bytes 12292
  328.2 8.8 %copy-start.11 = (f32[128]{0:T(128)S(1)}, f32[128]{0:T(128)}, u32[]{:S(2)}) copy-start(f32[128]{0:T(128)} %copy-done.10) | copy-start | bytes 1540
  336.0 103.7 %collective-permute-start.1 = (bf16[3,2,768,512]{2,1,0,3:T(2,128)(2,1)}, bf16[3,2,768,512]{2,1,0,3:T(2,128)(2,1)}, u32[]{:S(2)}, u32[]{:S(2)}) collective-permute-start(bf16[3,2,768,512]{2,1,0,3:T(2,128)(2,1)} %dynamic-slice_bitcast_fusion), channel_id=1, source_target_pairs={{0,64},{64,0},{1,65},{65,1},{2,66},{66,2},{3,67},{67,3},{4,68},{68... | collective-permute-start | bytes 14155784 | tf_op jit(solution)/shard_map/ppermute | solution.py:171
  337.7 66.6 %copy-start.4 = (pred[1152,128]{1,0:T(8,128)(4,1)S(1)}, pred[1152,128]{1,0:T(8,128)(4,1)}, u32[]{:S(2)}) copy-start(pred[1152,128]{1,0:T(8,128)(4,1)} %copy-done.3) | copy-start | bytes 442372
  404.3 43.3 %copy-start.1 = (bf16[128,2048]{1,0:T(8,128)(2,1)S(1)}, bf16[128,2048]{1,0:T(8,128)(2,1)}, u32[]{:S(2)}) copy-start(bf16[128,2048]{1,0:T(8,128)(2,1)} %param.7) | copy-start | bytes 1572868
  (1 other events, 0.5 us)

commit v5 on v4

--- a/solution.py
+++ b/solution.py
@@ -103,21 +103,20 @@
         jnp.einsum("nemh,deh->nemd", gate_grad, w_gate, preferred_element_type=jnp.float32)
         + jnp.einsum("nemh,deh->nemd", up_grad, w_up, preferred_element_type=jnp.float32)
     ).astype(jnp.bfloat16)
-    back_rows = lax.all_to_all(
-        row_grad.reshape(send_shape), ("xlo", "expert"),
-        split_axis=0,
-        concat_axis=0,
-        tiled=True,
-        axis_index_groups=groups,
-    ).reshape(slot_count, model_width)
-    back_probs = lax.all_to_all(
-        prob_part.reshape(owners, local_experts * capacity),
+    lane_pad = 128
+    prob_cols = jnp.pad(prob_part[..., None], ((0, 0),) * 3 + ((0, lane_pad - 1),))
+    back = lax.all_to_all(
+        jnp.concatenate([row_grad, prob_cols], axis=3).reshape(
+            owners, local_experts * capacity, model_width + lane_pad
+        ),
         ("xlo", "expert"),
         split_axis=0,
         concat_axis=0,
         tiled=True,
         axis_index_groups=groups,
-    ).reshape(slot_count)
+    ).reshape(slot_count, model_width + lane_pad)
+    back_rows = back[:, :model_width]
+    back_probs = back[:, model_width]
 
     input_grad = lax.dot_general(
         dispatch, back_rows, (((0,), (0,)), ((), ())), preferred_element_type=jnp.float32
@@ -130,49 +129,36 @@
     block_count = xlo_count * core_count
     block_rows = model_width // block_count
     blocks = []
-    for block in range(block_count):
-        rows = slice(block * block_rows, (block + 1) * block_rows)
+    for xlo_side, core_side in ((1, 1), (0, 1), (1, 0), (0, 0)):
+        block = (xlo ^ xlo_side) * core_count + (core ^ core_side)
+        tokens_rows = lax.dynamic_slice_in_dim(recv_tokens, block * block_rows, block_rows, 3)
+        scaled_rows = lax.dynamic_slice_in_dim(recv_scaled, block * block_rows, block_rows, 3)
         blocks.append(
             jnp.stack(
                 [
                     jnp.einsum(
-                        "nemh,nemd->ehd",
-                        gate_grad,
-                        recv_tokens[..., rows],
-                        preferred_element_type=jnp.float32,
+                        "nemh,nemd->ehd", gate_grad, tokens_rows, preferred_element_type=jnp.float32
                     ),
                     jnp.einsum(
-                        "nemh,nemd->ehd",
-                        up_grad,
-                        recv_tokens[..., rows],
-                        preferred_element_type=jnp.float32,
+                        "nemh,nemd->ehd", up_grad, tokens_rows, preferred_element_type=jnp.float32
                     ),
                     jnp.einsum(
-                        "nemh,nemd->ehd",
-                        hidden,
-                        recv_scaled[..., rows],
-                        preferred_element_type=jnp.float32,
+                        "nemh,nemd->ehd", hidden, scaled_rows, preferred_element_type=jnp.float32
                     ),
                 ]
-            )
+            ).astype(jnp.bfloat16)
         )
-    grads = jnp.stack(blocks).astype(jnp.bfloat16)
-    grads = grads.reshape((xlo_count, core_count) + grads.shape[1:])
 
     core_pairs = [(i, (i + 1) % core_count) for i in range(core_count)]
-    sibling = lax.dynamic_index_in_dim(grads, 1 - core, axis=1, keepdims=False)
-    own = lax.dynamic_index_in_dim(grads, core, axis=1, keepdims=False)
-    summed = (
-        own.astype(jnp.float32) + lax.ppermute(sibling, "core", core_pairs).astype(jnp.float32)
-    ).astype(jnp.bfloat16)
-
     xlo_pairs = [(i, (i + 1) % xlo_count) for i in range(xlo_count)]
-    mine = lax.dynamic_index_in_dim(summed, xlo, axis=0, keepdims=False)
-    theirs = lax.ppermute(
-        lax.dynamic_index_in_dim(summed, 1 - xlo, axis=0, keepdims=False), "xlo", xlo_pairs
+    from_sibling = lax.ppermute(jnp.stack(blocks[:2]), "core", core_pairs)
+    summed = (jnp.stack(blocks[2:]).astype(jnp.float32) + from_sibling.astype(jnp.float32)).astype(
+        jnp.bfloat16
     )
+    theirs = lax.ppermute(summed[0], "xlo", xlo_pairs)
     shares = jnp.transpose(
-        (mine.astype(jnp.float32) + theirs.astype(jnp.float32)).astype(jnp.bfloat16), (3, 0, 1, 2)
+        (summed[1].astype(jnp.float32) + theirs.astype(jnp.float32)).astype(jnp.bfloat16),
+        (3, 0, 1, 2),
     )
     return (input_grad, router_grad, shares)
 

time: 456 us -> 401 us (0.88)
  local copies, waits for them, and re-layouts: 103 us -> 57.9 us
  starting transfers between devices: 41.9 us -> 33.7 us
    dynamic_slice x2 -> x0, local copies, waits for them, and re-layouts: 30.6 us -> none  [the longest x1 23.9 us: per_device(): sibling = lax.dynamic_index_in_dim(grads, 1 - core, axis=1, keepdims=False)]
    all_to_all x2 -> x1, waiting for transfers between devices: 59.4 us -> 49.7 us  [per_device(): lax.all_to_all(jnp.concatenate([row_grad, prob_cols], axis=3).reshape(own...]
    all_to_all x2 -> x1, starting transfers between devices: 20.1 us -> 10.9 us  [per_device(): lax.all_to_all(jnp.concatenate([row_grad, prob_cols], axis=3).reshape(own...]
    ppermute x2, waiting for transfers between devices: 31.3 us -> 39.9 us  [the longest x1 39.9 us: per_device(): theirs = lax.ppermute(summed[0], 'xlo', xlo_pairs)]
    unnamed x42 -> x57, local copies, waits for them, and re-layouts: 26.4 us -> 18 us
    convert_element_type x2 -> x1, other arithmetic: 12.5 us -> 6.91 us  [per_device(): (jnp.stack(blocks[2:]).astype(jnp.float32) + from_sibling.astype(jnp.floa...]
    squeeze x1, local copies, waits for them, and re-layouts: 7.81 us -> 2.69 us  [per_device(): theirs = lax.ppermute(summed[0], 'xlo', xlo_pairs)]
  transfers between devices with their start and end apart: 6 -> 5, of which waited for: 4 -> 4; matrix products, arithmetic and copies ran while one was open for 26% -> 24% of each run, Pallas kernels for 0% -> 0%
where the time goes in v5:
time: 401 us; the launch traced here: 394 us
  waiting for transfers between devices  195 us (49%)
  matrix products  78 us (19%)
  local copies, waits for them, and re-layouts  57.9 us (14%)
  starting transfers between devices  33.7 us (8%)
  other arithmetic  27.4 us (7%)
    all_to_all x1, waiting for transfers between devices, per_device(): lax.all_to_all(send_tokens.reshape(send_shape), ('xlo', 'expert'), split_...  57.3 us
    all_to_all x1, waiting for transfers between devices, per_device(): lax.all_to_all(jnp.concatenate([row_grad, prob_cols], axis=3).reshape(own...  49.7 us
    all_to_all x1, waiting for transfers between devices, per_device(): lax.all_to_all(send_scaled.reshape(send_shape), ('xlo', 'expert'), split_...  48.1 us
    ppermute x1, waiting for transfers between devices, per_device(): theirs = lax.ppermute(summed[0], 'xlo', xlo_pairs)  39.9 us
    unnamed x57, local copies, waits for them, and re-layouts  18 us
    all_to_all x1, starting transfers between devices, per_device(): lax.all_to_all(send_scaled.reshape(send_shape), ('xlo', 'expert'), split_...  11 us
    all_to_all x1, starting transfers between devices, per_device(): lax.all_to_all(jnp.concatenate([row_grad, prob_cols], axis=3).reshape(own...  10.9 us
    dot_general x1, matrix products, per_device(): jnp.einsum('nemh,deh->nemd', gate_grad, w_gate, preferred_element_type=jn...  10.9 us
  transfers between devices with their start and end apart: 5, of which 4 were waited for; matrix products, arithmetic and copies ran while one was open for 24% of the time, Pallas kernels for 0%

profile of v5, /device:TPU:0, one launch (start us, length us, event | category | flops | bytes accessed | tf_op | source)
XLA Modules:
  0.0 393.8 jit_solution(16861951846506389146)
XLA Ops:
  3.1 4.2 %fusion.18 = pred[1152,128]{1,0:T(8,128)(4,1)S(1)} fusion(s32[128,8]{0,1:T(8,128)S(1)} %fusion.71), kind=kLoop, calls=%fused_computation.31 | loop fusion | flops 2211840 | bytes 151552 | tf_op jit(solution)/shard_map/reduce_or | solution.py:61
  10.9 7.2 %reshape.355 = bf16[32,36,2048]{2,1,0:T(8,128)(2,1)} reshape(bf16[1152,2048]{1,0:T(8,128)(2,1)} %convolution_convert_fusion) | data formatting | bytes 9437184 | tf_op jit(solution)/shard_map/reshape | solution.py:72
  18.1 10.9 %all-to-all-start.1 = ((bf16[32,36,2048]{2,1,0:T(8,128)(2,1)}), bf16[32,36,2048]{2,1,0:T(8,128)(2,1)}, u32[]{:S(2)}, u32[]{:S(2)}) async-start(bf16[32,36,2048]{2,1,0:T(8,128)(2,1)} %reshape.355), calls=%async_computation.1 | async-start | bytes 10485760 | tf_op jit(solution)/shard_map/all_to_all | solution.py:71
  34.1 7.3 %reshape.353 = bf16[32,36,2048]{2,1,0:T(8,128)(2,1)} reshape(bf16[1152,2048]{1,0:T(8,128)(2,1)} %fusion.2) | data formatting | bytes 9437184 | tf_op jit(solution)/shard_map/reshape | solution.py:79
  41.4 57.3 %all-to-all-done.1 = bf16[32,36,2048]{2,1,0:T(8,128)(2,1)} async-done(((bf16[32,36,2048]{2,1,0:T(8,128)(2,1)}), bf16[32,36,2048]{2,1,0:T(8,128)(2,1)}, u32[]{:S(2)}, u32[]{:S(2)}) %all-to-all-start.1) | async-done | bytes 4718624 | tf_op jit(solution)/shard_map/all_to_all | solution.py:71
  98.7 11.0 %all-to-all-start = ((bf16[32,36,2048]{2,1,0:T(8,128)(2,1)}), bf16[32,36,2048]{2,1,0:T(8,128)(2,1)}, u32[]{:S(2)}, u32[]{:S(2)}) async-start(bf16[32,36,2048]{2,1,0:T(8,128)(2,1)} %reshape.353), calls=%async_computation | async-start | bytes 10485760 | tf_op jit(solution)/shard_map/all_to_all | solution.py:78
  109.7 5.2 %copy.78 = bf16[32,36,2048]{2,0,1:T(8,128)(2,1)S(1)} copy(bf16[32,36,2048]{2,1,0:T(8,128)(2,1)} %all-to-all-done.1) | data formatting | bytes 9437184 | tf_op jit(solution)/shard_map/all_to_all | solution.py:71
  114.9 10.1 %fusion.11 = f32[2,32,18,768]{3,1,2,0:T(8,128)} fusion(bf16[32,2,18,2048]{3,0,2,1:T(8,128)(2,1)S(1)} %bitcast.172, bf16[2048,2,768,1]{2,1,0,3:T(2,128)(2,1)} %bitcast.197), kind=kOutput, calls=%fused_computation.18 | convolution fusion | flops 3623878656 | bytes 14548992 | tf_op jit(solution)/shard_map/nemd,deh->nemh/dot_general | solution.py:90
  125.1 5.6 %fusion.7 = f32[2,32,18,768]{3,1,2,0:T(8,128)} fusion(bf16[32,2,18,2048]{3,0,2,1:T(8,128)(2,1)S(1)} %bitcast.173, bf16[2048,2,768,1]{2,1,0,3:T(2,128)(2,1)S(1)} %bitcast.196), kind=kOutput, calls=%fused_computation.14 | convolution fusion | flops 3623878656 | bytes 14548992 | tf_op jit(solution)/shard_map/nemd,deh->nemh/dot_general | solution.py:89
  130.7 48.1 %all-to-all-done = bf16[32,36,2048]{2,1,0:T(8,128)(2,1)} async-done(((bf16[32,36,2048]{2,1,0:T(8,128)(2,1)}), bf16[32,36,2048]{2,1,0:T(8,128)(2,1)}, u32[]{:S(2)}, u32[]{:S(2)}) %all-to-all-start) | async-done | bytes 4718624 | tf_op jit(solution)/shard_map/all_to_all | solution.py:78
  178.8 5.2 %copy.76 = bf16[32,36,2048]{2,0,1:T(8,128)(2,1)S(1)} copy(bf16[32,36,2048]{2,1,0:T(8,128)(2,1)} %all-to-all-done) | data formatting | bytes 9437184 | tf_op jit(solution)/shard_map/all_to_all | solution.py:78
  184.0 10.8 %fusion.31 = (bf16[32,2,18]{0,2,1:T(8,128)(2,1)S(1)}, bf16[32,2,18,768]{3,0,2,1:T(8,128)(2,1)S(1)}, bf16[32,2,18,768]{3,0,2,1:T(8,128)(2,1)S(1)}, bf16[32,2,18,768]{3,0,2,1:T(8,128)(2,1)S(1)}) fusion(f32[2,32,18,768]{3,1,2,0:T(8,128)S(1)} %copy-done.17, f32[2,32,18,768]{3,1,2,0:T(8,128)} %fusion.7, bf16[32,2,18,2048]{3,0,2,1:T(8,128)(2,1)S(1)} %bitcast.186, ...), kind=kOutput, calls=%fused_computation.50 | convolution fusion | flops 3639802880 | bytes 23398656 | tf_op jit(solution)/shard_map/nemd,deh->nemh/dot_general | solution.py:94
  204.3 4.7 %maximum_maximum_fusion = bf16[2,3,2,768,512]{4,3,2,1,0:T(8,128)(2,1)} fusion(bf16[1,1,2,768,512]{4,3,2,1,0:T(8,128)(2,1)S(1)} %fusion.46, bf16[1,1,2,768,512]{4,3,2,1,0:T(8,128)(2,1)S(1)} %fusion.45, bf16[1,1,2,768,512]{4,3,2,1,0:T(8,128)(2,1)S(1)} %fusion.44, bf16[1,1,2,768,512]{4,3,2,1,0:T(8,128)(2,1)S(1)} %fusion.43, ...), kind=kLoop, calls=%fused_computation.4 | loop fusion | flops 23592960 | bytes 18874368 | tf_op jit(solution)/shard_map/stack | solution.py:154
  209.6 10.9 %fusion.5 = f32[2,32,18,2048]{3,1,2,0:T(8,128)} fusion(bf16[32,2,18,768]{3,0,2,1:T(8,128)(2,1)} %copy-done.15, bf16[2048,2,768,1]{2,1,0,3:T(2,128)(2,1)} %bitcast.193), kind=kOutput, calls=%fused_computation.12 | convolution fusion | flops 3623878656 | bytes 17498112 | tf_op jit(solution)/shard_map/nemh,deh->nemd/dot_general | solution.py:103
  220.5 8.4 %fusion.14 = bf16[32,2,18,2048]{3,0,2,1:T(8,128)(2,1)S(1)} fusion(f32[2,32,18,2048]{3,1,2,0:T(8,128)} %fusion.5, bf16[32,2,18,768]{3,0,2,1:T(8,128)(2,1)S(1)} %get-tuple-element.21, bf16[2048,2,768,1]{2,1,0,3:T(2,128)(2,1)} %bitcast.198), kind=kOutput, calls=%fused_computation.21 | convolution fusion | flops 3628597248 | bytes 22216704 | tf_op jit(solution)/shard_map/nemh,deh->nemd/dot_general | solution.py:104
  229.4 4.1 %copy.85 = bf16[32,36,2176]{2,1,0:T(8,128)(2,1)} copy(bf16[32,36,2176]{2,0,1:T(8,128)(2,1)S(1)} %bitcast.171) | data formatting | bytes 10027008 | tf_op jit(solution)/shard_map/reshape | solution.py:109
  233.6 10.9 %all-to-all-start.2 = ((bf16[32,36,2176]{2,1,0:T(8,128)(2,1)}), bf16[32,36,2176]{2,1,0:T(8,128)(2,1)}, u32[]{:S(2)}, u32[]{:S(2)}) async-start(bf16[32,36,2176]{2,1,0:T(8,128)(2,1)} %copy.85), calls=%async_computation.2 | async-start | bytes 11141120 | tf_op jit(solution)/shard_map/all_to_all | solution.py:108
  256.7 6.9 %add_convert_fusion = bf16[2,3,2,768,512]{4,3,2,1,0:T(8,128)(2,1)S(1)} fusion(bf16[2,3,2,768,512]{4,3,2,1,0:T(8,128)(2,1)} %collective-permute-done, bf16[1,1,2,768,512]{4,3,2,1,0:T(8,128)(2,1)S(1)} %fusion.40, bf16[1,1,2,768,512]{4,3,2,1,0:T(8,128)(2,1)S(1)} %fusion.39, bf16[1,1,2,768,512]{4,3,2,1,0:T(8,128)(2,1)S(1)} %fusion.38, ...), kind=kLoop, calls=%fused_computation | loop fusion | flops 42467328 | bytes 28311552 | tf_op jit(solution)/shard_map/convert_element_type | solution.py:155
  269.4 49.7 %all-to-all-done.2 = bf16[32,36,2176]{2,1,0:T(8,128)(2,1)} async-done(((bf16[32,36,2176]{2,1,0:T(8,128)(2,1)}), bf16[32,36,2176]{2,1,0:T(8,128)(2,1)}, u32[]{:S(2)}, u32[]{:S(2)}) %all-to-all-start.2) | async-done | bytes 5013536 | tf_op jit(solution)/shard_map/all_to_all | solution.py:108
  319.1 7.4 %reshape.358 = bf16[1152,2176]{1,0:T(8,128)(2,1)} reshape(bf16[32,36,2176]{2,1,0:T(8,128)(2,1)} %all-to-all-done.2) | data formatting | bytes 10027008 | tf_op jit(solution)/shard_map/reshape | solution.py:117
  329.3 4.0 %fusion.32 = bf16[128,2048]{1,0:T(8,128)(2,1)} fusion(pred[1152,128]{1,0:T(8,128)(4,1)S(1)} %copy-done.6, bf16[1152,2176]{1,0:T(8,128)(2,1)} %reshape.358), kind=kOutput, calls=%fused_computation.63 | convolution fusion | flops 604241920 | bytes 5390336 | tf_op jit(solution)/shard_map/dot_general | solution.py:121
  333.3 39.9 %collective-permute-done.1 = bf16[3,2,768,512]{3,2,1,0:T(8,128)(2,1)} collective-permute-done((bf16[3,2,768,512]{3,2,1,0:T(8,128)(2,1)}, bf16[3,2,768,512]{3,2,1,0:T(8,128)(2,1)}, u32[]{:S(2)}, u32[]{:S(2)}) %collective-permute-start.1) | collective-permute-done | bytes 4718624 | tf_op jit(solution)/shard_map/ppermute | solution.py:158
  373.3 7.6 %fusion.15 = bf16[512,3,2,768]{0,3,2,1:T(8,128)(2,1)} fusion(bf16[3,2,768,512]{3,2,1,0:T(8,128)(2,1)} %collective-permute-done.1, bf16[2,3,2,768,512]{4,3,2,1,0:T(8,128)(2,1)} %copy-done.2), kind=kLoop, calls=%fused_computation.22 | loop fusion | flops 9437184 | bytes 14155776 | tf_op jit(solution)/shard_map/transpose | solution.py:159
  380.9 12.4 %copy.87 = bf16[512,3,2,768]{3,2,1,0:T(2,128)(2,1)} copy(bf16[512,3,2,768]{0,3,2,1:T(8,128)(2,1)} %fusion.15) | data formatting | bytes 9437184
  (95 shorter events, 42.0 us)
Async XLA Ops:
  0.6 6.7 %copy-start = (bf16[128,2048]{1,0:T(8,128)(2,1)S(1)}, bf16[128,2048]{1,0:T(8,128)(2,1)}, u32[]{:S(2)}) copy-start(bf16[128,2048]{1,0:T(8,128)(2,1)} %param.7) | copy-start | bytes 1572868
  7.3 23.2 %copy-start.5 = (pred[1152,128]{1,0:T(8,128)(4,1)}, pred[1152,128]{1,0:T(8,128)(4,1)S(1)}, u32[]{:S(2)}) copy-start(pred[1152,128]{1,0:T(8,128)(4,1)S(1)} %fusion.18) | copy-start | bytes 442372
  18.1 10.9 %copy-start.14 = (f32[128,8]{0,1:T(8,128)S(1)}, f32[128,8]{0,1:T(8,128)}, u32[]{:S(2)}) copy-start(f32[128,8]{0,1:T(8,128)} %param.9) | copy-start | bytes 12292
  18.1 12.4 %copy-start.9 = (bf16[128,2048]{1,0:T(8,128)(2,1)S(1)}, bf16[128,2048]{1,0:T(8,128)(2,1)}, u32[]{:S(2)}) copy-start(bf16[128,2048]{1,0:T(8,128)(2,1)} %param.8) | copy-start | bytes 1572868
  18.1 80.6 %all-to-all-start.1 = ((bf16[32,36,2048]{2,1,0:T(8,128)(2,1)}), bf16[32,36,2048]{2,1,0:T(8,128)(2,1)}, u32[]{:S(2)}, u32[]{:S(2)}) async-start(bf16[32,36,2048]{2,1,0:T(8,128)(2,1)} %reshape.355), calls=%async_computation.1 | async-start | bytes 10485760 | tf_op jit(solution)/shard_map/all_to_all | solution.py:71
  29.1 5.0 %copy-start.7 = (f32[128,8]{1,0:T(8,128)}, f32[128,8]{1,0:T(8,128)S(1)}, u32[]{:S(2)}) copy-start(f32[128,8]{1,0:T(8,128)S(1)} %copy.75) | copy-start | bytes 12292
  30.0 11.4 %copy-start.10 = (s32[1024]{0:T(1024)}, s32[1024]{0:T(1024)S(1)}, u32[]{:S(2)}) copy-start(s32[1024]{0:T(1024)S(1)} %fusion.82) | copy-start | bytes 12292
  98.7 80.1 %all-to-all-start = ((bf16[32,36,2048]{2,1,0:T(8,128)(2,1)}), bf16[32,36,2048]{2,1,0:T(8,128)(2,1)}, u32[]{:S(2)}, u32[]{:S(2)}) async-start(bf16[32,36,2048]{2,1,0:T(8,128)(2,1)} %reshape.353), calls=%async_computation | async-start | bytes 10485760 | tf_op jit(solution)/shard_map/all_to_all | solution.py:78
  109.7 15.4 %slice-start.4 = ((s8[6291456]{0:T(1024)(128)(4,1)}), s8[4194304]{0:T(1024)(128)(4,1)S(1)}, s32[]{:S(2)}) async-start(s8[6291456]{0:T(1024)(128)(4,1)} %bitcast.194), calls=%async_computation.7 | async-start | bytes 8388608
  114.9 10.1 %copy-start.3 = (bf16[32,36,2048]{2,0,1:T(8,128)(2,1)}, bf16[32,36,2048]{2,0,1:T(8,128)(2,1)S(1)}, u32[]{:S(2)}) copy-start(bf16[32,36,2048]{2,0,1:T(8,128)(2,1)S(1)} %copy.78) | copy-start | bytes 14155780
  114.9 10.1 %slice-start.5 = ((s8[6291456]{0:T(1024)(128)(4,1)}), s8[2097152]{0:T(1024)(128)(4,1)S(1)}, s32[]{:S(2)}) async-start(s8[6291456]{0:T(1024)(128)(4,1)} %bitcast.194), calls=%async_computation.8 | async-start | bytes 4194304
  178.8 5.2 %copy-start.17 = (f32[2,32,18,768]{3,1,2,0:T(8,128)S(1)}, f32[2,32,18,768]{3,1,2,0:T(8,128)}, u32[]{:S(2)}) copy-start(f32[2,32,18,768]{3,1,2,0:T(8,128)} %fusion.11) | copy-start | bytes 10616836
  184.0 12.3 %copy-start.4 = (bf16[32,36,2048]{2,0,1:T(8,128)(2,1)}, bf16[32,36,2048]{2,0,1:T(8,128)(2,1)S(1)}, u32[]{:S(2)}) copy-start(bf16[32,36,2048]{2,0,1:T(8,128)(2,1)S(1)} %copy.76) | copy-start | bytes 14155780
  194.9 5.1 %copy-start.15 = (bf16[32,2,18,768]{3,0,2,1:T(8,128)(2,1)}, bf16[32,2,18,768]{3,0,2,1:T(8,128)(2,1)S(1)}, u32[]{:S(2)}) copy-start(bf16[32,2,18,768]{3,0,2,1:T(8,128)(2,1)S(1)} %get-tuple-element.20) | copy-start | bytes 5308420
  209.0 47.7 %collective-permute-start = (bf16[2,3,2,768,512]{4,3,2,1,0:T(8,128)(2,1)}, bf16[2,3,2,768,512]{4,3,2,1,0:T(8,128)(2,1)}, u32[]{:S(2)}, u32[]{:S(2)}) collective-permute-start(bf16[2,3,2,768,512]{4,3,2,1,0:T(8,128)(2,1)} %maximum_maximum_fusion), channel_id=1, source_target_pairs={{0,32},{32,0},{1,33},{33,1},{2,34},{34,2},{3,35},{35,3},{4,36},{36... | collective-permute-start | bytes 28311560 | tf_op jit(solution)/shard_map/ppermute | solution.py:154
  233.6 14.4 %slice-start.2 = ((s8[4718592]{0:T(1024)(128)(4,1)}), s8[524288]{0:T(1024)(128)(4,1)S(1)}, s32[]{:S(2)}) async-start(s8[4718592]{0:T(1024)(128)(4,1)} %bitcast.180), calls=%async_computation.5 | async-start | bytes 1048576
  233.6 85.5 %all-to-all-start.2 = ((bf16[32,36,2176]{2,1,0:T(8,128)(2,1)}), bf16[32,36,2176]{2,1,0:T(8,128)(2,1)}, u32[]{:S(2)}, u32[]{:S(2)}) async-start(bf16[32,36,2176]{2,1,0:T(8,128)(2,1)} %copy.85), calls=%async_computation.2 | async-start | bytes 11141120 | tf_op jit(solution)/shard_map/all_to_all | solution.py:108
  263.6 5.1 %copy-start.2 = (bf16[2,3,2,768,512]{4,3,2,1,0:T(8,128)(2,1)}, bf16[2,3,2,768,512]{4,3,2,1,0:T(8,128)(2,1)S(1)}, u32[]{:S(2)}) copy-start(bf16[2,3,2,768,512]{4,3,2,1,0:T(8,128)(2,1)S(1)} %add_convert_fusion) | copy-start | bytes 28311556
  268.7 59.0 %copy-start.11 = (s32[1024]{0:T(1024)S(1)}, s32[1024]{0:T(1024)}, u32[]{:S(2)}) copy-start(s32[1024]{0:T(1024)} %copy-done.10) | copy-start | bytes 12292
  268.7 59.8 %copy-start.8 = (f32[128,8]{1,0:T(8,128)S(1)}, f32[128,8]{1,0:T(8,128)}, u32[]{:S(2)}) copy-start(f32[128,8]{1,0:T(8,128)} %copy-done.7) | copy-start | bytes 12292
  268.7 59.8 %copy-start.13 = (f32[128]{0:T(128)S(1)}, f32[128]{0:T(128)}, u32[]{:S(2)}) copy-start(f32[128]{0:T(128)} %copy-done.12) | copy-start | bytes 1540
  268.7 60.6 %copy-start.6 = (pred[1152,128]{1,0:T(8,128)(4,1)S(1)}, pred[1152,128]{1,0:T(8,128)(4,1)}, u32[]{:S(2)}) copy-start(pred[1152,128]{1,0:T(8,128)(4,1)} %copy-done.5) | copy-start | bytes 442372
  268.7 104.6 %collective-permute-start.1 = (bf16[3,2,768,512]{3,2,1,0:T(8,128)(2,1)}, bf16[3,2,768,512]{3,2,1,0:T(8,128)(2,1)}, u32[]{:S(2)}, u32[]{:S(2)}) collective-permute-start(bf16[3,2,768,512]{3,2,1,0:T(8,128)(2,1)} %slice_bitcast_fusion), channel_id=1, source_target_pairs={{0,64},{64,0},{1,65},{65,1},{2,66},{66,2},{3,67},{67,3},{4,68},{68... | collective-permute-start | bytes 14155784 | tf_op jit(solution)/shard_map/ppermute | solution.py:158
  373.3 20.0 %copy-start.1 = (bf16[128,2048]{1,0:T(8,128)(2,1)S(1)}, bf16[128,2048]{1,0:T(8,128)(2,1)}, u32[]{:S(2)}) copy-start(bf16[128,2048]{1,0:T(8,128)(2,1)} %param.7) | copy-start | bytes 1572868
  (7 other events, 16.2 us)

commit v6 on v5

--- a/solution.py
+++ b/solution.py
@@ -62,26 +62,22 @@
     dispatch = token_hit.astype(jnp.bfloat16)
     slot_weight = jnp.sum(jnp.where(pair_hit, flat_weights[None, :], 0.0), axis=1)
 
-    send_shape = (owners, local_experts * capacity, model_width)
+    send_shape = (owners, local_experts * capacity, 2 * model_width)
     send_tokens = jnp.dot(dispatch, tokens_in, preferred_element_type=jnp.float32).astype(
         jnp.bfloat16
     )
     send_grads = jnp.dot(dispatch, out_grad, preferred_element_type=jnp.float32)
     send_scaled = (slot_weight[:, None] * send_grads).astype(jnp.bfloat16)
-    recv_tokens = lax.all_to_all(
-        send_tokens.reshape(send_shape), ("xlo", "expert"),
+    recv = lax.all_to_all(
+        jnp.concatenate([send_tokens, send_scaled], axis=1).reshape(send_shape),
+        ("xlo", "expert"),
         split_axis=0,
         concat_axis=0,
         tiled=True,
         axis_index_groups=groups,
     )
-    recv_scaled = lax.all_to_all(
-        send_scaled.reshape(send_shape), ("xlo", "expert"),
-        split_axis=0,
-        concat_axis=0,
-        tiled=True,
-        axis_index_groups=groups,
-    )
+    recv_tokens = recv[..., :model_width]
+    recv_scaled = recv[..., model_width:]
     block_shape = (owners, local_experts, capacity, model_width)
     recv_tokens = recv_tokens.reshape(block_shape)
     recv_scaled = recv_scaled.reshape(block_shape)
@@ -128,38 +124,31 @@
 
     block_count = xlo_count * core_count
     block_rows = model_width // block_count
-    blocks = []
-    for xlo_side, core_side in ((1, 1), (0, 1), (1, 0), (0, 0)):
-        block = (xlo ^ xlo_side) * core_count + (core ^ core_side)
-        tokens_rows = lax.dynamic_slice_in_dim(recv_tokens, block * block_rows, block_rows, 3)
-        scaled_rows = lax.dynamic_slice_in_dim(recv_scaled, block * block_rows, block_rows, 3)
-        blocks.append(
-            jnp.stack(
-                [
-                    jnp.einsum(
-                        "nemh,nemd->ehd", gate_grad, tokens_rows, preferred_element_type=jnp.float32
-                    ),
-                    jnp.einsum(
-                        "nemh,nemd->ehd", up_grad, tokens_rows, preferred_element_type=jnp.float32
-                    ),
-                    jnp.einsum(
-                        "nemh,nemd->ehd", hidden, scaled_rows, preferred_element_type=jnp.float32
-                    ),
-                ]
-            ).astype(jnp.bfloat16)
-        )
-
     core_pairs = [(i, (i + 1) % core_count) for i in range(core_count)]
     xlo_pairs = [(i, (i + 1) % xlo_count) for i in range(xlo_count)]
-    from_sibling = lax.ppermute(jnp.stack(blocks[:2]), "core", core_pairs)
-    summed = (jnp.stack(blocks[2:]).astype(jnp.float32) + from_sibling.astype(jnp.float32)).astype(
-        jnp.bfloat16
-    )
-    theirs = lax.ppermute(summed[0], "xlo", xlo_pairs)
-    shares = jnp.transpose(
-        (summed[1].astype(jnp.float32) + theirs.astype(jnp.float32)).astype(jnp.bfloat16),
-        (3, 0, 1, 2),
-    )
+    order = ((1, 1), (0, 1), (1, 0), (0, 0))
+    starts = [((xlo ^ a) * core_count + (core ^ c)) * block_rows for a, c in order]
+    shares = []
+    for left, right in ((gate_grad, recv_tokens), (up_grad, recv_tokens), (hidden, recv_scaled)):
+        blocks = [
+            jnp.einsum(
+                "nemh,nemd->ehd",
+                left,
+                lax.dynamic_slice_in_dim(right, at, block_rows, 3),
+                preferred_element_type=jnp.float32,
+            ).astype(jnp.bfloat16)
+            for at in starts
+        ]
+        from_sibling = lax.ppermute(jnp.stack(blocks[:2]), "core", core_pairs)
+        summed = (
+            jnp.stack(blocks[2:]).astype(jnp.float32) + from_sibling.astype(jnp.float32)
+        ).astype(jnp.bfloat16)
+        theirs = lax.ppermute(jnp.transpose(summed[0], (2, 0, 1)), "xlo", xlo_pairs)
+        mine = jnp.transpose(summed[1], (2, 0, 1))
+        shares.append(
+            (mine.astype(jnp.float32) + theirs.astype(jnp.float32)).astype(jnp.bfloat16)
+        )
+    shares = jnp.stack(shares, axis=1)
     return (input_grad, router_grad, shares)
 
 

time: 401 us -> 463 us (1.15)
  waiting for transfers between devices: 195 us -> 239 us
  starting transfers between devices: 33.7 us -> 45.2 us
  other arithmetic: 27.4 us -> 33 us
    ppermute x1 -> x3, waiting for transfers between devices: 39.9 us -> 92.9 us  [per_device(): theirs = lax.ppermute(jnp.transpose(summed[0], (2, 0, 1)), 'xlo', xlo_pairs)]
    all_to_all x1, waiting for transfers between devices: 49.7 us -> 0.01 us  [per_device(): lax.all_to_all(jnp.concatenate([row_grad, prob_cols], axis=3).reshape(own...]
    all_to_all x2 -> x1, waiting for transfers between devices: 105 us -> 146 us  [per_device(): lax.all_to_all(jnp.concatenate([send_tokens, send_scaled], axis=1).reshap...]
    slice x0 -> x3, local copies, waits for them, and re-layouts: none -> 18.2 us  [the longest x2 15.4 us: per_device(): recv_tokens = recv[..., :model_width]]
    all_to_all x1, starting transfers between devices: 10.9 us -> 24.6 us  [per_device(): lax.all_to_all(jnp.concatenate([row_grad, prob_cols], axis=3).reshape(own...]
    all_to_all x2 -> x1, starting transfers between devices: 21.8 us -> 11.2 us  [per_device(): lax.all_to_all(jnp.concatenate([send_tokens, send_scaled], axis=1).reshap...]
    all_to_all x2 -> x0, local copies, waits for them, and re-layouts: 10.4 us -> none  [the longest x1 5.22 us: per_device(): lax.all_to_all(send_tokens.reshape(send_shape), ('xlo', 'expert'), split_...]
    ppermute x1 -> x3, starting transfers between devices: 0.74 us -> 8.91 us  [per_device(): theirs = lax.ppermute(jnp.transpose(summed[0], (2, 0, 1)), 'xlo', xlo_pairs)]
  transfers between devices with their start and end apart: 5 -> 8, of which waited for: 4 -> 4; matrix products, arithmetic and copies ran while one was open for 24% -> 11% of each run, Pallas kernels for 0% -> 0%
where the time goes in v6:
time: 463 us; the launch traced here: 456 us
  waiting for transfers between devices  239 us (52%)
  matrix products  77.1 us (17%)
  local copies, waits for them, and re-layouts  59.4 us (13%)
  starting transfers between devices  45.2 us (10%)
  other arithmetic  33 us (7%)
    all_to_all x1, waiting for transfers between devices, per_device(): lax.all_to_all(jnp.concatenate([send_tokens, send_scaled], axis=1).reshap...  146 us
    ppermute x3, waiting for transfers between devices, per_device(): theirs = lax.ppermute(jnp.transpose(summed[0], (2, 0, 1)), 'xlo', xlo_pairs)  92.9 us
    all_to_all x1, starting transfers between devices, per_device(): lax.all_to_all(jnp.concatenate([row_grad, prob_cols], axis=3).reshape(own...  24.6 us
    dot_general x12, matrix products, per_device(): jnp.einsum('nemh,nemd->ehd', left, lax.dynamic_slice_in_dim(right, at, bl...  24.3 us
    slice x2, local copies, waits for them, and re-layouts, per_device(): recv_tokens = recv[..., :model_width]  15.4 us
    unnamed x57, local copies, waits for them, and re-layouts  15.4 us
    reshape x1, local copies, waits for them, and re-layouts, per_device(): jnp.concatenate([send_tokens, send_scaled], axis=1).reshape(send_shape)  13.2 us
    dot_general x1, matrix products, per_device(): jnp.einsum('nemd,deh->nemh', recv_scaled, w_down, preferred_element_type=...  12.1 us
  transfers between devices with their start and end apart: 8, of which 4 were waited for; matrix products, arithmetic and copies ran while one was open for 11% of the time, Pallas kernels for 0%

profile of v6, /device:TPU:0, one launch (start us, length us, event | category | flops | bytes accessed | tf_op | source)
XLA Modules:
  0.0 455.6 jit_solution(174528777755860220)
XLA Ops:
  4.8 4.2 fusion.16
  12.4 4.4 pad_maximum_fusion
  16.8 13.2 %reshape.162 = bf16[32,36,4096]{2,1,0:T(8,128)(2,1)} reshape(bf16[1152,4096]{1,0:T(8,128)(2,1)} %pad_maximum_fusion) | data formatting | bytes 18874368 | tf_op jit(solution)/shard_map/reshape | solution.py:72
  29.9 11.2 %all-to-all-start = ((bf16[32,36,4096]{2,1,0:T(8,128)(2,1)}), bf16[32,36,4096]{2,1,0:T(8,128)(2,1)}, u32[]{:S(2)}, u32[]{:S(2)}) async-start(bf16[32,36,4096]{2,1,0:T(8,128)(2,1)} %reshape.162), calls=%async_computation | async-start | bytes 20971520 | tf_op jit(solution)/shard_map/all_to_all | solution.py:71
  41.1 146.2 %all-to-all-done = bf16[32,36,4096]{2,1,0:T(8,128)(2,1)} async-done(((bf16[32,36,4096]{2,1,0:T(8,128)(2,1)}), bf16[32,36,4096]{2,1,0:T(8,128)(2,1)}, u32[]{:S(2)}, u32[]{:S(2)}) %all-to-all-start) | async-done | bytes 9437216 | tf_op jit(solution)/shard_map/all_to_all | solution.py:71
  187.3 10.2 %fusion.115 = (bf16[32,36,2048]{2,1,0:T(8,128)(2,1)}, bf16[32,36,2048]{2,1,0:T(8,128)(2,1)}) fusion(bf16[32,36,4096]{2,1,0:T(8,128)(2,1)} %all-to-all-done), kind=kLoop, calls=%fused_computation.197 | loop fusion | bytes 18874368 | tf_op jit(solution)/shard_map/slice | solution.py:79
  197.5 5.2 %copy.78 = bf16[32,36,2048]{2,0,1:T(8,128)(2,1)S(1)} copy(bf16[32,36,2048]{2,1,0:T(8,128)(2,1)} %get-tuple-element.21) | data formatting | bytes 9437184 | tf_op jit(solution)/shard_map/slice | solution.py:79
  202.7 8.6 %fusion.10 = f32[2,32,18,768]{3,1,2,0:T(8,128)} fusion(bf16[32,2,18,2048]{3,0,2,1:T(8,128)(2,1)S(1)} %bitcast.227, bf16[2048,2,768,1]{2,1,0,3:T(2,128)(2,1)} %bitcast.243), kind=kOutput, calls=%fused_computation.18 | convolution fusion | flops 3623878656 | bytes 14548992 | tf_op jit(solution)/shard_map/nemd,deh->nemh/dot_general | solution.py:86
  211.4 5.7 %fusion.6 = f32[2,32,18,768]{3,1,2,0:T(8,128)} fusion(bf16[32,2,18,2048]{3,0,2,1:T(8,128)(2,1)S(1)} %bitcast.228, bf16[2048,2,768,1]{2,1,0,3:T(2,128)(2,1)S(1)} %bitcast.242), kind=kOutput, calls=%fused_computation.14 | convolution fusion | flops 3623878656 | bytes 14548992 | tf_op jit(solution)/shard_map/nemd,deh->nemh/dot_general | solution.py:85
  219.8 12.1 %fusion.29 = (bf16[32,2,18]{0,2,1:T(8,128)(2,1)S(1)}, bf16[32,2,18,768]{3,0,2,1:T(8,128)(2,1)}, bf16[32,2,18,768]{3,0,2,1:T(8,128)(2,1)S(1)}, bf16[32,2,18,768]{3,0,2,1:T(8,128)(2,1)S(1)}) fusion(f32[2,32,18,768]{3,1,2,0:T(8,128)} %fusion.10, f32[2,32,18,768]{3,1,2,0:T(8,128)} %fusion.6, bf16[32,2,18,2048]{3,0,2,1:T(8,128)(2,1)S(1)} %bitcast.222, ...), kind=kOutput, calls=%fused_computation.48 | convolution fusion | flops 3639802880 | bytes 23398656 | tf_op jit(solution)/shard_map/nemd,deh->nemh/dot_general | solution.py:90
  250.2 9.1 %fusion.4 = f32[2,32,18,2048]{3,1,2,0:T(8,128)} fusion(bf16[32,2,18,768]{3,0,2,1:T(8,128)(2,1)S(1)} %copy-done.19, bf16[2048,2,768,1]{2,1,0,3:T(2,128)(2,1)} %bitcast.239), kind=kOutput, calls=%fused_computation.12 | convolution fusion | flops 3623878656 | bytes 17498112 | tf_op jit(solution)/shard_map/nemh,deh->nemd/dot_general | solution.py:99
  265.6 9.8 %fusion.13 = bf16[32,2,18,2048]{3,0,2,1:T(8,128)(2,1)} fusion(f32[2,32,18,2048]{3,1,2,0:T(8,128)} %fusion.4, bf16[32,2,18,768]{3,0,2,1:T(8,128)(2,1)S(1)} %copy-done.17, bf16[2048,2,768,1]{2,1,0,3:T(2,128)(2,1)} %bitcast.244), kind=kOutput, calls=%fused_computation.21 | convolution fusion | flops 3628597248 | bytes 22216704 | tf_op jit(solution)/shard_map/nemh,deh->nemd/dot_general | solution.py:100
  275.7 2.9 fusion.12
  278.6 4.2 copy.85
  282.8 24.6 %all-to-all-start.1 = ((bf16[32,36,2176]{2,1,0:T(8,128)(2,1)}), bf16[32,36,2176]{2,1,0:T(8,128)(2,1)}, u32[]{:S(2)}, u32[]{:S(2)}) async-start(bf16[32,36,2176]{2,1,0:T(8,128)(2,1)} %copy.85), calls=%async_computation.1 | async-start | bytes 11141120 | tf_op jit(solution)/shard_map/all_to_all | solution.py:104
  307.4 3.4 fusion.50
  316.7 6.7 %collective-permute-start.1 = (bf16[512,2,768]{0,2,1:T(8,128)(2,1)S(1)}, bf16[512,2,768]{0,2,1:T(8,128)(2,1)S(1)}, u32[]{:S(2)}, u32[]{:S(2)}) collective-permute-start(bf16[512,2,768]{0,2,1:T(8,128)(2,1)S(1)} %slice_bitcast_fusion.4), channel_id=1, source_target_pairs={{0,64},{64,0},{1,65},{65,1},{2,66},{66,2},{3,67},{67,3},{4,68},{68... | collective-permute-start | bytes 4718600 | tf_op jit(solution)/shard_map/ppermute | solution.py:146
  327.6 2.9 add_convert_fusion.1
  331.5 27.1 %collective-permute-done.1 = bf16[512,2,768]{0,2,1:T(8,128)(2,1)S(1)} collective-permute-done((bf16[512,2,768]{0,2,1:T(8,128)(2,1)S(1)}, bf16[512,2,768]{0,2,1:T(8,128)(2,1)S(1)}, u32[]{:S(2)}, u32[]{:S(2)}) %collective-permute-start.1) | collective-permute-done | bytes 1572896 | tf_op jit(solution)/shard_map/ppermute | solution.py:146
  359.1 33.3 %collective-permute-done.3 = bf16[512,2,768]{0,2,1:T(8,128)(2,1)S(1)} collective-permute-done((bf16[512,2,768]{0,2,1:T(8,128)(2,1)S(1)}, bf16[512,2,768]{0,2,1:T(8,128)(2,1)S(1)}, u32[]{:S(2)}, u32[]{:S(2)}) %collective-permute-start.3) | collective-permute-done | bytes 1572896 | tf_op jit(solution)/shard_map/ppermute | solution.py:146
  392.8 32.6 %collective-permute-done.5 = bf16[512,2,768]{0,2,1:T(8,128)(2,1)S(1)} collective-permute-done((bf16[512,2,768]{0,2,1:T(8,128)(2,1)S(1)}, bf16[512,2,768]{0,2,1:T(8,128)(2,1)S(1)}, u32[]{:S(2)}, u32[]{:S(2)}) %collective-permute-start.5) | collective-permute-done | bytes 1572896 | tf_op jit(solution)/shard_map/ppermute | solution.py:146
  428.2 12.4 %copy.87 = bf16[512,3,2,768]{3,2,1,0:T(2,128)(2,1)} copy(bf16[512,3,2,768]{0,3,2,1:T(8,128)(2,1)} %pad_maximum_fusion.1) | data formatting | bytes 9437184
  440.7 7.6 %reshape.166 = bf16[1152,2176]{1,0:T(8,128)(2,1)} reshape(bf16[32,36,2176]{2,1,0:T(8,128)(2,1)} %all-to-all-done.1) | data formatting | bytes 10027008 | tf_op jit(solution)/shard_map/reshape | solution.py:113
  449.4 4.1 fusion.36
  (110 shorter events, 52.4 us)
Async XLA Ops:
  0.6 8.9 %copy-start = (bf16[128,2048]{1,0:T(8,128)(2,1)S(1)}, bf16[128,2048]{1,0:T(8,128)(2,1)}, u32[]{:S(2)}) copy-start(bf16[128,2048]{1,0:T(8,128)(2,1)} %param.7) | copy-start | bytes 1572868
  2.3 8.7 %copy-start.11 = (s32[1024]{0:T(1024)}, s32[1024]{0:T(1024)S(1)}, u32[]{:S(2)}) copy-start(s32[1024]{0:T(1024)S(1)} %fusion.89) | copy-start | bytes 12292
  3.1 7.9 %copy-start.8 = (f32[128,8]{1,0:T(8,128)}, f32[128,8]{1,0:T(8,128)S(1)}, u32[]{:S(2)}) copy-start(f32[128,8]{1,0:T(8,128)S(1)} %copy.75) | copy-start | bytes 12292
  29.9 157.4 %all-to-all-start = ((bf16[32,36,4096]{2,1,0:T(8,128)(2,1)}), bf16[32,36,4096]{2,1,0:T(8,128)(2,1)}, u32[]{:S(2)}, u32[]{:S(2)}) async-start(bf16[32,36,4096]{2,1,0:T(8,128)(2,1)} %reshape.162), calls=%async_computation | async-start | bytes 20971520 | tf_op jit(solution)/shard_map/all_to_all | solution.py:71
  197.5 13.9 %slice-start.2 = ((s8[6291456]{0:T(1024)(128)(4,1)}), s8[4194304]{0:T(1024)(128)(4,1)S(1)}, s32[]{:S(2)}) async-start(s8[6291456]{0:T(1024)(128)(4,1)} %bitcast.240), calls=%async_computation.4 | async-start | bytes 8388608
  202.7 8.7 %slice-start.3 = ((s8[6291456]{0:T(1024)(128)(4,1)}), s8[2097152]{0:T(1024)(128)(4,1)S(1)}, s32[]{:S(2)}) async-start(s8[6291456]{0:T(1024)(128)(4,1)} %bitcast.240), calls=%async_computation.5 | async-start | bytes 4194304
  202.7 14.3 %slice-start = ((s8[5242880]{0:T(1024)(128)(4,1)}), s8[4194304]{0:T(1024)(128)(4,1)S(1)}, s32[]{:S(2)}) async-start(s8[5242880]{0:T(1024)(128)(4,1)} %bitcast.219), calls=%async_computation.2 | async-start | bytes 8388608
  211.4 5.7 %slice-start.1 = ((s8[5242880]{0:T(1024)(128)(4,1)}), s8[1048576]{0:T(1024)(128)(4,1)S(1)}, s32[]{:S(2)}) async-start(s8[5242880]{0:T(1024)(128)(4,1)} %bitcast.219), calls=%async_computation.3 | async-start | bytes 2097152
  219.8 28.6 %copy-start.2 = (bf16[32,36,2048]{2,0,1:T(8,128)(2,1)}, bf16[32,36,2048]{2,0,1:T(8,128)(2,1)S(1)}, u32[]{:S(2)}) copy-start(bf16[32,36,2048]{2,0,1:T(8,128)(2,1)S(1)} %copy.76) | copy-start | bytes 14155780
  232.0 4.3 copy-start.15
  261.2 52.5 %collective-permute-start = (bf16[2,2,768,512]{3,2,1,0:T(8,128)(2,1)}, bf16[2,2,768,512]{3,2,1,0:T(8,128)(2,1)}, u32[]{:S(2)}, u32[]{:S(2)}) collective-permute-start(bf16[2,2,768,512]{3,2,1,0:T(8,128)(2,1)} %pad_maximum_fusion.2), channel_id=1, source_target_pairs={{0,32},{32,0},{1,33},{33,1},{2,34},{34,2},{3,35},{35,3},{4,36},{36... | collective-permute-start | bytes 9437192 | tf_op jit(solution)/shard_map/ppermute | solution.py:142
  263.1 60.3 %collective-permute-start.2 = (bf16[2,2,768,512]{3,2,1,0:T(8,128)(2,1)}, bf16[2,2,768,512]{3,2,1,0:T(8,128)(2,1)}, u32[]{:S(2)}, u32[]{:S(2)}) collective-permute-start(bf16[2,2,768,512]{3,2,1,0:T(8,128)(2,1)} %pad_maximum_fusion.3), channel_id=1, source_target_pairs={{0,32},{32,0},{1,33},{33,1},{2,34},{34,2},{3,35},{35,3},{4,36},{36... | collective-permute-start | bytes 9437192 | tf_op jit(solution)/shard_map/ppermute | solution.py:142
  265.6 62.1 %collective-permute-start.4 = (bf16[2,2,768,512]{3,2,1,0:T(8,128)(2,1)}, bf16[2,2,768,512]{3,2,1,0:T(8,128)(2,1)}, u32[]{:S(2)}, u32[]{:S(2)}) collective-permute-start(bf16[2,2,768,512]{3,2,1,0:T(8,128)(2,1)} %pad_maximum_fusion.4), channel_id=1, source_target_pairs={{0,32},{32,0},{1,33},{33,1},{2,34},{34,2},{3,35},{35,3},{4,36},{36... | collective-permute-start | bytes 9437192 | tf_op jit(solution)/shard_map/ppermute | solution.py:142
  282.8 157.9 %all-to-all-start.1 = ((bf16[32,36,2176]{2,1,0:T(8,128)(2,1)}), bf16[32,36,2176]{2,1,0:T(8,128)(2,1)}, u32[]{:S(2)}, u32[]{:S(2)}) async-start(bf16[32,36,2176]{2,1,0:T(8,128)(2,1)} %copy.85), calls=%async_computation.1 | async-start | bytes 11141120 | tf_op jit(solution)/shard_map/all_to_all | solution.py:104
  307.4 3.4 copy-start.21
  316.6 6.9 %copy-start.5 = (bf16[1,2,768,512]{3,2,1,0:T(8,128)(2,1)S(1)}, bf16[1,2,768,512]{3,2,1,0:T(8,128)(2,1)}, u32[]{:S(2)}) copy-start(bf16[1,2,768,512]{3,2,1,0:T(8,128)(2,1)} %fusion.47) | copy-start | bytes 4718596
  316.7 41.9 %collective-permute-start.1 = (bf16[512,2,768]{0,2,1:T(8,128)(2,1)S(1)}, bf16[512,2,768]{0,2,1:T(8,128)(2,1)S(1)}, u32[]{:S(2)}, u32[]{:S(2)}) collective-permute-start(bf16[512,2,768]{0,2,1:T(8,128)(2,1)S(1)} %slice_bitcast_fusion.4), channel_id=1, source_target_pairs={{0,64},{64,0},{1,65},{65,1},{2,66},{66,2},{3,67},{67,3},{4,68},{68... | collective-permute-start | bytes 4718600 | tf_op jit(solution)/shard_map/ppermute | solution.py:146
  326.4 66.0 %collective-permute-start.3 = (bf16[512,2,768]{0,2,1:T(8,128)(2,1)S(1)}, bf16[512,2,768]{0,2,1:T(8,128)(2,1)S(1)}, u32[]{:S(2)}, u32[]{:S(2)}) collective-permute-start(bf16[512,2,768]{0,2,1:T(8,128)(2,1)S(1)} %slice_bitcast_fusion.2), channel_id=1, source_target_pairs={{0,64},{64,0},{1,65},{65,1},{2,66},{66,2},{3,67},{67,3},{4,68},{68... | collective-permute-start | bytes 4718600 | tf_op jit(solution)/shard_map/ppermute | solution.py:146
  330.6 94.7 %collective-permute-start.5 = (bf16[512,2,768]{0,2,1:T(8,128)(2,1)S(1)}, bf16[512,2,768]{0,2,1:T(8,128)(2,1)S(1)}, u32[]{:S(2)}, u32[]{:S(2)}) collective-permute-start(bf16[512,2,768]{0,2,1:T(8,128)(2,1)S(1)} %slice_bitcast_fusion), channel_id=1, source_target_pairs={{0,64},{64,0},{1,65},{65,1},{2,66},{66,2},{3,67},{67,3},{4,68},{68... | collective-permute-start | bytes 4718600 | tf_op jit(solution)/shard_map/ppermute | solution.py:146
  440.6 8.8 %copy-start.4 = (pred[1152,128]{1,0:T(8,128)(4,1)S(1)}, pred[1152,128]{1,0:T(8,128)(4,1)}, u32[]{:S(2)}) copy-start(pred[1152,128]{1,0:T(8,128)(4,1)} %copy-done.3) | copy-start | bytes 442372
  448.2 6.9 %copy-start.1 = (bf16[128,2048]{1,0:T(8,128)(2,1)S(1)}, bf16[128,2048]{1,0:T(8,128)(2,1)}, u32[]{:S(2)}) copy-start(bf16[128,2048]{1,0:T(8,128)(2,1)} %param.7) | copy-start | bytes 1572868
  449.4 4.1 copy-start.12
  449.4 4.9 %copy-start.9 = (f32[128,8]{1,0:T(8,128)S(1)}, f32[128,8]{1,0:T(8,128)}, u32[]{:S(2)}) copy-start(f32[128,8]{1,0:T(8,128)} %copy-done.8) | copy-start | bytes 12292
  449.4 4.9 %copy-start.14 = (f32[128]{0:T(128)S(1)}, f32[128]{0:T(128)}, u32[]{:S(2)}) copy-start(f32[128]{0:T(128)} %copy-done.13) | copy-start | bytes 1540
  (10 other events, 20.3 us)

commit v7 on v5

--- a/solution.py
+++ b/solution.py
@@ -99,6 +99,43 @@
         hidden_grad * up_pre * sigmoid_gate * (1.0 + gate_pre * (1.0 - sigmoid_gate))
     ).astype(jnp.bfloat16)
     up_grad = (hidden_grad * active).astype(jnp.bfloat16)
+    block_count = xlo_count * core_count
+    block_rows = model_width // block_count
+    blocks = []
+    for xlo_side, core_side in ((1, 1), (0, 1), (1, 0), (0, 0)):
+        block = (xlo ^ xlo_side) * core_count + (core ^ core_side)
+        tokens_rows = lax.dynamic_slice_in_dim(recv_tokens, block * block_rows, block_rows, 3)
+        scaled_rows = lax.dynamic_slice_in_dim(recv_scaled, block * block_rows, block_rows, 3)
+        blocks.append(
+            jnp.stack(
+                [
+                    jnp.einsum(
+                        "nemh,nemd->ehd", gate_grad, tokens_rows, preferred_element_type=jnp.float32
+                    ),
+                    jnp.einsum(
+                        "nemh,nemd->ehd", up_grad, tokens_rows, preferred_element_type=jnp.float32
+                    ),
+                    jnp.einsum(
+                        "nemh,nemd->ehd", hidden, scaled_rows, preferred_element_type=jnp.float32
+                    ),
+                ]
+            ).astype(jnp.bfloat16)
+        )
+
+    to_sibling, own_blocks, gate_grad, up_grad = lax.optimization_barrier(
+        (jnp.stack(blocks[:2]), jnp.stack(blocks[2:]), gate_grad, up_grad)
+    )
+
+    core_pairs = [(i, (i + 1) % core_count) for i in range(core_count)]
+    xlo_pairs = [(i, (i + 1) % xlo_count) for i in range(xlo_count)]
+    from_sibling = lax.ppermute(to_sibling, "core", core_pairs)
+    summed = (own_blocks.astype(jnp.float32) + from_sibling.astype(jnp.float32)).astype(
+        jnp.bfloat16
+    )
+    theirs = lax.ppermute(jnp.transpose(summed[0], (3, 0, 1, 2)), "xlo", xlo_pairs)
+    mine = jnp.transpose(summed[1], (3, 0, 1, 2))
+    shares = (mine.astype(jnp.float32) + theirs.astype(jnp.float32)).astype(jnp.bfloat16)
+
     row_grad = (
         jnp.einsum("nemh,deh->nemd", gate_grad, w_gate, preferred_element_type=jnp.float32)
         + jnp.einsum("nemh,deh->nemd", up_grad, w_up, preferred_element_type=jnp.float32)
@@ -126,40 +163,6 @@
     ).reshape(tok_rows, topk_count)
     router_grad = pair_probs - weights * jnp.sum(pair_probs, axis=1, keepdims=True)
 
-    block_count = xlo_count * core_count
-    block_rows = model_width // block_count
-    blocks = []
-    for xlo_side, core_side in ((1, 1), (0, 1), (1, 0), (0, 0)):
-        block = (xlo ^ xlo_side) * core_count + (core ^ core_side)
-        tokens_rows = lax.dynamic_slice_in_dim(recv_tokens, block * block_rows, block_rows, 3)
-        scaled_rows = lax.dynamic_slice_in_dim(recv_scaled, block * block_rows, block_rows, 3)
-        blocks.append(
-            jnp.stack(
-                [
-                    jnp.einsum(
-                        "nemh,nemd->ehd", gate_grad, tokens_rows, preferred_element_type=jnp.float32
-                    ),
-                    jnp.einsum(
-                        "nemh,nemd->ehd", up_grad, tokens_rows, preferred_element_type=jnp.float32
-                    ),
-                    jnp.einsum(
-                        "nemh,nemd->ehd", hidden, scaled_rows, preferred_element_type=jnp.float32
-                    ),
-                ]
-            ).astype(jnp.bfloat16)
-        )
-
-    core_pairs = [(i, (i + 1) % core_count) for i in range(core_count)]
-    xlo_pairs = [(i, (i + 1) % xlo_count) for i in range(xlo_count)]
-    from_sibling = lax.ppermute(jnp.stack(blocks[:2]), "core", core_pairs)
-    summed = (jnp.stack(blocks[2:]).astype(jnp.float32) + from_sibling.astype(jnp.float32)).astype(
-        jnp.bfloat16
-    )
-    theirs = lax.ppermute(summed[0], "xlo", xlo_pairs)
-    shares = jnp.transpose(
-        (summed[1].astype(jnp.float32) + theirs.astype(jnp.float32)).astype(jnp.bfloat16),
-        (3, 0, 1, 2),
-    )
     return (input_grad, router_grad, shares)
 
 

time: 401 us -> 400 us (level)
    ppermute x2, waiting for transfers between devices: 39.9 us -> 28.3 us  [the longest x1 28.3 us: per_device(): lax.ppermute(jnp.transpose(summed[0], (3, 0, 1, 2)), 'xlo', xlo_pairs)]
    all_to_all x1, waiting for transfers between devices: 49.7 us -> 61.3 us  [per_device(): lax.all_to_all(jnp.concatenate([row_grad, prob_cols], axis=3).reshape(own...]
    convert_element_type x1 -> x2, other arithmetic: 6.91 us -> 15.4 us  [the longest x1 7.79 us: per_device(): (own_blocks.astype(jnp.float32) + from_sibling.astype(jnp.float32)).astyp...]
    transpose x1 -> x0, other arithmetic: 7.6 us -> none  [per_device(): jnp.transpose((summed[1].astype(jnp.float32) + theirs.astype(jnp.float32)...]
    unnamed x57 -> x45, local copies, waits for them, and re-layouts: 18 us -> 17 us
  transfers between devices with their start and end apart: 5 -> 5, of which waited for: 4 -> 4; matrix products, arithmetic and copies ran while one was open for 24% -> 21% of each run, Pallas kernels for 0% -> 0%
where the time goes in v7:
time: 400 us; the launch traced here: 393 us
  waiting for transfers between devices  196 us (49%)
  matrix products  75.1 us (19%)
  local copies, waits for them, and re-layouts  56.8 us (14%)
  starting transfers between devices  32.8 us (8%)
  other arithmetic  31.2 us (8%)
    all_to_all x1, waiting for transfers between devices, per_device(): lax.all_to_all(jnp.concatenate([row_grad, prob_cols], axis=3).reshape(own...  61.3 us
    all_to_all x1, waiting for transfers between devices, per_device(): lax.all_to_all(send_tokens.reshape(send_shape), ('xlo', 'expert'), split_...  57.3 us
    all_to_all x1, waiting for transfers between devices, per_device(): lax.all_to_all(send_scaled.reshape(send_shape), ('xlo', 'expert'), split_...  48.7 us
    ppermute x1, waiting for transfers between devices, per_device(): lax.ppermute(jnp.transpose(summed[0], (3, 0, 1, 2)), 'xlo', xlo_pairs)  28.3 us
    unnamed x45, local copies, waits for them, and re-layouts  17 us
    dot_general x1, matrix products, per_device(): jnp.einsum('nemd,deh->nemh', recv_scaled, w_down, preferred_element_type=...  10.9 us
    dot_general x1, matrix products, per_device(): jnp.einsum('nemh,deh->nemd', gate_grad, w_gate, preferred_element_type=jn...  10.9 us
    all_to_all x1, starting transfers between devices, per_device(): lax.all_to_all(send_tokens.reshape(send_shape), ('xlo', 'expert'), split_...  10.9 us
  transfers between devices with their start and end apart: 5, of which 4 were waited for; matrix products, arithmetic and copies ran while one was open for 21% of the time, Pallas kernels for 0%

profile of v7, /device:TPU:0, one launch (start us, length us, event | category | flops | bytes accessed | tf_op | source)
XLA Modules:
  0.0 392.8 jit_solution(4184431385106669751)
XLA Ops:
  3.1 4.2 %fusion.18 = pred[1152,128]{1,0:T(8,128)(4,1)S(1)} fusion(s32[128,8]{0,1:T(8,128)S(1)} %fusion.71), kind=kLoop, calls=%fused_computation.32 | loop fusion | flops 2211840 | bytes 151552 | tf_op jit(solution)/shard_map/reduce_or | solution.py:61
  10.9 7.2 %reshape.355 = bf16[32,36,2048]{2,1,0:T(8,128)(2,1)} reshape(bf16[1152,2048]{1,0:T(8,128)(2,1)} %convolution_convert_fusion) | data formatting | bytes 9437184 | tf_op jit(solution)/shard_map/reshape | solution.py:72
  18.1 10.9 %all-to-all-start.1 = ((bf16[32,36,2048]{2,1,0:T(8,128)(2,1)}), bf16[32,36,2048]{2,1,0:T(8,128)(2,1)}, u32[]{:S(2)}, u32[]{:S(2)}) async-start(bf16[32,36,2048]{2,1,0:T(8,128)(2,1)} %reshape.355), calls=%async_computation.1 | async-start | bytes 10485760 | tf_op jit(solution)/shard_map/all_to_all | solution.py:71
  34.1 7.2 %reshape.353 = bf16[32,36,2048]{2,1,0:T(8,128)(2,1)} reshape(bf16[1152,2048]{1,0:T(8,128)(2,1)} %fusion.3) | data formatting | bytes 9437184 | tf_op jit(solution)/shard_map/reshape | solution.py:79
  41.3 57.3 %all-to-all-done.1 = bf16[32,36,2048]{2,1,0:T(8,128)(2,1)} async-done(((bf16[32,36,2048]{2,1,0:T(8,128)(2,1)}), bf16[32,36,2048]{2,1,0:T(8,128)(2,1)}, u32[]{:S(2)}, u32[]{:S(2)}) %all-to-all-start.1) | async-done | bytes 4718624 | tf_op jit(solution)/shard_map/all_to_all | solution.py:71
  98.6 10.7 %all-to-all-start = ((bf16[32,36,2048]{2,1,0:T(8,128)(2,1)}), bf16[32,36,2048]{2,1,0:T(8,128)(2,1)}, u32[]{:S(2)}, u32[]{:S(2)}) async-start(bf16[32,36,2048]{2,1,0:T(8,128)(2,1)} %reshape.353), calls=%async_computation | async-start | bytes 10485760 | tf_op jit(solution)/shard_map/all_to_all | solution.py:78
  109.4 5.2 %copy.78 = bf16[32,36,2048]{2,0,1:T(8,128)(2,1)S(1)} copy(bf16[32,36,2048]{2,1,0:T(8,128)(2,1)} %all-to-all-done.1) | data formatting | bytes 9437184 | tf_op jit(solution)/shard_map/all_to_all | solution.py:71
  114.6 10.1 %fusion.12 = f32[2,32,18,768]{3,1,2,0:T(8,128)} fusion(bf16[32,2,18,2048]{3,0,2,1:T(8,128)(2,1)S(1)} %bitcast.178, bf16[2048,2,768,1]{2,1,0,3:T(2,128)(2,1)} %bitcast.201), kind=kOutput, calls=%fused_computation.20 | convolution fusion | flops 3623878656 | bytes 14548992 | tf_op jit(solution)/shard_map/nemd,deh->nemh/dot_general | solution.py:90
  124.7 5.6 %fusion.8 = f32[2,32,18,768]{3,1,2,0:T(8,128)} fusion(bf16[32,2,18,2048]{3,0,2,1:T(8,128)(2,1)S(1)} %bitcast.179, bf16[2048,2,768,1]{2,1,0,3:T(2,128)(2,1)S(1)} %bitcast.200), kind=kOutput, calls=%fused_computation.16 | convolution fusion | flops 3623878656 | bytes 14548992 | tf_op jit(solution)/shard_map/nemd,deh->nemh/dot_general | solution.py:89
  130.3 48.7 %all-to-all-done = bf16[32,36,2048]{2,1,0:T(8,128)(2,1)} async-done(((bf16[32,36,2048]{2,1,0:T(8,128)(2,1)}), bf16[32,36,2048]{2,1,0:T(8,128)(2,1)}, u32[]{:S(2)}, u32[]{:S(2)}) %all-to-all-start) | async-done | bytes 4718624 | tf_op jit(solution)/shard_map/all_to_all | solution.py:78
  179.1 5.2 %copy.76 = bf16[32,36,2048]{2,0,1:T(8,128)(2,1)S(1)} copy(bf16[32,36,2048]{2,1,0:T(8,128)(2,1)} %all-to-all-done) | data formatting | bytes 9437184 | tf_op jit(solution)/shard_map/all_to_all | solution.py:78
  184.3 10.9 %fusion.31 = (bf16[32,2,18]{0,2,1:T(8,128)(2,1)S(1)}, bf16[32,2,18,768]{3,0,2,1:T(8,128)(2,1)}, bf16[32,2,18,768]{3,0,2,1:T(8,128)(2,1)S(1)}, bf16[32,2,18,768]{3,0,2,1:T(8,128)(2,1)S(1)}) fusion(f32[2,32,18,768]{3,1,2,0:T(8,128)} %fusion.12, f32[2,32,18,768]{3,1,2,0:T(8,128)} %fusion.8, bf16[32,2,18,2048]{3,0,2,1:T(8,128)(2,1)S(1)} %bitcast.190, ...), kind=kOutput, calls=%fused_computation.51 | convolution fusion | flops 3639802880 | bytes 23398656 | tf_op jit(solution)/shard_map/nemd,deh->nemh/dot_general | solution.py:94
  212.8 7.6 %maximum_maximum_fusion = (bf16[2,3,2,768,512]{4,3,2,1,0:T(8,128)(2,1)}, bf16[2,3,2,768,512]{4,3,2,1,0:T(8,128)(2,1)}) fusion(bf16[1,1,2,768,512]{4,3,2,1,0:T(8,128)(2,1)S(1)} %fusion.40, bf16[1,1,2,768,512]{4,3,2,1,0:T(8,128)(2,1)S(1)} %fusion.39, bf16[1,1,2,768,512]{4,3,2,1,0:T(8,128)(2,1)S(1)} %fusion.38, bf16[1,1,2,768,512]{4,3,2,1,0:T(8,128)(2,1)S(1)} %fusion.37, ...), kind=kLoop, calls=%fused_computation.4 | loop fusion | flops 47185920 | bytes 37748736 | tf_op jit(solution)/shard_map/stack | solution.py:126
  220.8 10.9 %fusion.6 = f32[2,32,18,2048]{3,1,2,0:T(8,128)} fusion(bf16[32,2,18,768]{3,0,2,1:T(8,128)(2,1)} %copy-done.14, bf16[2048,2,768,1]{2,1,0,3:T(2,128)(2,1)} %bitcast.197), kind=kOutput, calls=%fused_computation.14 | convolution fusion | flops 3623878656 | bytes 17498112 | tf_op jit(solution)/shard_map/nemh,deh->nemd/dot_general | solution.py:140
  231.7 8.4 %fusion.15 = bf16[32,2,18,2048]{3,0,2,1:T(8,128)(2,1)S(1)} fusion(f32[2,32,18,2048]{3,1,2,0:T(8,128)} %fusion.6, bf16[32,2,18,768]{3,0,2,1:T(8,128)(2,1)S(1)} %get-tuple-element.8, bf16[2048,2,768,1]{2,1,0,3:T(2,128)(2,1)} %bitcast.202), kind=kOutput, calls=%fused_computation.23 | convolution fusion | flops 3628597248 | bytes 22216704 | tf_op jit(solution)/shard_map/nemh,deh->nemd/dot_general | solution.py:141
  240.6 4.1 %copy.85 = bf16[32,36,2176]{2,1,0:T(8,128)(2,1)} copy(bf16[32,36,2176]{2,0,1:T(8,128)(2,1)S(1)} %bitcast.177) | data formatting | bytes 10027008 | tf_op jit(solution)/shard_map/reshape | solution.py:146
  244.7 10.7 %all-to-all-start.2 = ((bf16[32,36,2176]{2,1,0:T(8,128)(2,1)}), bf16[32,36,2176]{2,1,0:T(8,128)(2,1)}, u32[]{:S(2)}, u32[]{:S(2)}) async-start(bf16[32,36,2176]{2,1,0:T(8,128)(2,1)} %copy.85), calls=%async_computation.2 | async-start | bytes 11141120 | tf_op jit(solution)/shard_map/all_to_all | solution.py:145
  255.4 7.8 %add_convert_fusion = bf16[2,3,2,768,512]{4,3,2,1,0:T(8,128)(2,1)S(1)} fusion(bf16[2,3,2,768,512]{4,3,2,1,0:T(8,128)(2,1)} %collective-permute-done, bf16[2,3,2,768,512]{4,3,2,1,0:T(8,128)(2,1)} %get-tuple-element.9), kind=kLoop, calls=%fused_computation | loop fusion | flops 18874368 | bytes 28311552 | tf_op jit(solution)/shard_map/convert_element_type | solution.py:132
  268.8 61.3 %all-to-all-done.2 = bf16[32,36,2176]{2,1,0:T(8,128)(2,1)} async-done(((bf16[32,36,2176]{2,1,0:T(8,128)(2,1)}), bf16[32,36,2176]{2,1,0:T(8,128)(2,1)}, u32[]{:S(2)}, u32[]{:S(2)}) %all-to-all-start.2) | async-done | bytes 5013536 | tf_op jit(solution)/shard_map/all_to_all | solution.py:145
  330.1 7.4 %reshape.358 = bf16[1152,2176]{1,0:T(8,128)(2,1)} reshape(bf16[32,36,2176]{2,1,0:T(8,128)(2,1)} %all-to-all-done.2) | data formatting | bytes 10027008 | tf_op jit(solution)/shard_map/reshape | solution.py:154
  340.3 4.0 %fusion.32 = bf16[128,2048]{1,0:T(8,128)(2,1)} fusion(pred[1152,128]{1,0:T(8,128)(4,1)S(1)} %copy-done.5, bf16[1152,2176]{1,0:T(8,128)(2,1)} %reshape.358), kind=kOutput, calls=%fused_computation.64 | convolution fusion | flops 604241920 | bytes 5390336 | tf_op jit(solution)/shard_map/dot_general | solution.py:158
  344.3 28.3 %collective-permute-done.1 = bf16[512,3,2,768]{0,3,2,1:T(8,128)(2,1)} collective-permute-done((bf16[512,3,2,768]{0,3,2,1:T(8,128)(2,1)}, bf16[512,3,2,768]{0,3,2,1:T(8,128)(2,1)}, u32[]{:S(2)}, u32[]{:S(2)}) %collective-permute-start.1) | collective-permute-done | bytes 4718624 | tf_op jit(solution)/shard_map/ppermute | solution.py:135
  372.6 7.6 %fusion.2 = bf16[512,3,2,768]{0,3,2,1:T(8,128)(2,1)} fusion(bf16[512,3,2,768]{0,3,2,1:T(8,128)(2,1)} %collective-permute-done.1, bf16[2,3,2,768,512]{4,3,2,1,0:T(8,128)(2,1)} %copy-done.2), kind=kLoop, calls=%fused_computation.8 | loop fusion | flops 9437184 | bytes 14155776 | tf_op jit(solution)/shard_map/convert_element_type | solution.py:137
  380.2 12.4 %copy.87 = bf16[512,3,2,768]{3,2,1,0:T(2,128)(2,1)} copy(bf16[512,3,2,768]{0,3,2,1:T(8,128)(2,1)} %fusion.2) | data formatting | bytes 9437184
  (82 shorter events, 37.7 us)
Async XLA Ops:
  0.6 6.7 %copy-start = (bf16[128,2048]{1,0:T(8,128)(2,1)S(1)}, bf16[128,2048]{1,0:T(8,128)(2,1)}, u32[]{:S(2)}) copy-start(bf16[128,2048]{1,0:T(8,128)(2,1)} %param.7) | copy-start | bytes 1572868
  7.3 23.2 %copy-start.4 = (pred[1152,128]{1,0:T(8,128)(4,1)}, pred[1152,128]{1,0:T(8,128)(4,1)S(1)}, u32[]{:S(2)}) copy-start(pred[1152,128]{1,0:T(8,128)(4,1)S(1)} %fusion.18) | copy-start | bytes 442372
  18.1 10.9 %copy-start.13 = (f32[128,8]{0,1:T(8,128)S(1)}, f32[128,8]{0,1:T(8,128)}, u32[]{:S(2)}) copy-start(f32[128,8]{0,1:T(8,128)} %param.9) | copy-start | bytes 12292
  18.1 12.4 %copy-start.8 = (bf16[128,2048]{1,0:T(8,128)(2,1)S(1)}, bf16[128,2048]{1,0:T(8,128)(2,1)}, u32[]{:S(2)}) copy-start(bf16[128,2048]{1,0:T(8,128)(2,1)} %param.8) | copy-start | bytes 1572868
  18.1 80.5 %all-to-all-start.1 = ((bf16[32,36,2048]{2,1,0:T(8,128)(2,1)}), bf16[32,36,2048]{2,1,0:T(8,128)(2,1)}, u32[]{:S(2)}, u32[]{:S(2)}) async-start(bf16[32,36,2048]{2,1,0:T(8,128)(2,1)} %reshape.355), calls=%async_computation.1 | async-start | bytes 10485760 | tf_op jit(solution)/shard_map/all_to_all | solution.py:71
  29.0 5.0 %copy-start.6 = (f32[128,8]{1,0:T(8,128)}, f32[128,8]{1,0:T(8,128)S(1)}, u32[]{:S(2)}) copy-start(f32[128,8]{1,0:T(8,128)S(1)} %copy.75) | copy-start | bytes 12292
  29.9 11.4 %copy-start.9 = (s32[1024]{0:T(1024)}, s32[1024]{0:T(1024)S(1)}, u32[]{:S(2)}) copy-start(s32[1024]{0:T(1024)S(1)} %fusion.82) | copy-start | bytes 12292
  98.6 80.5 %all-to-all-start = ((bf16[32,36,2048]{2,1,0:T(8,128)(2,1)}), bf16[32,36,2048]{2,1,0:T(8,128)(2,1)}, u32[]{:S(2)}, u32[]{:S(2)}) async-start(bf16[32,36,2048]{2,1,0:T(8,128)(2,1)} %reshape.353), calls=%async_computation | async-start | bytes 10485760 | tf_op jit(solution)/shard_map/all_to_all | solution.py:78
  109.4 15.4 %slice-start.2 = ((s8[6291456]{0:T(1024)(128)(4,1)}), s8[4194304]{0:T(1024)(128)(4,1)S(1)}, s32[]{:S(2)}) async-start(s8[6291456]{0:T(1024)(128)(4,1)} %bitcast.198), calls=%async_computation.5 | async-start | bytes 8388608
  114.6 10.1 %copy-start.3 = (bf16[32,36,2048]{2,0,1:T(8,128)(2,1)}, bf16[32,36,2048]{2,0,1:T(8,128)(2,1)S(1)}, u32[]{:S(2)}) copy-start(bf16[32,36,2048]{2,0,1:T(8,128)(2,1)S(1)} %copy.78) | copy-start | bytes 14155780
  114.6 10.1 %slice-start.3 = ((s8[6291456]{0:T(1024)(128)(4,1)}), s8[2097152]{0:T(1024)(128)(4,1)S(1)}, s32[]{:S(2)}) async-start(s8[6291456]{0:T(1024)(128)(4,1)} %bitcast.198), calls=%async_computation.6 | async-start | bytes 4194304
  179.1 16.2 %slice-start = ((s8[4718592]{0:T(1024)(128)(4,1)}), s8[4194304]{0:T(1024)(128)(4,1)S(1)}, s32[]{:S(2)}) async-start(s8[4718592]{0:T(1024)(128)(4,1)} %bitcast.180), calls=%async_computation.3 | async-start | bytes 8388608
  184.3 11.0 %slice-start.1 = ((s8[4718592]{0:T(1024)(128)(4,1)}), s8[524288]{0:T(1024)(128)(4,1)S(1)}, s32[]{:S(2)}) async-start(s8[4718592]{0:T(1024)(128)(4,1)} %bitcast.180), calls=%async_computation.4 | async-start | bytes 1048576
  195.3 13.0 %copy-start.14 = (bf16[32,2,18,768]{3,0,2,1:T(8,128)(2,1)}, bf16[32,2,18,768]{3,0,2,1:T(8,128)(2,1)S(1)}, u32[]{:S(2)}) copy-start(bf16[32,2,18,768]{3,0,2,1:T(8,128)(2,1)S(1)} %get-tuple-element.7) | copy-start | bytes 5308420
  199.6 1.5 copy-start.15
  220.4 34.9 %collective-permute-start = (bf16[2,3,2,768,512]{4,3,2,1,0:T(8,128)(2,1)}, bf16[2,3,2,768,512]{4,3,2,1,0:T(8,128)(2,1)}, u32[]{:S(2)}, u32[]{:S(2)}) collective-permute-start(bf16[2,3,2,768,512]{4,3,2,1,0:T(8,128)(2,1)} %get-tuple-element.10), channel_id=1, source_target_pairs={{0,32},{32,0},{1,33},{33,1},{2,34},{34,2},{3,35},{35,3},{4,36},{36... | collective-permute-start | bytes 28311560 | tf_op jit(solution)/shard_map/ppermute | solution.py:131
  244.7 85.4 %all-to-all-start.2 = ((bf16[32,36,2176]{2,1,0:T(8,128)(2,1)}), bf16[32,36,2176]{2,1,0:T(8,128)(2,1)}, u32[]{:S(2)}, u32[]{:S(2)}) async-start(bf16[32,36,2176]{2,1,0:T(8,128)(2,1)} %copy.85), calls=%async_computation.2 | async-start | bytes 11141120 | tf_op jit(solution)/shard_map/all_to_all | solution.py:145
  263.2 5.1 %copy-start.2 = (bf16[2,3,2,768,512]{4,3,2,1,0:T(8,128)(2,1)}, bf16[2,3,2,768,512]{4,3,2,1,0:T(8,128)(2,1)S(1)}, u32[]{:S(2)}) copy-start(bf16[2,3,2,768,512]{4,3,2,1,0:T(8,128)(2,1)S(1)} %add_convert_fusion) | copy-start | bytes 28311556
  268.3 70.4 %copy-start.10 = (s32[1024]{0:T(1024)S(1)}, s32[1024]{0:T(1024)}, u32[]{:S(2)}) copy-start(s32[1024]{0:T(1024)} %copy-done.9) | copy-start | bytes 12292
  268.3 71.2 %copy-start.7 = (f32[128,8]{1,0:T(8,128)S(1)}, f32[128,8]{1,0:T(8,128)}, u32[]{:S(2)}) copy-start(f32[128,8]{1,0:T(8,128)} %copy-done.6) | copy-start | bytes 12292
  268.3 71.2 %copy-start.12 = (f32[128]{0:T(128)S(1)}, f32[128]{0:T(128)}, u32[]{:S(2)}) copy-start(f32[128]{0:T(128)} %copy-done.11) | copy-start | bytes 1540
  268.3 72.0 %copy-start.5 = (pred[1152,128]{1,0:T(8,128)(4,1)S(1)}, pred[1152,128]{1,0:T(8,128)(4,1)}, u32[]{:S(2)}) copy-start(pred[1152,128]{1,0:T(8,128)(4,1)} %copy-done.4) | copy-start | bytes 442372
  268.3 104.3 %collective-permute-start.1 = (bf16[512,3,2,768]{0,3,2,1:T(8,128)(2,1)}, bf16[512,3,2,768]{0,3,2,1:T(8,128)(2,1)}, u32[]{:S(2)}, u32[]{:S(2)}) collective-permute-start(bf16[512,3,2,768]{0,3,2,1:T(8,128)(2,1)} %slice_bitcast_fusion), channel_id=1, source_target_pairs={{0,64},{64,0},{1,65},{65,1},{2,66},{66,2},{3,67},{67,3},{4,68},{68... | collective-permute-start | bytes 14155784 | tf_op jit(solution)/shard_map/ppermute | solution.py:135
  372.6 20.0 %copy-start.1 = (bf16[128,2048]{1,0:T(8,128)(2,1)S(1)}, bf16[128,2048]{1,0:T(8,128)(2,1)}, u32[]{:S(2)}) copy-start(bf16[128,2048]{1,0:T(8,128)(2,1)} %param.7) | copy-start | bytes 1572868
  (1 other events, 0.5 us)

commit v8 on v7

--- a/solution.py
+++ b/solution.py
@@ -101,40 +101,42 @@
     up_grad = (hidden_grad * active).astype(jnp.bfloat16)
     block_count = xlo_count * core_count
     block_rows = model_width // block_count
-    blocks = []
-    for xlo_side, core_side in ((1, 1), (0, 1), (1, 0), (0, 0)):
-        block = (xlo ^ xlo_side) * core_count + (core ^ core_side)
-        tokens_rows = lax.dynamic_slice_in_dim(recv_tokens, block * block_rows, block_rows, 3)
-        scaled_rows = lax.dynamic_slice_in_dim(recv_scaled, block * block_rows, block_rows, 3)
-        blocks.append(
-            jnp.stack(
-                [
-                    jnp.einsum(
-                        "nemh,nemd->ehd", gate_grad, tokens_rows, preferred_element_type=jnp.float32
-                    ),
-                    jnp.einsum(
-                        "nemh,nemd->ehd", up_grad, tokens_rows, preferred_element_type=jnp.float32
-                    ),
-                    jnp.einsum(
-                        "nemh,nemd->ehd", hidden, scaled_rows, preferred_element_type=jnp.float32
-                    ),
-                ]
+    starts = [
+        ((xlo ^ xlo_side) * core_count + (core ^ core_side)) * block_rows
+        for xlo_side, core_side in ((1, 1), (0, 1), (1, 0), (0, 0))
+    ]
+
+    def blocks_of(left, right):
+        blocks = [
+            jnp.einsum(
+                "nemh,nemd->ehd",
+                left,
+                lax.dynamic_slice_in_dim(right, at, block_rows, 3),
+                preferred_element_type=jnp.float32,
             ).astype(jnp.bfloat16)
-        )
+            for at in starts
+        ]
+        return jnp.stack(blocks[:2]), jnp.stack(blocks[2:])
 
-    to_sibling, own_blocks, gate_grad, up_grad = lax.optimization_barrier(
-        (jnp.stack(blocks[:2]), jnp.stack(blocks[2:]), gate_grad, up_grad)
+    gate_sib, gate_own, up_grad, hidden = lax.optimization_barrier(
+        blocks_of(gate_grad, recv_tokens) + (up_grad, hidden)
+    )
+    up_sib, up_own, hidden = lax.optimization_barrier(
+        blocks_of(up_grad, recv_tokens) + (hidden,)
+    )
+    down_sib, down_own, gate_grad, up_grad = lax.optimization_barrier(
+        blocks_of(hidden, recv_scaled) + (gate_grad, up_grad)
     )
 
     core_pairs = [(i, (i + 1) % core_count) for i in range(core_count)]
     xlo_pairs = [(i, (i + 1) % xlo_count) for i in range(xlo_count)]
-    from_sibling = lax.ppermute(to_sibling, "core", core_pairs)
-    summed = (own_blocks.astype(jnp.float32) + from_sibling.astype(jnp.float32)).astype(
-        jnp.bfloat16
-    )
-    theirs = lax.ppermute(jnp.transpose(summed[0], (3, 0, 1, 2)), "xlo", xlo_pairs)
-    mine = jnp.transpose(summed[1], (3, 0, 1, 2))
-    shares = (mine.astype(jnp.float32) + theirs.astype(jnp.float32)).astype(jnp.bfloat16)
+    shares = jnp.zeros((block_rows, 3, local_experts, hidden_width), jnp.bfloat16)
+    for kind, (sib, own) in enumerate(((gate_sib, gate_own), (up_sib, up_own), (down_sib, down_own))):
+        from_sibling = lax.ppermute(sib, "core", core_pairs)
+        summed = (own.astype(jnp.float32) + from_sibling.astype(jnp.float32)).astype(jnp.bfloat16)
+        theirs = lax.ppermute(summed[0], "xlo", xlo_pairs)
+        share = (summed[1].astype(jnp.float32) + theirs.astype(jnp.float32)).astype(jnp.bfloat16)
+        shares = lax.dynamic_update_index_in_dim(shares, jnp.transpose(share, (2, 0, 1)), kind, 1)
 
     row_grad = (
         jnp.einsum("nemh,deh->nemd", gate_grad, w_gate, preferred_element_type=jnp.float32)

time: 400 us -> 401 us (level)
  matrix products: 75.1 us -> 69.6 us
    all_to_all x1, waiting for transfers between devices: 61.3 us -> 0.01 us  [per_device(): lax.all_to_all(jnp.concatenate([row_grad, prob_cols], axis=3).reshape(own...]
    ppermute x2 -> x6, waiting for transfers between devices: 28.3 us -> 89.3 us  [the longest x3 89.3 us: per_device(): theirs = lax.ppermute(summed[0], 'xlo', xlo_pairs)]
    convert_element_type x2 -> x3, other arithmetic: 15.4 us -> 9.47 us  [per_device(): (own.astype(jnp.float32) + from_sibling.astype(jnp.float32)).astype(jnp.b...]
    dot_general x1, matrix products: 10.9 us -> 6.29 us  [per_device(): jnp.einsum('nemh,deh->nemd', gate_grad, w_gate, preferred_element_type=jn...]
    another operation x1 -> x5, other arithmetic: 7.62 us -> 10.9 us  [blocks_of(): return (jnp.stack(blocks[:2]), jnp.stack(blocks[2:]))]
    unnamed x45 -> x57, local copies, waits for them, and re-layouts: 17 us -> 17.8 us
  transfers between devices with their start and end apart: 5 -> 9, of which waited for: 4 -> 4; matrix products, arithmetic and copies ran while one was open for 21% -> 21% of each run, Pallas kernels for 0% -> 0%
where the time goes in v8:
time: 401 us; the launch traced here: 394 us
  waiting for transfers between devices  195 us (49%)
  matrix products  69.6 us (17%)
  local copies, waits for them, and re-layouts  57.8 us (14%)
  other arithmetic  34.6 us (9%)
  starting transfers between devices  34.4 us (9%)
    ppermute x3, waiting for transfers between devices, per_device(): theirs = lax.ppermute(summed[0], 'xlo', xlo_pairs)  89.3 us
    all_to_all x1, waiting for transfers between devices, per_device(): lax.all_to_all(send_tokens.reshape(send_shape), ('xlo', 'expert'), split_...  57.3 us
    all_to_all x1, waiting for transfers between devices, per_device(): lax.all_to_all(send_scaled.reshape(send_shape), ('xlo', 'expert'), split_...  48.8 us
    unnamed x57, local copies, waits for them, and re-layouts  17.8 us
    dot_general x12, matrix products, blocks_of(): jnp.einsum('nemh,nemd->ehd', left, lax.dynamic_slice_in_dim(right, at, bl...  17.2 us
    all_to_all x1, starting transfers between devices, per_device(): lax.all_to_all(send_scaled.reshape(send_shape), ('xlo', 'expert'), split_...  11 us
    another operation x5, other arithmetic, blocks_of(): return (jnp.stack(blocks[:2]), jnp.stack(blocks[2:]))  10.9 us
    all_to_all x1, starting transfers between devices, per_device(): lax.all_to_all(send_tokens.reshape(send_shape), ('xlo', 'expert'), split_...  10.9 us
  transfers between devices with their start and end apart: 9, of which 4 were waited for; matrix products, arithmetic and copies ran while one was open for 21% of the time, Pallas kernels for 0%

profile of v8, /device:TPU:0, one launch (start us, length us, event | category | flops | bytes accessed | tf_op | source)
XLA Modules:
  0.0 393.5 jit_solution(11640739060194391458)
XLA Ops:
  3.1 4.2 %fusion.16 = pred[1152,128]{1,0:T(8,128)(4,1)S(1)} fusion(s32[128,8]{0,1:T(8,128)S(1)} %fusion.77), kind=kLoop, calls=%fused_computation.27 | loop fusion | flops 2211840 | bytes 151552 | tf_op jit(solution)/shard_map/reduce_or | solution.py:61
  7.3 3.6 convolution_convert_fusion
  10.9 7.2 %reshape.167 = bf16[32,36,2048]{2,1,0:T(8,128)(2,1)} reshape(bf16[1152,2048]{1,0:T(8,128)(2,1)} %convolution_convert_fusion) | data formatting | bytes 9437184 | tf_op jit(solution)/shard_map/reshape | solution.py:72
  18.1 10.9 %all-to-all-start.1 = ((bf16[32,36,2048]{2,1,0:T(8,128)(2,1)}), bf16[32,36,2048]{2,1,0:T(8,128)(2,1)}, u32[]{:S(2)}, u32[]{:S(2)}) async-start(bf16[32,36,2048]{2,1,0:T(8,128)(2,1)} %reshape.167), calls=%async_computation.1 | async-start | bytes 10485760 | tf_op jit(solution)/shard_map/all_to_all | solution.py:71
  30.5 3.6 fusion.1
  34.1 7.2 %reshape.165 = bf16[32,36,2048]{2,1,0:T(8,128)(2,1)} reshape(bf16[1152,2048]{1,0:T(8,128)(2,1)} %fusion.1) | data formatting | bytes 9437184 | tf_op jit(solution)/shard_map/reshape | solution.py:79
  41.3 57.3 %all-to-all-done.1 = bf16[32,36,2048]{2,1,0:T(8,128)(2,1)} async-done(((bf16[32,36,2048]{2,1,0:T(8,128)(2,1)}), bf16[32,36,2048]{2,1,0:T(8,128)(2,1)}, u32[]{:S(2)}, u32[]{:S(2)}) %all-to-all-start.1) | async-done | bytes 4718624 | tf_op jit(solution)/shard_map/all_to_all | solution.py:71
  98.6 11.0 %all-to-all-start = ((bf16[32,36,2048]{2,1,0:T(8,128)(2,1)}), bf16[32,36,2048]{2,1,0:T(8,128)(2,1)}, u32[]{:S(2)}, u32[]{:S(2)}) async-start(bf16[32,36,2048]{2,1,0:T(8,128)(2,1)} %reshape.165), calls=%async_computation | async-start | bytes 10485760 | tf_op jit(solution)/shard_map/all_to_all | solution.py:78
  109.7 5.2 %copy.78 = bf16[32,36,2048]{2,0,1:T(8,128)(2,1)S(1)} copy(bf16[32,36,2048]{2,1,0:T(8,128)(2,1)} %all-to-all-done.1) | data formatting | bytes 9437184 | tf_op jit(solution)/shard_map/all_to_all | solution.py:71
  114.9 10.1 %fusion.10 = f32[2,32,18,768]{3,1,2,0:T(8,128)} fusion(bf16[32,2,18,2048]{3,0,2,1:T(8,128)(2,1)S(1)} %bitcast.205, bf16[2048,2,768,1]{2,1,0,3:T(2,128)(2,1)} %bitcast.225), kind=kOutput, calls=%fused_computation.17 | convolution fusion | flops 3623878656 | bytes 14548992 | tf_op jit(solution)/shard_map/nemd,deh->nemh/dot_general | solution.py:90
  125.0 5.6 %fusion.6 = f32[2,32,18,768]{3,1,2,0:T(8,128)} fusion(bf16[32,2,18,2048]{3,0,2,1:T(8,128)(2,1)S(1)} %bitcast.206, bf16[2048,2,768,1]{2,1,0,3:T(2,128)(2,1)S(1)} %bitcast.221), kind=kOutput, calls=%fused_computation.13 | convolution fusion | flops 3623878656 | bytes 14548992 | tf_op jit(solution)/shard_map/nemd,deh->nemh/dot_general | solution.py:89
  130.6 48.8 %all-to-all-done = bf16[32,36,2048]{2,1,0:T(8,128)(2,1)} async-done(((bf16[32,36,2048]{2,1,0:T(8,128)(2,1)}), bf16[32,36,2048]{2,1,0:T(8,128)(2,1)}, u32[]{:S(2)}, u32[]{:S(2)}) %all-to-all-start) | async-done | bytes 4718624 | tf_op jit(solution)/shard_map/all_to_all | solution.py:78
  179.4 5.2 %copy.76 = bf16[32,36,2048]{2,0,1:T(8,128)(2,1)S(1)} copy(bf16[32,36,2048]{2,1,0:T(8,128)(2,1)} %all-to-all-done) | data formatting | bytes 9437184 | tf_op jit(solution)/shard_map/all_to_all | solution.py:78
  184.6 10.7 %fusion.29 = (bf16[32,2,18]{0,2,1:T(8,128)(2,1)S(1)}, bf16[32,2,18,768]{3,0,2,1:T(8,128)(2,1)}, bf16[32,2,18,768]{3,0,2,1:T(8,128)(2,1)S(1)}, bf16[32,2,18,768]{3,0,2,1:T(8,128)(2,1)S(1)}) fusion(f32[2,32,18,768]{3,1,2,0:T(8,128)} %fusion.10, f32[2,32,18,768]{3,1,2,0:T(8,128)} %fusion.6, bf16[32,2,18,2048]{3,0,2,1:T(8,128)(2,1)S(1)} %bitcast.200, ...), kind=kOutput, calls=%fused_computation.46 | convolution fusion | flops 3639802880 | bytes 23398656 | tf_op jit(solution)/shard_map/nemd,deh->nemh/dot_general | solution.py:94
  224.6 6.3 %fusion.4 = f32[2,32,18,2048]{3,1,2,0:T(8,128)} fusion(bf16[32,2,18,768]{3,0,2,1:T(8,128)(2,1)S(1)} %copy-done.16, bf16[2048,2,768,1]{2,1,0,3:T(2,128)(2,1)S(1)} %bitcast.224), kind=kOutput, calls=%fused_computation.11 | convolution fusion | flops 3623878656 | bytes 17498112 | tf_op jit(solution)/shard_map/nemh,deh->nemd/dot_general | solution.py:142
  230.8 8.0 %fusion.13 = bf16[32,2,18,2048]{3,0,2,1:T(8,128)(2,1)} fusion(f32[2,32,18,2048]{3,1,2,0:T(8,128)} %fusion.4, bf16[32,2,18,768]{3,0,2,1:T(8,128)(2,1)S(1)} %get-tuple-element.18, bf16[2048,2,768,1]{2,1,0,3:T(2,128)(2,1)S(1)} %bitcast.228), kind=kOutput, calls=%fused_computation.20 | convolution fusion | flops 3628597248 | bytes 22216704 | tf_op jit(solution)/shard_map/nemh,deh->nemd/dot_general | solution.py:143
  242.1 4.2 %copy.85 = bf16[32,36,2176]{2,1,0:T(8,128)(2,1)} copy(bf16[32,36,2176]{2,0,1:T(8,128)(2,1)S(1)} %bitcast.199) | data formatting | bytes 10027008 | tf_op jit(solution)/shard_map/reshape | solution.py:148
  246.2 10.5 %all-to-all-start.2 = ((bf16[32,36,2176]{2,1,0:T(8,128)(2,1)}), bf16[32,36,2176]{2,1,0:T(8,128)(2,1)}, u32[]{:S(2)}, u32[]{:S(2)}) async-start(bf16[32,36,2176]{2,1,0:T(8,128)(2,1)} %copy.85), calls=%async_computation.2 | async-start | bytes 11141120 | tf_op jit(solution)/shard_map/all_to_all | solution.py:147
  256.7 3.8 add_convert_fusion.2
  270.8 60.8 %collective-permute-done.1 = bf16[2,768,512]{2,1,0:T(8,128)(2,1)S(1)} collective-permute-done((bf16[2,768,512]{2,1,0:T(8,128)(2,1)S(1)}, bf16[2,768,512]{2,1,0:T(8,128)(2,1)S(1)}, u32[]{:S(2)}, u32[]{:S(2)}) %collective-permute-start.1) | collective-permute-done | bytes 1572896 | tf_op jit(solution)/shard_map/ppermute | solution.py:137
  336.2 28.4 %collective-permute-done.5 = bf16[2,768,512]{2,1,0:T(8,128)(2,1)S(1)} collective-permute-done((bf16[2,768,512]{2,1,0:T(8,128)(2,1)S(1)}, bf16[2,768,512]{2,1,0:T(8,128)(2,1)S(1)}, u32[]{:S(2)}, u32[]{:S(2)}) %collective-permute-start.5) | collective-permute-done | bytes 1572896 | tf_op jit(solution)/shard_map/ppermute | solution.py:137
  366.2 12.4 %copy.87 = bf16[512,3,2,768]{3,2,1,0:T(2,128)(2,1)} copy(bf16[512,3,2,768]{0,3,2,1:T(8,128)(2,1)} %fusion.40) | data formatting | bytes 9437184
  378.6 7.5 %reshape.170 = bf16[1152,2176]{1,0:T(8,128)(2,1)} reshape(bf16[32,36,2176]{2,1,0:T(8,128)(2,1)} %all-to-all-done.2) | data formatting | bytes 10027008 | tf_op jit(solution)/shard_map/reshape | solution.py:156
  387.4 4.1 %fusion.33 = bf16[128,2048]{1,0:T(8,128)(2,1)} fusion(pred[1152,128]{1,0:T(8,128)(4,1)S(1)} %copy-done.6, bf16[1152,2176]{1,0:T(8,128)(2,1)} %reshape.170), kind=kOutput, calls=%fused_computation.71 | convolution fusion | flops 604241920 | bytes 5390336 | tf_op jit(solution)/shard_map/dot_general | solution.py:160
  (115 shorter events, 55.4 us)
Async XLA Ops:
  0.6 6.7 %copy-start = (bf16[128,2048]{1,0:T(8,128)(2,1)S(1)}, bf16[128,2048]{1,0:T(8,128)(2,1)}, u32[]{:S(2)}) copy-start(bf16[128,2048]{1,0:T(8,128)(2,1)} %param.7) | copy-start | bytes 1572868
  7.3 23.2 %copy-start.5 = (pred[1152,128]{1,0:T(8,128)(4,1)}, pred[1152,128]{1,0:T(8,128)(4,1)S(1)}, u32[]{:S(2)}) copy-start(pred[1152,128]{1,0:T(8,128)(4,1)S(1)} %fusion.16) | copy-start | bytes 442372
  18.1 10.9 %copy-start.14 = (f32[128,8]{0,1:T(8,128)S(1)}, f32[128,8]{0,1:T(8,128)}, u32[]{:S(2)}) copy-start(f32[128,8]{0,1:T(8,128)} %param.9) | copy-start | bytes 12292
  18.1 12.4 %copy-start.9 = (bf16[128,2048]{1,0:T(8,128)(2,1)S(1)}, bf16[128,2048]{1,0:T(8,128)(2,1)}, u32[]{:S(2)}) copy-start(bf16[128,2048]{1,0:T(8,128)(2,1)} %param.8) | copy-start | bytes 1572868
  18.1 80.6 %all-to-all-start.1 = ((bf16[32,36,2048]{2,1,0:T(8,128)(2,1)}), bf16[32,36,2048]{2,1,0:T(8,128)(2,1)}, u32[]{:S(2)}, u32[]{:S(2)}) async-start(bf16[32,36,2048]{2,1,0:T(8,128)(2,1)} %reshape.167), calls=%async_computation.1 | async-start | bytes 10485760 | tf_op jit(solution)/shard_map/all_to_all | solution.py:71
  98.6 80.7 %all-to-all-start = ((bf16[32,36,2048]{2,1,0:T(8,128)(2,1)}), bf16[32,36,2048]{2,1,0:T(8,128)(2,1)}, u32[]{:S(2)}, u32[]{:S(2)}) async-start(bf16[32,36,2048]{2,1,0:T(8,128)(2,1)} %reshape.165), calls=%async_computation | async-start | bytes 10485760 | tf_op jit(solution)/shard_map/all_to_all | solution.py:78
  109.7 15.4 %slice-start.2 = ((s8[6291456]{0:T(1024)(128)(4,1)}), s8[4194304]{0:T(1024)(128)(4,1)S(1)}, s32[]{:S(2)}) async-start(s8[6291456]{0:T(1024)(128)(4,1)} %bitcast.219), calls=%async_computation.5 | async-start | bytes 8388608
  114.9 10.1 %copy-start.4 = (bf16[32,36,2048]{2,0,1:T(8,128)(2,1)}, bf16[32,36,2048]{2,0,1:T(8,128)(2,1)S(1)}, u32[]{:S(2)}) copy-start(bf16[32,36,2048]{2,0,1:T(8,128)(2,1)S(1)} %copy.78) | copy-start | bytes 14155780
  114.9 10.1 %slice-start.3 = ((s8[6291456]{0:T(1024)(128)(4,1)}), s8[2097152]{0:T(1024)(128)(4,1)S(1)}, s32[]{:S(2)}) async-start(s8[6291456]{0:T(1024)(128)(4,1)} %bitcast.219), calls=%async_computation.6 | async-start | bytes 4194304
  179.4 15.9 %slice-start = ((s8[4718592]{0:T(1024)(128)(4,1)}), s8[4194304]{0:T(1024)(128)(4,1)S(1)}, s32[]{:S(2)}) async-start(s8[4718592]{0:T(1024)(128)(4,1)} %bitcast.207), calls=%async_computation.3 | async-start | bytes 8388608
  184.6 10.7 %slice-start.1 = ((s8[4718592]{0:T(1024)(128)(4,1)}), s8[524288]{0:T(1024)(128)(4,1)S(1)}, s32[]{:S(2)}) async-start(s8[4718592]{0:T(1024)(128)(4,1)} %bitcast.207), calls=%async_computation.4 | async-start | bytes 1048576
  217.0 7.5 %slice-start.4 = ((s8[6291456]{0:T(1024)(128)(4,1)}), s8[4194304]{0:T(1024)(128)(4,1)S(1)}, s32[]{:S(2)}) async-start(s8[6291456]{0:T(1024)(128)(4,1)} %bitcast.222), calls=%async_computation.7 | async-start | bytes 8388608
  218.4 6.1 %slice-start.5 = ((s8[6291456]{0:T(1024)(128)(4,1)}), s8[2097152]{0:T(1024)(128)(4,1)S(1)}, s32[]{:S(2)}) async-start(s8[6291456]{0:T(1024)(128)(4,1)} %bitcast.222), calls=%async_computation.8 | async-start | bytes 4194304
  221.8 9.1 %slice-start.6 = ((s8[6291456]{0:T(1024)(128)(4,1)}), s8[4194304]{0:T(1024)(128)(4,1)S(1)}, s32[]{:S(2)}) async-start(s8[6291456]{0:T(1024)(128)(4,1)} %bitcast.226), calls=%async_computation.9 | async-start | bytes 8388608
  223.8 7.1 %slice-start.7 = ((s8[6291456]{0:T(1024)(128)(4,1)}), s8[2097152]{0:T(1024)(128)(4,1)S(1)}, s32[]{:S(2)}) async-start(s8[6291456]{0:T(1024)(128)(4,1)} %bitcast.226), calls=%async_computation.10 | async-start | bytes 4194304
  223.8 42.0 %collective-permute-start.4 = (bf16[2,2,768,512]{3,2,1,0:T(8,128)(2,1)}, bf16[2,2,768,512]{3,2,1,0:T(8,128)(2,1)}, u32[]{:S(2)}, u32[]{:S(2)}) collective-permute-start(bf16[2,2,768,512]{3,2,1,0:T(8,128)(2,1)} %pad_maximum_fusion.4), channel_id=1, source_target_pairs={{0,32},{32,0},{1,33},{33,1},{2,34},{34,2},{3,35},{35,3},{4,36},{36... | collective-permute-start | bytes 9437192 | tf_op jit(solution)/shard_map/ppermute | solution.py:135
  223.8 32.9 %collective-permute-start.2 = (bf16[2,2,768,512]{3,2,1,0:T(8,128)(2,1)}, bf16[2,2,768,512]{3,2,1,0:T(8,128)(2,1)}, u32[]{:S(2)}, u32[]{:S(2)}) collective-permute-start(bf16[2,2,768,512]{3,2,1,0:T(8,128)(2,1)} %pad_maximum_fusion.2), channel_id=1, source_target_pairs={{0,32},{32,0},{1,33},{33,1},{2,34},{34,2},{3,35},{35,3},{4,36},{36... | collective-permute-start | bytes 9437192 | tf_op jit(solution)/shard_map/ppermute | solution.py:135
  224.3 36.5 %collective-permute-start = (bf16[2,2,768,512]{3,2,1,0:T(8,128)(2,1)}, bf16[2,2,768,512]{3,2,1,0:T(8,128)(2,1)}, u32[]{:S(2)}, u32[]{:S(2)}) collective-permute-start(bf16[2,2,768,512]{3,2,1,0:T(8,128)(2,1)} %get-tuple-element.20), channel_id=1, source_target_pairs={{0,32},{32,0},{1,33},{33,1},{2,34},{34,2},{3,35},{35,3},{4,36},{36... | collective-permute-start | bytes 9437192 | tf_op jit(solution)/shard_map/ppermute | solution.py:135
  246.2 132.4 %all-to-all-start.2 = ((bf16[32,36,2176]{2,1,0:T(8,128)(2,1)}), bf16[32,36,2176]{2,1,0:T(8,128)(2,1)}, u32[]{:S(2)}, u32[]{:S(2)}) async-start(bf16[32,36,2176]{2,1,0:T(8,128)(2,1)} %copy.85), calls=%async_computation.2 | async-start | bytes 11141120 | tf_op jit(solution)/shard_map/all_to_all | solution.py:147
  260.6 74.0 %collective-permute-start.3 = (bf16[2,768,512]{2,1,0:T(8,128)(2,1)S(1)}, bf16[2,768,512]{2,1,0:T(8,128)(2,1)S(1)}, u32[]{:S(2)}, u32[]{:S(2)}) collective-permute-start(bf16[2,768,512]{2,1,0:T(8,128)(2,1)S(1)} %slice_bitcast_fusion.2), channel_id=1, source_target_pairs={{0,64},{64,0},{1,65},{65,1},{2,66},{66,2},{3,67},{67,3},{4,68},{68... | collective-permute-start | bytes 4718600 | tf_op jit(solution)/shard_map/ppermute | solution.py:137
  265.4 66.3 %collective-permute-start.1 = (bf16[2,768,512]{2,1,0:T(8,128)(2,1)S(1)}, bf16[2,768,512]{2,1,0:T(8,128)(2,1)S(1)}, u32[]{:S(2)}, u32[]{:S(2)}) collective-permute-start(bf16[2,768,512]{2,1,0:T(8,128)(2,1)S(1)} %slice_bitcast_fusion.4), channel_id=1, source_target_pairs={{0,64},{64,0},{1,65},{65,1},{2,66},{66,2},{3,67},{67,3},{4,68},{68... | collective-permute-start | bytes 4718600 | tf_op jit(solution)/shard_map/ppermute | solution.py:137
  270.1 94.5 %collective-permute-start.5 = (bf16[2,768,512]{2,1,0:T(8,128)(2,1)S(1)}, bf16[2,768,512]{2,1,0:T(8,128)(2,1)S(1)}, u32[]{:S(2)}, u32[]{:S(2)}) collective-permute-start(bf16[2,768,512]{2,1,0:T(8,128)(2,1)S(1)} %slice_bitcast_fusion), channel_id=1, source_target_pairs={{0,64},{64,0},{1,65},{65,1},{2,66},{66,2},{3,67},{67,3},{4,68},{68... | collective-permute-start | bytes 4718600 | tf_op jit(solution)/shard_map/ppermute | solution.py:137
  378.6 8.7 %copy-start.6 = (pred[1152,128]{1,0:T(8,128)(4,1)S(1)}, pred[1152,128]{1,0:T(8,128)(4,1)}, u32[]{:S(2)}) copy-start(pred[1152,128]{1,0:T(8,128)(4,1)} %copy-done.5) | copy-start | bytes 442372
  386.1 6.9 %copy-start.1 = (bf16[128,2048]{1,0:T(8,128)(2,1)S(1)}, bf16[128,2048]{1,0:T(8,128)(2,1)}, u32[]{:S(2)}) copy-start(bf16[128,2048]{1,0:T(8,128)(2,1)} %param.7) | copy-start | bytes 1572868
  (11 other events, 36.6 us)

commit v9 on v8

--- a/solution.py
+++ b/solution.py
@@ -118,21 +118,22 @@
         ]
         return jnp.stack(blocks[:2]), jnp.stack(blocks[2:])
 
-    gate_sib, gate_own, up_grad, hidden = lax.optimization_barrier(
-        blocks_of(gate_grad, recv_tokens) + (up_grad, hidden)
+    core_pairs = [(i, (i + 1) % core_count) for i in range(core_count)]
+    xlo_pairs = [(i, (i + 1) % xlo_count) for i in range(xlo_count)]
+    gate_sib, gate_own = blocks_of(gate_grad, recv_tokens)
+    gate_from, up_grad, hidden = lax.optimization_barrier(
+        (lax.ppermute(gate_sib, "core", core_pairs), up_grad, hidden)
     )
-    up_sib, up_own, hidden = lax.optimization_barrier(
-        blocks_of(up_grad, recv_tokens) + (hidden,)
-    )
+    up_sib, up_own = blocks_of(up_grad, recv_tokens)
+    up_from, hidden = lax.optimization_barrier((lax.ppermute(up_sib, "core", core_pairs), hidden))
     down_sib, down_own, gate_grad, up_grad = lax.optimization_barrier(
         blocks_of(hidden, recv_scaled) + (gate_grad, up_grad)
     )
+    down_from = lax.ppermute(down_sib, "core", core_pairs)
 
-    core_pairs = [(i, (i + 1) % core_count) for i in range(core_count)]
-    xlo_pairs = [(i, (i + 1) % xlo_count) for i in range(xlo_count)]
     shares = jnp.zeros((block_rows, 3, local_experts, hidden_width), jnp.bfloat16)
-    for kind, (sib, own) in enumerate(((gate_sib, gate_own), (up_sib, up_own), (down_sib, down_own))):
-        from_sibling = lax.ppermute(sib, "core", core_pairs)
+    pieces = ((gate_from, gate_own), (up_from, up_own), (down_from, down_own))
+    for kind, (from_sibling, own) in enumerate(pieces):
         summed = (own.astype(jnp.float32) + from_sibling.astype(jnp.float32)).astype(jnp.bfloat16)
         theirs = lax.ppermute(summed[0], "xlo", xlo_pairs)
         share = (summed[1].astype(jnp.float32) + theirs.astype(jnp.float32)).astype(jnp.bfloat16)

time: 401 us -> 378 us (0.943)
  waiting for transfers between devices: 195 us -> 170 us
  matrix products: 69.6 us -> 79.3 us
  other arithmetic: 34.6 us -> 26 us
    ppermute x3, waiting for transfers between devices: 89.3 us -> 57.8 us  [per_device(): theirs = lax.ppermute(summed[0], 'xlo', xlo_pairs)]
    dot_general x12, matrix products: 17.2 us -> 23.3 us  [blocks_of(): jnp.einsum('nemh,nemd->ehd', left, lax.dynamic_slice_in_dim(right, at, bl...]
    ppermute x3, waiting for transfers between devices: 0.01 us -> 5.65 us  [the longest x1 5.65 us: per_device(): lax.ppermute(gate_sib, 'core', core_pairs)]
    another operation x5 -> x4, other arithmetic: 10.9 us -> 6.08 us  [blocks_of(): return (jnp.stack(blocks[:2]), jnp.stack(blocks[2:]))]
    dot_general x1, matrix products: 5.59 us -> 10.2 us  [per_device(): jnp.einsum('nemd,deh->nemh', recv_tokens, w_gate, preferred_element_type=...]
    dot_general x1, matrix products: 10.1 us -> 5.6 us  [per_device(): jnp.einsum('nemd,deh->nemh', recv_tokens, w_up, preferred_element_type=jn...]
    ppermute x3, starting transfers between devices: 1.31 us -> 5.35 us  [per_device(): theirs = lax.ppermute(summed[0], 'xlo', xlo_pairs)]
    unnamed x57 -> x69, local copies, waits for them, and re-layouts: 17.8 us -> 17.3 us
  transfers between devices with their start and end apart: 9 -> 9, of which waited for: 4 -> 5; matrix products, arithmetic and copies ran while one was open for 21% -> 28% of each run, Pallas kernels for 0% -> 0%
where the time goes in v9:
time: 378 us; the launch traced here: 371 us
  waiting for transfers between devices  170 us (45%)
  matrix products  79.3 us (21%)
  local copies, waits for them, and re-layouts  57.4 us (15%)
  starting transfers between devices  37 us (10%)
  other arithmetic  26 us (7%)
    ppermute x3, waiting for transfers between devices, per_device(): theirs = lax.ppermute(summed[0], 'xlo', xlo_pairs)  57.8 us
    all_to_all x1, waiting for transfers between devices, per_device(): lax.all_to_all(send_tokens.reshape(send_shape), ('xlo', 'expert'), split_...  57.3 us
    all_to_all x1, waiting for transfers between devices, per_device(): lax.all_to_all(send_scaled.reshape(send_shape), ('xlo', 'expert'), split_...  48.7 us
    dot_general x12, matrix products, blocks_of(): jnp.einsum('nemh,nemd->ehd', left, lax.dynamic_slice_in_dim(right, at, bl...  23.3 us
    unnamed x69, local copies, waits for them, and re-layouts  17.3 us
    dot_general x1, matrix products, per_device(): jnp.einsum('nemd,deh->nemh', recv_scaled, w_down, preferred_element_type=...  12.3 us
    all_to_all x1, starting transfers between devices, per_device(): lax.all_to_all(send_scaled.reshape(send_shape), ('xlo', 'expert'), split_...  11 us
    all_to_all x1, starting transfers between devices, per_device(): lax.all_to_all(send_tokens.reshape(send_shape), ('xlo', 'expert'), split_...  10.9 us
  transfers between devices with their start and end apart: 9, of which 5 were waited for; matrix products, arithmetic and copies ran while one was open for 28% of the time, Pallas kernels for 0%

profile of v9, /device:TPU:0, one launch (start us, length us, event | category | flops | bytes accessed | tf_op | source)
XLA Modules:
  0.0 371.0 jit_solution(14272536574041455373)
XLA Ops:
  3.1 4.2 %fusion.16 = pred[1152,128]{1,0:T(8,128)(4,1)S(1)} fusion(s32[128,8]{0,1:T(8,128)S(1)} %fusion.77), kind=kLoop, calls=%fused_computation.27 | loop fusion | flops 2211840 | bytes 151552 | tf_op jit(solution)/shard_map/reduce_or | solution.py:61
  10.9 7.2 %reshape.167 = bf16[32,36,2048]{2,1,0:T(8,128)(2,1)} reshape(bf16[1152,2048]{1,0:T(8,128)(2,1)} %convolution_convert_fusion) | data formatting | bytes 9437184 | tf_op jit(solution)/shard_map/reshape | solution.py:72
  18.1 10.9 %all-to-all-start.1 = ((bf16[32,36,2048]{2,1,0:T(8,128)(2,1)}), bf16[32,36,2048]{2,1,0:T(8,128)(2,1)}, u32[]{:S(2)}, u32[]{:S(2)}) async-start(bf16[32,36,2048]{2,1,0:T(8,128)(2,1)} %reshape.167), calls=%async_computation.1 | async-start | bytes 10485760 | tf_op jit(solution)/shard_map/all_to_all | solution.py:71
  30.5 3.6 fusion.1
  34.1 7.3 %reshape.165 = bf16[32,36,2048]{2,1,0:T(8,128)(2,1)} reshape(bf16[1152,2048]{1,0:T(8,128)(2,1)} %fusion.1) | data formatting | bytes 9437184 | tf_op jit(solution)/shard_map/reshape | solution.py:79
  41.3 57.3 %all-to-all-done.1 = bf16[32,36,2048]{2,1,0:T(8,128)(2,1)} async-done(((bf16[32,36,2048]{2,1,0:T(8,128)(2,1)}), bf16[32,36,2048]{2,1,0:T(8,128)(2,1)}, u32[]{:S(2)}, u32[]{:S(2)}) %all-to-all-start.1) | async-done | bytes 4718624 | tf_op jit(solution)/shard_map/all_to_all | solution.py:71
  98.6 11.0 %all-to-all-start = ((bf16[32,36,2048]{2,1,0:T(8,128)(2,1)}), bf16[32,36,2048]{2,1,0:T(8,128)(2,1)}, u32[]{:S(2)}, u32[]{:S(2)}) async-start(bf16[32,36,2048]{2,1,0:T(8,128)(2,1)} %reshape.165), calls=%async_computation | async-start | bytes 10485760 | tf_op jit(solution)/shard_map/all_to_all | solution.py:78
  109.7 5.2 %copy.78 = bf16[32,36,2048]{2,0,1:T(8,128)(2,1)S(1)} copy(bf16[32,36,2048]{2,1,0:T(8,128)(2,1)} %all-to-all-done.1) | data formatting | bytes 9437184 | tf_op jit(solution)/shard_map/all_to_all | solution.py:71
  114.9 10.2 %fusion.6 = f32[2,32,18,768]{3,1,2,0:T(8,128)} fusion(bf16[32,2,18,2048]{3,0,2,1:T(8,128)(2,1)S(1)} %bitcast.200, bf16[2048,2,768,1]{2,1,0,3:T(2,128)(2,1)} %bitcast.221), kind=kOutput, calls=%fused_computation.13 | convolution fusion | flops 3623878656 | bytes 14548992 | tf_op jit(solution)/shard_map/nemd,deh->nemh/dot_general | solution.py:89
  125.1 5.6 %fusion.10 = f32[2,32,18,768]{3,1,2,0:T(8,128)} fusion(bf16[32,2,18,2048]{3,0,2,1:T(8,128)(2,1)S(1)} %bitcast.201, bf16[2048,2,768,1]{2,1,0,3:T(2,128)(2,1)S(1)} %bitcast.228), kind=kOutput, calls=%fused_computation.17 | convolution fusion | flops 3623878656 | bytes 14548992 | tf_op jit(solution)/shard_map/nemd,deh->nemh/dot_general | solution.py:90
  130.7 48.7 %all-to-all-done = bf16[32,36,2048]{2,1,0:T(8,128)(2,1)} async-done(((bf16[32,36,2048]{2,1,0:T(8,128)(2,1)}), bf16[32,36,2048]{2,1,0:T(8,128)(2,1)}, u32[]{:S(2)}, u32[]{:S(2)}) %all-to-all-start) | async-done | bytes 4718624 | tf_op jit(solution)/shard_map/all_to_all | solution.py:78
  179.4 5.2 %copy.76 = bf16[32,36,2048]{2,0,1:T(8,128)(2,1)S(1)} copy(bf16[32,36,2048]{2,1,0:T(8,128)(2,1)} %all-to-all-done) | data formatting | bytes 9437184 | tf_op jit(solution)/shard_map/all_to_all | solution.py:78
  184.6 12.3 %fusion.29 = (bf16[32,2,18]{0,2,1:T(8,128)(2,1)S(1)}, bf16[32,2,18,768]{3,0,2,1:T(8,128)(2,1)}, bf16[32,2,18,768]{3,0,2,1:T(8,128)(2,1)S(1)}, bf16[32,2,18,768]{3,0,2,1:T(8,128)(2,1)S(1)}) fusion(f32[2,32,18,768]{3,1,2,0:T(8,128)} %fusion.10, f32[2,32,18,768]{3,1,2,0:T(8,128)} %fusion.6, bf16[32,2,18,2048]{3,0,2,1:T(8,128)(2,1)S(1)} %bitcast.212, ...), kind=kOutput, calls=%fused_computation.46 | convolution fusion | flops 3639802880 | bytes 23398656 | tf_op jit(solution)/shard_map/nemd,deh->nemh/dot_general | solution.py:94
  200.3 5.6 %collective-permute-done = bf16[2,2,768,512]{3,2,1,0:T(8,128)(2,1)S(1)} collective-permute-done((bf16[2,2,768,512]{3,2,1,0:T(8,128)(2,1)S(1)}, bf16[2,2,768,512]{3,2,1,0:T(8,128)(2,1)S(1)}, u32[]{:S(2)}, u32[]{:S(2)}) %collective-permute-start) | collective-permute-done | bytes 3145760 | tf_op jit(solution)/shard_map/ppermute | solution.py:125
  218.5 4.2 %collective-permute-start.2 = (bf16[2,768,512]{2,1,0:T(8,128)(2,1)S(1)}, bf16[2,768,512]{2,1,0:T(8,128)(2,1)}, u32[]{:S(2)}, u32[]{:S(2)}) collective-permute-start(bf16[2,768,512]{2,1,0:T(8,128)(2,1)S(1)} %slice_bitcast_fusion.4), channel_id=1, source_target_pairs={{0,64},{64,0},{1,65},{65,1},{2,66},{66,2},{3,67},{67,3},{4,68},{68... | collective-permute-start | bytes 4718600 | tf_op jit(solution)/shard_map/ppermute | solution.py:138
  232.7 6.3 %fusion.4 = f32[2,32,18,2048]{3,1,2,0:T(8,128)} fusion(bf16[32,2,18,768]{3,0,2,1:T(8,128)(2,1)S(1)} %copy-done.22, bf16[2048,2,768,1]{2,1,0,3:T(2,128)(2,1)S(1)} %bitcast.224), kind=kOutput, calls=%fused_computation.11 | convolution fusion | flops 3623878656 | bytes 17498112 | tf_op jit(solution)/shard_map/nemh,deh->nemd/dot_general | solution.py:143
  239.1 9.9 %fusion.13 = bf16[32,2,18,2048]{3,0,2,1:T(8,128)(2,1)S(1)} fusion(f32[2,32,18,2048]{3,1,2,0:T(8,128)} %fusion.4, bf16[32,2,18,768]{3,0,2,1:T(8,128)(2,1)} %copy-done.19, bf16[2048,2,768,1]{2,1,0,3:T(2,128)(2,1)} %bitcast.225), kind=kOutput, calls=%fused_computation.20 | convolution fusion | flops 3628597248 | bytes 22216704 | tf_op jit(solution)/shard_map/nemh,deh->nemd/dot_general | solution.py:144
  249.5 4.1 %copy.85 = bf16[32,36,2176]{2,1,0:T(8,128)(2,1)} copy(bf16[32,36,2176]{2,0,1:T(8,128)(2,1)S(1)} %bitcast.199) | data formatting | bytes 10027008 | tf_op jit(solution)/shard_map/reshape | solution.py:149
  253.6 9.0 %all-to-all-start.2 = ((bf16[32,36,2176]{2,1,0:T(8,128)(2,1)}), bf16[32,36,2176]{2,1,0:T(8,128)(2,1)}, u32[]{:S(2)}, u32[]{:S(2)}) async-start(bf16[32,36,2176]{2,1,0:T(8,128)(2,1)} %copy.85), calls=%async_computation.2 | async-start | bytes 11141120 | tf_op jit(solution)/shard_map/all_to_all | solution.py:148
  282.6 26.8 %collective-permute-done.3 = bf16[2,768,512]{2,1,0:T(8,128)(2,1)S(1)} collective-permute-done((bf16[2,768,512]{2,1,0:T(8,128)(2,1)S(1)}, bf16[2,768,512]{2,1,0:T(8,128)(2,1)S(1)}, u32[]{:S(2)}, u32[]{:S(2)}) %collective-permute-start.3) | collective-permute-done | bytes 1572896 | tf_op jit(solution)/shard_map/ppermute | solution.py:138
  311.0 31.0 %collective-permute-done.5 = bf16[2,768,512]{2,1,0:T(8,128)(2,1)S(1)} collective-permute-done((bf16[2,768,512]{2,1,0:T(8,128)(2,1)S(1)}, bf16[2,768,512]{2,1,0:T(8,128)(2,1)S(1)}, u32[]{:S(2)}, u32[]{:S(2)}) %collective-permute-start.5) | collective-permute-done | bytes 1572896 | tf_op jit(solution)/shard_map/ppermute | solution.py:138
  343.7 12.4 %copy.87 = bf16[512,3,2,768]{3,2,1,0:T(2,128)(2,1)} copy(bf16[512,3,2,768]{0,3,2,1:T(8,128)(2,1)} %fusion.40) | data formatting | bytes 9437184
  356.1 7.5 %reshape.170 = bf16[1152,2176]{1,0:T(8,128)(2,1)} reshape(bf16[32,36,2176]{2,1,0:T(8,128)(2,1)} %all-to-all-done.2) | data formatting | bytes 10027008 | tf_op jit(solution)/shard_map/reshape | solution.py:157
  364.8 4.1 %fusion.33 = bf16[128,2048]{1,0:T(8,128)(2,1)} fusion(pred[1152,128]{1,0:T(8,128)(4,1)S(1)} %copy-done.10, bf16[1152,2176]{1,0:T(8,128)(2,1)} %reshape.170), kind=kOutput, calls=%fused_computation.69 | convolution fusion | flops 604241920 | bytes 5390336 | tf_op jit(solution)/shard_map/dot_general | solution.py:161
  (126 shorter events, 59.6 us)
Async XLA Ops:
  7.3 23.2 %copy-start.9 = (pred[1152,128]{1,0:T(8,128)(4,1)}, pred[1152,128]{1,0:T(8,128)(4,1)S(1)}, u32[]{:S(2)}) copy-start(pred[1152,128]{1,0:T(8,128)(4,1)S(1)} %fusion.16) | copy-start | bytes 442372
  18.1 10.9 %copy-start.18 = (f32[128,8]{0,1:T(8,128)S(1)}, f32[128,8]{0,1:T(8,128)}, u32[]{:S(2)}) copy-start(f32[128,8]{0,1:T(8,128)} %param.9) | copy-start | bytes 12292
  18.1 12.4 %copy-start.13 = (bf16[128,2048]{1,0:T(8,128)(2,1)S(1)}, bf16[128,2048]{1,0:T(8,128)(2,1)}, u32[]{:S(2)}) copy-start(bf16[128,2048]{1,0:T(8,128)(2,1)} %param.8) | copy-start | bytes 1572868
  18.1 80.6 %all-to-all-start.1 = ((bf16[32,36,2048]{2,1,0:T(8,128)(2,1)}), bf16[32,36,2048]{2,1,0:T(8,128)(2,1)}, u32[]{:S(2)}, u32[]{:S(2)}) async-start(bf16[32,36,2048]{2,1,0:T(8,128)(2,1)} %reshape.167), calls=%async_computation.1 | async-start | bytes 10485760 | tf_op jit(solution)/shard_map/all_to_all | solution.py:71
  98.6 80.7 %all-to-all-start = ((bf16[32,36,2048]{2,1,0:T(8,128)(2,1)}), bf16[32,36,2048]{2,1,0:T(8,128)(2,1)}, u32[]{:S(2)}, u32[]{:S(2)}) async-start(bf16[32,36,2048]{2,1,0:T(8,128)(2,1)} %reshape.165), calls=%async_computation | async-start | bytes 10485760 | tf_op jit(solution)/shard_map/all_to_all | solution.py:78
  109.6 15.4 %slice-start.6 = ((s8[6291456]{0:T(1024)(128)(4,1)}), s8[4194304]{0:T(1024)(128)(4,1)S(1)}, s32[]{:S(2)}) async-start(s8[6291456]{0:T(1024)(128)(4,1)} %bitcast.226), calls=%async_computation.9 | async-start | bytes 8388608
  114.9 10.2 %copy-start.5 = (bf16[32,36,2048]{2,0,1:T(8,128)(2,1)}, bf16[32,36,2048]{2,0,1:T(8,128)(2,1)S(1)}, u32[]{:S(2)}) copy-start(bf16[32,36,2048]{2,0,1:T(8,128)(2,1)S(1)} %copy.78) | copy-start | bytes 14155780
  114.9 10.2 %slice-start.7 = ((s8[6291456]{0:T(1024)(128)(4,1)}), s8[2097152]{0:T(1024)(128)(4,1)S(1)}, s32[]{:S(2)}) async-start(s8[6291456]{0:T(1024)(128)(4,1)} %bitcast.226), calls=%async_computation.10 | async-start | bytes 4194304
  179.4 17.6 %slice-start = ((s8[4718592]{0:T(1024)(128)(4,1)}), s8[4194304]{0:T(1024)(128)(4,1)S(1)}, s32[]{:S(2)}) async-start(s8[4718592]{0:T(1024)(128)(4,1)} %bitcast.206), calls=%async_computation.3 | async-start | bytes 8388608
  184.6 12.3 %copy-start.6 = (bf16[32,36,2048]{2,0,1:T(8,128)(2,1)}, bf16[32,36,2048]{2,0,1:T(8,128)(2,1)S(1)}, u32[]{:S(2)}) copy-start(bf16[32,36,2048]{2,0,1:T(8,128)(2,1)S(1)} %copy.76) | copy-start | bytes 14155780
  184.6 12.4 %slice-start.1 = ((s8[4718592]{0:T(1024)(128)(4,1)}), s8[524288]{0:T(1024)(128)(4,1)S(1)}, s32[]{:S(2)}) async-start(s8[4718592]{0:T(1024)(128)(4,1)} %bitcast.206), calls=%async_computation.4 | async-start | bytes 1048576
  196.9 10.4 %copy-start.19 = (bf16[32,2,18,768]{3,0,2,1:T(8,128)(2,1)}, bf16[32,2,18,768]{3,0,2,1:T(8,128)(2,1)S(1)}, u32[]{:S(2)}) copy-start(bf16[32,2,18,768]{3,0,2,1:T(8,128)(2,1)S(1)} %get-tuple-element.16) | copy-start | bytes 5308420
  196.9 17.6 %copy-start.21 = (bf16[32,2,18,768]{3,0,2,1:T(8,128)(2,1)}, bf16[32,2,18,768]{3,0,2,1:T(8,128)(2,1)S(1)}, u32[]{:S(2)}) copy-start(bf16[32,2,18,768]{3,0,2,1:T(8,128)(2,1)S(1)} %get-tuple-element.15) | copy-start | bytes 5308420
  200.2 5.7 %collective-permute-start = (bf16[2,2,768,512]{3,2,1,0:T(8,128)(2,1)S(1)}, bf16[2,2,768,512]{3,2,1,0:T(8,128)(2,1)S(1)}, u32[]{:S(2)}, u32[]{:S(2)}) collective-permute-start(bf16[2,2,768,512]{3,2,1,0:T(8,128)(2,1)S(1)} %pad_maximum_fusion), channel_id=1, source_target_pairs={{0,32},{32,0},{1,33},{33,1},{2,34},{34,2},{3,35},{35,3},{4,36},{36... | collective-permute-start | bytes 9437192 | tf_op jit(solution)/shard_map/ppermute | solution.py:125
  211.0 11.7 %collective-permute-start.1 = (bf16[2,2,768,512]{3,2,1,0:T(8,128)(2,1)}, bf16[2,2,768,512]{3,2,1,0:T(8,128)(2,1)}, u32[]{:S(2)}, u32[]{:S(2)}) collective-permute-start(bf16[2,2,768,512]{3,2,1,0:T(8,128)(2,1)} %pad_maximum_fusion.1), channel_id=1, source_target_pairs={{0,32},{32,0},{1,33},{33,1},{2,34},{34,2},{3,35},{35,3},{4,36},{36... | collective-permute-start | bytes 9437192 | tf_op jit(solution)/shard_map/ppermute | solution.py:128
  211.7 11.0 %slice-start.2 = ((s8[4718592]{0:T(1024)(128)(4,1)}), s8[4194304]{0:T(1024)(128)(4,1)S(1)}, s32[]{:S(2)}) async-start(s8[4718592]{0:T(1024)(128)(4,1)} %bitcast.213), calls=%async_computation.5 | async-start | bytes 8388608
  214.6 8.1 %slice-start.3 = ((s8[4718592]{0:T(1024)(128)(4,1)}), s8[524288]{0:T(1024)(128)(4,1)S(1)}, s32[]{:S(2)}) async-start(s8[4718592]{0:T(1024)(128)(4,1)} %bitcast.213), calls=%async_computation.6 | async-start | bytes 1048576
  218.5 58.7 %collective-permute-start.2 = (bf16[2,768,512]{2,1,0:T(8,128)(2,1)S(1)}, bf16[2,768,512]{2,1,0:T(8,128)(2,1)}, u32[]{:S(2)}, u32[]{:S(2)}) collective-permute-start(bf16[2,768,512]{2,1,0:T(8,128)(2,1)S(1)} %slice_bitcast_fusion.4), channel_id=1, source_target_pairs={{0,64},{64,0},{1,65},{65,1},{2,66},{66,2},{3,67},{67,3},{4,68},{68... | collective-permute-start | bytes 4718600 | tf_op jit(solution)/shard_map/ppermute | solution.py:138
  225.6 7.1 %slice-start.4 = ((s8[6291456]{0:T(1024)(128)(4,1)}), s8[4194304]{0:T(1024)(128)(4,1)S(1)}, s32[]{:S(2)}) async-start(s8[6291456]{0:T(1024)(128)(4,1)} %bitcast.222), calls=%async_computation.7 | async-start | bytes 8388608
  232.4 39.8 %collective-permute-start.4 = (bf16[2,2,768,512]{3,2,1,0:T(8,128)(2,1)}, bf16[2,2,768,512]{3,2,1,0:T(8,128)(2,1)}, u32[]{:S(2)}, u32[]{:S(2)}) collective-permute-start(bf16[2,2,768,512]{3,2,1,0:T(8,128)(2,1)} %pad_maximum_fusion.2), channel_id=1, source_target_pairs={{0,32},{32,0},{1,33},{33,1},{2,34},{34,2},{3,35},{35,3},{4,36},{36... | collective-permute-start | bytes 9437192 | tf_op jit(solution)/shard_map/ppermute | solution.py:132
  253.6 102.5 %all-to-all-start.2 = ((bf16[32,36,2176]{2,1,0:T(8,128)(2,1)}), bf16[32,36,2176]{2,1,0:T(8,128)(2,1)}, u32[]{:S(2)}, u32[]{:S(2)}) async-start(bf16[32,36,2176]{2,1,0:T(8,128)(2,1)} %copy.85), calls=%async_computation.2 | async-start | bytes 11141120 | tf_op jit(solution)/shard_map/all_to_all | solution.py:148
  271.8 37.6 %collective-permute-start.3 = (bf16[2,768,512]{2,1,0:T(8,128)(2,1)S(1)}, bf16[2,768,512]{2,1,0:T(8,128)(2,1)S(1)}, u32[]{:S(2)}, u32[]{:S(2)}) collective-permute-start(bf16[2,768,512]{2,1,0:T(8,128)(2,1)S(1)} %slice_bitcast_fusion.2), channel_id=1, source_target_pairs={{0,64},{64,0},{1,65},{65,1},{2,66},{66,2},{3,67},{67,3},{4,68},{68... | collective-permute-start | bytes 4718600 | tf_op jit(solution)/shard_map/ppermute | solution.py:138
  276.5 65.5 %collective-permute-start.5 = (bf16[2,768,512]{2,1,0:T(8,128)(2,1)S(1)}, bf16[2,768,512]{2,1,0:T(8,128)(2,1)S(1)}, u32[]{:S(2)}, u32[]{:S(2)}) collective-permute-start(bf16[2,768,512]{2,1,0:T(8,128)(2,1)S(1)} %slice_bitcast_fusion), channel_id=1, source_target_pairs={{0,64},{64,0},{1,65},{65,1},{2,66},{66,2},{3,67},{67,3},{4,68},{68... | collective-permute-start | bytes 4718600 | tf_op jit(solution)/shard_map/ppermute | solution.py:138
  356.1 8.7 %copy-start.10 = (pred[1152,128]{1,0:T(8,128)(4,1)S(1)}, pred[1152,128]{1,0:T(8,128)(4,1)}, u32[]{:S(2)}) copy-start(pred[1152,128]{1,0:T(8,128)(4,1)} %copy-done.9) | copy-start | bytes 442372
  (17 other events, 67.0 us)

commit v10 on v6

v10 whole, which is shorter than its diff:
```python
import jax
import jax.numpy as jnp
from jax import lax
from jax.sharding import Mesh
from jax.sharding import PartitionSpec as P


def combine_weights(gate_logits):
    raised = jnp.exp(gate_logits)
    return raised / jnp.sum(raised, axis=1, keepdims=True)


def diagonal_groups(xlo_count, owners, hi_stride):
    groups = [[], []]
    for xlo in range(xlo_count):
        for holder in range(owners):
            groups[xlo ^ ((holder // hi_stride) % 2)].append(xlo * owners + holder)
    return groups


def per_device(tokens_in, out_grad, gate_logits, route_ids, w_gate, w_up, w_down):
    tok_rows, model_width = tokens_in.shape
    topk_count = route_ids.shape[1]
    local_experts = w_gate.shape[1]
    hidden_width = w_gate.shape[2]
    xlo_count = lax.axis_size("xlo")
    core_count = lax.axis_size("core")
    owners = lax.axis_size("expert")
    expert_count = local_experts * owners
    capacity = 9 * tok_rows * topk_count // (8 * expert_count)
    pair_count = tok_rows * topk_count
    slot_count = expert_count * capacity
    xlo = lax.axis_index("xlo")
    core = lax.axis_index("core")
    hi_stride = 4
    group_half = owners // 2
    my_xhi = (lax.axis_index("expert") // hi_stride) % 2
    my_group = xlo ^ my_xhi
    groups = diagonal_groups(xlo_count, owners, hi_stride)

    weights = combine_weights(gate_logits)
    flat_ids = route_ids.reshape(-1)
    flat_weights = weights.reshape(-1)

    onehot = (flat_ids[:, None] == jnp.arange(expert_count, dtype=jnp.int32)[None, :]).astype(
        jnp.bfloat16
    )
    pos = jnp.arange(pair_count, dtype=jnp.int32)
    earlier = (pos[None, :] < pos[:, None]).astype(jnp.bfloat16)
    before = jnp.dot(earlier, onehot, preferred_element_type=jnp.float32)
    slot_rank = jnp.sum(before * onehot.astype(jnp.float32), axis=1).astype(jnp.int32)
    holder = flat_ids // local_experts
    holder_xhi = (holder // hi_stride) % 2
    group_pos = (my_group ^ holder_xhi) * group_half + (holder // (2 * hi_stride)) * hi_stride + (
        holder % hi_stride
    )
    slot_of_pair = (group_pos * local_experts + flat_ids % local_experts) * capacity + slot_rank

    slot_ids = jnp.arange(slot_count, dtype=jnp.int32)
    pair_hit = slot_of_pair[None, :] == slot_ids[:, None]
    token_hit = jnp.any(pair_hit.reshape(slot_count, tok_rows, topk_count), axis=2)
    dispatch = token_hit.astype(jnp.bfloat16)
    slot_weight = jnp.sum(jnp.where(pair_hit, flat_weights[None, :], 0.0), axis=1)

    block_count = xlo_count * core_count
    block_rows = model_width // block_count
    starts = [
        ((xlo ^ xlo_side) * core_count + (core ^ core_side)) * block_rows
        for xlo_side, core_side in ((1, 1), (0, 1), (1, 0), (0, 0))
    ]
    core_pairs = [(i, (i + 1) % core_count) for i in range(core_count)]
    xlo_pairs = [(i, (i + 1) % xlo_count) for i in range(xlo_count)]
    lane_pad = 128
    expert_slots = owners * capacity
    dispatch = dispatch.reshape(owners, local_experts, capacity, tok_rows)
    slot_weight = slot_weight.reshape(owners, local_experts, capacity)
    pair_hit = pair_hit.reshape(owners, local_experts, capacity, pair_count)

    shares = jnp.zeros((block_rows, 3, local_experts, hidden_width), jnp.bfloat16)
    combined = jnp.zeros((tok_rows, model_width), jnp.float32)
    pair_probs = jnp.zeros((pair_count,), jnp.float32)
    for local in range(local_experts):
        picks = dispatch[:, local].reshape(expert_slots, tok_rows)
        send_tokens = jnp.dot(picks, tokens_in, preferred_element_type=jnp.float32)
        send_grads = jnp.dot(picks, out_grad, preferred_element_type=jnp.float32)
        send_scaled = slot_weight[:, local].reshape(expert_slots, 1) * send_grads
        send = jnp.concatenate([send_tokens, send_scaled], axis=1).astype(jnp.bfloat16)
        recv = lax.all_to_all(
            send.reshape(owners, capacity, 2 * model_width),
            ("xlo", "expert"),
            split_axis=0,
            concat_axis=0,
            tiled=True,
            axis_index_groups=groups,
        ).reshape(expert_slots, 2 * model_width)
        rows_in = recv[:, :model_width]
        rows_scaled = recv[:, model_width:]
        wg = w_gate[:, local]
        wu = w_up[:, local]
        wd = w_down[:, local]

        gate_pre = jnp.dot(rows_in, wg, preferred_element_type=jnp.float32)
        up_pre = jnp.dot(rows_in, wu, preferred_element_type=jnp.float32)
        sigmoid_gate = jax.nn.sigmoid(gate_pre)
        active = gate_pre * sigmoid_gate
        hidden = (active * up_pre).astype(jnp.bfloat16)
        hidden_grad = jnp.dot(rows_scaled, wd, preferred_element_type=jnp.float32)
        prob_part = jnp.sum(hidden_grad * hidden.astype(jnp.float32), axis=1).astype(
            jnp.bfloat16
        )
        gate_grad = (
            hidden_grad * up_pre * sigmoid_gate * (1.0 + gate_pre * (1.0 - sigmoid_gate))
        ).astype(jnp.bfloat16)
        up_grad = (hidden_grad * active).astype(jnp.bfloat16)

        blocks = [
            jnp.stack(
                [
                    lax.dot_general(
                        left,
                        lax.dynamic_slice_in_dim(right, at, block_rows, 1),
                        (((0,), (0,)), ((), ())),
                        preferred_element_type=jnp.float32,
                    )
                    for left, right in (
                        (gate_grad, rows_in),
                        (up_grad, rows_in),
                        (hidden, rows_scaled),
                    )
                ]
            ).astype(jnp.bfloat16)
            for at in starts
        ]
        to_sibling, own_blocks, gate_grad, up_grad = lax.optimization_barrier(
            (jnp.stack(blocks[:2]), jnp.stack(blocks[2:]), gate_grad, up_grad)
        )
        from_sibling = lax.ppermute(to_sibling, "core", core_pairs)
        summed = (own_blocks.astype(jnp.float32) + from_sibling.astype(jnp.float32)).astype(
            jnp.bfloat16
        )
        theirs = lax.ppermute(summed[0], "xlo", xlo_pairs)
        share = (summed[1].astype(jnp.float32) + theirs.astype(jnp.float32)).astype(jnp.bfloat16)
        shares = lax.dynamic_update_index_in_dim(
            shares, jnp.transpose(share, (2, 0, 1)), local, 2
        )

        row_grad = (
            jnp.dot(gate_grad, wg.T, preferred_element_type=jnp.float32)
            + jnp.dot(up_grad, wu.T, preferred_element_type=jnp.float32)
        ).astype(jnp.bfloat16)
        prob_cols = jnp.pad(prob_part[:, None], ((0, 0), (0, lane_pad - 1)))
        back = lax.all_to_all(
            jnp.concatenate([row_grad, prob_cols], axis=1).reshape(
                owners, capacity, model_width + lane_pad
            ),
            ("xlo", "expert"),
            split_axis=0,
            concat_axis=0,
            tiled=True,
            axis_index_groups=groups,
        ).reshape(expert_slots, model_width + lane_pad)
        combined = combined + lax.dot_general(
            picks, back[:, :model_width], (((0,), (0,)), ((), ())),
            preferred_element_type=jnp.float32,
        )
        hits = pair_hit[:, local].reshape(expert_slots, pair_count)
        pair_probs = pair_probs + jnp.sum(
            jnp.where(hits, back[:, model_width].astype(jnp.float32)[:, None], 0.0), axis=0
        )

    input_grad = combined.astype(jnp.bfloat16)
    pair_probs = pair_probs.reshape(tok_rows, topk_count)
    router_grad = pair_probs - weights * jnp.sum(pair_probs, axis=1, keepdims=True)

    return (input_grad, router_grad, shares)


def solution(mesh):
    dp_count, expert_devs = mesh.devices.shape
    core_count = 2
    split_mesh = Mesh(
        mesh.devices.reshape(dp_count // core_count, core_count, expert_devs),
        ("xlo", "core", "expert"),
    )
    rows = ("xlo", "core", "expert")
    in_specs = (
        P(rows, None),
        P(rows, None),
        P(rows, None),
        P(rows, None),
        P(None, "expert", None),
        P(None, "expert", None),
        P(None, "expert", None),
    )
    out_specs = (
        P(rows, None),
        P(rows, None),
        P(("xlo", "core"), None, "expert", None),
    )
    return jax.shard_map(
        per_device, mesh=split_mesh, in_specs=in_specs, out_specs=out_specs, check_vma=False
    )
```

time: 463 us -> 472 us (1.019)
  local copies, waits for them, and re-layouts: 59.4 us -> 116 us
  waiting for transfers between devices: 239 us -> 188 us
  matrix products: 77.1 us -> 69.6 us
  other arithmetic: 33 us -> 38.8 us
    ppermute x6 -> x4, waiting for transfers between devices: 93 us -> 63.6 us  [the longest x2 63.6 us: per_device(): theirs = lax.ppermute(summed[0], 'xlo', xlo_pairs)]
    concatenate x0 -> x6, local copies, waits for them, and re-layouts: none -> 23.8 us  [per_device(): jnp.concatenate([send_tokens, send_scaled], axis=1).astype(jnp.bfloat16)]
    all_to_all x2 -> x4, waiting for transfers between devices: 146 us -> 125 us  [the longest x2 79.2 us: per_device(): lax.all_to_all(send.reshape(owners, capacity, 2 * model_width), ('xlo', '...]
    slice x3 -> x7, local copies, waits for them, and re-layouts: 18.2 us -> 38.3 us  [the longest x1 14.4 us: per_device(): wg = w_gate[:, local]]
    dot_general x20 -> x40, matrix products: 76.5 us -> 69 us  [the longest x24 27.5 us: per_device(): lax.dot_general(left, lax.dynamic_slice_in_dim(right, at, block_rows, 1),...]
    concatenate x2 -> x4, other arithmetic: 7.29 us -> 1.54 us  [the longest x2 1.11 us: per_device(): jnp.concatenate([send_tokens, send_scaled], axis=1).astype(jnp.bfloat16)]
    broadcast_in_dim x1 -> x4, other arithmetic: 1.19 us -> 6.6 us  [the longest x2 5.37 us: per_device(): lax.dynamic_update_index_in_dim(shares, jnp.transpose(share, (2, 0, 1)),...]
    reshape x4 -> x8, local copies, waits for them, and re-layouts: 24.9 us -> 28.8 us  [the longest x2 16.1 us: per_device(): recv = lax.all_to_all(send.reshape(owners, capacity, 2 * model_width), ('...]
  transfers between devices with their start and end apart: 8 -> 8, of which waited for: 4 -> 6; matrix products, arithmetic and copies ran while one was open for 11% -> 31% of each run, Pallas kernels for 0% -> 0%
where the time goes in v10:
time: 472 us; the launch traced here: 463 us
  waiting for transfers between devices  188 us (40%)
  local copies, waits for them, and re-layouts  116 us (25%)
  matrix products  69.6 us (15%)
  starting transfers between devices  48 us (10%)
  other arithmetic  38.8 us (8%)
    all_to_all x2, waiting for transfers between devices, per_device(): lax.all_to_all(send.reshape(owners, capacity, 2 * model_width), ('xlo', '...  79.2 us
    ppermute x2, waiting for transfers between devices, per_device(): theirs = lax.ppermute(summed[0], 'xlo', xlo_pairs)  63.6 us
    all_to_all x2, waiting for transfers between devices, per_device(): lax.all_to_all(jnp.concatenate([row_grad, prob_cols], axis=1).reshape(own...  45.5 us
    dot_general x24, matrix products, per_device(): lax.dot_general(left, lax.dynamic_slice_in_dim(right, at, block_rows, 1),...  27.5 us
    concatenate x6, local copies, waits for them, and re-layouts, per_device(): jnp.concatenate([send_tokens, send_scaled], axis=1).astype(jnp.bfloat16)  23.8 us
    all_to_all x2, starting transfers between devices, per_device(): lax.all_to_all(send.reshape(owners, capacity, 2 * model_width), ('xlo', '...  21.5 us
    unnamed x118, local copies, waits for them, and re-layouts  18.8 us
    reshape x2, local copies, waits for them, and re-layouts, per_device(): recv = lax.all_to_all(send.reshape(owners, capacity, 2 * model_width), ('...  16.1 us
  transfers between devices with their start and end apart: 8, of which 6 were waited for; matrix products, arithmetic and copies ran while one was open for 31% of the time, Pallas kernels for 0%

profile of v10, /device:TPU:0, one launch (start us, length us, event | category | flops | bytes accessed | tf_op | source)
XLA Modules:
  0.0 462.7 jit_solution(4182478578796114729)
XLA Ops:
  19.4 5.3 %copy.93 = bf16[32,18,4096]{2,1,0:T(8,128)(2,1)} copy(bf16[32,18,4096]{2,0,1:T(8,128)(2,1)S(1)} %pad_maximum_fusion) | data formatting | bytes 9437184 | tf_op jit(solution)/shard_map/concatenate | solution.py:87
  24.7 10.9 %all-to-all-start = ((bf16[32,18,4096]{2,1,0:T(8,128)(2,1)}), bf16[32,18,4096]{2,1,0:T(8,128)(2,1)}, u32[]{:S(2)}, u32[]{:S(2)}) async-start(bf16[32,18,4096]{2,1,0:T(8,128)(2,1)} %copy.93), calls=%async_computation | async-start | bytes 12582912 | tf_op jit(solution)/shard_map/all_to_all | solution.py:88
  48.3 5.4 %copy.101 = bf16[32,18,4096]{2,1,0:T(8,128)(2,1)} copy(bf16[32,18,4096]{2,0,1:T(8,128)(2,1)S(1)} %pad_maximum_fusion.1) | data formatting | bytes 9437184 | tf_op jit(solution)/shard_map/concatenate | solution.py:87
  53.7 14.4 %fusion.140 = (bf16[2048,1,768]{2,1,0:T(2,128)(2,1)}, bf16[2048,1,768]{2,1,0:T(2,128)(2,1)}) fusion(bf16[2048,2,768]{2,1,0:T(2,128)(2,1)} %param.11), kind=kLoop, calls=%fused_computation.257 | loop fusion | bytes 12582912 | tf_op jit(solution)/shard_map/slice | solution.py:98
  68.2 10.0 %fusion.141 = (bf16[2048,1,768]{2,1,0:T(2,128)(2,1)}, bf16[2048,1,768]{2,1,0:T(2,128)(2,1)}) fusion(bf16[2048,2,768]{2,1,0:T(2,128)(2,1)S(1)} %bitcast.142), kind=kLoop, calls=%fused_computation.258 | loop fusion | bytes 12582912 | tf_op jit(solution)/shard_map/slice | solution.py:99
  78.2 10.1 %fusion.142 = (bf16[2048,1,768]{2,1,0:T(2,128)(2,1)}, bf16[2048,1,768]{2,1,0:T(2,128)(2,1)}) fusion(bf16[2048,2,768]{2,1,0:T(2,128)(2,1)S(1)} %bitcast.144), kind=kLoop, calls=%fused_computation.259 | loop fusion | bytes 12582912 | tf_op jit(solution)/shard_map/slice | solution.py:100
  88.3 31.6 %all-to-all-done = bf16[32,18,4096]{2,1,0:T(8,128)(2,1)} async-done(((bf16[32,18,4096]{2,1,0:T(8,128)(2,1)}), bf16[32,18,4096]{2,1,0:T(8,128)(2,1)}, u32[]{:S(2)}, u32[]{:S(2)}) %all-to-all-start) | async-done | bytes 4718624 | tf_op jit(solution)/shard_map/all_to_all | solution.py:88
  120.0 10.5 %all-to-all-start.2 = ((bf16[32,18,4096]{2,1,0:T(8,128)(2,1)}), bf16[32,18,4096]{2,1,0:T(8,128)(2,1)}, u32[]{:S(2)}, u32[]{:S(2)}) async-start(bf16[32,18,4096]{2,1,0:T(8,128)(2,1)} %copy.101), calls=%async_computation.2 | async-start | bytes 12582912 | tf_op jit(solution)/shard_map/all_to_all | solution.py:88
  130.5 8.2 %reshape.612 = bf16[576,4096]{1,0:T(8,128)(2,1)} reshape(bf16[32,18,4096]{2,1,0:T(8,128)(2,1)} %all-to-all-done) | data formatting | bytes 9437184 | tf_op jit(solution)/shard_map/reshape | solution.py:95
  138.8 5.6 %fusion.44 = f32[576,768]{1,0:T(8,128)S(1)} fusion(bf16[2048,1,768]{2,1,0:T(2,128)(2,1)} %get-tuple-element.43, bf16[576,4096]{1,0:T(8,128)(2,1)} %reshape.612), kind=kOutput, calls=%fused_computation.114 | convolution fusion | flops 1811939328 | bytes 10420224 | tf_op jit(solution)/shard_map/dot_general | solution.py:102
  168.3 47.5 %all-to-all-done.2 = bf16[32,18,4096]{2,1,0:T(8,128)(2,1)} async-done(((bf16[32,18,4096]{2,1,0:T(8,128)(2,1)}), bf16[32,18,4096]{2,1,0:T(8,128)(2,1)}, u32[]{:S(2)}, u32[]{:S(2)}) %all-to-all-start.2) | async-done | bytes 4718624 | tf_op jit(solution)/shard_map/all_to_all | solution.py:88
  215.8 7.9 %reshape.615 = bf16[576,4096]{1,0:T(8,128)(2,1)} reshape(bf16[32,18,4096]{2,1,0:T(8,128)(2,1)} %all-to-all-done.2) | data formatting | bytes 9437184 | tf_op jit(solution)/shard_map/reshape | solution.py:95
  227.4 5.1 %fusion.45 = f32[576,768]{1,0:T(8,128)S(1)} fusion(bf16[2048,1,768]{2,1,0:T(2,128)(2,1)} %get-tuple-element.44, bf16[576,4096]{1,0:T(8,128)(2,1)S(1)} %copy-done.4), kind=kOutput, calls=%fused_computation.115 | convolution fusion | flops 1811939328 | bytes 7274496 | tf_op jit(solution)/shard_map/dot_general | solution.py:103
  248.3 4.7 %maximum_maximum_fusion = (bf16[2,3,768,512]{3,2,1,0:T(8,128)(2,1)}, bf16[2,3,768,512]{3,2,1,0:T(8,128)(2,1)}) fusion(bf16[1,1,768,512]{3,2,1,0:T(8,128)(2,1)S(1)} %copy-done.17, bf16[1,1,768,512]{3,2,1,0:T(8,128)(2,1)S(1)} %copy-done.16, bf16[1,1,768,512]{3,2,1,0:T(8,128)(2,1)S(1)} %copy-done.15, bf16[1,1,768,512]{3,2,1,0:T(8,128)(2,1)S(1)} %copy-done.14, ...), kind=kLoop, calls=%fused_computation.6 | loop fusion | flops 23592960 | bytes 18874368 | tf_op jit(solution)/shard_map/stack | solution.py:135
  265.1 6.8 %all-to-all-start.3 = ((bf16[32,18,2176]{2,1,0:T(8,128)(2,1)}), bf16[32,18,2176]{2,1,0:T(8,128)(2,1)}, u32[]{:S(2)}, u32[]{:S(2)}) async-start(bf16[32,18,2176]{2,1,0:T(8,128)(2,1)} %reshape.616), calls=%async_computation.3 | async-start | bytes 6684672 | tf_op jit(solution)/shard_map/all_to_all | solution.py:152
  272.1 5.0 %fusion.43 = f32[576,2048]{1,0:T(8,128)S(1)} fusion(bf16[576,768]{1,0:T(8,128)(2,1)S(1)} %copy-done.29, bf16[2048,1,768]{2,1,0:T(2,128)(2,1)} %get-tuple-element.43), kind=kOutput, calls=%fused_computation.113 | convolution fusion | flops 1811939328 | bytes 8749056 | tf_op jit(solution)/shard_map/dot_general | solution.py:148
  281.8 35.3 %all-to-all-done.3 = bf16[32,18,2176]{2,1,0:T(8,128)(2,1)} async-done(((bf16[32,18,2176]{2,1,0:T(8,128)(2,1)}), bf16[32,18,2176]{2,1,0:T(8,128)(2,1)}, u32[]{:S(2)}, u32[]{:S(2)}) %all-to-all-start.3) | async-done | bytes 2506784 | tf_op jit(solution)/shard_map/all_to_all | solution.py:152
  317.1 7.1 %all-to-all-start.1 = ((bf16[32,18,2176]{2,1,0:T(8,128)(2,1)}), bf16[32,18,2176]{2,1,0:T(8,128)(2,1)}, u32[]{:S(2)}, u32[]{:S(2)}) async-start(bf16[32,18,2176]{2,1,0:T(8,128)(2,1)} %reshape.613), calls=%async_computation.1 | async-start | bytes 6684672 | tf_op jit(solution)/shard_map/all_to_all | solution.py:152
  324.3 5.5 %add_convert_fusion.1 = bf16[2,3,768,512]{3,2,1,0:T(8,128)(2,1)S(1)} fusion(bf16[2,3,768,512]{3,2,1,0:T(8,128)(2,1)} %collective-permute-done, bf16[2,3,768,512]{3,2,1,0:T(8,128)(2,1)} %get-tuple-element.15), kind=kLoop, calls=%fused_computation.1 | loop fusion | flops 9437184 | bytes 14155776 | tf_op jit(solution)/shard_map/convert_element_type | solution.py:138
  331.5 11.8 %collective-permute-start.1 = (bf16[3,768,512]{2,1,0:T(8,128)(2,1)}, bf16[3,768,512]{2,1,0:T(8,128)(2,1)}, u32[]{:S(2)}, u32[]{:S(2)}) collective-permute-start(bf16[3,768,512]{2,1,0:T(8,128)(2,1)} %slice_bitcast_fusion.2), channel_id=1, source_target_pairs={{0,64},{64,0},{1,65},{65,1},{2,66},{66,2},{3,67},{67,3},{4,68},{68... | collective-permute-start | bytes 7077896 | tf_op jit(solution)/shard_map/ppermute | solution.py:141
  355.5 10.2 %all-to-all-done.1 = bf16[32,18,2176]{2,1,0:T(8,128)(2,1)} async-done(((bf16[32,18,2176]{2,1,0:T(8,128)(2,1)}), bf16[32,18,2176]{2,1,0:T(8,128)(2,1)}, u32[]{:S(2)}, u32[]{:S(2)}) %all-to-all-start.1) | async-done | bytes 2506784 | tf_op jit(solution)/shard_map/all_to_all | solution.py:152
  378.3 17.6 %collective-permute-done.1 = bf16[3,768,512]{2,1,0:T(8,128)(2,1)} collective-permute-done((bf16[3,768,512]{2,1,0:T(8,128)(2,1)}, bf16[3,768,512]{2,1,0:T(8,128)(2,1)}, u32[]{:S(2)}, u32[]{:S(2)}) %collective-permute-start.1) | collective-permute-done | bytes 2359328 | tf_op jit(solution)/shard_map/ppermute | solution.py:141
  398.9 46.0 %collective-permute-done.3 = bf16[3,768,512]{2,1,0:T(8,128)(2,1)} collective-permute-done((bf16[3,768,512]{2,1,0:T(8,128)(2,1)}, bf16[3,768,512]{2,1,0:T(8,128)(2,1)}, u32[]{:S(2)}, u32[]{:S(2)}) %collective-permute-start.3) | collective-permute-done | bytes 2359328 | tf_op jit(solution)/shard_map/ppermute | solution.py:141
  449.8 12.4 %copy.109 = bf16[512,3,2,768]{3,2,1,0:T(2,128)(2,1)} copy(bf16[512,3,2,768]{0,3,1,2:T(8,128)(2,1)} %pad_maximum_fusion.2) | data formatting | bytes 9437184
  (225 shorter events, 125.3 us)
Async XLA Ops:
  0.6 17.4 %copy-start = (bf16[128,2048]{1,0:T(8,128)(2,1)S(1)}, bf16[128,2048]{1,0:T(8,128)(2,1)}, u32[]{:S(2)}) copy-start(bf16[128,2048]{1,0:T(8,128)(2,1)} %param.7) | copy-start | bytes 1572868
  24.7 95.3 %all-to-all-start = ((bf16[32,18,4096]{2,1,0:T(8,128)(2,1)}), bf16[32,18,4096]{2,1,0:T(8,128)(2,1)}, u32[]{:S(2)}, u32[]{:S(2)}) async-start(bf16[32,18,4096]{2,1,0:T(8,128)(2,1)} %copy.93), calls=%async_computation | async-start | bytes 12582912 | tf_op jit(solution)/shard_map/all_to_all | solution.py:88
  48.3 19.8 %slice-start = ((s8[6291456]{0:T(1024)(128)(4,1)}), s8[2097152]{0:T(1024)(128)(4,1)S(1)}, s32[]{:S(2)}) async-start(s8[6291456]{0:T(1024)(128)(4,1)} %bitcast.141), calls=%async_computation.4 | async-start | bytes 4194304
  53.7 14.4 %slice-start.1 = ((s8[6291456]{0:T(1024)(128)(4,1)}), s8[4194304]{0:T(1024)(128)(4,1)S(1)}, s32[]{:S(2)}) async-start(s8[6291456]{0:T(1024)(128)(4,1)} %bitcast.141), calls=%async_computation.5 | async-start | bytes 8388608
  53.7 24.5 %slice-start.2 = ((s8[6291456]{0:T(1024)(128)(4,1)}), s8[4194304]{0:T(1024)(128)(4,1)S(1)}, s32[]{:S(2)}) async-start(s8[6291456]{0:T(1024)(128)(4,1)} %bitcast.143), calls=%async_computation.6 | async-start | bytes 8388608
  120.0 95.8 %all-to-all-start.2 = ((bf16[32,18,4096]{2,1,0:T(8,128)(2,1)}), bf16[32,18,4096]{2,1,0:T(8,128)(2,1)}, u32[]{:S(2)}, u32[]{:S(2)}) async-start(bf16[32,18,4096]{2,1,0:T(8,128)(2,1)} %copy.101), calls=%async_computation.2 | async-start | bytes 12582912 | tf_op jit(solution)/shard_map/all_to_all | solution.py:88
  130.5 13.9 %slice-start.8 = ((s8[6291456]{0:T(1024)(128)(4,1)}), s8[2097152]{0:T(1024)(128)(4,1)S(1)}, s32[]{:S(2)}) async-start(s8[6291456]{0:T(1024)(128)(4,1)} %bitcast.149), calls=%async_computation.12 | async-start | bytes 4194304
  150.4 12.8 %copy-start.28 = (bf16[576,768]{1,0:T(8,128)(2,1)}, bf16[576,768]{1,0:T(8,128)(2,1)S(1)}, u32[]{:S(2)}) copy-start(bf16[576,768]{1,0:T(8,128)(2,1)S(1)} %get-tuple-element.11) | copy-start | bytes 2654212
  150.4 14.5 %copy-start.26 = (bf16[576,768]{1,0:T(8,128)(2,1)}, bf16[576,768]{1,0:T(8,128)(2,1)S(1)}, u32[]{:S(2)}) copy-start(bf16[576,768]{1,0:T(8,128)(2,1)S(1)} %get-tuple-element.12) | copy-start | bytes 2654212
  253.0 71.3 %collective-permute-start = (bf16[2,3,768,512]{3,2,1,0:T(8,128)(2,1)}, bf16[2,3,768,512]{3,2,1,0:T(8,128)(2,1)}, u32[]{:S(2)}, u32[]{:S(2)}) collective-permute-start(bf16[2,3,768,512]{3,2,1,0:T(8,128)(2,1)} %get-tuple-element.16), channel_id=1, source_target_pairs={{0,32},{32,0},{1,33},{33,1},{2,34},{34,2},{3,35},{35,3},{4,36},{36... | collective-permute-start | bytes 14155784 | tf_op jit(solution)/shard_map/ppermute | solution.py:137
  257.6 85.8 %collective-permute-start.2 = (bf16[2,3,768,512]{3,2,1,0:T(8,128)(2,1)}, bf16[2,3,768,512]{3,2,1,0:T(8,128)(2,1)}, u32[]{:S(2)}, u32[]{:S(2)}) collective-permute-start(bf16[2,3,768,512]{3,2,1,0:T(8,128)(2,1)} %get-tuple-element.18), channel_id=1, source_target_pairs={{0,32},{32,0},{1,33},{33,1},{2,34},{34,2},{3,35},{35,3},{4,36},{36... | collective-permute-start | bytes 14155784 | tf_op jit(solution)/shard_map/ppermute | solution.py:137
  265.1 52.0 %all-to-all-start.3 = ((bf16[32,18,2176]{2,1,0:T(8,128)(2,1)}), bf16[32,18,2176]{2,1,0:T(8,128)(2,1)}, u32[]{:S(2)}, u32[]{:S(2)}) async-start(bf16[32,18,2176]{2,1,0:T(8,128)(2,1)} %reshape.616), calls=%async_computation.3 | async-start | bytes 6684672 | tf_op jit(solution)/shard_map/all_to_all | solution.py:152
  317.1 26.2 %slice-start.6 = ((s8[4718592]{0:T(1024)(128)(4,1)}), s8[524288]{0:T(1024)(128)(4,1)S(1)}, s32[]{:S(2)}) async-start(s8[4718592]{0:T(1024)(128)(4,1)} %bitcast.147), calls=%async_computation.10 | async-start | bytes 1048576
  317.1 48.5 %all-to-all-start.1 = ((bf16[32,18,2176]{2,1,0:T(8,128)(2,1)}), bf16[32,18,2176]{2,1,0:T(8,128)(2,1)}, u32[]{:S(2)}, u32[]{:S(2)}) async-start(bf16[32,18,2176]{2,1,0:T(8,128)(2,1)} %reshape.613), calls=%async_computation.1 | async-start | bytes 6684672 | tf_op jit(solution)/shard_map/all_to_all | solution.py:152
  324.3 19.1 %slice-start.7 = ((s8[4718592]{0:T(1024)(128)(4,1)}), s8[4194304]{0:T(1024)(128)(4,1)S(1)}, s32[]{:S(2)}) async-start(s8[4718592]{0:T(1024)(128)(4,1)} %bitcast.147), calls=%async_computation.11 | async-start | bytes 8388608
  329.8 17.3 %copy-start.2 = (bf16[2,3,768,512]{3,2,1,0:T(8,128)(2,1)}, bf16[2,3,768,512]{3,2,1,0:T(8,128)(2,1)S(1)}, u32[]{:S(2)}) copy-start(bf16[2,3,768,512]{3,2,1,0:T(8,128)(2,1)S(1)} %add_convert_fusion.1) | copy-start | bytes 14155780
  331.5 64.3 %collective-permute-start.1 = (bf16[3,768,512]{2,1,0:T(8,128)(2,1)}, bf16[3,768,512]{2,1,0:T(8,128)(2,1)}, u32[]{:S(2)}, u32[]{:S(2)}) collective-permute-start(bf16[3,768,512]{2,1,0:T(8,128)(2,1)} %slice_bitcast_fusion.2), channel_id=1, source_target_pairs={{0,64},{64,0},{1,65},{65,1},{2,66},{66,2},{3,67},{67,3},{4,68},{68... | collective-permute-start | bytes 7077896 | tf_op jit(solution)/shard_map/ppermute | solution.py:141
  350.0 94.9 %collective-permute-start.3 = (bf16[3,768,512]{2,1,0:T(8,128)(2,1)}, bf16[3,768,512]{2,1,0:T(8,128)(2,1)}, u32[]{:S(2)}, u32[]{:S(2)}) collective-permute-start(bf16[3,768,512]{2,1,0:T(8,128)(2,1)} %slice_bitcast_fusion), channel_id=1, source_target_pairs={{0,64},{64,0},{1,65},{65,1},{2,66},{66,2},{3,67},{67,3},{4,68},{68... | collective-permute-start | bytes 7077896 | tf_op jit(solution)/shard_map/ppermute | solution.py:141
  355.5 18.1 %copy-start.8 = (f32[128,8]{1,0:T(8,128)S(1)}, f32[128,8]{1,0:T(8,128)}, u32[]{:S(2)}) copy-start(f32[128,8]{1,0:T(8,128)} %copy-done.7) | copy-start | bytes 12292
  355.5 18.1 %copy-start.25 = (f32[128]{0:T(128)S(1)}, f32[128]{0:T(128)}, u32[]{:S(2)}) copy-start(f32[128]{0:T(128)} %copy-done.24) | copy-start | bytes 1540
  355.5 18.9 %copy-start.20 = (pred[576,128]{1,0:T(32,128)(4,1)S(1)}, pred[576,128]{1,0:T(32,128)(4,1)}, u32[]{:S(2)}) copy-start(pred[576,128]{1,0:T(32,128)(4,1)} %reshape_squeeze.4) | copy-start | bytes 221188
  374.4 70.5 %slice-start.4 = ((s8[4718592]{0:T(1024)(128)(4,1)}), s8[4194304]{0:T(1024)(128)(4,1)S(1)}, s32[]{:S(2)}) async-start(s8[4718592]{0:T(1024)(128)(4,1)} %bitcast.145), calls=%async_computation.8 | async-start | bytes 8388608
  376.8 68.0 %slice-start.5 = ((s8[4718592]{0:T(1024)(128)(4,1)}), s8[524288]{0:T(1024)(128)(4,1)S(1)}, s32[]{:S(2)}) async-start(s8[4718592]{0:T(1024)(128)(4,1)} %bitcast.145), calls=%async_computation.9 | async-start | bytes 1048576
  447.2 15.0 %copy-start.1 = (bf16[128,2048]{1,0:T(8,128)(2,1)S(1)}, bf16[128,2048]{1,0:T(8,128)(2,1)}, u32[]{:S(2)}) copy-start(bf16[128,2048]{1,0:T(8,128)(2,1)} %param.7) | copy-start | bytes 1572868
  (41 other events, 198.1 us)

commit v11 on v9

--- a/solution.py
+++ b/solution.py
@@ -1,6 +1,7 @@
 import jax
 import jax.numpy as jnp
 from jax import lax
+from jax.experimental.layout import Layout, with_layout_constraint
 from jax.sharding import Mesh
 from jax.sharding import PartitionSpec as P
 
@@ -131,14 +132,15 @@
     )
     down_from = lax.ppermute(down_sib, "core", core_pairs)
 
-    shares = jnp.zeros((block_rows, 3, local_experts, hidden_width), jnp.bfloat16)
+    shares = []
     pieces = ((gate_from, gate_own), (up_from, up_own), (down_from, down_own))
     for kind, (from_sibling, own) in enumerate(pieces):
         summed = (own.astype(jnp.float32) + from_sibling.astype(jnp.float32)).astype(jnp.bfloat16)
         theirs = lax.ppermute(summed[0], "xlo", xlo_pairs)
         share = (summed[1].astype(jnp.float32) + theirs.astype(jnp.float32)).astype(jnp.bfloat16)
-        shares = lax.dynamic_update_index_in_dim(shares, jnp.transpose(share, (2, 0, 1)), kind, 1)
+        shares.append(with_layout_constraint(jnp.transpose(share, (2, 0, 1)), Layout((0, 1, 2))))
 
+    shares = with_layout_constraint(jnp.stack(shares, axis=1), Layout((0, 1, 2, 3)))
     row_grad = (
         jnp.einsum("nemh,deh->nemd", gate_grad, w_gate, preferred_element_type=jnp.float32)
         + jnp.einsum("nemh,deh->nemd", up_grad, w_up, preferred_element_type=jnp.float32)

time: 378 us -> 482 us (1.28)
  local copies, waits for them, and re-layouts: 57.4 us -> 103 us
  other arithmetic: 26 us -> 68.6 us
  matrix products: 79.3 us -> 102 us
  waiting for transfers between devices: 170 us -> 163 us
    unnamed x69 -> x78, local copies, waits for them, and re-layouts: 17.3 us -> 61 us
    another operation x4 -> x3, other arithmetic: 6.08 us -> 27.4 us  [blocks_of(): return (jnp.stack(blocks[:2]), jnp.stack(blocks[2:]))]
    dot_general x12, matrix products: 23.3 us -> 44 us  [blocks_of(): jnp.einsum('nemh,nemd->ehd', left, lax.dynamic_slice_in_dim(right, at, bl...]
    another operation x0 -> x4, other arithmetic: none -> 15.2 us  [per_device(): jnp.stack(shares, axis=1)]
    convert_element_type x3, other arithmetic: 6.63 us -> 17.7 us  [per_device(): (own.astype(jnp.float32) + from_sibling.astype(jnp.float32)).astype(jnp.b...]
  transfers between devices with their start and end apart: 9 -> 9, of which waited for: 5 -> 5; matrix products, arithmetic and copies ran while one was open for 28% -> 37% of each run, Pallas kernels for 0% -> 0%
where the time goes in v11:
time: 482 us; the launch traced here: 474 us
  waiting for transfers between devices  163 us (34%)
  local copies, waits for them, and re-layouts  103 us (21%)
  matrix products  102 us (21%)
  other arithmetic  68.6 us (14%)
  starting transfers between devices  36.1 us (7%)
    unnamed x78, local copies, waits for them, and re-layouts  61 us
    all_to_all x1, waiting for transfers between devices, per_device(): lax.all_to_all(send_tokens.reshape(send_shape), ('xlo', 'expert'), split_...  57.3 us
    ppermute x3, waiting for transfers between devices, per_device(): theirs = lax.ppermute(summed[0], 'xlo', xlo_pairs)  55.8 us
    all_to_all x1, waiting for transfers between devices, per_device(): lax.all_to_all(send_scaled.reshape(send_shape), ('xlo', 'expert'), split_...  48.4 us
    dot_general x12, matrix products, blocks_of(): jnp.einsum('nemh,nemd->ehd', left, lax.dynamic_slice_in_dim(right, at, bl...  44 us
    another operation x3, other arithmetic, blocks_of(): return (jnp.stack(blocks[:2]), jnp.stack(blocks[2:]))  27.4 us
    convert_element_type x3, other arithmetic, per_device(): (own.astype(jnp.float32) + from_sibling.astype(jnp.float32)).astype(jnp.b...  17.7 us
    another operation x4, other arithmetic, per_device(): jnp.stack(shares, axis=1)  15.2 us
  transfers between devices with their start and end apart: 9, of which 5 were waited for; matrix products, arithmetic and copies ran while one was open for 37% of the time, Pallas kernels for 0%

profile of v11, /device:TPU:0, one launch (start us, length us, event | category | flops | bytes accessed | tf_op | source)
XLA Modules:
  0.0 474.0 jit_solution(15910338433597582326)
XLA Ops:
  10.9 7.2 %reshape.167 = bf16[32,36,2048]{2,1,0:T(8,128)(2,1)} reshape(bf16[1152,2048]{1,0:T(8,128)(2,1)} %convolution_convert_fusion) | data formatting | bytes 9437184 | tf_op jit(solution)/shard_map/reshape | solution.py:73
  18.1 10.9 %all-to-all-start.1 = ((bf16[32,36,2048]{2,1,0:T(8,128)(2,1)}), bf16[32,36,2048]{2,1,0:T(8,128)(2,1)}, u32[]{:S(2)}, u32[]{:S(2)}) async-start(bf16[32,36,2048]{2,1,0:T(8,128)(2,1)} %reshape.167), calls=%async_computation.1 | async-start | bytes 10485760 | tf_op jit(solution)/shard_map/all_to_all | solution.py:72
  34.2 7.2 %reshape.165 = bf16[32,36,2048]{2,1,0:T(8,128)(2,1)} reshape(bf16[1152,2048]{1,0:T(8,128)(2,1)} %fusion.1) | data formatting | bytes 9437184 | tf_op jit(solution)/shard_map/reshape | solution.py:80
  41.4 57.3 %all-to-all-done.1 = bf16[32,36,2048]{2,1,0:T(8,128)(2,1)} async-done(((bf16[32,36,2048]{2,1,0:T(8,128)(2,1)}), bf16[32,36,2048]{2,1,0:T(8,128)(2,1)}, u32[]{:S(2)}, u32[]{:S(2)}) %all-to-all-start.1) | async-done | bytes 4718624 | tf_op jit(solution)/shard_map/all_to_all | solution.py:72
  98.7 10.7 %all-to-all-start = ((bf16[32,36,2048]{2,1,0:T(8,128)(2,1)}), bf16[32,36,2048]{2,1,0:T(8,128)(2,1)}, u32[]{:S(2)}, u32[]{:S(2)}) async-start(bf16[32,36,2048]{2,1,0:T(8,128)(2,1)} %reshape.165), calls=%async_computation | async-start | bytes 10485760 | tf_op jit(solution)/shard_map/all_to_all | solution.py:79
  109.4 5.2 %copy.122 = bf16[32,36,2048]{2,0,1:T(8,128)(2,1)S(1)} copy(bf16[32,36,2048]{2,1,0:T(8,128)(2,1)} %all-to-all-done.1) | data formatting | bytes 9437184 | tf_op jit(solution)/shard_map/all_to_all | solution.py:72
  114.7 10.1 %fusion.10 = f32[2,32,18,768]{3,1,2,0:T(8,128)} fusion(bf16[32,2,18,2048]{3,0,2,1:T(8,128)(2,1)S(1)} %bitcast.191, bf16[2048,2,768,1]{2,1,0,3:T(2,128)(2,1)} %bitcast.209), kind=kOutput, calls=%fused_computation.17 | convolution fusion | flops 3623878656 | bytes 14548992 | tf_op jit(solution)/shard_map/nemd,deh->nemh/dot_general | solution.py:91
  124.8 5.6 %fusion.6 = f32[2,32,18,768]{3,1,2,0:T(8,128)} fusion(bf16[32,2,18,2048]{3,0,2,1:T(8,128)(2,1)S(1)} %bitcast.192, bf16[2048,2,768,1]{2,1,0,3:T(2,128)(2,1)S(1)} %bitcast.208), kind=kOutput, calls=%fused_computation.13 | convolution fusion | flops 3623878656 | bytes 14548992 | tf_op jit(solution)/shard_map/nemd,deh->nemh/dot_general | solution.py:90
  130.5 48.4 %all-to-all-done = bf16[32,36,2048]{2,1,0:T(8,128)(2,1)} async-done(((bf16[32,36,2048]{2,1,0:T(8,128)(2,1)}), bf16[32,36,2048]{2,1,0:T(8,128)(2,1)}, u32[]{:S(2)}, u32[]{:S(2)}) %all-to-all-start) | async-done | bytes 4718624 | tf_op jit(solution)/shard_map/all_to_all | solution.py:79
  178.9 5.2 %copy.120 = bf16[32,36,2048]{2,0,1:T(8,128)(2,1)S(1)} copy(bf16[32,36,2048]{2,1,0:T(8,128)(2,1)} %all-to-all-done) | data formatting | bytes 9437184 | tf_op jit(solution)/shard_map/all_to_all | solution.py:79
  184.1 12.0 %fusion.29 = (bf16[32,2,18]{0,2,1:T(8,128)(2,1)S(1)}, bf16[32,2,18,768]{3,0,2,1:T(8,128)(2,1)}, bf16[32,2,18,768]{3,0,2,1:T(8,128)(2,1)S(1)}, bf16[32,2,18,768]{3,0,2,1:T(8,128)(2,1)}) fusion(f32[2,32,18,768]{3,1,2,0:T(8,128)S(1)} %copy-done.22, f32[2,32,18,768]{3,1,2,0:T(8,128)S(1)} %copy-done.23, bf16[32,2,18,2048]{3,0,2,1:T(8,128)(2,1)S(1)} %bitcast.184, ...), kind=kOutput, calls=%fused_computation.47 | convolution fusion | flops 3639802880 | bytes 23398656 | tf_op jit(solution)/shard_map/nemd,deh->nemh/dot_general | solution.py:95
  214.6 7.8 %pad_maximum_fusion.1 = bf16[2,2,768,512]{2,1,3,0:T(2,128)(2,1)} fusion(bf16[1,2,768,512]{2,1,3,0:T(2,128)(2,1)} %bitcast.182, bf16[1,2,768,512]{2,1,3,0:T(2,128)(2,1)S(1)} %bitcast.180), kind=kLoop, calls=%fused_computation.48 | loop fusion | flops 1572864 | bytes 6291456 | tf_op jit(solution)/shard_map/stack | solution.py:120
  242.7 7.9 %pad_maximum_fusion.2 = bf16[2,2,768,512]{2,1,3,0:T(2,128)(2,1)} fusion(bf16[1,2,768,512]{2,1,3,0:T(2,128)(2,1)} %bitcast.183, bf16[1,2,768,512]{2,1,3,0:T(2,128)(2,1)S(1)} %bitcast.181), kind=kLoop, calls=%fused_computation.49 | loop fusion | flops 1572864 | bytes 6291456 | tf_op jit(solution)/shard_map/stack | solution.py:120
  263.9 6.3 %add_convert_fusion.3 = bf16[2,2,768,512]{2,1,3,0:T(2,128)(2,1)S(1)} fusion(bf16[2,2,768,512]{2,1,3,0:T(2,128)(2,1)} %collective-permute-done, bf16[1,2,768,512]{2,1,3,0:T(2,128)(2,1)} %bitcast.176, bf16[1,2,768,512]{2,1,3,0:T(2,128)(2,1)S(1)} %bitcast.174), kind=kLoop, calls=%fused_computation.10 | loop fusion | flops 7864320 | bytes 9437184 | tf_op jit(solution)/shard_map/convert_element_type | solution.py:138
  329.6 11.7 %pad_maximum_fusion.3 = (bf16[2,2,768,512]{2,1,3,0:T(2,128)(2,1)}, bf16[2,2,768,512]{2,1,3,0:T(2,128)(2,1)}) fusion(bf16[1,2,768,512]{2,1,3,0:T(2,128)(2,1)} %bitcast.179, bf16[1,2,768,512]{2,1,3,0:T(2,128)(2,1)} %bitcast.178, bf16[1,2,768,512]{2,1,3,0:T(2,128)(2,1)} %bitcast.177, bf16[1,2,768,512]{2,1,3,0:T(2,128)(2,1)} %bitcast.175), kind=kLoop, calls=%fused_computation.50 | loop fusion | flops 3145728 | bytes 12582912 | tf_op jit(solution)/shard_map/stack | solution.py:120
  341.8 9.0 %fusion.4 = f32[2,32,18,2048]{3,1,2,0:T(8,128)} fusion(bf16[32,2,18,768]{3,0,2,1:T(8,128)(2,1)S(1)} %copy-done.21, bf16[2048,2,768,1]{2,1,0,3:T(2,128)(2,1)} %bitcast.205), kind=kOutput, calls=%fused_computation.11 | convolution fusion | flops 3623878656 | bytes 17498112 | tf_op jit(solution)/shard_map/nemh,deh->nemd/dot_general | solution.py:145
  350.9 9.9 %fusion.13 = bf16[32,2,18,2048]{3,0,2,1:T(8,128)(2,1)S(1)} fusion(f32[2,32,18,2048]{3,1,2,0:T(8,128)} %fusion.4, bf16[32,2,18,768]{3,0,2,1:T(8,128)(2,1)} %get-tuple-element.16, bf16[2048,2,768,1]{2,1,0,3:T(2,128)(2,1)} %bitcast.210), kind=kOutput, calls=%fused_computation.20 | convolution fusion | flops 3628597248 | bytes 22216704 | tf_op jit(solution)/shard_map/nemh,deh->nemd/dot_general | solution.py:146
  365.4 6.9 %all-to-all-start.2 = ((bf16[32,36,2176]{2,1,0:T(8,128)(2,1)}), bf16[32,36,2176]{2,1,0:T(8,128)(2,1)}, u32[]{:S(2)}, u32[]{:S(2)}) async-start(bf16[32,36,2176]{2,1,0:T(8,128)(2,1)} %copy.137), calls=%async_computation.2 | async-start | bytes 11141120 | tf_op jit(solution)/shard_map/all_to_all | solution.py:150
  372.4 6.3 %add_convert_fusion.2 = bf16[2,2,768,512]{2,1,3,0:T(2,128)(2,1)S(1)} fusion(bf16[2,2,768,512]{2,1,3,0:T(2,128)(2,1)} %collective-permute-done.1, bf16[1,2,768,512]{2,1,3,0:T(2,128)(2,1)} %bitcast.173, bf16[1,2,768,512]{2,1,3,0:T(2,128)(2,1)S(1)} %bitcast.172), kind=kLoop, calls=%fused_computation.9 | loop fusion | flops 7864320 | bytes 9437184 | tf_op jit(solution)/shard_map/convert_element_type | solution.py:138
  381.1 5.1 %add_convert_fusion.1 = bf16[2,2,768,512]{2,1,3,0:T(2,128)(2,1)S(1)} fusion(bf16[2,2,768,512]{2,1,3,0:T(2,128)(2,1)} %collective-permute-done.4, bf16[2,2,768,512]{2,1,3,0:T(2,128)(2,1)S(1)} %copy-done.4), kind=kLoop, calls=%fused_computation.8 | loop fusion | flops 6291456 | bytes 9437184 | tf_op jit(solution)/shard_map/convert_element_type | solution.py:138
  391.4 26.0 %collective-permute-done.3 = bf16[2,768,512]{1,0,2:T(2,128)(2,1)} collective-permute-done((bf16[2,768,512]{1,0,2:T(2,128)(2,1)S(1)}, bf16[2,768,512]{1,0,2:T(2,128)(2,1)}, u32[]{:S(2)}, u32[]{:S(2)}) %collective-permute-start.3) | collective-permute-done | bytes 1572896 | tf_op jit(solution)/shard_map/ppermute | solution.py:139
  420.4 29.8 %collective-permute-done.5 = bf16[2,768,512]{1,0,2:T(2,128)(2,1)S(1)} collective-permute-done((bf16[2,768,512]{1,0,2:T(2,128)(2,1)S(1)}, bf16[2,768,512]{1,0,2:T(2,128)(2,1)S(1)}, u32[]{:S(2)}, u32[]{:S(2)}) %collective-permute-start.5) | collective-permute-done | bytes 1572896 | tf_op jit(solution)/shard_map/ppermute | solution.py:139
  451.8 7.5 %pad_maximum_fusion = bf16[512,3,2,768]{3,2,1,0:T(2,128)(2,1)} fusion(bf16[512,1,2,768]{3,2,1,0:T(2,128)(2,1)S(1)} %fusion.38, bf16[512,1,2,768]{3,2,1,0:T(2,128)(2,1)S(1)} %fusion.37, bf16[512,1,2,768]{3,2,1,0:T(2,128)(2,1)S(1)} %fusion.36), kind=kLoop, calls=%fused_computation.23 | loop fusion | flops 4718592 | bytes 9437184 | tf_op jit(solution)/shard_map/stack | solution.py:143
  459.3 7.5 %reshape.170 = bf16[1152,2176]{1,0:T(8,128)(2,1)} reshape(bf16[32,36,2176]{2,1,0:T(8,128)(2,1)} %all-to-all-done.2) | data formatting | bytes 10027008 | tf_op jit(solution)/shard_map/reshape | solution.py:159
  (133 shorter events, 150.9 us)
Async XLA Ops:
  0.6 6.7 %copy-start = (bf16[128,2048]{1,0:T(8,128)(2,1)S(1)}, bf16[128,2048]{1,0:T(8,128)(2,1)}, u32[]{:S(2)}) copy-start(bf16[128,2048]{1,0:T(8,128)(2,1)} %param.7) | copy-start | bytes 1572868
  7.3 23.3 %copy-start.7 = (pred[1152,128]{1,0:T(8,128)(4,1)}, pred[1152,128]{1,0:T(8,128)(4,1)S(1)}, u32[]{:S(2)}) copy-start(pred[1152,128]{1,0:T(8,128)(4,1)S(1)} %fusion.16) | copy-start | bytes 442372
  18.1 10.9 %copy-start.16 = (f32[128,8]{0,1:T(8,128)S(1)}, f32[128,8]{0,1:T(8,128)}, u32[]{:S(2)}) copy-start(f32[128,8]{0,1:T(8,128)} %param.9) | copy-start | bytes 12292
  18.1 12.5 %copy-start.11 = (bf16[128,2048]{1,0:T(8,128)(2,1)S(1)}, bf16[128,2048]{1,0:T(8,128)(2,1)}, u32[]{:S(2)}) copy-start(bf16[128,2048]{1,0:T(8,128)(2,1)} %param.8) | copy-start | bytes 1572868
  18.1 80.5 %all-to-all-start.1 = ((bf16[32,36,2048]{2,1,0:T(8,128)(2,1)}), bf16[32,36,2048]{2,1,0:T(8,128)(2,1)}, u32[]{:S(2)}, u32[]{:S(2)}) async-start(bf16[32,36,2048]{2,1,0:T(8,128)(2,1)} %reshape.167), calls=%async_computation.1 | async-start | bytes 10485760 | tf_op jit(solution)/shard_map/all_to_all | solution.py:72
  98.7 80.2 %all-to-all-start = ((bf16[32,36,2048]{2,1,0:T(8,128)(2,1)}), bf16[32,36,2048]{2,1,0:T(8,128)(2,1)}, u32[]{:S(2)}, u32[]{:S(2)}) async-start(bf16[32,36,2048]{2,1,0:T(8,128)(2,1)} %reshape.165), calls=%async_computation | async-start | bytes 10485760 | tf_op jit(solution)/shard_map/all_to_all | solution.py:79
  109.4 15.4 %slice-start.4 = ((s8[6291456]{0:T(1024)(128)(4,1)}), s8[4194304]{0:T(1024)(128)(4,1)S(1)}, s32[]{:S(2)}) async-start(s8[6291456]{0:T(1024)(128)(4,1)} %bitcast.206), calls=%async_computation.7 | async-start | bytes 8388608
  114.7 10.2 %copy-start.6 = (bf16[32,36,2048]{2,0,1:T(8,128)(2,1)}, bf16[32,36,2048]{2,0,1:T(8,128)(2,1)S(1)}, u32[]{:S(2)}) copy-start(bf16[32,36,2048]{2,0,1:T(8,128)(2,1)S(1)} %copy.122) | copy-start | bytes 14155780
  114.7 10.1 %slice-start.5 = ((s8[6291456]{0:T(1024)(128)(4,1)}), s8[2097152]{0:T(1024)(128)(4,1)S(1)}, s32[]{:S(2)}) async-start(s8[6291456]{0:T(1024)(128)(4,1)} %bitcast.206), calls=%async_computation.8 | async-start | bytes 4194304
  184.1 12.0 %copy-start.5 = (bf16[32,36,2048]{2,0,1:T(8,128)(2,1)}, bf16[32,36,2048]{2,0,1:T(8,128)(2,1)S(1)}, u32[]{:S(2)}) copy-start(bf16[32,36,2048]{2,0,1:T(8,128)(2,1)S(1)} %copy.120) | copy-start | bytes 14155780
  214.6 14.0 %slice-start.2 = ((s8[4718592]{0:T(1024)(128)(4,1)}), s8[524288]{0:T(1024)(128)(4,1)S(1)}, s32[]{:S(2)}) async-start(s8[4718592]{0:T(1024)(128)(4,1)} %bitcast.199), calls=%async_computation.5 | async-start | bytes 1048576
  222.4 6.2 %collective-permute-start = (bf16[2,2,768,512]{2,1,3,0:T(2,128)(2,1)}, bf16[2,2,768,512]{2,1,3,0:T(2,128)(2,1)}, u32[]{:S(2)}, u32[]{:S(2)}) collective-permute-start(bf16[2,2,768,512]{2,1,3,0:T(2,128)(2,1)} %pad_maximum_fusion.1), channel_id=1, source_target_pairs={{0,32},{32,0},{1,33},{33,1},{2,34},{34,2},{3,35},{35,3},{4,36},{36... | collective-permute-start | bytes 9437192 | tf_op jit(solution)/shard_map/ppermute | solution.py:126
  242.7 8.0 %copy-start.20 = (bf16[32,2,18,768]{3,0,2,1:T(8,128)(2,1)S(1)}, bf16[32,2,18,768]{3,0,2,1:T(8,128)(2,1)}, u32[]{:S(2)}) copy-start(bf16[32,2,18,768]{3,0,2,1:T(8,128)(2,1)} %copy-done.19) | copy-start | bytes 5308420
  250.6 45.3 %collective-permute-start.1 = (bf16[2,2,768,512]{2,1,3,0:T(2,128)(2,1)}, bf16[2,2,768,512]{2,1,3,0:T(2,128)(2,1)}, u32[]{:S(2)}, u32[]{:S(2)}) collective-permute-start(bf16[2,2,768,512]{2,1,3,0:T(2,128)(2,1)} %pad_maximum_fusion.2), channel_id=1, source_target_pairs={{0,32},{32,0},{1,33},{33,1},{2,34},{34,2},{3,35},{35,3},{4,36},{36... | collective-permute-start | bytes 9437192 | tf_op jit(solution)/shard_map/ppermute | solution.py:129
  271.8 6.8 %copy-start.18 = (bf16[32,2,18,768]{3,0,2,1:T(8,128)(2,1)S(1)}, bf16[32,2,18,768]{3,0,2,1:T(8,128)(2,1)}, u32[]{:S(2)}) copy-start(bf16[32,2,18,768]{3,0,2,1:T(8,128)(2,1)} %get-tuple-element.16) | copy-start | bytes 5308420
  274.1 114.2 %collective-permute-start.2 = (bf16[2,768,512]{1,0,2:T(2,128)(2,1)}, bf16[2,768,512]{1,0,2:T(2,128)(2,1)}, u32[]{:S(2)}, u32[]{:S(2)}) collective-permute-start(bf16[2,768,512]{1,0,2:T(2,128)(2,1)} %slice_bitcast_fusion.4), channel_id=1, source_target_pairs={{0,64},{64,0},{1,65},{65,1},{2,66},{66,2},{3,67},{67,3},{4,68},{68... | collective-permute-start | bytes 4718600 | tf_op jit(solution)/shard_map/ppermute | solution.py:139
  295.8 8.5 %slice-start = ((s8[4718592]{0:T(1024)(128)(4,1)}), s8[4194304]{0:T(1024)(128)(4,1)S(1)}, s32[]{:S(2)}) async-start(s8[4718592]{0:T(1024)(128)(4,1)} %bitcast.187), calls=%async_computation.3 | async-start | bytes 8388608
  329.6 12.2 %copy-start.21 = (bf16[32,2,18,768]{3,0,2,1:T(8,128)(2,1)S(1)}, bf16[32,2,18,768]{3,0,2,1:T(8,128)(2,1)}, u32[]{:S(2)}) copy-start(bf16[32,2,18,768]{3,0,2,1:T(8,128)(2,1)} %copy-done.19) | copy-start | bytes 5308420
  341.4 39.7 %collective-permute-start.4 = (bf16[2,2,768,512]{2,1,3,0:T(2,128)(2,1)}, bf16[2,2,768,512]{2,1,3,0:T(2,128)(2,1)}, u32[]{:S(2)}, u32[]{:S(2)}) collective-permute-start(bf16[2,2,768,512]{2,1,3,0:T(2,128)(2,1)} %get-tuple-element.20), channel_id=1, source_target_pairs={{0,32},{32,0},{1,33},{33,1},{2,34},{34,2},{3,35},{35,3},{4,36},{36... | collective-permute-start | bytes 9437192 | tf_op jit(solution)/shard_map/ppermute | solution.py:133
  365.4 93.9 %all-to-all-start.2 = ((bf16[32,36,2176]{2,1,0:T(8,128)(2,1)}), bf16[32,36,2176]{2,1,0:T(8,128)(2,1)}, u32[]{:S(2)}, u32[]{:S(2)}) async-start(bf16[32,36,2176]{2,1,0:T(8,128)(2,1)} %copy.137), calls=%async_computation.2 | async-start | bytes 11141120 | tf_op jit(solution)/shard_map/all_to_all | solution.py:150
  379.7 37.6 %collective-permute-start.3 = (bf16[2,768,512]{1,0,2:T(2,128)(2,1)S(1)}, bf16[2,768,512]{1,0,2:T(2,128)(2,1)}, u32[]{:S(2)}, u32[]{:S(2)}) collective-permute-start(bf16[2,768,512]{1,0,2:T(2,128)(2,1)S(1)} %slice_bitcast_fusion.2), channel_id=1, source_target_pairs={{0,64},{64,0},{1,65},{65,1},{2,66},{66,2},{3,67},{67,3},{4,68},{68... | collective-permute-start | bytes 4718600 | tf_op jit(solution)/shard_map/ppermute | solution.py:139
  387.3 62.9 %collective-permute-start.5 = (bf16[2,768,512]{1,0,2:T(2,128)(2,1)S(1)}, bf16[2,768,512]{1,0,2:T(2,128)(2,1)S(1)}, u32[]{:S(2)}, u32[]{:S(2)}) collective-permute-start(bf16[2,768,512]{1,0,2:T(2,128)(2,1)S(1)} %slice_bitcast_fusion), channel_id=1, source_target_pairs={{0,64},{64,0},{1,65},{65,1},{2,66},{66,2},{3,67},{67,3},{4,68},{68... | collective-permute-start | bytes 4718600 | tf_op jit(solution)/shard_map/ppermute | solution.py:139
  459.3 8.7 %copy-start.8 = (pred[1152,128]{1,0:T(8,128)(4,1)S(1)}, pred[1152,128]{1,0:T(8,128)(4,1)}, u32[]{:S(2)}) copy-start(pred[1152,128]{1,0:T(8,128)(4,1)} %copy-done.7) | copy-start | bytes 442372
  466.9 6.9 %copy-start.1 = (bf16[128,2048]{1,0:T(8,128)(2,1)S(1)}, bf16[128,2048]{1,0:T(8,128)(2,1)}, u32[]{:S(2)}) copy-start(bf16[128,2048]{1,0:T(8,128)(2,1)} %param.7) | copy-start | bytes 1572868
  (16 other events, 62.2 us)

commit v12 on v9

--- a/solution.py
+++ b/solution.py
@@ -120,21 +120,21 @@
 
     core_pairs = [(i, (i + 1) % core_count) for i in range(core_count)]
     xlo_pairs = [(i, (i + 1) % xlo_count) for i in range(xlo_count)]
-    gate_sib, gate_own = blocks_of(gate_grad, recv_tokens)
-    gate_from, up_grad, hidden = lax.optimization_barrier(
-        (lax.ppermute(gate_sib, "core", core_pairs), up_grad, hidden)
+    def core_sum(sib, own):
+        from_sibling = lax.ppermute(sib, "core", core_pairs)
+        return (own.astype(jnp.float32) + from_sibling.astype(jnp.float32)).astype(jnp.bfloat16)
+
+    gate_sum, up_grad, hidden = lax.optimization_barrier(
+        (core_sum(*blocks_of(gate_grad, recv_tokens)), up_grad, hidden)
     )
-    up_sib, up_own = blocks_of(up_grad, recv_tokens)
-    up_from, hidden = lax.optimization_barrier((lax.ppermute(up_sib, "core", core_pairs), hidden))
+    up_sum, hidden = lax.optimization_barrier((core_sum(*blocks_of(up_grad, recv_tokens)), hidden))
     down_sib, down_own, gate_grad, up_grad = lax.optimization_barrier(
         blocks_of(hidden, recv_scaled) + (gate_grad, up_grad)
     )
-    down_from = lax.ppermute(down_sib, "core", core_pairs)
+    down_sum = core_sum(down_sib, down_own)
 
     shares = jnp.zeros((block_rows, 3, local_experts, hidden_width), jnp.bfloat16)
-    pieces = ((gate_from, gate_own), (up_from, up_own), (down_from, down_own))
-    for kind, (from_sibling, own) in enumerate(pieces):
-        summed = (own.astype(jnp.float32) + from_sibling.astype(jnp.float32)).astype(jnp.bfloat16)
+    for kind, summed in enumerate((gate_sum, up_sum, down_sum)):
         theirs = lax.ppermute(summed[0], "xlo", xlo_pairs)
         share = (summed[1].astype(jnp.float32) + theirs.astype(jnp.float32)).astype(jnp.bfloat16)
         shares = lax.dynamic_update_index_in_dim(shares, jnp.transpose(share, (2, 0, 1)), kind, 1)

time: 378 us -> 411 us (1.087)
  waiting for transfers between devices: 170 us -> 200 us
  other arithmetic: 26 us -> 30.6 us
    ppermute x3, waiting for transfers between devices: 57.8 us -> 92.9 us  [per_device(): theirs = lax.ppermute(summed[0], 'xlo', xlo_pairs)]
    convert_element_type x3, other arithmetic: 6.63 us -> 11.9 us  [core_sum(): (own.astype(jnp.float32) + from_sibling.astype(jnp.float32)).astype(jnp.b...]
    ppermute x3, waiting for transfers between devices: 5.65 us -> 0.92 us  [core_sum(): from_sibling = lax.ppermute(sib, 'core', core_pairs)]
    dot_general x1, matrix products: 10.2 us -> 5.66 us  [per_device(): jnp.einsum('nemd,deh->nemh', recv_tokens, w_gate, preferred_element_type=...]
    dot_general x1, matrix products: 5.6 us -> 10.1 us  [per_device(): jnp.einsum('nemd,deh->nemh', recv_tokens, w_up, preferred_element_type=jn...]
    unnamed x69 -> x67, local copies, waits for them, and re-layouts: 17.3 us -> 16.6 us
  transfers between devices with their start and end apart: 9 -> 9, of which waited for: 5 -> 6; matrix products, arithmetic and copies ran while one was open for 28% -> 21% of each run, Pallas kernels for 0% -> 0%
where the time goes in v12:
time: 411 us; the launch traced here: 404 us
  waiting for transfers between devices  200 us (49%)
  matrix products  77.9 us (19%)
  local copies, waits for them, and re-layouts  58.1 us (14%)
  starting transfers between devices  35.9 us (9%)
  other arithmetic  30.6 us (7%)
    ppermute x3, waiting for transfers between devices, per_device(): theirs = lax.ppermute(summed[0], 'xlo', xlo_pairs)  92.9 us
    all_to_all x1, waiting for transfers between devices, per_device(): lax.all_to_all(send_tokens.reshape(send_shape), ('xlo', 'expert'), split_...  57.4 us
    all_to_all x1, waiting for transfers between devices, per_device(): lax.all_to_all(send_scaled.reshape(send_shape), ('xlo', 'expert'), split_...  48.7 us
    dot_general x12, matrix products, blocks_of(): jnp.einsum('nemh,nemd->ehd', left, lax.dynamic_slice_in_dim(right, at, bl...  23.4 us
    unnamed x67, local copies, waits for them, and re-layouts  16.6 us
    dot_general x1, matrix products, per_device(): jnp.einsum('nemd,deh->nemh', recv_scaled, w_down, preferred_element_type=...  12.3 us
    convert_element_type x3, other arithmetic, core_sum(): (own.astype(jnp.float32) + from_sibling.astype(jnp.float32)).astype(jnp.b...  11.9 us
    all_to_all x1, starting transfers between devices, per_device(): lax.all_to_all(send_scaled.reshape(send_shape), ('xlo', 'expert'), split_...  11 us
  transfers between devices with their start and end apart: 9, of which 6 were waited for; matrix products, arithmetic and copies ran while one was open for 21% of the time, Pallas kernels for 0%

profile of v12, /device:TPU:0, one launch (start us, length us, event | category | flops | bytes accessed | tf_op | source)
XLA Modules:
  0.0 404.2 jit_solution(14835497900109326907)
XLA Ops:
  3.1 4.2 %fusion.16 = pred[1152,128]{1,0:T(8,128)(4,1)S(1)} fusion(s32[128,8]{0,1:T(8,128)S(1)} %fusion.77), kind=kLoop, calls=%fused_computation.27 | loop fusion | flops 2211840 | bytes 151552 | tf_op jit(solution)/shard_map/reduce_or | solution.py:61
  10.9 7.2 %reshape.167 = bf16[32,36,2048]{2,1,0:T(8,128)(2,1)} reshape(bf16[1152,2048]{1,0:T(8,128)(2,1)} %convolution_convert_fusion) | data formatting | bytes 9437184 | tf_op jit(solution)/shard_map/reshape | solution.py:72
  18.0 10.9 %all-to-all-start.1 = ((bf16[32,36,2048]{2,1,0:T(8,128)(2,1)}), bf16[32,36,2048]{2,1,0:T(8,128)(2,1)}, u32[]{:S(2)}, u32[]{:S(2)}) async-start(bf16[32,36,2048]{2,1,0:T(8,128)(2,1)} %reshape.167), calls=%async_computation.1 | async-start | bytes 10485760 | tf_op jit(solution)/shard_map/all_to_all | solution.py:71
  34.0 7.2 %reshape.165 = bf16[32,36,2048]{2,1,0:T(8,128)(2,1)} reshape(bf16[1152,2048]{1,0:T(8,128)(2,1)} %fusion.1) | data formatting | bytes 9437184 | tf_op jit(solution)/shard_map/reshape | solution.py:79
  41.3 57.4 %all-to-all-done.1 = bf16[32,36,2048]{2,1,0:T(8,128)(2,1)} async-done(((bf16[32,36,2048]{2,1,0:T(8,128)(2,1)}), bf16[32,36,2048]{2,1,0:T(8,128)(2,1)}, u32[]{:S(2)}, u32[]{:S(2)}) %all-to-all-start.1) | async-done | bytes 4718624 | tf_op jit(solution)/shard_map/all_to_all | solution.py:71
  98.6 11.0 %all-to-all-start = ((bf16[32,36,2048]{2,1,0:T(8,128)(2,1)}), bf16[32,36,2048]{2,1,0:T(8,128)(2,1)}, u32[]{:S(2)}, u32[]{:S(2)}) async-start(bf16[32,36,2048]{2,1,0:T(8,128)(2,1)} %reshape.165), calls=%async_computation | async-start | bytes 10485760 | tf_op jit(solution)/shard_map/all_to_all | solution.py:78
  109.7 5.2 %copy.78 = bf16[32,36,2048]{2,0,1:T(8,128)(2,1)S(1)} copy(bf16[32,36,2048]{2,1,0:T(8,128)(2,1)} %all-to-all-done.1) | data formatting | bytes 9437184 | tf_op jit(solution)/shard_map/all_to_all | solution.py:71
  114.9 10.1 %fusion.10 = f32[2,32,18,768]{3,1,2,0:T(8,128)} fusion(bf16[32,2,18,2048]{3,0,2,1:T(8,128)(2,1)S(1)} %bitcast.203, bf16[2048,2,768,1]{2,1,0,3:T(2,128)(2,1)} %bitcast.225), kind=kOutput, calls=%fused_computation.17 | convolution fusion | flops 3623878656 | bytes 14548992 | tf_op jit(solution)/shard_map/nemd,deh->nemh/dot_general | solution.py:90
  125.0 5.7 %fusion.6 = f32[2,32,18,768]{3,1,2,0:T(8,128)} fusion(bf16[32,2,18,2048]{3,0,2,1:T(8,128)(2,1)S(1)} %bitcast.204, bf16[2048,2,768,1]{2,1,0,3:T(2,128)(2,1)S(1)} %bitcast.221), kind=kOutput, calls=%fused_computation.13 | convolution fusion | flops 3623878656 | bytes 14548992 | tf_op jit(solution)/shard_map/nemd,deh->nemh/dot_general | solution.py:89
  130.7 48.7 %all-to-all-done = bf16[32,36,2048]{2,1,0:T(8,128)(2,1)} async-done(((bf16[32,36,2048]{2,1,0:T(8,128)(2,1)}), bf16[32,36,2048]{2,1,0:T(8,128)(2,1)}, u32[]{:S(2)}, u32[]{:S(2)}) %all-to-all-start) | async-done | bytes 4718624 | tf_op jit(solution)/shard_map/all_to_all | solution.py:78
  179.4 5.2 %copy.76 = bf16[32,36,2048]{2,0,1:T(8,128)(2,1)S(1)} copy(bf16[32,36,2048]{2,1,0:T(8,128)(2,1)} %all-to-all-done) | data formatting | bytes 9437184 | tf_op jit(solution)/shard_map/all_to_all | solution.py:78
  184.6 12.3 %fusion.29 = (bf16[32,2,18]{0,2,1:T(8,128)(2,1)S(1)}, bf16[32,2,18,768]{3,0,2,1:T(8,128)(2,1)}, bf16[32,2,18,768]{3,0,2,1:T(8,128)(2,1)S(1)}, bf16[32,2,18,768]{3,0,2,1:T(8,128)(2,1)S(1)}) fusion(f32[2,32,18,768]{3,1,2,0:T(8,128)} %fusion.10, f32[2,32,18,768]{3,1,2,0:T(8,128)} %fusion.6, bf16[32,2,18,2048]{3,0,2,1:T(8,128)(2,1)S(1)} %bitcast.196, ...), kind=kOutput, calls=%fused_computation.46 | convolution fusion | flops 3639802880 | bytes 23398656 | tf_op jit(solution)/shard_map/nemd,deh->nemh/dot_general | solution.py:94
  210.4 4.4 %add_convert_fusion.3 = bf16[2,2,768,512]{3,2,1,0:T(8,128)(2,1)} fusion(bf16[2,2,768,512]{3,2,1,0:T(8,128)(2,1)} %collective-permute-done, bf16[1,2,768,512]{3,2,1,0:T(8,128)(2,1)S(1)} %fusion.42, bf16[1,2,768,512]{3,2,1,0:T(8,128)(2,1)S(1)} %fusion.41), kind=kLoop, calls=%fused_computation.10 | loop fusion | flops 7864320 | bytes 9437184 | tf_op jit(solution)/shard_map/convert_element_type | solution.py:125
  226.0 4.6 %add_convert_fusion.2 = bf16[2,2,768,512]{3,2,1,0:T(8,128)(2,1)} fusion(bf16[2,2,768,512]{3,2,1,0:T(8,128)(2,1)} %collective-permute-done.1, bf16[1,2,768,512]{3,2,1,0:T(8,128)(2,1)S(1)} %fusion.46, bf16[1,2,768,512]{3,2,1,0:T(8,128)(2,1)S(1)} %fusion.45), kind=kLoop, calls=%fused_computation.9 | loop fusion | flops 7864320 | bytes 9437184 | tf_op jit(solution)/shard_map/convert_element_type | solution.py:125
  240.1 6.3 %fusion.4 = f32[2,32,18,2048]{3,1,2,0:T(8,128)} fusion(bf16[32,2,18,768]{3,0,2,1:T(8,128)(2,1)S(1)} %copy-done.19, bf16[2048,2,768,1]{2,1,0,3:T(2,128)(2,1)S(1)} %bitcast.224), kind=kOutput, calls=%fused_computation.11 | convolution fusion | flops 3623878656 | bytes 17498112 | tf_op jit(solution)/shard_map/nemh,deh->nemd/dot_general | solution.py:143
  246.4 8.4 %fusion.13 = bf16[32,2,18,2048]{3,0,2,1:T(8,128)(2,1)S(1)} fusion(f32[2,32,18,2048]{3,1,2,0:T(8,128)} %fusion.4, bf16[32,2,18,768]{3,0,2,1:T(8,128)(2,1)S(1)} %get-tuple-element.16, bf16[2048,2,768,1]{2,1,0,3:T(2,128)(2,1)} %bitcast.226), kind=kOutput, calls=%fused_computation.20 | convolution fusion | flops 3628597248 | bytes 22216704 | tf_op jit(solution)/shard_map/nemh,deh->nemd/dot_general | solution.py:144
  255.3 4.1 %copy.85 = bf16[32,36,2176]{2,1,0:T(8,128)(2,1)} copy(bf16[32,36,2176]{2,0,1:T(8,128)(2,1)S(1)} %bitcast.195) | data formatting | bytes 10027008 | tf_op jit(solution)/shard_map/reshape | solution.py:149
  259.5 10.4 %all-to-all-start.2 = ((bf16[32,36,2176]{2,1,0:T(8,128)(2,1)}), bf16[32,36,2176]{2,1,0:T(8,128)(2,1)}, u32[]{:S(2)}, u32[]{:S(2)}) async-start(bf16[32,36,2176]{2,1,0:T(8,128)(2,1)} %copy.85), calls=%async_computation.2 | async-start | bytes 11141120 | tf_op jit(solution)/shard_map/all_to_all | solution.py:148
  277.8 31.1 %collective-permute-done.2 = bf16[2,768,512]{2,1,0:T(8,128)(2,1)S(1)} collective-permute-done((bf16[2,768,512]{2,1,0:T(8,128)(2,1)S(1)}, bf16[2,768,512]{2,1,0:T(8,128)(2,1)S(1)}, u32[]{:S(2)}, u32[]{:S(2)}) %collective-permute-start.2) | collective-permute-done | bytes 1572896 | tf_op jit(solution)/shard_map/ppermute | solution.py:138
  311.9 30.8 %collective-permute-done.3 = bf16[2,768,512]{2,1,0:T(8,128)(2,1)S(1)} collective-permute-done((bf16[2,768,512]{2,1,0:T(8,128)(2,1)S(1)}, bf16[2,768,512]{2,1,0:T(8,128)(2,1)S(1)}, u32[]{:S(2)}, u32[]{:S(2)}) %collective-permute-start.3) | collective-permute-done | bytes 1572896 | tf_op jit(solution)/shard_map/ppermute | solution.py:138
  344.2 31.0 %collective-permute-done.5 = bf16[2,768,512]{2,1,0:T(8,128)(2,1)S(1)} collective-permute-done((bf16[2,768,512]{2,1,0:T(8,128)(2,1)S(1)}, bf16[2,768,512]{2,1,0:T(8,128)(2,1)S(1)}, u32[]{:S(2)}, u32[]{:S(2)}) %collective-permute-start.5) | collective-permute-done | bytes 1572896 | tf_op jit(solution)/shard_map/ppermute | solution.py:138
  376.9 12.4 %copy.87 = bf16[512,3,2,768]{3,2,1,0:T(2,128)(2,1)} copy(bf16[512,3,2,768]{0,3,2,1:T(8,128)(2,1)} %fusion.40) | data formatting | bytes 9437184
  389.3 7.5 %reshape.170 = bf16[1152,2176]{1,0:T(8,128)(2,1)} reshape(bf16[32,36,2176]{2,1,0:T(8,128)(2,1)} %all-to-all-done.2) | data formatting | bytes 10027008 | tf_op jit(solution)/shard_map/reshape | solution.py:157
  398.0 4.1 %fusion.33 = bf16[128,2048]{1,0:T(8,128)(2,1)} fusion(pred[1152,128]{1,0:T(8,128)(4,1)S(1)} %copy-done.8, bf16[1152,2176]{1,0:T(8,128)(2,1)} %reshape.170), kind=kOutput, calls=%fused_computation.69 | convolution fusion | flops 604241920 | bytes 5390336 | tf_op jit(solution)/shard_map/dot_general | solution.py:161
  (124 shorter events, 62.3 us)
Async XLA Ops:
  0.6 6.7 %copy-start = (bf16[128,2048]{1,0:T(8,128)(2,1)S(1)}, bf16[128,2048]{1,0:T(8,128)(2,1)}, u32[]{:S(2)}) copy-start(bf16[128,2048]{1,0:T(8,128)(2,1)} %param.7) | copy-start | bytes 1572868
  7.3 23.1 %copy-start.7 = (pred[1152,128]{1,0:T(8,128)(4,1)}, pred[1152,128]{1,0:T(8,128)(4,1)S(1)}, u32[]{:S(2)}) copy-start(pred[1152,128]{1,0:T(8,128)(4,1)S(1)} %fusion.16) | copy-start | bytes 442372
  18.0 10.9 %copy-start.16 = (f32[128,8]{0,1:T(8,128)S(1)}, f32[128,8]{0,1:T(8,128)}, u32[]{:S(2)}) copy-start(f32[128,8]{0,1:T(8,128)} %param.9) | copy-start | bytes 12292
  18.0 12.4 %copy-start.11 = (bf16[128,2048]{1,0:T(8,128)(2,1)S(1)}, bf16[128,2048]{1,0:T(8,128)(2,1)}, u32[]{:S(2)}) copy-start(bf16[128,2048]{1,0:T(8,128)(2,1)} %param.8) | copy-start | bytes 1572868
  18.0 80.6 %all-to-all-start.1 = ((bf16[32,36,2048]{2,1,0:T(8,128)(2,1)}), bf16[32,36,2048]{2,1,0:T(8,128)(2,1)}, u32[]{:S(2)}, u32[]{:S(2)}) async-start(bf16[32,36,2048]{2,1,0:T(8,128)(2,1)} %reshape.167), calls=%async_computation.1 | async-start | bytes 10485760 | tf_op jit(solution)/shard_map/all_to_all | solution.py:71
  98.6 80.7 %all-to-all-start = ((bf16[32,36,2048]{2,1,0:T(8,128)(2,1)}), bf16[32,36,2048]{2,1,0:T(8,128)(2,1)}, u32[]{:S(2)}, u32[]{:S(2)}) async-start(bf16[32,36,2048]{2,1,0:T(8,128)(2,1)} %reshape.165), calls=%async_computation | async-start | bytes 10485760 | tf_op jit(solution)/shard_map/all_to_all | solution.py:78
  109.6 15.4 %slice-start.6 = ((s8[6291456]{0:T(1024)(128)(4,1)}), s8[4194304]{0:T(1024)(128)(4,1)S(1)}, s32[]{:S(2)}) async-start(s8[6291456]{0:T(1024)(128)(4,1)} %bitcast.219), calls=%async_computation.9 | async-start | bytes 8388608
  114.9 10.1 %copy-start.6 = (bf16[32,36,2048]{2,0,1:T(8,128)(2,1)}, bf16[32,36,2048]{2,0,1:T(8,128)(2,1)S(1)}, u32[]{:S(2)}) copy-start(bf16[32,36,2048]{2,0,1:T(8,128)(2,1)S(1)} %copy.78) | copy-start | bytes 14155780
  114.9 10.1 %slice-start.7 = ((s8[6291456]{0:T(1024)(128)(4,1)}), s8[2097152]{0:T(1024)(128)(4,1)S(1)}, s32[]{:S(2)}) async-start(s8[6291456]{0:T(1024)(128)(4,1)} %bitcast.219), calls=%async_computation.10 | async-start | bytes 4194304
  179.4 18.8 %slice-start.2 = ((s8[4718592]{0:T(1024)(128)(4,1)}), s8[4194304]{0:T(1024)(128)(4,1)S(1)}, s32[]{:S(2)}) async-start(s8[4718592]{0:T(1024)(128)(4,1)} %bitcast.208), calls=%async_computation.5 | async-start | bytes 8388608
  184.6 12.3 %copy-start.5 = (bf16[32,36,2048]{2,0,1:T(8,128)(2,1)}, bf16[32,36,2048]{2,0,1:T(8,128)(2,1)S(1)}, u32[]{:S(2)}) copy-start(bf16[32,36,2048]{2,0,1:T(8,128)(2,1)S(1)} %copy.76) | copy-start | bytes 14155780
  184.6 13.5 %slice-start.3 = ((s8[4718592]{0:T(1024)(128)(4,1)}), s8[524288]{0:T(1024)(128)(4,1)S(1)}, s32[]{:S(2)}) async-start(s8[4718592]{0:T(1024)(128)(4,1)} %bitcast.208), calls=%async_computation.6 | async-start | bytes 1048576
  204.4 6.0 %collective-permute-start = (bf16[2,2,768,512]{3,2,1,0:T(8,128)(2,1)}, bf16[2,2,768,512]{3,2,1,0:T(8,128)(2,1)}, u32[]{:S(2)}, u32[]{:S(2)}) collective-permute-start(bf16[2,2,768,512]{3,2,1,0:T(8,128)(2,1)} %pad_maximum_fusion), channel_id=1, source_target_pairs={{0,32},{32,0},{1,33},{33,1},{2,34},{34,2},{3,35},{35,3},{4,36},{36... | collective-permute-start | bytes 9437192 | tf_op jit(solution)/shard_map/ppermute | solution.py:124
  219.7 6.3 %collective-permute-start.1 = (bf16[2,2,768,512]{3,2,1,0:T(8,128)(2,1)}, bf16[2,2,768,512]{3,2,1,0:T(8,128)(2,1)}, u32[]{:S(2)}, u32[]{:S(2)}) collective-permute-start(bf16[2,2,768,512]{3,2,1,0:T(8,128)(2,1)} %pad_maximum_fusion.1), channel_id=1, source_target_pairs={{0,32},{32,0},{1,33},{33,1},{2,34},{34,2},{3,35},{35,3},{4,36},{36... | collective-permute-start | bytes 9437192 | tf_op jit(solution)/shard_map/ppermute | solution.py:124
  220.4 10.3 %slice-start = ((s8[4718592]{0:T(1024)(128)(4,1)}), s8[4194304]{0:T(1024)(128)(4,1)S(1)}, s32[]{:S(2)}) async-start(s8[4718592]{0:T(1024)(128)(4,1)} %bitcast.197), calls=%async_computation.3 | async-start | bytes 8388608
  223.2 7.4 %slice-start.1 = ((s8[4718592]{0:T(1024)(128)(4,1)}), s8[524288]{0:T(1024)(128)(4,1)S(1)}, s32[]{:S(2)}) async-start(s8[4718592]{0:T(1024)(128)(4,1)} %bitcast.197), calls=%async_computation.4 | async-start | bytes 1048576
  239.4 34.4 %collective-permute-start.4 = (bf16[2,2,768,512]{3,2,1,0:T(8,128)(2,1)}, bf16[2,2,768,512]{3,2,1,0:T(8,128)(2,1)}, u32[]{:S(2)}, u32[]{:S(2)}) collective-permute-start(bf16[2,2,768,512]{3,2,1,0:T(8,128)(2,1)} %get-tuple-element.20), channel_id=1, source_target_pairs={{0,32},{32,0},{1,33},{33,1},{2,34},{34,2},{3,35},{35,3},{4,36},{36... | collective-permute-start | bytes 9437192 | tf_op jit(solution)/shard_map/ppermute | solution.py:124
  259.5 129.8 %all-to-all-start.2 = ((bf16[32,36,2176]{2,1,0:T(8,128)(2,1)}), bf16[32,36,2176]{2,1,0:T(8,128)(2,1)}, u32[]{:S(2)}, u32[]{:S(2)}) async-start(bf16[32,36,2176]{2,1,0:T(8,128)(2,1)} %copy.85), calls=%async_computation.2 | async-start | bytes 11141120 | tf_op jit(solution)/shard_map/all_to_all | solution.py:148
  271.6 37.4 %collective-permute-start.2 = (bf16[2,768,512]{2,1,0:T(8,128)(2,1)S(1)}, bf16[2,768,512]{2,1,0:T(8,128)(2,1)S(1)}, u32[]{:S(2)}, u32[]{:S(2)}) collective-permute-start(bf16[2,768,512]{2,1,0:T(8,128)(2,1)S(1)} %slice_bitcast_fusion.3), channel_id=1, source_target_pairs={{0,64},{64,0},{1,65},{65,1},{2,66},{66,2},{3,67},{67,3},{4,68},{68... | collective-permute-start | bytes 4718600 | tf_op jit(solution)/shard_map/ppermute | solution.py:138
  272.4 70.3 %collective-permute-start.3 = (bf16[2,768,512]{2,1,0:T(8,128)(2,1)S(1)}, bf16[2,768,512]{2,1,0:T(8,128)(2,1)S(1)}, u32[]{:S(2)}, u32[]{:S(2)}) collective-permute-start(bf16[2,768,512]{2,1,0:T(8,128)(2,1)S(1)} %slice_bitcast_fusion.2), channel_id=1, source_target_pairs={{0,64},{64,0},{1,65},{65,1},{2,66},{66,2},{3,67},{67,3},{4,68},{68... | collective-permute-start | bytes 4718600 | tf_op jit(solution)/shard_map/ppermute | solution.py:138
  276.7 32.2 %copy-start.2 = (bf16[2,2,768,512]{3,2,1,0:T(8,128)(2,1)S(1)}, bf16[2,2,768,512]{3,2,1,0:T(8,128)(2,1)}, u32[]{:S(2)}) copy-start(bf16[2,2,768,512]{3,2,1,0:T(8,128)(2,1)} %add_convert_fusion.3) | copy-start | bytes 9437188
  276.9 98.4 %collective-permute-start.5 = (bf16[2,768,512]{2,1,0:T(8,128)(2,1)S(1)}, bf16[2,768,512]{2,1,0:T(8,128)(2,1)S(1)}, u32[]{:S(2)}, u32[]{:S(2)}) collective-permute-start(bf16[2,768,512]{2,1,0:T(8,128)(2,1)S(1)} %slice_bitcast_fusion), channel_id=1, source_target_pairs={{0,64},{64,0},{1,65},{65,1},{2,66},{66,2},{3,67},{67,3},{4,68},{68... | collective-permute-start | bytes 4718600 | tf_op jit(solution)/shard_map/ppermute | solution.py:138
  389.3 8.7 %copy-start.8 = (pred[1152,128]{1,0:T(8,128)(4,1)S(1)}, pred[1152,128]{1,0:T(8,128)(4,1)}, u32[]{:S(2)}) copy-start(pred[1152,128]{1,0:T(8,128)(4,1)} %copy-done.7) | copy-start | bytes 442372
  396.8 6.9 %copy-start.1 = (bf16[128,2048]{1,0:T(8,128)(2,1)S(1)}, bf16[128,2048]{1,0:T(8,128)(2,1)}, u32[]{:S(2)}) copy-start(bf16[128,2048]{1,0:T(8,128)(2,1)} %param.7) | copy-start | bytes 1572868
  (16 other events, 63.3 us)

commit v13 on v9

--- a/solution.py
+++ b/solution.py
@@ -63,11 +63,14 @@
     slot_weight = jnp.sum(jnp.where(pair_hit, flat_weights[None, :], 0.0), axis=1)
 
     send_shape = (owners, local_experts * capacity, model_width)
-    send_tokens = jnp.dot(dispatch, tokens_in, preferred_element_type=jnp.float32).astype(
-        jnp.bfloat16
-    )
-    send_grads = jnp.dot(dispatch, out_grad, preferred_element_type=jnp.float32)
-    send_scaled = (slot_weight[:, None] * send_grads).astype(jnp.bfloat16)
+    picks = dispatch.reshape(owners, local_experts * capacity, tok_rows)
+    send_tokens = jnp.einsum(
+        "nst,td->nsd", picks, tokens_in, preferred_element_type=jnp.float32
+    ).astype(jnp.bfloat16)
+    send_grads = jnp.einsum("nst,td->nsd", picks, out_grad, preferred_element_type=jnp.float32)
+    send_scaled = (
+        slot_weight.reshape(owners, local_experts * capacity, 1) * send_grads
+    ).astype(jnp.bfloat16)
     recv_tokens = lax.all_to_all(
         send_tokens.reshape(send_shape), ("xlo", "expert"),
         split_axis=0,

time: 378 us -> 371 us (0.981)
  local copies, waits for them, and re-layouts: 57.4 us -> 43.7 us
  waiting for transfers between devices: 170 us -> 176 us
    reshape x2 -> x1, local copies, waits for them, and re-layouts: 14.4 us -> 0.06 us  [per_device(): picks = dispatch.reshape(owners, local_experts * capacity, tok_rows)]
    all_to_all x1, waiting for transfers between devices: 57.3 us -> 63.6 us  [per_device(): lax.all_to_all(send_tokens.reshape(send_shape), ('xlo', 'expert'), split_...]
  transfers between devices with their start and end apart: 9 -> 9, of which waited for: 5 -> 5; matrix products, arithmetic and copies ran while one was open for 28% -> 26% of each run, Pallas kernels for 0% -> 0%
where the time goes in v13:
time: 371 us; the launch traced here: 364 us
  waiting for transfers between devices  176 us (47%)
  matrix products  79.9 us (22%)
  local copies, waits for them, and re-layouts  43.7 us (12%)
  starting transfers between devices  37 us (10%)
  other arithmetic  26 us (7%)
    all_to_all x1, waiting for transfers between devices, per_device(): lax.all_to_all(send_tokens.reshape(send_shape), ('xlo', 'expert'), split_...  63.6 us
    ppermute x3, waiting for transfers between devices, per_device(): theirs = lax.ppermute(summed[0], 'xlo', xlo_pairs)  57.8 us
    all_to_all x1, waiting for transfers between devices, per_device(): lax.all_to_all(send_scaled.reshape(send_shape), ('xlo', 'expert'), split_...  48.7 us
    dot_general x12, matrix products, blocks_of(): jnp.einsum('nemh,nemd->ehd', left, lax.dynamic_slice_in_dim(right, at, bl...  23.3 us
    unnamed x69, local copies, waits for them, and re-layouts  18 us
    dot_general x1, matrix products, per_device(): jnp.einsum('nemd,deh->nemh', recv_scaled, w_down, preferred_element_type=...  12.3 us
    all_to_all x1, starting transfers between devices, per_device(): lax.all_to_all(send_scaled.reshape(send_shape), ('xlo', 'expert'), split_...  11.1 us
    all_to_all x1, starting transfers between devices, per_device(): lax.all_to_all(send_tokens.reshape(send_shape), ('xlo', 'expert'), split_...  10.9 us
  transfers between devices with their start and end apart: 9, of which 5 were waited for; matrix products, arithmetic and copies ran while one was open for 26% of the time, Pallas kernels for 0%

profile of v13, /device:TPU:0, one launch (start us, length us, event | category | flops | bytes accessed | tf_op | source)
XLA Modules:
  0.0 364.2 jit_solution(12643763702900234282)
XLA Ops:
  3.1 4.2 %fusion.15 = pred[1152,128]{1,0:T(8,128)(4,1)S(1)} fusion(s32[128,8]{0,1:T(8,128)S(1)} %fusion.78), kind=kLoop, calls=%fused_computation.25 | loop fusion | flops 2211840 | bytes 151552 | tf_op jit(solution)/shard_map/reduce_or | solution.py:61
  7.4 3.8 %convolution_convert_fusion = bf16[32,36,2048]{2,1,0:T(8,128)(2,1)} fusion(pred[32,36,128]{2,1,0:T(8,128)(4,1)S(1)} %reshape.163, bf16[128,2048]{1,0:T(8,128)(2,1)S(1)} %copy-done), kind=kOutput, calls=%fused_computation.28 | convolution fusion | flops 606339072 | bytes 5390336 | tf_op jit(solution)/shard_map/nst,td->nsd/dot_general | solution.py:67
  11.2 10.9 %all-to-all-start.1 = ((bf16[32,36,2048]{2,1,0:T(8,128)(2,1)}), bf16[32,36,2048]{2,1,0:T(8,128)(2,1)}, u32[]{:S(2)}, u32[]{:S(2)}) async-start(bf16[32,36,2048]{2,1,0:T(8,128)(2,1)} %convolution_convert_fusion), calls=%async_computation.1 | async-start | bytes 10485760 | tf_op jit(solution)/shard_map/all_to_all | solution.py:74
  24.3 3.9 %multiply_convert_fusion = bf16[32,36,2048]{2,1,0:T(8,128)(2,1)} fusion(f32[32,36]{1,0:T(8,128)S(1)} %mul.130, pred[32,36,128]{2,1,0:T(8,128)(4,1)S(1)} %reshape.163, bf16[128,2048]{1,0:T(8,128)(2,1)S(1)} %copy-done.13), kind=kOutput, calls=%fused_computation | convolution fusion | flops 608698368 | bytes 5394944 | tf_op jit(solution)/shard_map/nst,td->nsd/dot_general | solution.py:70
  28.2 63.6 %all-to-all-done.1 = bf16[32,36,2048]{2,1,0:T(8,128)(2,1)} async-done(((bf16[32,36,2048]{2,1,0:T(8,128)(2,1)}), bf16[32,36,2048]{2,1,0:T(8,128)(2,1)}, u32[]{:S(2)}, u32[]{:S(2)}) %all-to-all-start.1) | async-done | bytes 4718624 | tf_op jit(solution)/shard_map/all_to_all | solution.py:74
  91.8 11.1 %all-to-all-start = ((bf16[32,36,2048]{2,1,0:T(8,128)(2,1)}), bf16[32,36,2048]{2,1,0:T(8,128)(2,1)}, u32[]{:S(2)}, u32[]{:S(2)}) async-start(bf16[32,36,2048]{2,1,0:T(8,128)(2,1)} %multiply_convert_fusion), calls=%async_computation | async-start | bytes 10485760 | tf_op jit(solution)/shard_map/all_to_all | solution.py:81
  102.9 5.2 %copy.87 = bf16[32,36,2048]{2,0,1:T(8,128)(2,1)S(1)} copy(bf16[32,36,2048]{2,1,0:T(8,128)(2,1)} %all-to-all-done.1) | data formatting | bytes 9437184 | tf_op jit(solution)/shard_map/all_to_all | solution.py:74
  108.1 10.2 %fusion.5 = f32[2,32,18,768]{3,1,2,0:T(8,128)} fusion(bf16[32,2,18,2048]{3,0,2,1:T(8,128)(2,1)S(1)} %bitcast.204, bf16[2048,2,768,1]{2,1,0,3:T(2,128)(2,1)} %bitcast.225), kind=kOutput, calls=%fused_computation.11 | convolution fusion | flops 3623878656 | bytes 14548992 | tf_op jit(solution)/shard_map/nemd,deh->nemh/dot_general | solution.py:92
  118.3 5.6 %fusion.9 = f32[2,32,18,768]{3,1,2,0:T(8,128)} fusion(bf16[32,2,18,2048]{3,0,2,1:T(8,128)(2,1)S(1)} %bitcast.205, bf16[2048,2,768,1]{2,1,0,3:T(2,128)(2,1)S(1)} %bitcast.232), kind=kOutput, calls=%fused_computation.15 | convolution fusion | flops 3623878656 | bytes 14548992 | tf_op jit(solution)/shard_map/nemd,deh->nemh/dot_general | solution.py:93
  123.9 48.7 %all-to-all-done = bf16[32,36,2048]{2,1,0:T(8,128)(2,1)} async-done(((bf16[32,36,2048]{2,1,0:T(8,128)(2,1)}), bf16[32,36,2048]{2,1,0:T(8,128)(2,1)}, u32[]{:S(2)}, u32[]{:S(2)}) %all-to-all-start) | async-done | bytes 4718624 | tf_op jit(solution)/shard_map/all_to_all | solution.py:81
  172.6 5.2 %copy.85 = bf16[32,36,2048]{2,0,1:T(8,128)(2,1)S(1)} copy(bf16[32,36,2048]{2,1,0:T(8,128)(2,1)} %all-to-all-done) | data formatting | bytes 9437184 | tf_op jit(solution)/shard_map/all_to_all | solution.py:81
  177.9 12.3 %fusion.28 = (bf16[32,2,18]{0,2,1:T(8,128)(2,1)S(1)}, bf16[32,2,18,768]{3,0,2,1:T(8,128)(2,1)}, bf16[32,2,18,768]{3,0,2,1:T(8,128)(2,1)S(1)}, bf16[32,2,18,768]{3,0,2,1:T(8,128)(2,1)S(1)}) fusion(f32[2,32,18,768]{3,1,2,0:T(8,128)} %fusion.9, f32[2,32,18,768]{3,1,2,0:T(8,128)} %fusion.5, bf16[32,2,18,2048]{3,0,2,1:T(8,128)(2,1)S(1)} %bitcast.216, ...), kind=kOutput, calls=%fused_computation.45 | convolution fusion | flops 3639802880 | bytes 23398656 | tf_op jit(solution)/shard_map/nemd,deh->nemh/dot_general | solution.py:97
  193.5 5.6 %collective-permute-done = bf16[2,2,768,512]{3,2,1,0:T(8,128)(2,1)S(1)} collective-permute-done((bf16[2,2,768,512]{3,2,1,0:T(8,128)(2,1)S(1)}, bf16[2,2,768,512]{3,2,1,0:T(8,128)(2,1)S(1)}, u32[]{:S(2)}, u32[]{:S(2)}) %collective-permute-start) | collective-permute-done | bytes 3145760 | tf_op jit(solution)/shard_map/ppermute | solution.py:128
  211.8 4.1 %collective-permute-start.2 = (bf16[2,768,512]{2,1,0:T(8,128)(2,1)S(1)}, bf16[2,768,512]{2,1,0:T(8,128)(2,1)}, u32[]{:S(2)}, u32[]{:S(2)}) collective-permute-start(bf16[2,768,512]{2,1,0:T(8,128)(2,1)S(1)} %slice_bitcast_fusion.4), channel_id=1, source_target_pairs={{0,64},{64,0},{1,65},{65,1},{2,66},{66,2},{3,67},{67,3},{4,68},{68... | collective-permute-start | bytes 4718600 | tf_op jit(solution)/shard_map/ppermute | solution.py:141
  225.9 6.3 %fusion.3 = f32[2,32,18,2048]{3,1,2,0:T(8,128)} fusion(bf16[32,2,18,768]{3,0,2,1:T(8,128)(2,1)S(1)} %copy-done.22, bf16[2048,2,768,1]{2,1,0,3:T(2,128)(2,1)S(1)} %bitcast.228), kind=kOutput, calls=%fused_computation.9 | convolution fusion | flops 3623878656 | bytes 17498112 | tf_op jit(solution)/shard_map/nemh,deh->nemd/dot_general | solution.py:146
  232.2 9.9 %fusion.12 = bf16[32,2,18,2048]{3,0,2,1:T(8,128)(2,1)S(1)} fusion(f32[2,32,18,2048]{3,1,2,0:T(8,128)} %fusion.3, bf16[32,2,18,768]{3,0,2,1:T(8,128)(2,1)} %copy-done.19, bf16[2048,2,768,1]{2,1,0,3:T(2,128)(2,1)} %bitcast.229), kind=kOutput, calls=%fused_computation.18 | convolution fusion | flops 3628597248 | bytes 22216704 | tf_op jit(solution)/shard_map/nemh,deh->nemd/dot_general | solution.py:147
  242.7 4.1 %copy.94 = bf16[32,36,2176]{2,1,0:T(8,128)(2,1)} copy(bf16[32,36,2176]{2,0,1:T(8,128)(2,1)S(1)} %bitcast.203) | data formatting | bytes 10027008 | tf_op jit(solution)/shard_map/reshape | solution.py:152
  246.8 9.1 %all-to-all-start.2 = ((bf16[32,36,2176]{2,1,0:T(8,128)(2,1)}), bf16[32,36,2176]{2,1,0:T(8,128)(2,1)}, u32[]{:S(2)}, u32[]{:S(2)}) async-start(bf16[32,36,2176]{2,1,0:T(8,128)(2,1)} %copy.94), calls=%async_computation.2 | async-start | bytes 11141120 | tf_op jit(solution)/shard_map/all_to_all | solution.py:151
  255.9 3.4 fusion.51
  275.9 26.8 %collective-permute-done.3 = bf16[2,768,512]{2,1,0:T(8,128)(2,1)S(1)} collective-permute-done((bf16[2,768,512]{2,1,0:T(8,128)(2,1)S(1)}, bf16[2,768,512]{2,1,0:T(8,128)(2,1)S(1)}, u32[]{:S(2)}, u32[]{:S(2)}) %collective-permute-start.3) | collective-permute-done | bytes 1572896 | tf_op jit(solution)/shard_map/ppermute | solution.py:141
  304.2 31.0 %collective-permute-done.5 = bf16[2,768,512]{2,1,0:T(8,128)(2,1)S(1)} collective-permute-done((bf16[2,768,512]{2,1,0:T(8,128)(2,1)S(1)}, bf16[2,768,512]{2,1,0:T(8,128)(2,1)S(1)}, u32[]{:S(2)}, u32[]{:S(2)}) %collective-permute-start.5) | collective-permute-done | bytes 1572896 | tf_op jit(solution)/shard_map/ppermute | solution.py:141
  336.9 12.4 %copy.96 = bf16[512,3,2,768]{3,2,1,0:T(2,128)(2,1)} copy(bf16[512,3,2,768]{0,3,2,1:T(8,128)(2,1)} %fusion.39) | data formatting | bytes 9437184
  349.3 7.5 %reshape.167 = bf16[1152,2176]{1,0:T(8,128)(2,1)} reshape(bf16[32,36,2176]{2,1,0:T(8,128)(2,1)} %all-to-all-done.2) | data formatting | bytes 10027008 | tf_op jit(solution)/shard_map/reshape | solution.py:160
  358.0 4.1 %fusion.32 = bf16[128,2048]{1,0:T(8,128)(2,1)} fusion(pred[1152,128]{1,0:T(8,128)(4,1)S(1)} %copy-done.12, bf16[1152,2176]{1,0:T(8,128)(2,1)} %reshape.167), kind=kOutput, calls=%fused_computation.68 | convolution fusion | flops 604241920 | bytes 5390336 | tf_op jit(solution)/shard_map/dot_general | solution.py:164
  (126 shorter events, 53.4 us)
Async XLA Ops:
  11.2 10.9 %copy-start.18 = (f32[128,8]{0,1:T(8,128)S(1)}, f32[128,8]{0,1:T(8,128)}, u32[]{:S(2)}) copy-start(f32[128,8]{0,1:T(8,128)} %param.9) | copy-start | bytes 12292
  11.2 13.1 %copy-start.13 = (bf16[128,2048]{1,0:T(8,128)(2,1)S(1)}, bf16[128,2048]{1,0:T(8,128)(2,1)}, u32[]{:S(2)}) copy-start(bf16[128,2048]{1,0:T(8,128)(2,1)} %param.8) | copy-start | bytes 1572868
  11.2 80.5 %all-to-all-start.1 = ((bf16[32,36,2048]{2,1,0:T(8,128)(2,1)}), bf16[32,36,2048]{2,1,0:T(8,128)(2,1)}, u32[]{:S(2)}, u32[]{:S(2)}) async-start(bf16[32,36,2048]{2,1,0:T(8,128)(2,1)} %convolution_convert_fusion), calls=%async_computation.1 | async-start | bytes 10485760 | tf_op jit(solution)/shard_map/all_to_all | solution.py:74
  22.2 69.6 %copy-start.9 = (f32[128,8]{1,0:T(8,128)}, f32[128,8]{1,0:T(8,128)S(1)}, u32[]{:S(2)}) copy-start(f32[128,8]{1,0:T(8,128)S(1)} %copy.84) | copy-start | bytes 12292
  91.8 80.8 %all-to-all-start = ((bf16[32,36,2048]{2,1,0:T(8,128)(2,1)}), bf16[32,36,2048]{2,1,0:T(8,128)(2,1)}, u32[]{:S(2)}, u32[]{:S(2)}) async-start(bf16[32,36,2048]{2,1,0:T(8,128)(2,1)} %multiply_convert_fusion), calls=%async_computation | async-start | bytes 10485760 | tf_op jit(solution)/shard_map/all_to_all | solution.py:81
  102.9 15.4 %slice-start.6 = ((s8[6291456]{0:T(1024)(128)(4,1)}), s8[4194304]{0:T(1024)(128)(4,1)S(1)}, s32[]{:S(2)}) async-start(s8[6291456]{0:T(1024)(128)(4,1)} %bitcast.230), calls=%async_computation.9 | async-start | bytes 8388608
  108.1 10.2 %copy-start.5 = (bf16[32,36,2048]{2,0,1:T(8,128)(2,1)}, bf16[32,36,2048]{2,0,1:T(8,128)(2,1)S(1)}, u32[]{:S(2)}) copy-start(bf16[32,36,2048]{2,0,1:T(8,128)(2,1)S(1)} %copy.87) | copy-start | bytes 14155780
  108.1 10.2 %slice-start.7 = ((s8[6291456]{0:T(1024)(128)(4,1)}), s8[2097152]{0:T(1024)(128)(4,1)S(1)}, s32[]{:S(2)}) async-start(s8[6291456]{0:T(1024)(128)(4,1)} %bitcast.230), calls=%async_computation.10 | async-start | bytes 4194304
  172.6 17.6 %slice-start = ((s8[4718592]{0:T(1024)(128)(4,1)}), s8[4194304]{0:T(1024)(128)(4,1)S(1)}, s32[]{:S(2)}) async-start(s8[4718592]{0:T(1024)(128)(4,1)} %bitcast.210), calls=%async_computation.3 | async-start | bytes 8388608
  177.8 12.3 %copy-start.6 = (bf16[32,36,2048]{2,0,1:T(8,128)(2,1)}, bf16[32,36,2048]{2,0,1:T(8,128)(2,1)S(1)}, u32[]{:S(2)}) copy-start(bf16[32,36,2048]{2,0,1:T(8,128)(2,1)S(1)} %copy.85) | copy-start | bytes 14155780
  177.8 12.4 %slice-start.1 = ((s8[4718592]{0:T(1024)(128)(4,1)}), s8[524288]{0:T(1024)(128)(4,1)S(1)}, s32[]{:S(2)}) async-start(s8[4718592]{0:T(1024)(128)(4,1)} %bitcast.210), calls=%async_computation.4 | async-start | bytes 1048576
  190.2 10.4 %copy-start.19 = (bf16[32,2,18,768]{3,0,2,1:T(8,128)(2,1)}, bf16[32,2,18,768]{3,0,2,1:T(8,128)(2,1)S(1)}, u32[]{:S(2)}) copy-start(bf16[32,2,18,768]{3,0,2,1:T(8,128)(2,1)S(1)} %get-tuple-element.16) | copy-start | bytes 5308420
  190.2 17.6 %copy-start.21 = (bf16[32,2,18,768]{3,0,2,1:T(8,128)(2,1)}, bf16[32,2,18,768]{3,0,2,1:T(8,128)(2,1)S(1)}, u32[]{:S(2)}) copy-start(bf16[32,2,18,768]{3,0,2,1:T(8,128)(2,1)S(1)} %get-tuple-element.15) | copy-start | bytes 5308420
  193.4 5.7 %collective-permute-start = (bf16[2,2,768,512]{3,2,1,0:T(8,128)(2,1)S(1)}, bf16[2,2,768,512]{3,2,1,0:T(8,128)(2,1)S(1)}, u32[]{:S(2)}, u32[]{:S(2)}) collective-permute-start(bf16[2,2,768,512]{3,2,1,0:T(8,128)(2,1)S(1)} %pad_maximum_fusion), channel_id=1, source_target_pairs={{0,32},{32,0},{1,33},{33,1},{2,34},{34,2},{3,35},{35,3},{4,36},{36... | collective-permute-start | bytes 9437192 | tf_op jit(solution)/shard_map/ppermute | solution.py:128
  204.3 11.6 %collective-permute-start.1 = (bf16[2,2,768,512]{3,2,1,0:T(8,128)(2,1)}, bf16[2,2,768,512]{3,2,1,0:T(8,128)(2,1)}, u32[]{:S(2)}, u32[]{:S(2)}) collective-permute-start(bf16[2,2,768,512]{3,2,1,0:T(8,128)(2,1)} %pad_maximum_fusion.1), channel_id=1, source_target_pairs={{0,32},{32,0},{1,33},{33,1},{2,34},{34,2},{3,35},{35,3},{4,36},{36... | collective-permute-start | bytes 9437192 | tf_op jit(solution)/shard_map/ppermute | solution.py:131
  204.9 11.0 %slice-start.2 = ((s8[4718592]{0:T(1024)(128)(4,1)}), s8[4194304]{0:T(1024)(128)(4,1)S(1)}, s32[]{:S(2)}) async-start(s8[4718592]{0:T(1024)(128)(4,1)} %bitcast.217), calls=%async_computation.5 | async-start | bytes 8388608
  207.8 8.1 %slice-start.3 = ((s8[4718592]{0:T(1024)(128)(4,1)}), s8[524288]{0:T(1024)(128)(4,1)S(1)}, s32[]{:S(2)}) async-start(s8[4718592]{0:T(1024)(128)(4,1)} %bitcast.217), calls=%async_computation.6 | async-start | bytes 1048576
  211.8 58.7 %collective-permute-start.2 = (bf16[2,768,512]{2,1,0:T(8,128)(2,1)S(1)}, bf16[2,768,512]{2,1,0:T(8,128)(2,1)}, u32[]{:S(2)}, u32[]{:S(2)}) collective-permute-start(bf16[2,768,512]{2,1,0:T(8,128)(2,1)S(1)} %slice_bitcast_fusion.4), channel_id=1, source_target_pairs={{0,64},{64,0},{1,65},{65,1},{2,66},{66,2},{3,67},{67,3},{4,68},{68... | collective-permute-start | bytes 4718600 | tf_op jit(solution)/shard_map/ppermute | solution.py:141
  218.8 7.1 %slice-start.4 = ((s8[6291456]{0:T(1024)(128)(4,1)}), s8[4194304]{0:T(1024)(128)(4,1)S(1)}, s32[]{:S(2)}) async-start(s8[6291456]{0:T(1024)(128)(4,1)} %bitcast.226), calls=%async_computation.7 | async-start | bytes 8388608
  225.6 39.9 %collective-permute-start.4 = (bf16[2,2,768,512]{3,2,1,0:T(8,128)(2,1)}, bf16[2,2,768,512]{3,2,1,0:T(8,128)(2,1)}, u32[]{:S(2)}, u32[]{:S(2)}) collective-permute-start(bf16[2,2,768,512]{3,2,1,0:T(8,128)(2,1)} %pad_maximum_fusion.2), channel_id=1, source_target_pairs={{0,32},{32,0},{1,33},{33,1},{2,34},{34,2},{3,35},{35,3},{4,36},{36... | collective-permute-start | bytes 9437192 | tf_op jit(solution)/shard_map/ppermute | solution.py:135
  246.8 102.5 %all-to-all-start.2 = ((bf16[32,36,2176]{2,1,0:T(8,128)(2,1)}), bf16[32,36,2176]{2,1,0:T(8,128)(2,1)}, u32[]{:S(2)}, u32[]{:S(2)}) async-start(bf16[32,36,2176]{2,1,0:T(8,128)(2,1)} %copy.94), calls=%async_computation.2 | async-start | bytes 11141120 | tf_op jit(solution)/shard_map/all_to_all | solution.py:151
  265.0 37.7 %collective-permute-start.3 = (bf16[2,768,512]{2,1,0:T(8,128)(2,1)S(1)}, bf16[2,768,512]{2,1,0:T(8,128)(2,1)S(1)}, u32[]{:S(2)}, u32[]{:S(2)}) collective-permute-start(bf16[2,768,512]{2,1,0:T(8,128)(2,1)S(1)} %slice_bitcast_fusion.2), channel_id=1, source_target_pairs={{0,64},{64,0},{1,65},{65,1},{2,66},{66,2},{3,67},{67,3},{4,68},{68... | collective-permute-start | bytes 4718600 | tf_op jit(solution)/shard_map/ppermute | solution.py:141
  269.7 65.5 %collective-permute-start.5 = (bf16[2,768,512]{2,1,0:T(8,128)(2,1)S(1)}, bf16[2,768,512]{2,1,0:T(8,128)(2,1)S(1)}, u32[]{:S(2)}, u32[]{:S(2)}) collective-permute-start(bf16[2,768,512]{2,1,0:T(8,128)(2,1)S(1)} %slice_bitcast_fusion), channel_id=1, source_target_pairs={{0,64},{64,0},{1,65},{65,1},{2,66},{66,2},{3,67},{67,3},{4,68},{68... | collective-permute-start | bytes 4718600 | tf_op jit(solution)/shard_map/ppermute | solution.py:141
  349.3 8.7 %copy-start.12 = (pred[1152,128]{1,0:T(8,128)(4,1)S(1)}, pred[1152,128]{1,0:T(8,128)(4,1)}, u32[]{:S(2)}) copy-start(pred[1152,128]{1,0:T(8,128)(4,1)} %copy-done.11) | copy-start | bytes 442372
  (17 other events, 62.3 us)

commit v14 on v13

--- a/solution.py
+++ b/solution.py
@@ -157,15 +157,17 @@
         concat_axis=0,
         tiled=True,
         axis_index_groups=groups,
-    ).reshape(slot_count, model_width + lane_pad)
-    back_rows = back[:, :model_width]
-    back_probs = back[:, model_width]
-
-    input_grad = lax.dot_general(
-        dispatch, back_rows, (((0,), (0,)), ((), ())), preferred_element_type=jnp.float32
+    )
+    input_grad = jnp.einsum(
+        "nst,nsd->td", picks, back[..., :model_width], preferred_element_type=jnp.float32
     ).astype(jnp.bfloat16)
     pair_probs = jnp.sum(
-        jnp.where(pair_hit, back_probs.astype(jnp.float32)[:, None], 0.0), axis=0
+        jnp.where(
+            pair_hit.reshape(owners, local_experts * capacity, pair_count),
+            back[..., model_width].astype(jnp.float32)[..., None],
+            0.0,
+        ),
+        axis=(0, 1),
     ).reshape(tok_rows, topk_count)
     router_grad = pair_probs - weights * jnp.sum(pair_probs, axis=1, keepdims=True)
 

time: 371 us -> 364 us (0.981)
  local copies, waits for them, and re-layouts: 43.7 us -> 36.8 us
    reshape x2 -> x1, local copies, waits for them, and re-layouts: 7.56 us -> 0.08 us  [per_device(): pair_probs = jnp.sum(jnp.where(pair_hit.reshape(owners, local_experts * c...]
  transfers between devices with their start and end apart: 9 -> 9, of which waited for: 5 -> 5; matrix products, arithmetic and copies ran while one was open for 26% -> 27% of each run, Pallas kernels for 0% -> 0%
where the time goes in v14:
time: 364 us; the launch traced here: 357 us
  waiting for transfers between devices  176 us (48%)
  matrix products  80.1 us (22%)
  starting transfers between devices  37 us (10%)
  local copies, waits for them, and re-layouts  36.8 us (10%)
  other arithmetic  25.9 us (7%)
    all_to_all x1, waiting for transfers between devices, per_device(): lax.all_to_all(send_tokens.reshape(send_shape), ('xlo', 'expert'), split_...  63.5 us
    ppermute x3, waiting for transfers between devices, per_device(): theirs = lax.ppermute(summed[0], 'xlo', xlo_pairs)  57.8 us
    all_to_all x1, waiting for transfers between devices, per_device(): lax.all_to_all(send_scaled.reshape(send_shape), ('xlo', 'expert'), split_...  48.7 us
    dot_general x12, matrix products, blocks_of(): jnp.einsum('nemh,nemd->ehd', left, lax.dynamic_slice_in_dim(right, at, bl...  23.3 us
    unnamed x69, local copies, waits for them, and re-layouts  18.2 us
    dot_general x1, matrix products, per_device(): jnp.einsum('nemd,deh->nemh', recv_scaled, w_down, preferred_element_type=...  12.3 us
    all_to_all x1, starting transfers between devices, per_device(): lax.all_to_all(send_scaled.reshape(send_shape), ('xlo', 'expert'), split_...  11.1 us
    all_to_all x1, starting transfers between devices, per_device(): lax.all_to_all(send_tokens.reshape(send_shape), ('xlo', 'expert'), split_...  10.9 us
  transfers between devices with their start and end apart: 9, of which 5 were waited for; matrix products, arithmetic and copies ran while one was open for 27% of the time, Pallas kernels for 0%

profile of v14, /device:TPU:0, one launch (start us, length us, event | category | flops | bytes accessed | tf_op | source)
XLA Modules:
  0.0 357.1 jit_solution(10934783123804808201)
XLA Ops:
  3.1 4.2 %fusion.15 = pred[1152,128]{1,0:T(8,128)(4,1)S(1)} fusion(s32[128,8]{0,1:T(8,128)S(1)} %fusion.81), kind=kLoop, calls=%fused_computation.25 | loop fusion | flops 2211840 | bytes 151552 | tf_op jit(solution)/shard_map/reduce_or | solution.py:61
  7.4 3.8 %convolution_convert_fusion = bf16[32,36,2048]{2,1,0:T(8,128)(2,1)} fusion(pred[32,36,128]{2,1,0:T(8,128)(4,1)S(1)} %reshape.175, bf16[128,2048]{1,0:T(8,128)(2,1)S(1)} %copy-done), kind=kOutput, calls=%fused_computation.28 | convolution fusion | flops 606339072 | bytes 5390336 | tf_op jit(solution)/shard_map/nst,td->nsd/dot_general | solution.py:67
  11.2 10.9 %all-to-all-start.1 = ((bf16[32,36,2048]{2,1,0:T(8,128)(2,1)}), bf16[32,36,2048]{2,1,0:T(8,128)(2,1)}, u32[]{:S(2)}, u32[]{:S(2)}) async-start(bf16[32,36,2048]{2,1,0:T(8,128)(2,1)} %convolution_convert_fusion), calls=%async_computation.1 | async-start | bytes 10485760 | tf_op jit(solution)/shard_map/all_to_all | solution.py:74
  24.4 3.9 %multiply_convert_fusion = bf16[32,36,2048]{2,1,0:T(8,128)(2,1)} fusion(f32[32,36]{1,0:T(8,128)S(1)} %mul.130, pred[32,36,128]{2,1,0:T(8,128)(4,1)S(1)} %reshape.175, bf16[128,2048]{1,0:T(8,128)(2,1)S(1)} %copy-done.13), kind=kOutput, calls=%fused_computation | convolution fusion | flops 608698368 | bytes 5394944 | tf_op jit(solution)/shard_map/nst,td->nsd/dot_general | solution.py:70
  28.3 63.5 %all-to-all-done.1 = bf16[32,36,2048]{2,1,0:T(8,128)(2,1)} async-done(((bf16[32,36,2048]{2,1,0:T(8,128)(2,1)}), bf16[32,36,2048]{2,1,0:T(8,128)(2,1)}, u32[]{:S(2)}, u32[]{:S(2)}) %all-to-all-start.1) | async-done | bytes 4718624 | tf_op jit(solution)/shard_map/all_to_all | solution.py:74
  91.8 11.1 %all-to-all-start = ((bf16[32,36,2048]{2,1,0:T(8,128)(2,1)}), bf16[32,36,2048]{2,1,0:T(8,128)(2,1)}, u32[]{:S(2)}, u32[]{:S(2)}) async-start(bf16[32,36,2048]{2,1,0:T(8,128)(2,1)} %multiply_convert_fusion), calls=%async_computation | async-start | bytes 10485760 | tf_op jit(solution)/shard_map/all_to_all | solution.py:81
  102.9 5.2 %copy.89 = bf16[32,36,2048]{2,0,1:T(8,128)(2,1)S(1)} copy(bf16[32,36,2048]{2,1,0:T(8,128)(2,1)} %all-to-all-done.1) | data formatting | bytes 9437184 | tf_op jit(solution)/shard_map/all_to_all | solution.py:74
  108.1 10.2 %fusion.5 = f32[2,32,18,768]{3,1,2,0:T(8,128)} fusion(bf16[32,2,18,2048]{3,0,2,1:T(8,128)(2,1)S(1)} %bitcast.209, bf16[2048,2,768,1]{2,1,0,3:T(2,128)(2,1)} %bitcast.231), kind=kOutput, calls=%fused_computation.11 | convolution fusion | flops 3623878656 | bytes 14548992 | tf_op jit(solution)/shard_map/nemd,deh->nemh/dot_general | solution.py:92
  118.3 5.6 %fusion.9 = f32[2,32,18,768]{3,1,2,0:T(8,128)} fusion(bf16[32,2,18,2048]{3,0,2,1:T(8,128)(2,1)S(1)} %bitcast.210, bf16[2048,2,768,1]{2,1,0,3:T(2,128)(2,1)S(1)} %bitcast.238), kind=kOutput, calls=%fused_computation.15 | convolution fusion | flops 3623878656 | bytes 14548992 | tf_op jit(solution)/shard_map/nemd,deh->nemh/dot_general | solution.py:93
  123.9 48.7 %all-to-all-done = bf16[32,36,2048]{2,1,0:T(8,128)(2,1)} async-done(((bf16[32,36,2048]{2,1,0:T(8,128)(2,1)}), bf16[32,36,2048]{2,1,0:T(8,128)(2,1)}, u32[]{:S(2)}, u32[]{:S(2)}) %all-to-all-start) | async-done | bytes 4718624 | tf_op jit(solution)/shard_map/all_to_all | solution.py:81
  172.6 5.2 %copy.87 = bf16[32,36,2048]{2,0,1:T(8,128)(2,1)S(1)} copy(bf16[32,36,2048]{2,1,0:T(8,128)(2,1)} %all-to-all-done) | data formatting | bytes 9437184 | tf_op jit(solution)/shard_map/all_to_all | solution.py:81
  177.8 12.3 %fusion.28 = (bf16[32,2,18]{0,2,1:T(8,128)(2,1)S(1)}, bf16[32,2,18,768]{3,0,2,1:T(8,128)(2,1)}, bf16[32,2,18,768]{3,0,2,1:T(8,128)(2,1)S(1)}, bf16[32,2,18,768]{3,0,2,1:T(8,128)(2,1)S(1)}) fusion(f32[2,32,18,768]{3,1,2,0:T(8,128)} %fusion.9, f32[2,32,18,768]{3,1,2,0:T(8,128)} %fusion.5, bf16[32,2,18,2048]{3,0,2,1:T(8,128)(2,1)S(1)} %bitcast.221, ...), kind=kOutput, calls=%fused_computation.45 | convolution fusion | flops 3639802880 | bytes 23398656 | tf_op jit(solution)/shard_map/nemd,deh->nemh/dot_general | solution.py:97
  193.5 5.6 %collective-permute-done = bf16[2,2,768,512]{3,2,1,0:T(8,128)(2,1)S(1)} collective-permute-done((bf16[2,2,768,512]{3,2,1,0:T(8,128)(2,1)S(1)}, bf16[2,2,768,512]{3,2,1,0:T(8,128)(2,1)S(1)}, u32[]{:S(2)}, u32[]{:S(2)}) %collective-permute-start) | collective-permute-done | bytes 3145760 | tf_op jit(solution)/shard_map/ppermute | solution.py:128
  207.8 2.9 fusion.51
  211.8 4.1 %collective-permute-start.2 = (bf16[2,768,512]{2,1,0:T(8,128)(2,1)S(1)}, bf16[2,768,512]{2,1,0:T(8,128)(2,1)}, u32[]{:S(2)}, u32[]{:S(2)}) collective-permute-start(bf16[2,768,512]{2,1,0:T(8,128)(2,1)S(1)} %slice_bitcast_fusion.4), channel_id=1, source_target_pairs={{0,64},{64,0},{1,65},{65,1},{2,66},{66,2},{3,67},{67,3},{4,68},{68... | collective-permute-start | bytes 4718600 | tf_op jit(solution)/shard_map/ppermute | solution.py:141
  225.9 6.3 %fusion.3 = f32[2,32,18,2048]{3,1,2,0:T(8,128)} fusion(bf16[32,2,18,768]{3,0,2,1:T(8,128)(2,1)S(1)} %copy-done.22, bf16[2048,2,768,1]{2,1,0,3:T(2,128)(2,1)S(1)} %bitcast.234), kind=kOutput, calls=%fused_computation.9 | convolution fusion | flops 3623878656 | bytes 17498112 | tf_op jit(solution)/shard_map/nemh,deh->nemd/dot_general | solution.py:146
  232.2 9.9 %fusion.14 = bf16[32,2,18,2048]{3,0,2,1:T(8,128)(2,1)S(1)} fusion(f32[2,32,18,2048]{3,1,2,0:T(8,128)} %fusion.3, bf16[32,2,18,768]{3,0,2,1:T(8,128)(2,1)} %copy-done.19, bf16[2048,2,768,1]{2,1,0,3:T(2,128)(2,1)} %bitcast.235), kind=kOutput, calls=%fused_computation.20 | convolution fusion | flops 3628597248 | bytes 22216704 | tf_op jit(solution)/shard_map/nemh,deh->nemd/dot_general | solution.py:147
  242.7 4.1 %copy.96 = bf16[32,36,2176]{2,1,0:T(8,128)(2,1)} copy(bf16[32,36,2176]{2,0,1:T(8,128)(2,1)S(1)} %bitcast.208) | data formatting | bytes 10027008 | tf_op jit(solution)/shard_map/reshape | solution.py:152
  246.8 9.1 %all-to-all-start.2 = ((bf16[32,36,2176]{2,1,0:T(8,128)(2,1)}), bf16[32,36,2176]{2,1,0:T(8,128)(2,1)}, u32[]{:S(2)}, u32[]{:S(2)}) async-start(bf16[32,36,2176]{2,1,0:T(8,128)(2,1)} %copy.96), calls=%async_computation.2 | async-start | bytes 11141120 | tf_op jit(solution)/shard_map/all_to_all | solution.py:151
  255.9 3.4 fusion.54
  275.9 26.8 %collective-permute-done.3 = bf16[2,768,512]{2,1,0:T(8,128)(2,1)S(1)} collective-permute-done((bf16[2,768,512]{2,1,0:T(8,128)(2,1)S(1)}, bf16[2,768,512]{2,1,0:T(8,128)(2,1)S(1)}, u32[]{:S(2)}, u32[]{:S(2)}) %collective-permute-start.3) | collective-permute-done | bytes 1572896 | tf_op jit(solution)/shard_map/ppermute | solution.py:141
  304.3 31.0 %collective-permute-done.5 = bf16[2,768,512]{2,1,0:T(8,128)(2,1)S(1)} collective-permute-done((bf16[2,768,512]{2,1,0:T(8,128)(2,1)S(1)}, bf16[2,768,512]{2,1,0:T(8,128)(2,1)S(1)}, u32[]{:S(2)}, u32[]{:S(2)}) %collective-permute-start.5) | collective-permute-done | bytes 1572896 | tf_op jit(solution)/shard_map/ppermute | solution.py:141
  336.9 12.5 %copy.99 = bf16[512,3,2,768]{3,2,1,0:T(2,128)(2,1)} copy(bf16[512,3,2,768]{0,3,2,1:T(8,128)(2,1)} %fusion.42) | data formatting | bytes 9437184
  352.4 4.2 %fusion.35 = bf16[128,2048]{1,0:T(8,128)(2,1)} fusion(pred[32,36,128]{2,1,0:T(8,128)(4,1)S(1)} %copy-done.10, bf16[32,36,2176]{2,1,0:T(8,128)(2,1)} %all-to-all-done.2), kind=kOutput, calls=%fused_computation.69 | convolution fusion | flops 604241920 | bytes 5914624 | tf_op jit(solution)/shard_map/nst,nsd->td/dot_general | solution.py:161
  (127 shorter events, 50.8 us)
Async XLA Ops:
  7.4 17.0 %copy-start.9 = (pred[32,36,128]{2,1,0:T(8,128)(4,1)}, pred[32,36,128]{2,1,0:T(8,128)(4,1)S(1)}, u32[]{:S(2)}) copy-start(pred[32,36,128]{2,1,0:T(8,128)(4,1)S(1)} %reshape.175) | copy-start | bytes 442372
  11.2 10.9 %copy-start.18 = (f32[128,8]{0,1:T(8,128)S(1)}, f32[128,8]{0,1:T(8,128)}, u32[]{:S(2)}) copy-start(f32[128,8]{0,1:T(8,128)} %param.9) | copy-start | bytes 12292
  11.2 13.2 %copy-start.13 = (bf16[128,2048]{1,0:T(8,128)(2,1)S(1)}, bf16[128,2048]{1,0:T(8,128)(2,1)}, u32[]{:S(2)}) copy-start(bf16[128,2048]{1,0:T(8,128)(2,1)} %param.8) | copy-start | bytes 1572868
  11.2 80.5 %all-to-all-start.1 = ((bf16[32,36,2048]{2,1,0:T(8,128)(2,1)}), bf16[32,36,2048]{2,1,0:T(8,128)(2,1)}, u32[]{:S(2)}, u32[]{:S(2)}) async-start(bf16[32,36,2048]{2,1,0:T(8,128)(2,1)} %convolution_convert_fusion), calls=%async_computation.1 | async-start | bytes 10485760 | tf_op jit(solution)/shard_map/all_to_all | solution.py:74
  22.2 69.6 %copy-start.11 = (f32[128,8]{1,0:T(8,128)}, f32[128,8]{1,0:T(8,128)S(1)}, u32[]{:S(2)}) copy-start(f32[128,8]{1,0:T(8,128)S(1)} %copy.86) | copy-start | bytes 12292
  91.8 80.8 %all-to-all-start = ((bf16[32,36,2048]{2,1,0:T(8,128)(2,1)}), bf16[32,36,2048]{2,1,0:T(8,128)(2,1)}, u32[]{:S(2)}, u32[]{:S(2)}) async-start(bf16[32,36,2048]{2,1,0:T(8,128)(2,1)} %multiply_convert_fusion), calls=%async_computation | async-start | bytes 10485760 | tf_op jit(solution)/shard_map/all_to_all | solution.py:81
  102.9 15.4 %slice-start.6 = ((s8[6291456]{0:T(1024)(128)(4,1)}), s8[4194304]{0:T(1024)(128)(4,1)S(1)}, s32[]{:S(2)}) async-start(s8[6291456]{0:T(1024)(128)(4,1)} %bitcast.236), calls=%async_computation.9 | async-start | bytes 8388608
  172.6 17.6 %slice-start = ((s8[4718592]{0:T(1024)(128)(4,1)}), s8[4194304]{0:T(1024)(128)(4,1)S(1)}, s32[]{:S(2)}) async-start(s8[4718592]{0:T(1024)(128)(4,1)} %bitcast.215), calls=%async_computation.3 | async-start | bytes 8388608
  177.8 12.4 %copy-start.6 = (bf16[32,36,2048]{2,0,1:T(8,128)(2,1)}, bf16[32,36,2048]{2,0,1:T(8,128)(2,1)S(1)}, u32[]{:S(2)}) copy-start(bf16[32,36,2048]{2,0,1:T(8,128)(2,1)S(1)} %copy.87) | copy-start | bytes 14155780
  177.8 12.4 %slice-start.1 = ((s8[4718592]{0:T(1024)(128)(4,1)}), s8[524288]{0:T(1024)(128)(4,1)S(1)}, s32[]{:S(2)}) async-start(s8[4718592]{0:T(1024)(128)(4,1)} %bitcast.215), calls=%async_computation.4 | async-start | bytes 1048576
  190.2 10.4 %copy-start.19 = (bf16[32,2,18,768]{3,0,2,1:T(8,128)(2,1)}, bf16[32,2,18,768]{3,0,2,1:T(8,128)(2,1)S(1)}, u32[]{:S(2)}) copy-start(bf16[32,2,18,768]{3,0,2,1:T(8,128)(2,1)S(1)} %get-tuple-element.16) | copy-start | bytes 5308420
  190.2 17.6 %copy-start.21 = (bf16[32,2,18,768]{3,0,2,1:T(8,128)(2,1)}, bf16[32,2,18,768]{3,0,2,1:T(8,128)(2,1)S(1)}, u32[]{:S(2)}) copy-start(bf16[32,2,18,768]{3,0,2,1:T(8,128)(2,1)S(1)} %get-tuple-element.15) | copy-start | bytes 5308420
  193.4 5.7 %collective-permute-start = (bf16[2,2,768,512]{3,2,1,0:T(8,128)(2,1)S(1)}, bf16[2,2,768,512]{3,2,1,0:T(8,128)(2,1)S(1)}, u32[]{:S(2)}, u32[]{:S(2)}) collective-permute-start(bf16[2,2,768,512]{3,2,1,0:T(8,128)(2,1)S(1)} %pad_maximum_fusion), channel_id=1, source_target_pairs={{0,32},{32,0},{1,33},{33,1},{2,34},{34,2},{3,35},{35,3},{4,36},{36... | collective-permute-start | bytes 9437192 | tf_op jit(solution)/shard_map/ppermute | solution.py:128
  204.3 11.6 %collective-permute-start.1 = (bf16[2,2,768,512]{3,2,1,0:T(8,128)(2,1)}, bf16[2,2,768,512]{3,2,1,0:T(8,128)(2,1)}, u32[]{:S(2)}, u32[]{:S(2)}) collective-permute-start(bf16[2,2,768,512]{3,2,1,0:T(8,128)(2,1)} %pad_maximum_fusion.1), channel_id=1, source_target_pairs={{0,32},{32,0},{1,33},{33,1},{2,34},{34,2},{3,35},{35,3},{4,36},{36... | collective-permute-start | bytes 9437192 | tf_op jit(solution)/shard_map/ppermute | solution.py:131
  204.9 11.0 %slice-start.2 = ((s8[4718592]{0:T(1024)(128)(4,1)}), s8[4194304]{0:T(1024)(128)(4,1)S(1)}, s32[]{:S(2)}) async-start(s8[4718592]{0:T(1024)(128)(4,1)} %bitcast.222), calls=%async_computation.5 | async-start | bytes 8388608
  211.8 58.7 %collective-permute-start.2 = (bf16[2,768,512]{2,1,0:T(8,128)(2,1)S(1)}, bf16[2,768,512]{2,1,0:T(8,128)(2,1)}, u32[]{:S(2)}, u32[]{:S(2)}) collective-permute-start(bf16[2,768,512]{2,1,0:T(8,128)(2,1)S(1)} %slice_bitcast_fusion.4), channel_id=1, source_target_pairs={{0,64},{64,0},{1,65},{65,1},{2,66},{66,2},{3,67},{67,3},{4,68},{68... | collective-permute-start | bytes 4718600 | tf_op jit(solution)/shard_map/ppermute | solution.py:141
  225.6 39.8 %collective-permute-start.4 = (bf16[2,2,768,512]{3,2,1,0:T(8,128)(2,1)}, bf16[2,2,768,512]{3,2,1,0:T(8,128)(2,1)}, u32[]{:S(2)}, u32[]{:S(2)}) collective-permute-start(bf16[2,2,768,512]{3,2,1,0:T(8,128)(2,1)} %pad_maximum_fusion.2), channel_id=1, source_target_pairs={{0,32},{32,0},{1,33},{33,1},{2,34},{34,2},{3,35},{35,3},{4,36},{36... | collective-permute-start | bytes 9437192 | tf_op jit(solution)/shard_map/ppermute | solution.py:135
  246.8 102.6 %all-to-all-start.2 = ((bf16[32,36,2176]{2,1,0:T(8,128)(2,1)}), bf16[32,36,2176]{2,1,0:T(8,128)(2,1)}, u32[]{:S(2)}, u32[]{:S(2)}) async-start(bf16[32,36,2176]{2,1,0:T(8,128)(2,1)} %copy.96), calls=%async_computation.2 | async-start | bytes 11141120 | tf_op jit(solution)/shard_map/all_to_all | solution.py:151
  265.0 37.7 %collective-permute-start.3 = (bf16[2,768,512]{2,1,0:T(8,128)(2,1)S(1)}, bf16[2,768,512]{2,1,0:T(8,128)(2,1)S(1)}, u32[]{:S(2)}, u32[]{:S(2)}) collective-permute-start(bf16[2,768,512]{2,1,0:T(8,128)(2,1)S(1)} %slice_bitcast_fusion.2), channel_id=1, source_target_pairs={{0,64},{64,0},{1,65},{65,1},{2,66},{66,2},{3,67},{67,3},{4,68},{68... | collective-permute-start | bytes 4718600 | tf_op jit(solution)/shard_map/ppermute | solution.py:141
  269.8 65.5 %collective-permute-start.5 = (bf16[2,768,512]{2,1,0:T(8,128)(2,1)S(1)}, bf16[2,768,512]{2,1,0:T(8,128)(2,1)S(1)}, u32[]{:S(2)}, u32[]{:S(2)}) collective-permute-start(bf16[2,768,512]{2,1,0:T(8,128)(2,1)S(1)} %slice_bitcast_fusion), channel_id=1, source_target_pairs={{0,64},{64,0},{1,65},{65,1},{2,66},{66,2},{3,67},{67,3},{4,68},{68... | collective-permute-start | bytes 4718600 | tf_op jit(solution)/shard_map/ppermute | solution.py:141
  336.9 13.9 %copy-start.15 = (s32[1024]{0:T(1024)S(1)}, s32[1024]{0:T(1024)}, u32[]{:S(2)}) copy-start(s32[1024]{0:T(1024)} %copy-done.14) | copy-start | bytes 12292
  336.9 14.7 %copy-start.12 = (f32[128,8]{1,0:T(8,128)S(1)}, f32[128,8]{1,0:T(8,128)}, u32[]{:S(2)}) copy-start(f32[128,8]{1,0:T(8,128)} %copy-done.11) | copy-start | bytes 12292
  336.9 14.7 %copy-start.17 = (f32[128]{0:T(128)S(1)}, f32[128]{0:T(128)}, u32[]{:S(2)}) copy-start(f32[128]{0:T(128)} %copy-done.16) | copy-start | bytes 1540
  336.9 15.5 %copy-start.10 = (pred[32,36,128]{2,1,0:T(8,128)(4,1)S(1)}, pred[32,36,128]{2,1,0:T(8,128)(4,1)}, u32[]{:S(2)}) copy-start(pred[32,36,128]{2,1,0:T(8,128)(4,1)} %copy-done.9) | copy-start | bytes 442372
  (17 other events, 78.1 us)

commit v15 on v14

--- a/solution.py
+++ b/solution.py
@@ -1,6 +1,7 @@
 import jax
 import jax.numpy as jnp
 from jax import lax
+from jax.experimental.layout import Layout, with_layout_constraint
 from jax.sharding import Mesh
 from jax.sharding import PartitionSpec as P
 
@@ -140,7 +141,10 @@
         summed = (own.astype(jnp.float32) + from_sibling.astype(jnp.float32)).astype(jnp.bfloat16)
         theirs = lax.ppermute(summed[0], "xlo", xlo_pairs)
         share = (summed[1].astype(jnp.float32) + theirs.astype(jnp.float32)).astype(jnp.bfloat16)
-        shares = lax.dynamic_update_index_in_dim(shares, jnp.transpose(share, (2, 0, 1)), kind, 1)
+        shares = with_layout_constraint(
+            lax.dynamic_update_index_in_dim(shares, jnp.transpose(share, (2, 0, 1)), kind, 1),
+            Layout((0, 1, 2, 3)),
+        )
 
     row_grad = (
         jnp.einsum("nemh,deh->nemd", gate_grad, w_gate, preferred_element_type=jnp.float32)

time: 364 us -> 486 us (1.34)
  local copies, waits for them, and re-layouts: 36.8 us -> 87.8 us
  other arithmetic: 25.9 us -> 66.6 us
  matrix products: 80.1 us -> 102 us
  waiting for transfers between devices: 176 us -> 184 us
    unnamed x69 -> x76, local copies, waits for them, and re-layouts: 18.2 us -> 58.7 us
    another operation x4 -> x3, other arithmetic: 6.09 us -> 27.7 us  [blocks_of(): return (jnp.stack(blocks[:2]), jnp.stack(blocks[2:]))]
    dot_general x12, matrix products: 23.3 us -> 43.1 us  [blocks_of(): jnp.einsum('nemh,nemd->ehd', left, lax.dynamic_slice_in_dim(right, at, bl...]
    ppermute x3, waiting for transfers between devices: 57.8 us -> 72.2 us  [per_device(): theirs = lax.ppermute(summed[0], 'xlo', xlo_pairs)]
    convert_element_type x3, other arithmetic: 6.64 us -> 19.5 us  [per_device(): (own.astype(jnp.float32) + from_sibling.astype(jnp.float32)).astype(jnp.b...]
    squeeze x3, local copies, waits for them, and re-layouts: 0.31 us -> 8.27 us  [per_device(): theirs = lax.ppermute(summed[0], 'xlo', xlo_pairs)]
    ppermute x1, waiting for transfers between devices: 5.65 us -> 0.01 us  [per_device(): lax.ppermute(gate_sib, 'core', core_pairs)]
    dynamic_update_slice x2, other arithmetic: 3.18 us -> 8.34 us  [per_device(): lax.dynamic_update_index_in_dim(shares, jnp.transpose(share, (2, 0, 1)),...]
  transfers between devices with their start and end apart: 9 -> 9, of which waited for: 5 -> 5; matrix products, arithmetic and copies ran while one was open for 27% -> 26% of each run, Pallas kernels for 0% -> 0%
where the time goes in v15:
time: 486 us; the launch traced here: 478 us
  waiting for transfers between devices  184 us (38%)
  matrix products  102 us (21%)
  local copies, waits for them, and re-layouts  87.8 us (18%)
  other arithmetic  66.6 us (14%)
  starting transfers between devices  35.4 us (7%)
    ppermute x3, waiting for transfers between devices, per_device(): theirs = lax.ppermute(summed[0], 'xlo', xlo_pairs)  72.2 us
    all_to_all x1, waiting for transfers between devices, per_device(): lax.all_to_all(send_tokens.reshape(send_shape), ('xlo', 'expert'), split_...  63.6 us
    unnamed x76, local copies, waits for them, and re-layouts  58.7 us
    all_to_all x1, waiting for transfers between devices, per_device(): lax.all_to_all(send_scaled.reshape(send_shape), ('xlo', 'expert'), split_...  48.4 us
    dot_general x12, matrix products, blocks_of(): jnp.einsum('nemh,nemd->ehd', left, lax.dynamic_slice_in_dim(right, at, bl...  43.1 us
    another operation x3, other arithmetic, blocks_of(): return (jnp.stack(blocks[:2]), jnp.stack(blocks[2:]))  27.7 us
    convert_element_type x3, other arithmetic, per_device(): (own.astype(jnp.float32) + from_sibling.astype(jnp.float32)).astype(jnp.b...  19.5 us
    dot_general x1, matrix products, per_device(): jnp.einsum('nemd,deh->nemh', recv_scaled, w_down, preferred_element_type=...  11.7 us
  transfers between devices with their start and end apart: 9, of which 5 were waited for; matrix products, arithmetic and copies ran while one was open for 26% of the time, Pallas kernels for 0%

profile of v15, /device:TPU:0, one launch (start us, length us, event | category | flops | bytes accessed | tf_op | source)
XLA Modules:
  0.0 477.7 jit_solution(10369160751718018035)
XLA Ops:
  11.2 10.9 %all-to-all-start.1 = ((bf16[32,36,2048]{2,1,0:T(8,128)(2,1)}), bf16[32,36,2048]{2,1,0:T(8,128)(2,1)}, u32[]{:S(2)}, u32[]{:S(2)}) async-start(bf16[32,36,2048]{2,1,0:T(8,128)(2,1)} %convolution_convert_fusion), calls=%async_computation.1 | async-start | bytes 10485760 | tf_op jit(solution)/shard_map/all_to_all | solution.py:75
  28.2 63.6 %all-to-all-done.1 = bf16[32,36,2048]{2,1,0:T(8,128)(2,1)} async-done(((bf16[32,36,2048]{2,1,0:T(8,128)(2,1)}), bf16[32,36,2048]{2,1,0:T(8,128)(2,1)}, u32[]{:S(2)}, u32[]{:S(2)}) %all-to-all-start.1) | async-done | bytes 4718624 | tf_op jit(solution)/shard_map/all_to_all | solution.py:75
  91.8 10.6 %all-to-all-start = ((bf16[32,36,2048]{2,1,0:T(8,128)(2,1)}), bf16[32,36,2048]{2,1,0:T(8,128)(2,1)}, u32[]{:S(2)}, u32[]{:S(2)}) async-start(bf16[32,36,2048]{2,1,0:T(8,128)(2,1)} %multiply_convert_fusion), calls=%async_computation | async-start | bytes 10485760 | tf_op jit(solution)/shard_map/all_to_all | solution.py:82
  102.5 5.2 %copy.133 = bf16[32,36,2048]{2,0,1:T(8,128)(2,1)S(1)} copy(bf16[32,36,2048]{2,1,0:T(8,128)(2,1)} %all-to-all-done.1) | data formatting | bytes 9437184 | tf_op jit(solution)/shard_map/all_to_all | solution.py:75
  107.7 10.2 %fusion.5 = f32[2,32,18,768]{3,1,2,0:T(8,128)} fusion(bf16[32,2,18,2048]{3,0,2,1:T(8,128)(2,1)S(1)} %bitcast.204, bf16[2048,2,768,1]{2,1,0,3:T(2,128)(2,1)} %bitcast.217), kind=kOutput, calls=%fused_computation.11 | convolution fusion | flops 3623878656 | bytes 14548992 | tf_op jit(solution)/shard_map/nemd,deh->nemh/dot_general | solution.py:93
  117.9 5.6 %fusion.9 = f32[2,32,18,768]{3,1,2,0:T(8,128)} fusion(bf16[32,2,18,2048]{3,0,2,1:T(8,128)(2,1)S(1)} %bitcast.205, bf16[2048,2,768,1]{2,1,0,3:T(2,128)(2,1)S(1)} %bitcast.222), kind=kOutput, calls=%fused_computation.15 | convolution fusion | flops 3623878656 | bytes 14548992 | tf_op jit(solution)/shard_map/nemd,deh->nemh/dot_general | solution.py:94
  123.5 48.4 %all-to-all-done = bf16[32,36,2048]{2,1,0:T(8,128)(2,1)} async-done(((bf16[32,36,2048]{2,1,0:T(8,128)(2,1)}), bf16[32,36,2048]{2,1,0:T(8,128)(2,1)}, u32[]{:S(2)}, u32[]{:S(2)}) %all-to-all-start) | async-done | bytes 4718624 | tf_op jit(solution)/shard_map/all_to_all | solution.py:82
  171.9 5.2 %copy.131 = bf16[32,36,2048]{2,0,1:T(8,128)(2,1)S(1)} copy(bf16[32,36,2048]{2,1,0:T(8,128)(2,1)} %all-to-all-done) | data formatting | bytes 9437184 | tf_op jit(solution)/shard_map/all_to_all | solution.py:82
  177.2 11.7 %fusion.28 = (bf16[32,2,18]{0,2,1:T(8,128)(2,1)S(1)}, bf16[32,2,18,768]{3,0,2,1:T(8,128)(2,1)}, bf16[32,2,18,768]{3,0,2,1:T(8,128)(2,1)S(1)}, bf16[32,2,18,768]{3,0,2,1:T(8,128)(2,1)}) fusion(f32[2,32,18,768]{3,1,2,0:T(8,128)S(1)} %copy-done.24, f32[2,32,18,768]{3,1,2,0:T(8,128)S(1)} %copy-done.23, bf16[32,2,18,2048]{3,0,2,1:T(8,128)(2,1)S(1)} %bitcast.197, ...), kind=kOutput, calls=%fused_computation.45 | convolution fusion | flops 3639802880 | bytes 23398656 | tf_op jit(solution)/shard_map/nemd,deh->nemh/dot_general | solution.py:98
  207.3 7.9 %pad_maximum_fusion = bf16[2,2,768,512]{2,1,3,0:T(2,128)(2,1)} fusion(bf16[1,2,768,512]{2,1,3,0:T(2,128)(2,1)S(1)} %bitcast.193, bf16[1,2,768,512]{2,1,3,0:T(2,128)(2,1)} %bitcast.195), kind=kLoop, calls=%fused_computation.46 | loop fusion | flops 1572864 | bytes 6291456 | tf_op jit(solution)/shard_map/stack | solution.py:123
  234.6 5.0 %copy.186 = bf16[2,768,512]{1,0,2:T(2,128)(2,1)} copy(bf16[2,768,512]{2,1,0:T(8,128)(2,1)} %fusion.46) | data formatting | bytes 3145728
  239.6 8.0 %pad_maximum_fusion.1 = bf16[2,2,768,512]{2,1,3,0:T(2,128)(2,1)} fusion(bf16[1,2,768,512]{2,1,3,0:T(2,128)(2,1)} %bitcast.196, bf16[1,2,768,512]{2,1,3,0:T(2,128)(2,1)S(1)} %bitcast.194), kind=kLoop, calls=%fused_computation.47 | loop fusion | flops 1572864 | bytes 6291456 | tf_op jit(solution)/shard_map/stack | solution.py:123
  271.7 8.3 %add_convert_fusion.3 = bf16[2,2,768,512]{2,1,3,0:T(2,128)(2,1)} fusion(bf16[2,2,768,512]{2,1,3,0:T(2,128)(2,1)} %collective-permute-done, bf16[1,2,768,512]{2,1,3,0:T(2,128)(2,1)} %bitcast.187, bf16[1,2,768,512]{2,1,3,0:T(2,128)(2,1)} %bitcast.188), kind=kLoop, calls=%fused_computation.8 | loop fusion | flops 7864320 | bytes 9437184 | tf_op jit(solution)/shard_map/convert_element_type | solution.py:141
  291.7 5.0 %copy.190 = bf16[2,768,512]{1,0,2:T(2,128)(2,1)} copy(bf16[2,768,512]{2,1,0:T(8,128)(2,1)} %fusion.50) | data formatting | bytes 3145728
  301.7 5.0 %copy.187 = bf16[2,768,512]{1,0,2:T(2,128)(2,1)} copy(bf16[2,768,512]{2,1,0:T(8,128)(2,1)} %fusion.47) | data formatting | bytes 3145728
  311.7 11.8 %pad_maximum_fusion.2 = (bf16[2,2,768,512]{2,1,3,0:T(2,128)(2,1)}, bf16[2,2,768,512]{2,1,3,0:T(2,128)(2,1)}) fusion(bf16[1,2,768,512]{2,1,3,0:T(2,128)(2,1)} %bitcast.192, bf16[1,2,768,512]{2,1,3,0:T(2,128)(2,1)} %bitcast.191, bf16[1,2,768,512]{2,1,3,0:T(2,128)(2,1)} %bitcast.189, bf16[1,2,768,512]{2,1,3,0:T(2,128)(2,1)} %bitcast.190), kind=kLoop, calls=%fused_computation.48 | loop fusion | flops 3145728 | bytes 12582912 | tf_op jit(solution)/shard_map/stack | solution.py:123
  323.5 9.4 %fusion.3 = f32[2,32,18,2048]{3,1,2,0:T(8,128)} fusion(bf16[32,2,18,768]{3,0,2,1:T(8,128)(2,1)S(1)} %copy-done.22, bf16[2048,2,768,1]{2,1,0,3:T(2,128)(2,1)} %bitcast.218), kind=kOutput, calls=%fused_computation.9 | convolution fusion | flops 3623878656 | bytes 17498112 | tf_op jit(solution)/shard_map/nemh,deh->nemd/dot_general | solution.py:150
  332.9 9.9 %fusion.14 = bf16[32,2,18,2048]{3,0,2,1:T(8,128)(2,1)S(1)} fusion(f32[2,32,18,2048]{3,1,2,0:T(8,128)} %fusion.3, bf16[32,2,18,768]{3,0,2,1:T(8,128)(2,1)} %get-tuple-element.16, bf16[2048,2,768,1]{2,1,0,3:T(2,128)(2,1)} %bitcast.219), kind=kOutput, calls=%fused_computation.20 | convolution fusion | flops 3628597248 | bytes 22216704 | tf_op jit(solution)/shard_map/nemh,deh->nemd/dot_general | solution.py:151
  347.5 10.6 %all-to-all-start.2 = ((bf16[32,36,2176]{2,1,0:T(8,128)(2,1)}), bf16[32,36,2176]{2,1,0:T(8,128)(2,1)}, u32[]{:S(2)}, u32[]{:S(2)}) async-start(bf16[32,36,2176]{2,1,0:T(8,128)(2,1)} %copy.148), calls=%async_computation.2 | async-start | bytes 11141120 | tf_op jit(solution)/shard_map/all_to_all | solution.py:155
  362.2 6.1 %add_convert_fusion.2 = bf16[2,2,768,512]{2,1,3,0:T(2,128)(2,1)S(1)} fusion(bf16[2,2,768,512]{2,1,3,0:T(2,128)(2,1)} %collective-permute-done.1, bf16[1,2,768,512]{2,1,3,0:T(2,128)(2,1)S(1)} %bitcast.185, bf16[1,2,768,512]{2,1,3,0:T(2,128)(2,1)S(1)} %bitcast.186), kind=kLoop, calls=%fused_computation.7 | loop fusion | flops 7864320 | bytes 9437184 | tf_op jit(solution)/shard_map/convert_element_type | solution.py:141
  372.4 5.1 %add_convert_fusion.1 = bf16[2,2,768,512]{2,1,3,0:T(2,128)(2,1)S(1)} fusion(bf16[2,2,768,512]{2,1,3,0:T(2,128)(2,1)} %collective-permute-done.4, bf16[2,2,768,512]{2,1,3,0:T(2,128)(2,1)S(1)} %copy-done.3), kind=kLoop, calls=%fused_computation.6 | loop fusion | flops 6291456 | bytes 9437184 | tf_op jit(solution)/shard_map/convert_element_type | solution.py:141
  381.8 17.7 %collective-permute-done.2 = bf16[2,768,512]{1,0,2:T(2,128)(2,1)} collective-permute-done((bf16[2,768,512]{1,0,2:T(2,128)(2,1)}, bf16[2,768,512]{1,0,2:T(2,128)(2,1)}, u32[]{:S(2)}, u32[]{:S(2)}) %collective-permute-start.2) | collective-permute-done | bytes 1572896 | tf_op jit(solution)/shard_map/ppermute | solution.py:142
  407.5 25.7 %collective-permute-done.3 = bf16[2,768,512]{1,0,2:T(2,128)(2,1)} collective-permute-done((bf16[2,768,512]{1,0,2:T(2,128)(2,1)}, bf16[2,768,512]{1,0,2:T(2,128)(2,1)}, u32[]{:S(2)}, u32[]{:S(2)}) %collective-permute-start.3) | collective-permute-done | bytes 1572896 | tf_op jit(solution)/shard_map/ppermute | solution.py:142
  437.4 28.8 %collective-permute-done.5 = bf16[2,768,512]{1,0,2:T(2,128)(2,1)} collective-permute-done((bf16[2,768,512]{1,0,2:T(2,128)(2,1)}, bf16[2,768,512]{1,0,2:T(2,128)(2,1)}, u32[]{:S(2)}, u32[]{:S(2)}) %collective-permute-start.5) | collective-permute-done | bytes 1572896 | tf_op jit(solution)/shard_map/ppermute | solution.py:142
  (131 shorter events, 140.7 us)
Async XLA Ops:
  7.4 17.0 %copy-start.9 = (pred[32,36,128]{2,1,0:T(8,128)(4,1)}, pred[32,36,128]{2,1,0:T(8,128)(4,1)S(1)}, u32[]{:S(2)}) copy-start(pred[32,36,128]{2,1,0:T(8,128)(4,1)S(1)} %reshape.175) | copy-start | bytes 442372
  11.2 10.9 %copy-start.18 = (f32[128,8]{0,1:T(8,128)S(1)}, f32[128,8]{0,1:T(8,128)}, u32[]{:S(2)}) copy-start(f32[128,8]{0,1:T(8,128)} %param.9) | copy-start | bytes 12292
  11.2 13.1 %copy-start.13 = (bf16[128,2048]{1,0:T(8,128)(2,1)S(1)}, bf16[128,2048]{1,0:T(8,128)(2,1)}, u32[]{:S(2)}) copy-start(bf16[128,2048]{1,0:T(8,128)(2,1)} %param.8) | copy-start | bytes 1572868
  11.2 80.6 %all-to-all-start.1 = ((bf16[32,36,2048]{2,1,0:T(8,128)(2,1)}), bf16[32,36,2048]{2,1,0:T(8,128)(2,1)}, u32[]{:S(2)}, u32[]{:S(2)}) async-start(bf16[32,36,2048]{2,1,0:T(8,128)(2,1)} %convolution_convert_fusion), calls=%async_computation.1 | async-start | bytes 10485760 | tf_op jit(solution)/shard_map/all_to_all | solution.py:75
  22.2 69.6 %copy-start.11 = (f32[128,8]{1,0:T(8,128)}, f32[128,8]{1,0:T(8,128)S(1)}, u32[]{:S(2)}) copy-start(f32[128,8]{1,0:T(8,128)S(1)} %copy.130) | copy-start | bytes 12292
  91.8 80.1 %all-to-all-start = ((bf16[32,36,2048]{2,1,0:T(8,128)(2,1)}), bf16[32,36,2048]{2,1,0:T(8,128)(2,1)}, u32[]{:S(2)}, u32[]{:S(2)}) async-start(bf16[32,36,2048]{2,1,0:T(8,128)(2,1)} %multiply_convert_fusion), calls=%async_computation | async-start | bytes 10485760 | tf_op jit(solution)/shard_map/all_to_all | solution.py:82
  102.5 15.4 %slice-start.2 = ((s8[6291456]{0:T(1024)(128)(4,1)}), s8[4194304]{0:T(1024)(128)(4,1)S(1)}, s32[]{:S(2)}) async-start(s8[6291456]{0:T(1024)(128)(4,1)} %bitcast.220), calls=%async_computation.5 | async-start | bytes 8388608
  107.7 10.2 %copy-start.8 = (bf16[32,36,2048]{2,0,1:T(8,128)(2,1)}, bf16[32,36,2048]{2,0,1:T(8,128)(2,1)S(1)}, u32[]{:S(2)}) copy-start(bf16[32,36,2048]{2,0,1:T(8,128)(2,1)S(1)} %copy.133) | copy-start | bytes 14155780
  177.2 11.7 %copy-start.7 = (bf16[32,36,2048]{2,0,1:T(8,128)(2,1)}, bf16[32,36,2048]{2,0,1:T(8,128)(2,1)S(1)}, u32[]{:S(2)}) copy-start(bf16[32,36,2048]{2,0,1:T(8,128)(2,1)S(1)} %copy.131) | copy-start | bytes 14155780
  215.2 7.0 %collective-permute-start = (bf16[2,2,768,512]{2,1,3,0:T(2,128)(2,1)}, bf16[2,2,768,512]{2,1,3,0:T(2,128)(2,1)}, u32[]{:S(2)}, u32[]{:S(2)}) collective-permute-start(bf16[2,2,768,512]{2,1,3,0:T(2,128)(2,1)} %pad_maximum_fusion), channel_id=1, source_target_pairs={{0,32},{32,0},{1,33},{33,1},{2,34},{34,2},{3,35},{35,3},{4,36},{36... | collective-permute-start | bytes 9437192 | tf_op jit(solution)/shard_map/ppermute | solution.py:129
  247.6 32.3 %collective-permute-start.1 = (bf16[2,2,768,512]{2,1,3,0:T(2,128)(2,1)}, bf16[2,2,768,512]{2,1,3,0:T(2,128)(2,1)}, u32[]{:S(2)}, u32[]{:S(2)}) collective-permute-start(bf16[2,2,768,512]{2,1,3,0:T(2,128)(2,1)} %pad_maximum_fusion.1), channel_id=1, source_target_pairs={{0,32},{32,0},{1,33},{33,1},{2,34},{34,2},{3,35},{35,3},{4,36},{36... | collective-permute-start | bytes 9437192 | tf_op jit(solution)/shard_map/ppermute | solution.py:132
  271.6 12.2 %slice-start = ((s8[4718592]{0:T(1024)(128)(4,1)}), s8[4194304]{0:T(1024)(128)(4,1)S(1)}, s32[]{:S(2)}) async-start(s8[4718592]{0:T(1024)(128)(4,1)} %bitcast.199), calls=%async_computation.3 | async-start | bytes 8388608
  311.6 11.8 %copy-start.22 = (bf16[32,2,18,768]{3,0,2,1:T(8,128)(2,1)S(1)}, bf16[32,2,18,768]{3,0,2,1:T(8,128)(2,1)}, u32[]{:S(2)}) copy-start(bf16[32,2,18,768]{3,0,2,1:T(8,128)(2,1)} %copy-done.20) | copy-start | bytes 5308420
  323.4 49.0 %collective-permute-start.4 = (bf16[2,2,768,512]{2,1,3,0:T(2,128)(2,1)}, bf16[2,2,768,512]{2,1,3,0:T(2,128)(2,1)}, u32[]{:S(2)}, u32[]{:S(2)}) collective-permute-start(bf16[2,2,768,512]{2,1,3,0:T(2,128)(2,1)} %get-tuple-element.20), channel_id=1, source_target_pairs={{0,32},{32,0},{1,33},{33,1},{2,34},{34,2},{3,35},{35,3},{4,36},{36... | collective-permute-start | bytes 9437192 | tf_op jit(solution)/shard_map/ppermute | solution.py:136
  347.5 122.8 %all-to-all-start.2 = ((bf16[32,36,2176]{2,1,0:T(8,128)(2,1)}), bf16[32,36,2176]{2,1,0:T(8,128)(2,1)}, u32[]{:S(2)}, u32[]{:S(2)}) async-start(bf16[32,36,2176]{2,1,0:T(8,128)(2,1)} %copy.148), calls=%async_computation.2 | async-start | bytes 11141120 | tf_op jit(solution)/shard_map/all_to_all | solution.py:155
  361.9 37.5 %collective-permute-start.2 = (bf16[2,768,512]{1,0,2:T(2,128)(2,1)}, bf16[2,768,512]{1,0,2:T(2,128)(2,1)}, u32[]{:S(2)}, u32[]{:S(2)}) collective-permute-start(bf16[2,768,512]{1,0,2:T(2,128)(2,1)} %slice_bitcast_fusion.4), channel_id=1, source_target_pairs={{0,64},{64,0},{1,65},{65,1},{2,66},{66,2},{3,67},{67,3},{4,68},{68... | collective-permute-start | bytes 4718600 | tf_op jit(solution)/shard_map/ppermute | solution.py:142
  370.5 62.7 %collective-permute-start.3 = (bf16[2,768,512]{1,0,2:T(2,128)(2,1)}, bf16[2,768,512]{1,0,2:T(2,128)(2,1)}, u32[]{:S(2)}, u32[]{:S(2)}) collective-permute-start(bf16[2,768,512]{1,0,2:T(2,128)(2,1)} %slice_bitcast_fusion.2), channel_id=1, source_target_pairs={{0,64},{64,0},{1,65},{65,1},{2,66},{66,2},{3,67},{67,3},{4,68},{68... | collective-permute-start | bytes 4718600 | tf_op jit(solution)/shard_map/ppermute | solution.py:142
  379.3 20.2 %copy-start.2 = (bf16[2,2,768,512]{2,1,3,0:T(2,128)(2,1)S(1)}, bf16[2,2,768,512]{2,1,3,0:T(2,128)(2,1)}, u32[]{:S(2)}) copy-start(bf16[2,2,768,512]{2,1,3,0:T(2,128)(2,1)} %add_convert_fusion.3) | copy-start | bytes 9437188
  381.5 84.6 %collective-permute-start.5 = (bf16[2,768,512]{1,0,2:T(2,128)(2,1)}, bf16[2,768,512]{1,0,2:T(2,128)(2,1)}, u32[]{:S(2)}, u32[]{:S(2)}) collective-permute-start(bf16[2,768,512]{1,0,2:T(2,128)(2,1)} %slice_bitcast_fusion), channel_id=1, source_target_pairs={{0,64},{64,0},{1,65},{65,1},{2,66},{66,2},{3,67},{67,3},{4,68},{68... | collective-permute-start | bytes 4718600 | tf_op jit(solution)/shard_map/ppermute | solution.py:142
  407.5 58.6 %copy-start.5 = (bf16[2,2,768,512]{2,1,3,0:T(2,128)(2,1)S(1)}, bf16[2,2,768,512]{2,1,3,0:T(2,128)(2,1)}, u32[]{:S(2)}) copy-start(bf16[2,2,768,512]{2,1,3,0:T(2,128)(2,1)} %copy-done.4) | copy-start | bytes 9437188
  437.3 34.3 %copy-start.15 = (s32[1024]{0:T(1024)S(1)}, s32[1024]{0:T(1024)}, u32[]{:S(2)}) copy-start(s32[1024]{0:T(1024)} %copy-done.14) | copy-start | bytes 12292
  437.3 35.2 %copy-start.12 = (f32[128,8]{1,0:T(8,128)S(1)}, f32[128,8]{1,0:T(8,128)}, u32[]{:S(2)}) copy-start(f32[128,8]{1,0:T(8,128)} %copy-done.11) | copy-start | bytes 12292
  437.3 35.2 %copy-start.17 = (f32[128]{0:T(128)S(1)}, f32[128]{0:T(128)}, u32[]{:S(2)}) copy-start(f32[128]{0:T(128)} %copy-done.16) | copy-start | bytes 1540
  437.3 36.0 %copy-start.10 = (pred[32,36,128]{2,1,0:T(8,128)(4,1)S(1)}, pred[32,36,128]{2,1,0:T(8,128)(4,1)}, u32[]{:S(2)}) copy-start(pred[32,36,128]{2,1,0:T(8,128)(4,1)} %copy-done.9) | copy-start | bytes 442372
  (15 other events, 69.9 us)
